TPU v7x, 128 devices: a whole 4x4x4 slice. The times are simulated.
128 devices in a mesh: freq: 32 (over z, x_hi, y), dish: 4 (over x_lo, core).
Axes of the slice: x: 4 (x_hi: 2, x_lo: 2; x = x_hi * 2 + x_lo), y: 4, z: 4, core: 2. Of those that a mesh axis runs over, the one named last changes fastest.
Arguments:
- voltages: bfloat16 [256, 4, 2, 155648], P('freq', 'dish'), may hold values from -6 to 6
- feed_gains: bfloat16 [256, 4, 2, 8192], P('freq', 'dish'), may hold values from -4.1875 to 4.1875
- block_assign: int32 [32], replicated, may hold values from 0 to 31, each once
- grid_rows: int32 [4, 256], replicated, may hold values from 0 to 255, each once within a row
Outputs:
- beam_power: float32 [8192, 1024], P('freq', 'dish')
Inputs may be any that keep to these rules, and one draw needn't show every extreme that they name: block_assign names every channel block once. Each row of grid_rows names every grid row once.
All inputs are finite; a program needn't handle non-finite values.
Results may differ from a plain program's by a relative error of at most 0.0042.
Values may be sent and summed in bfloat16 or wider, within the bound.
No kernel may reach another device: no remote copies, remote signals or barrier semaphores. Data moves between devices by JAX's collectives and lax.ppermute only.
A program may use at most 128 MiB of HBM per device.

v0:
```python
import math

import jax
import jax.numpy as jnp
from jax import lax
from jax.experimental import pallas as pl
from jax.experimental.pallas import tpu as pltpu
from jax.sharding import PartitionSpec as P

NCHAN = 8192
CHA = 64
CHB = 128
TAPS = 4
FRAMES = 16


full_turn = 2.0 * math.pi


def fourier_table(row_index, col_index, modulus, scaling):
    phases = row_index[:, None] * col_index[None, :] % modulus
    angles = full_turn / modulus * phases.astype(jnp.float32)
    cosine_table = (jnp.cos(angles) * scaling).astype(jnp.bfloat16)
    sine_table = (jnp.sin(angles) * scaling).astype(jnp.bfloat16)
    upper_rows = jnp.stack([cosine_table, -sine_table], axis=1)
    lower_rows = jnp.stack([sine_table, cosine_table], axis=1)
    return jnp.stack([upper_rows, lower_rows], axis=0)


def filter_window():
    sample_index = jnp.arange(TAPS * NCHAN, dtype=jnp.float32)
    centred = (sample_index - TAPS * NCHAN / 2 + 0.5) / NCHAN
    taper_curve = 0.5 - 0.5 * jnp.cos(full_turn * (sample_index + 0.5) / (TAPS * NCHAN))
    shaped_window = (jnp.sinc(centred) * taper_curve).reshape(TAPS, NCHAN)
    energy = jnp.mean(jnp.sum(shaped_window * shaped_window, axis=0))
    return shaped_window / jnp.sqrt(energy)


def beam_tables(grid_line, grid_len, rows_per_device):
    positions = jnp.arange(grid_len, dtype=jnp.int32)
    phases = positions[:, None] * grid_line[None, :] % grid_len
    angles = full_turn / grid_len * phases.astype(jnp.float32)
    scaling = 1.0 / math.sqrt(grid_len)
    cosine_table = (jnp.cos(angles) * scaling).astype(jnp.bfloat16)
    sine_table = (jnp.sin(angles) * scaling).astype(jnp.bfloat16)
    real_rows = jnp.stack([cosine_table, sine_table], axis=2)
    imag_rows = jnp.stack([-sine_table, cosine_table], axis=2)
    table = jnp.stack([real_rows, imag_rows], axis=0)
    devices = grid_len // rows_per_device
    table = table.reshape(2, grid_len, devices, rows_per_device, 2)
    table = jnp.transpose(table, (0, 1, 3, 4, 2))
    return table.reshape(2 * grid_len, 2 * grid_len)


def channelize_kernel(v_ref, w_ref, t1_ref, tw_ref, t2_ref, g_ref, o_ref):
    cos_tw = tw_ref[0]
    sin_tw = tw_ref[1]
    t1 = t1_ref[...]
    t2_real = t2_ref[0]
    t2_imag = t2_ref[1]
    g_real = g_ref[0, 0]
    g_imag = g_ref[0, 1]
    half = t2_real.shape[0] // 2

    def one_frame(frame):
        acc = None
        for tap in range(TAPS):
            start = pl.multiple_of((frame + tap) * CHA, CHA)
            piece = v_ref[0, :, pl.ds(start, CHA), :].astype(jnp.float32)
            term = w_ref[tap][None] * piece
            acc = term if acc is None else acc + term
        block = acc.astype(jnp.bfloat16).reshape(2 * CHA, CHB)
        section = jnp.dot(t1, block, preferred_element_type=jnp.float32)
        sec_real = section[:CHA]
        sec_imag = section[CHA:]
        turned_real = sec_real * cos_tw - sec_imag * sin_tw
        turned_imag = sec_real * sin_tw + sec_imag * cos_tw
        return turned_real.astype(jnp.bfloat16), turned_imag.astype(jnp.bfloat16)

    def pair(step, carry):
        first_real, first_imag = one_frame(2 * step)
        second_real, second_imag = one_frame(2 * step + 1)
        both_real = jnp.concatenate([first_real, second_real], axis=0)
        both_imag = jnp.concatenate([first_imag, second_imag], axis=0)
        dims = (((1,), (1,)), ((), ()))
        spectrum = lax.dot_general(
            t2_real, both_real, dims, preferred_element_type=jnp.float32
        ) + lax.dot_general(t2_imag, both_imag, dims, preferred_element_type=jnp.float32)
        spec_real = spectrum[:half]
        spec_imag = spectrum[half:]
        out_real = spec_real * g_real - spec_imag * g_imag
        out_imag = spec_real * g_imag + spec_imag * g_real
        lanes = pl.ds(pl.multiple_of(step * 2 * CHA, 2 * CHA), 2 * CHA)
        o_ref[0, 0, :, lanes] = out_real.astype(o_ref.dtype)
        o_ref[0, 1, :, lanes] = out_imag.astype(o_ref.dtype)
        return carry

    lax.fori_loop(0, FRAMES // 2, pair, 0)


def beam_kernel(dish_count, x_ref, t_ref, c_ref, s_ref, o_ref, acc_ref):
    step = pl.program_id(0)
    rows = x_ref.shape[0] * x_ref.shape[1]
    devices = x_ref.shape[2] // dish_count
    grid_len = t_ref.shape[1] // 2

    @pl.when(step == 0)
    def _():
        acc_ref[...] = jnp.zeros_like(acc_ref)

    parts = []
    for d in range(dish_count):
        block = x_ref[:, :, pl.ds(d * devices, devices), :].reshape(rows * devices, x_ref.shape[3])
        sums = jnp.dot(t_ref[d], block, preferred_element_type=jnp.float32)
        sum_real = sums[:grid_len]
        sum_imag = sums[grid_len:]
        cos_d = c_ref[d]
        sin_d = s_ref[d]
        part_real = sum_real * cos_d - sum_imag * sin_d
        part_imag = sum_real * sin_d + sum_imag * cos_d
        parts.append(
            (
                part_real.astype(jnp.bfloat16).astype(jnp.float32),
                part_imag.astype(jnp.bfloat16).astype(jnp.float32),
            )
        )
    (a_re, a_im), (b_re, b_im), (c_re, c_im), (d_re, d_im) = parts
    beams = [
        (a_re + b_re + c_re + d_re, a_im + b_im + c_im + d_im),
        (a_re + b_im - c_re - d_im, a_im - b_re - c_im + d_re),
        (a_re - b_re + c_re - d_re, a_im - b_im + c_im - d_im),
        (a_re - b_im - c_re + d_im, a_im + b_re - c_im - d_re),
    ]
    for q in range(dish_count):
        beam_real, beam_imag = beams[q]
        acc_ref[q] += beam_real * beam_real + beam_imag * beam_imag

    @pl.when(step == pl.num_programs(0) - 1)
    def _():
        reversal = [
            int(format(s, "0%db" % (dish_count.bit_length() - 1))[::-1], 2)
            for s in range(dish_count)
        ]
        width = o_ref.shape[1]
        for s in range(dish_count):
            total = acc_ref[reversal[s]]
            total = total + pltpu.roll(total, width, 1)
            flipped = jnp.transpose(total, (1, 0))
            o_ref[s] = flipped[:width] * (0.25 / FRAMES)


def body(voltages, feed_gains, block_assign, grid_rows):
    dish_rows = voltages.shape[0]
    block_count = lax.axis_size("freq")
    dish_count = lax.axis_size("dish")
    block_width = NCHAN // block_count
    quarter = block_width // dish_count
    dests = block_count * dish_count
    grid_len = dish_rows * block_count
    total_dishes = grid_len * dish_count
    samples = voltages.shape[-1]

    dest = jnp.arange(dests, dtype=jnp.int32)
    dest_quarter = dest // block_count
    dest_block = jnp.take(block_assign, dest % block_count)
    dest_e = dest_block * dish_count + dest_quarter

    volts = voltages[:, 0].reshape(dish_rows, 2, samples // CHB, CHB)
    window = filter_window().reshape(TAPS, CHA, CHB)
    first_index = jnp.arange(CHA, dtype=jnp.int32)
    second_index = jnp.arange(CHB, dtype=jnp.int32)
    first_table = fourier_table(first_index, first_index, CHA, 1.0 / math.sqrt(CHA))
    first_table = jnp.transpose(first_table, (2, 3, 0, 1)).reshape(2 * CHA, 2 * CHA)
    angles = -(full_turn / NCHAN) * (first_index[:, None] * second_index[None, :] % NCHAN).astype(
        jnp.float32
    )
    twiddle = jnp.stack([jnp.cos(angles), jnp.sin(angles)], axis=0)
    second_table = fourier_table(second_index, second_index, CHB, 1.0 / math.sqrt(CHB))
    second_table = jnp.transpose(second_table, (0, 2, 3, 1))
    second_table = jnp.take(second_table, dest_e, axis=2).reshape(2, 2 * dests, CHB)
    gains = feed_gains[:, 0].reshape(dish_rows, 2, CHB, CHA).astype(jnp.float32)
    gains = jnp.take(gains, dest_e, axis=2)
    gains = jnp.concatenate([gains, gains], axis=3)

    channelized = pl.pallas_call(
        channelize_kernel,
        grid=(dish_rows,),
        in_specs=[
            pl.BlockSpec((1, 2, samples // CHB, CHB), lambda r: (r, 0, 0, 0)),
            pl.BlockSpec((TAPS, CHA, CHB), lambda r: (0, 0, 0)),
            pl.BlockSpec((2 * CHA, 2 * CHA), lambda r: (0, 0)),
            pl.BlockSpec((2, CHA, CHB), lambda r: (0, 0, 0)),
            pl.BlockSpec((2, 2 * dests, CHB), lambda r: (0, 0, 0)),
            pl.BlockSpec((1, 2, dests, 2 * CHA), lambda r: (r, 0, 0, 0)),
        ],
        out_specs=pl.BlockSpec((1, 2, dests, FRAMES * quarter), lambda r: (r, 0, 0, 0)),
        out_shape=jax.ShapeDtypeStruct((dish_rows, 2, dests, FRAMES * quarter), jnp.bfloat16),
    )(volts, window, first_table, twiddle, second_table, gains)

    gathered = lax.all_to_all(channelized, ("dish", "freq"), 2, 2, tiled=True)

    tables = jax.vmap(lambda line: beam_tables(line, grid_len, dish_rows))(grid_rows)
    feed_index = jnp.arange(dish_count, dtype=jnp.int32)
    positions = jnp.arange(grid_len, dtype=jnp.int32)
    twist_angles = -(full_turn / total_dishes) * (
        feed_index[:, None] * positions[None, :] % total_dishes
    ).astype(jnp.float32)
    twist_cos = jnp.cos(twist_angles)[:, :, None]
    twist_sin = jnp.sin(twist_angles)[:, :, None]
    lane_block = 2 * quarter
    steps = FRAMES * quarter // lane_block

    powers = pl.pallas_call(
        lambda *refs: beam_kernel(dish_count, *refs),
        grid=(steps,),
        in_specs=[
            pl.BlockSpec((dish_rows, 2, dests, lane_block), lambda f: (0, 0, 0, f)),
            pl.BlockSpec((dish_count, 2 * grid_len, 2 * grid_len), lambda f: (0, 0, 0)),
            pl.BlockSpec((dish_count, grid_len, 1), lambda f: (0, 0, 0)),
            pl.BlockSpec((dish_count, grid_len, 1), lambda f: (0, 0, 0)),
        ],
        out_specs=pl.BlockSpec((dish_count, quarter, grid_len), lambda f: (0, 0, 0)),
        out_shape=jax.ShapeDtypeStruct((dish_count, quarter, grid_len), jnp.float32),
        scratch_shapes=[pltpu.VMEM((dish_count, grid_len, lane_block), jnp.float32)],
    )(gathered, tables, twist_cos, twist_sin)

    received = lax.all_to_all(powers, "dish", 0, 0, tiled=True)
    return received.reshape(block_width, grid_len)


def solution(mesh):
    placed = (P("freq", "dish", None, None), P("freq", "dish", None, None), P(), P())
    return jax.shard_map(
        body, mesh=mesh, in_specs=placed, out_specs=P("freq", "dish"), check_vma=False
    )
```

profile of v0, /device:TPU:1, one launch (start us, length us, event | category | flops | bytes accessed | tf_op | source)
XLA Modules:
  0.0 147.7 jit_solution(9751153614340155290)
XLA Ops:
  0.7 1.2 gather_fusion
  2.4 1.2 fusion.30
  3.8 0.9 gather_fusion.1
  4.9 0.7 reshape.501.t1_ref
  6.6 0.7 gather_fusion.2
  7.7 1.3 pad_maximum_fusion.g_ref
  9.0 8.4 %reshape_squeeze.4.v_ref = bf16[8,2,1216,128]{3,2,1,0:T(8,128)(2,1)} reshape(bf16[8,1,2,155648]{3,2,1,0:T(2,128)(2,1)} %param.4) | data formatting | bytes 9961472 | tf_op jit(solution)/shard_map/reshape;squeeze | solution.py:168
  18.1 1.3 fusion.36.w_ref
  19.4 0.8 bitcast_select_fusion.t2_ref
  20.1 0.6 pad_maximum_fusion.1.tw_ref
  20.8 26.8 %shard_map.46 = bf16[8,2,128,1024]{3,2,1,0:T(8,128)(2,1)} custom-call(bf16[8,2,1216,128]{3,2,1,0:T(8,128)(2,1)} %reshape_squeeze.4.v_ref, f32[4,64,128]{2,1,0:T(8,128)} %fusion.36.w_ref, bf16[128,128]{1,0:T(8,128)(2,1)} %reshape.501.t1_ref, f32[2,64,128]{2,1,0:T(8,128)} %pad_maximum_fusion.1.tw_ref, bf16[2,256,128]{2,1,0:T(8,128)(2,1)} %bitcast_select_fusion.t2_ref, ...), custom_call_target="tpu_custom_call" | custom-call | tf_op jit(solution)/shard_map/pallas_call | solution.py:185
  47.5 8.5 %copy.30 = bf16[8,2,128,1024]{3,1,0,2:T(2,128)(2,1)} copy(bf16[8,2,128,1024]{3,2,1,0:T(8,128)(2,1)} %shard_map.46) | data formatting | bytes 8388608 | tf_op jit(solution)/shard_map/pallas_call | solution.py:185
  56.0 12.0 %all-to-all-start = ((bf16[8,2,128,1024]{3,1,0,2:T(2,128)(2,1)}), bf16[8,2,128,1024]{3,1,0,2:T(2,128)(2,1)}, u32[]{:S(2)}, u32[]{:S(2)}) async-start(bf16[8,2,128,1024]{3,1,0,2:T(2,128)(2,1)} %copy.30), calls=%async_computation | async-start | bytes 8388608 | tf_op jit(solution)/shard_map/all_to_all | solution.py:200
  68.0 4.3 %fusion.7 = bf16[4,256,256,1]{1,2,3,0:T(8,128)(2,1)S(1)} fusion(s32[4,256]{1,0:T(4,128)S(1)} %copy-done.2), kind=kLoop, calls=%fused_computation.34 | loop fusion | flops 4980736 | bytes 528384 | tf_op jit(solution)/shard_map/vmap()/neg | solution.py:47
  72.4 5.0 %multiply_convert_fusion = (bf16[4,256,256,1]{1,2,3,0:T(8,128)(2,1)S(1)}, bf16[4,256,256,1]{1,2,3,0:T(8,128)(2,1)S(1)}) fusion(s32[4,256]{1,0:T(4,128)S(1)} %copy-done.2), kind=kLoop, calls=%fused_computation.15 | loop fusion | flops 4718592 | bytes 1052672 | tf_op jit(solution)/shard_map/vmap()/convert_element_type | solution.py:45
  77.8 2.2 %copy.32 = bf16[4,2,256,8,2,32]{2,1,5,4,3,0:T(2,128)(2,1)S(1)} copy(bf16[4,2,256,8,2,32]{2,3,5,4,1,0:T(8,128)(2,1)S(1)} %maximum_bitcast_fusion) | data formatting | bytes 4194304 | tf_op jit(solution)/shard_map/vmap()/transpose | solution.py:51
  80.0 2.6 %reshape.503 = bf16[4,512,512]{1,2,0:T(8,128)(2,1)} reshape(bf16[4,2,256,8,2,32]{2,1,5,4,3,0:T(2,128)(2,1)S(1)} %copy.32) | data formatting | bytes 4194304 | tf_op jit(solution)/shard_map/vmap()/reshape | solution.py:52
  82.6 4.2 %copy.35.refs_1_ = bf16[4,512,512]{2,1,0:T(8,128)(2,1)} copy(bf16[4,512,512]{1,2,0:T(8,128)(2,1)} %reshape.503) | data formatting | bytes 4194304 | tf_op jit(solution)/shard_map/vmap()/reshape | solution.py:52
  87.0 2.7 %multiply_sine_fusion = (f32[4,256,1]{2,1,0:T(8,128)}, f32[4,256,1]{2,1,0:T(8,128)}) fusion(f32[4,256,1]{2,1,0:T(8,128)S(1)} %copy.33), kind=kLoop, calls=%fused_computation.20 | loop fusion | flops 1024 | bytes 12288 | tf_op jit(solution)/shard_map/sin | solution.py:209
  89.7 30.3 %all-to-all-done = bf16[8,2,128,1024]{3,1,0,2:T(2,128)(2,1)} async-done(((bf16[8,2,128,1024]{3,1,0,2:T(2,128)(2,1)}), bf16[8,2,128,1024]{3,1,0,2:T(2,128)(2,1)}, u32[]{:S(2)}, u32[]{:S(2)}) %all-to-all-start) | async-done | bytes 4194336 | tf_op jit(solution)/shard_map/all_to_all | solution.py:200
  120.0 6.5 %copy.34.refs_0_ = bf16[8,2,128,1024]{3,2,1,0:T(8,128)(2,1)} copy(bf16[8,2,128,1024]{3,1,0,2:T(2,128)(2,1)} %all-to-all-done) | data formatting | bytes 8388608 | tf_op jit(solution)/shard_map/all_to_all | solution.py:200
  126.5 10.9 %shard_map.47 = f32[4,64,256]{2,1,0:T(8,128)} custom-call(bf16[8,2,128,1024]{3,2,1,0:T(8,128)(2,1)} %copy.34.refs_0_, bf16[4,512,512]{2,1,0:T(8,128)(2,1)} %copy.35.refs_1_, f32[4,256,1]{2,1,0:T(8,128)} %get-tuple-element.6.refs_2_, f32[4,256,1]{2,1,0:T(8,128)} %get-tuple-element.5.refs_3_), custom_call_target="tpu_custom_call" | custom-call | tf_op jit(solution)/shard_map/pallas_call | solution.py:213
  137.4 9.6 %all_to_all.10 = f32[4,64,256]{2,1,0:T(8,128)S(1)} all-to-all(f32[4,64,256]{2,1,0:T(8,128)} %shard_map.47), channel_id=1, replica_groups=mesh['freq'=32,'dish'=4] {'dish'}, dimensions={0} | all-to-all | bytes 524288 | tf_op jit(solution)/shard_map/all_to_all | solution.py:227
  147.0 0.7 copy.42
  (31 shorter events, 3.3 us)
Async XLA Ops:
  0.0 0.7 copy-start
  0.0 5.6 %copy-start.1 = (bf16[8,1,2,8192]{3,2,1,0:T(2,128)(2,1)S(1)}, bf16[8,1,2,8192]{3,2,1,0:T(2,128)(2,1)}, u32[]{:S(2)}) copy-start(bf16[8,1,2,8192]{3,2,1,0:T(2,128)(2,1)} %param.5) | copy-start | bytes 786436
  56.0 12.0 %copy-start.2 = (s32[4,256]{1,0:T(4,128)S(1)}, s32[4,256]{1,0:T(4,128)}, u32[]{:S(2)}) copy-start(s32[4,256]{1,0:T(4,128)} %param.7) | copy-start | bytes 12292
  56.0 63.9 %all-to-all-start = ((bf16[8,2,128,1024]{3,1,0,2:T(2,128)(2,1)}), bf16[8,2,128,1024]{3,1,0,2:T(2,128)(2,1)}, u32[]{:S(2)}, u32[]{:S(2)}) async-start(bf16[8,2,128,1024]{3,1,0,2:T(2,128)(2,1)} %copy.30), calls=%async_computation | async-start | bytes 8388608 | tf_op jit(solution)/shard_map/all_to_all | solution.py:200
where the time goes:
time: 149 us; the launch traced here: 148 us
  local copies, waits for them, and re-layouts  38.1 us (26%)
  Pallas kernels  37.7 us (25%)
  waiting for transfers between devices  30.3 us (20%)
  other arithmetic  19.2 us (13%)
  starting transfers between devices  12 us (8%)
  blocking collectives  9.62 us (6%)
    all_to_all x1, waiting for transfers between devices, body(): gathered = lax.all_to_all(channelized, ('dish', 'freq'), 2, 2, tiled=True)  30.3 us
    pallas_call x1, Pallas kernels, body(): pl.pallas_call(channelize_kernel, grid=(dish_rows,), in_specs=[pl.BlockSp...  26.8 us
    all_to_all x1, starting transfers between devices, body(): gathered = lax.all_to_all(channelized, ('dish', 'freq'), 2, 2, tiled=True)  12 us
    pallas_call x1, Pallas kernels, body(): pl.pallas_call(lambda *refs: beam_kernel(dish_count, *refs), grid=(steps,...  10.9 us
    all_to_all x1, blocking collectives, body(): received = lax.all_to_all(powers, 'dish', 0, 0, tiled=True)  9.62 us
    pallas_call x1, local copies, waits for them, and re-layouts, body(): pl.pallas_call(channelize_kernel, grid=(dish_rows,), in_specs=[pl.BlockSp...  8.52 us
    another operation x1, local copies, waits for them, and re-layouts, body(): volts = voltages[:, 0].reshape(dish_rows, 2, samples // CHB, CHB)  8.39 us
    reshape x2, local copies, waits for them, and re-layouts, beam_tables(): return table.reshape(2 * grid_len, 2 * grid_len)  6.83 us
  transfers between devices with their start and end apart: 1, of which 1 were waited for; matrix products, arithmetic and copies ran while one was open for 15% of the time, Pallas kernels for 0%

commit v1 on v0

--- a/solution.py
+++ b/solution.py
@@ -1,3 +1,4 @@
+import functools
 import math
 
 import jax
@@ -36,23 +37,30 @@
     return shaped_window / jnp.sqrt(energy)
 
 
-def beam_tables(grid_line, grid_len, rows_per_device):
+def beam_tables(grid_rows, grid_len, rows_per_device):
     positions = jnp.arange(grid_len, dtype=jnp.int32)
-    phases = positions[:, None] * grid_line[None, :] % grid_len
+    phases = positions[:, None] * positions[None, :] % grid_len
     angles = full_turn / grid_len * phases.astype(jnp.float32)
     scaling = 1.0 / math.sqrt(grid_len)
-    cosine_table = (jnp.cos(angles) * scaling).astype(jnp.bfloat16)
-    sine_table = (jnp.sin(angles) * scaling).astype(jnp.bfloat16)
-    real_rows = jnp.stack([cosine_table, sine_table], axis=2)
-    imag_rows = jnp.stack([-sine_table, cosine_table], axis=2)
-    table = jnp.stack([real_rows, imag_rows], axis=0)
+    cosine_base = (jnp.cos(angles) * scaling).astype(jnp.bfloat16)
+    sine_base = (jnp.sin(angles) * scaling).astype(jnp.bfloat16)
     devices = grid_len // rows_per_device
-    table = table.reshape(2, grid_len, devices, rows_per_device, 2)
-    table = jnp.transpose(table, (0, 1, 3, 4, 2))
-    return table.reshape(2 * grid_len, 2 * grid_len)
-
-
-def channelize_kernel(v_ref, w_ref, t1_ref, tw_ref, t2_ref, g_ref, o_ref):
+    ordered_rows = jnp.transpose(
+        grid_rows.reshape(grid_rows.shape[0], devices, rows_per_device), (0, 2, 1)
+    ).reshape(grid_rows.shape[0], grid_len)
+    picks = (positions[None, :, None] == ordered_rows[:, None, :]).astype(jnp.bfloat16)
+    cosine_table = jnp.einsum(
+        "jg,dgm->djm", cosine_base, picks, preferred_element_type=jnp.float32
+    ).astype(jnp.bfloat16)
+    sine_table = jnp.einsum(
+        "jg,dgm->djm", sine_base, picks, preferred_element_type=jnp.float32
+    ).astype(jnp.bfloat16)
+    real_rows = jnp.concatenate([cosine_table, sine_table], axis=2)
+    imag_rows = jnp.concatenate([-sine_table, cosine_table], axis=2)
+    return jnp.concatenate([real_rows, imag_rows], axis=1)
+
+
+def channelize_kernel(first_pair, pairs, v_ref, w_ref, t1_ref, tw_ref, t2_ref, g_ref, o_ref):
     cos_tw = tw_ref[0]
     sin_tw = tw_ref[1]
     t1 = t1_ref[...]
@@ -90,27 +98,35 @@
         spec_imag = spectrum[half:]
         out_real = spec_real * g_real - spec_imag * g_imag
         out_imag = spec_real * g_imag + spec_imag * g_real
-        lanes = pl.ds(pl.multiple_of(step * 2 * CHA, 2 * CHA), 2 * CHA)
+        lanes = pl.ds(pl.multiple_of((step - first_pair) * 2 * CHA, 2 * CHA), 2 * CHA)
         o_ref[0, 0, :, lanes] = out_real.astype(o_ref.dtype)
-        o_ref[0, 1, :, lanes] = out_imag.astype(o_ref.dtype)
+        o_ref[1, 0, :, lanes] = out_imag.astype(o_ref.dtype)
         return carry
 
-    lax.fori_loop(0, FRAMES // 2, pair, 0)
-
-
-def beam_kernel(dish_count, x_ref, t_ref, c_ref, s_ref, o_ref, acc_ref):
+    lax.fori_loop(first_pair, first_pair + pairs, pair, 0)
+
+
+def beam_kernel(dish_count, carry_in, finish, *refs):
+    if carry_in:
+        x_ref, t_ref, c_ref, s_ref, init_ref, o_ref, acc_ref = refs
+    else:
+        x_ref, t_ref, c_ref, s_ref, o_ref, acc_ref = refs
     step = pl.program_id(0)
-    rows = x_ref.shape[0] * x_ref.shape[1]
+    rows = x_ref.shape[1]
     devices = x_ref.shape[2] // dish_count
     grid_len = t_ref.shape[1] // 2
+    lanes = x_ref.shape[3]
 
     @pl.when(step == 0)
     def _():
-        acc_ref[...] = jnp.zeros_like(acc_ref)
+        if carry_in:
+            acc_ref[...] = init_ref[...]
+        else:
+            acc_ref[...] = jnp.zeros_like(acc_ref)
 
     parts = []
     for d in range(dish_count):
-        block = x_ref[:, :, pl.ds(d * devices, devices), :].reshape(rows * devices, x_ref.shape[3])
+        block = x_ref[:, :, pl.ds(d * devices, devices), :].reshape(2 * rows * devices, lanes)
         sums = jnp.dot(t_ref[d], block, preferred_element_type=jnp.float32)
         sum_real = sums[:grid_len]
         sum_imag = sums[grid_len:]
@@ -137,6 +153,9 @@
 
     @pl.when(step == pl.num_programs(0) - 1)
     def _():
+        if not finish:
+            o_ref[...] = acc_ref[...]
+            return
         reversal = [
             int(format(s, "0%db" % (dish_count.bit_length() - 1))[::-1], 2)
             for s in range(dish_count)
@@ -182,24 +201,10 @@
     gains = jnp.take(gains, dest_e, axis=2)
     gains = jnp.concatenate([gains, gains], axis=3)
 
-    channelized = pl.pallas_call(
-        channelize_kernel,
-        grid=(dish_rows,),
-        in_specs=[
-            pl.BlockSpec((1, 2, samples // CHB, CHB), lambda r: (r, 0, 0, 0)),
-            pl.BlockSpec((TAPS, CHA, CHB), lambda r: (0, 0, 0)),
-            pl.BlockSpec((2 * CHA, 2 * CHA), lambda r: (0, 0)),
-            pl.BlockSpec((2, CHA, CHB), lambda r: (0, 0, 0)),
-            pl.BlockSpec((2, 2 * dests, CHB), lambda r: (0, 0, 0)),
-            pl.BlockSpec((1, 2, dests, 2 * CHA), lambda r: (r, 0, 0, 0)),
-        ],
-        out_specs=pl.BlockSpec((1, 2, dests, FRAMES * quarter), lambda r: (r, 0, 0, 0)),
-        out_shape=jax.ShapeDtypeStruct((dish_rows, 2, dests, FRAMES * quarter), jnp.bfloat16),
-    )(volts, window, first_table, twiddle, second_table, gains)
-
-    gathered = lax.all_to_all(channelized, ("dish", "freq"), 2, 2, tiled=True)
-
-    tables = jax.vmap(lambda line: beam_tables(line, grid_len, dish_rows))(grid_rows)
+    chunks = 2
+    pairs = FRAMES // 2 // chunks
+    chunk_lanes = pairs * 2 * quarter
+    tables = beam_tables(grid_rows, grid_len, dish_rows)
     feed_index = jnp.arange(dish_count, dtype=jnp.int32)
     positions = jnp.arange(grid_len, dtype=jnp.int32)
     twist_angles = -(full_turn / total_dishes) * (
@@ -208,21 +213,64 @@
     twist_cos = jnp.cos(twist_angles)[:, :, None]
     twist_sin = jnp.sin(twist_angles)[:, :, None]
     lane_block = 2 * quarter
-    steps = FRAMES * quarter // lane_block
-
-    powers = pl.pallas_call(
-        lambda *refs: beam_kernel(dish_count, *refs),
-        grid=(steps,),
-        in_specs=[
-            pl.BlockSpec((dish_rows, 2, dests, lane_block), lambda f: (0, 0, 0, f)),
+
+    def channelize_chunk(chunk):
+        return pl.pallas_call(
+            functools.partial(channelize_kernel, chunk * pairs, pairs),
+            grid=(dish_rows,),
+            in_specs=[
+                pl.BlockSpec((1, 2, samples // CHB, CHB), lambda r: (r, 0, 0, 0)),
+                pl.BlockSpec((TAPS, CHA, CHB), lambda r: (0, 0, 0)),
+                pl.BlockSpec((2 * CHA, 2 * CHA), lambda r: (0, 0)),
+                pl.BlockSpec((2, CHA, CHB), lambda r: (0, 0, 0)),
+                pl.BlockSpec((2, 2 * dests, CHB), lambda r: (0, 0, 0)),
+                pl.BlockSpec((1, 2, dests, 2 * CHA), lambda r: (r, 0, 0, 0)),
+            ],
+            out_specs=pl.BlockSpec((2, 1, dests, chunk_lanes), lambda r: (0, r, 0, 0)),
+            out_shape=jax.ShapeDtypeStruct((2, dish_rows, dests, chunk_lanes), jnp.bfloat16),
+            cost_estimate=pl.CostEstimate(
+                flops=int(dish_rows * pairs * 2 * 2 * 128 * 128 * 128 * 3),
+                bytes_accessed=int(voltages.size * 2 + 2 * dish_rows * dests * chunk_lanes * 2),
+                transcendentals=0,
+            ),
+        )(volts, window, first_table, twiddle, second_table, gains)
+
+    def beamform_chunk(received, carried, finish):
+        carry_in = carried is not None
+        in_specs = [
+            pl.BlockSpec((2, dish_rows, dests, lane_block), lambda f: (0, 0, 0, f)),
             pl.BlockSpec((dish_count, 2 * grid_len, 2 * grid_len), lambda f: (0, 0, 0)),
             pl.BlockSpec((dish_count, grid_len, 1), lambda f: (0, 0, 0)),
             pl.BlockSpec((dish_count, grid_len, 1), lambda f: (0, 0, 0)),
-        ],
-        out_specs=pl.BlockSpec((dish_count, quarter, grid_len), lambda f: (0, 0, 0)),
-        out_shape=jax.ShapeDtypeStruct((dish_count, quarter, grid_len), jnp.float32),
-        scratch_shapes=[pltpu.VMEM((dish_count, grid_len, lane_block), jnp.float32)],
-    )(gathered, tables, twist_cos, twist_sin)
+        ]
+        operands = [received, tables, twist_cos, twist_sin]
+        if carry_in:
+            in_specs.append(pl.BlockSpec((dish_count, grid_len, lane_block), lambda f: (0, 0, 0)))
+            operands.append(carried)
+        if finish:
+            out_shape = (dish_count, quarter, grid_len)
+        else:
+            out_shape = (dish_count, grid_len, lane_block)
+        return pl.pallas_call(
+            functools.partial(beam_kernel, dish_count, carry_in, finish),
+            grid=(chunk_lanes // lane_block,),
+            in_specs=in_specs,
+            out_specs=pl.BlockSpec(out_shape, lambda f: (0, 0, 0)),
+            out_shape=jax.ShapeDtypeStruct(out_shape, jnp.float32),
+            scratch_shapes=[pltpu.VMEM((dish_count, grid_len, lane_block), jnp.float32)],
+            cost_estimate=pl.CostEstimate(
+                flops=int(dish_count * 2 * 512 * 512 * chunk_lanes),
+                bytes_accessed=int(received.size * 2 + tables.size * 2),
+                transcendentals=0,
+            ),
+        )(*operands)
+
+    sent = [channelize_chunk(c) for c in range(chunks)]
+    arrived = [lax.all_to_all(s, ("dish", "freq"), 2, 2, tiled=True) for s in sent]
+    carried = None
+    for c in range(chunks):
+        carried = beamform_chunk(arrived[c], carried, c == chunks - 1)
+    powers = carried
 
     received = lax.all_to_all(powers, "dish", 0, 0, tiled=True)
     return received.reshape(block_width, grid_len)

time: 149 us -> 138 us (0.926)
  local copies, waits for them, and re-layouts: 38.1 us -> 29.1 us
  other arithmetic: 19.2 us -> 10.9 us
  waiting for transfers between devices: 30.3 us -> 24.2 us
  starting transfers between devices: 12 us -> 17.2 us
  Pallas kernels: 37.7 us -> 42.9 us
  matrix products: 0 us -> 2.82 us
    reshape x2 -> x1, local copies, waits for them, and re-layouts: 6.83 us -> 0.09 us  [beam_tables(): grid_rows.reshape(grid_rows.shape[0], devices, rows_per_device)]
    all_to_all x1 -> x2, waiting for transfers between devices: 30.3 us -> 24.2 us  [body(): lax.all_to_all(s, ('dish', 'freq'), 2, 2, tiled=True)]
    all_to_all x1 -> x2, starting transfers between devices: 12 us -> 17.2 us  [body(): lax.all_to_all(s, ('dish', 'freq'), 2, 2, tiled=True)]
    pallas_call x2 -> x4, Pallas kernels: 37.7 us -> 42.9 us  [the longest x2 29 us: channelize_chunk(): pl.pallas_call(functools.partial(channelize_kernel, chunk * pairs, pairs)...]
    convert_element_type x1 -> x0, other arithmetic: 5.03 us -> none  [beam_tables(): sine_table = (jnp.sin(angles) * scaling).astype(jnp.bfloat16)]
    neg x1 -> x0, other arithmetic: 4.33 us -> none  [beam_tables(): imag_rows = jnp.stack([-sine_table, cosine_table], axis=2)]
    dot_general x0 -> x2, matrix products: none -> 2.82 us  [the longest x1 1.41 us: beam_tables(): jnp.einsum('jg,dgm->djm', sine_base, picks, preferred_element_type=jnp.fl...]
    transpose x1, local copies, waits for them, and re-layouts: 2.18 us -> 0.07 us  [beam_tables(): jnp.transpose(grid_rows.reshape(grid_rows.shape[0], devices, rows_per_dev...]
  transfers between devices with their start and end apart: 1 -> 2, of which waited for: 1 -> 2; matrix products, arithmetic and copies ran while one was open for 15% -> 10% of each run, Pallas kernels for 0% -> 15%
where the time goes in v1:
time: 138 us
  Pallas kernels  42.9 us (31%)
  local copies, waits for them, and re-layouts  29.1 us (21%)
  waiting for transfers between devices  24.2 us (18%)
  starting transfers between devices  17.2 us (12%)
  other arithmetic  10.9 us (8%)
  blocking collectives  9.59 us (7%)
  matrix products  2.82 us (2%)
    pallas_call x2, Pallas kernels, channelize_chunk(): pl.pallas_call(functools.partial(channelize_kernel, chunk * pairs, pairs)...  29 us
    all_to_all x2, waiting for transfers between devices, body(): lax.all_to_all(s, ('dish', 'freq'), 2, 2, tiled=True)  24.2 us
    all_to_all x2, starting transfers between devices, body(): lax.all_to_all(s, ('dish', 'freq'), 2, 2, tiled=True)  17.2 us
    pallas_call x2, Pallas kernels, beamform_chunk(): pl.pallas_call(functools.partial(beam_kernel, dish_count, carry_in, finis...  14 us
    all_to_all x1, blocking collectives, body(): received = lax.all_to_all(powers, 'dish', 0, 0, tiled=True)  9.59 us
    another operation x1, local copies, waits for them, and re-layouts, body(): volts = voltages[:, 0].reshape(dish_rows, 2, samples // CHB, CHB)  8.38 us
    pallas_call x2, local copies, waits for them, and re-layouts, channelize_chunk(): pl.pallas_call(functools.partial(channelize_kernel, chunk * pairs, pairs)...  8.18 us
    all_to_all x2, local copies, waits for them, and re-layouts, body(): lax.all_to_all(s, ('dish', 'freq'), 2, 2, tiled=True)  6.59 us
  transfers between devices with their start and end apart: 2, of which 2 were waited for; matrix products, arithmetic and copies ran while one was open for 10% of the time, Pallas kernels for 15%

profile of v1, /device:TPU:1, one launch (start us, length us, event | category | flops | bytes accessed | tf_op | source)
XLA Modules:
  0.0 137.7 jit_solution(9716073780512288386)
XLA Ops:
  0.7 1.2 gather_fusion
  2.4 1.2 fusion.41
  3.8 0.9 gather_fusion.1
  7.6 1.3 pad_maximum_fusion.g_ref
  9.0 8.4 %reshape_squeeze.4.v_ref = bf16[8,2,1216,128]{3,2,1,0:T(8,128)(2,1)} reshape(bf16[8,1,2,155648]{3,2,1,0:T(2,128)(2,1)} %param.4) | data formatting | bytes 9961472 | tf_op jit(solution)/shard_map/reshape;squeeze | solution.py:187
  18.0 1.3 fusion.47.w_ref
  19.3 0.8 bitcast_select_fusion.t2_ref
  20.7 14.5 %shard_map.47 = bf16[2,8,128,512]{3,2,1,0:T(8,128)(2,1)} custom-call(bf16[8,2,1216,128]{3,2,1,0:T(8,128)(2,1)} %reshape_squeeze.4.v_ref, f32[4,64,128]{2,1,0:T(8,128)} %fusion.47.w_ref, bf16[128,128]{1,0:T(8,128)(2,1)} %reshape.432.t1_ref, f32[2,64,128]{2,1,0:T(8,128)} %pad_maximum_fusion.1.tw_ref, bf16[2,256,128]{2,1,0:T(8,128)(2,1)} %bitcast_select_fusion.t2_ref, ...), custom_call_target="tpu_custom_call" | custom-call | flops 805306368 | bytes 7077888 | tf_op jit(solution)/shard_map/pallas_call | solution.py:218
  35.2 4.1 %copy.39 = bf16[2,8,128,512]{3,1,0,2:T(8,128)(2,1)} copy(bf16[2,8,128,512]{3,2,1,0:T(8,128)(2,1)} %shard_map.47) | data formatting | bytes 4194304 | tf_op jit(solution)/shard_map/pallas_call | solution.py:218
  39.3 11.5 %all-to-all-start.1 = ((bf16[2,8,128,512]{3,1,0,2:T(8,128)(2,1)}), bf16[2,8,128,512]{3,1,0,2:T(8,128)(2,1)S(1)}, u32[]{:S(2)}, u32[]{:S(2)}) async-start(bf16[2,8,128,512]{3,1,0,2:T(8,128)(2,1)} %copy.39), calls=%async_computation.1 | async-start | bytes 4194304 | tf_op jit(solution)/shard_map/all_to_all | solution.py:269
  50.8 14.5 %shard_map.46 = bf16[2,8,128,512]{3,2,1,0:T(8,128)(2,1)} custom-call(bf16[8,2,1216,128]{3,2,1,0:T(8,128)(2,1)} %reshape_squeeze.4.v_ref, f32[4,64,128]{2,1,0:T(8,128)} %fusion.47.w_ref, bf16[128,128]{1,0:T(8,128)(2,1)} %reshape.432.t1_ref, f32[2,64,128]{2,1,0:T(8,128)} %pad_maximum_fusion.1.tw_ref, bf16[2,256,128]{2,1,0:T(8,128)(2,1)} %bitcast_select_fusion.t2_ref, ...), custom_call_target="tpu_custom_call" | custom-call | flops 805306368 | bytes 7077888 | tf_op jit(solution)/shard_map/pallas_call | solution.py:218
  65.3 4.1 %copy.34 = bf16[2,8,128,512]{3,1,0,2:T(8,128)(2,1)} copy(bf16[2,8,128,512]{3,2,1,0:T(8,128)(2,1)} %shard_map.46) | data formatting | bytes 4194304 | tf_op jit(solution)/shard_map/pallas_call | solution.py:218
  69.4 11.3 %all-to-all-done.1 = bf16[2,8,128,512]{3,1,0,2:T(8,128)(2,1)S(1)} async-done(((bf16[2,8,128,512]{3,1,0,2:T(8,128)(2,1)}), bf16[2,8,128,512]{3,1,0,2:T(8,128)(2,1)S(1)}, u32[]{:S(2)}, u32[]{:S(2)}) %all-to-all-start.1) | async-done | bytes 2097184 | tf_op jit(solution)/shard_map/all_to_all | solution.py:269
  80.7 5.7 %all-to-all-start = ((bf16[2,8,128,512]{3,1,0,2:T(8,128)(2,1)}), bf16[2,8,128,512]{3,1,0,2:T(8,128)(2,1)}, u32[]{:S(2)}, u32[]{:S(2)}) async-start(bf16[2,8,128,512]{3,1,0,2:T(8,128)(2,1)} %copy.34), calls=%async_computation | async-start | bytes 4194304 | tf_op jit(solution)/shard_map/all_to_all | solution.py:269
  86.9 1.4 %fusion = bf16[4,256,256]{2,1,0:T(8,128)(2,1)S(1)} fusion(s32[4,256]{1,0:T(4,128)S(1)} %eq.69), kind=kOutput, calls=%fused_computation.6 | convolution fusion | flops 135790592 | bytes 528384 | tf_op jit(solution)/shard_map/jg,dgm->djm/dot_general | solution.py:52
  88.3 1.4 %fusion.86 = (bf16[4,256,256]{2,1,0:T(8,128)(2,1)S(1)}, bf16[4,256,256]{2,1,0:T(8,128)(2,1)S(1)}) fusion(s32[4,256]{1,0:T(4,128)S(1)} %eq.69), kind=kOutput, calls=%fused_computation.164 | convolution fusion | flops 136052736 | bytes 1052672 | tf_op jit(solution)/shard_map/jg,dgm->djm/dot_general | solution.py:55
  89.8 1.5 %maximum_maximum_fusion.refs_1_ = bf16[4,512,512]{2,1,0:T(8,128)(2,1)} fusion(bf16[4,256,256]{2,1,0:T(8,128)(2,1)S(1)} %fusion, bf16[4,256,256]{2,1,0:T(8,128)(2,1)S(1)} %get-tuple-element.11, bf16[4,256,256]{2,1,0:T(8,128)(2,1)S(1)} %get-tuple-element.12), kind=kLoop, calls=%fused_computation.3 | loop fusion | flops 8388608 | bytes 3670016 | tf_op jit(solution)/shard_map/concatenate | solution.py:60
  91.3 2.7 %multiply_sine_fusion = (f32[4,256,1]{2,1,0:T(8,128)}, f32[4,256,1]{2,1,0:T(8,128)}) fusion(f32[4,256,1]{2,1,0:T(8,128)S(1)} %copy.38), kind=kLoop, calls=%fused_computation.14 | loop fusion | flops 1024 | bytes 12288 | tf_op jit(solution)/shard_map/sin | solution.py:214
  94.0 2.5 %copy.40.refs_0_ = bf16[2,8,128,512]{3,2,1,0:T(8,128)(2,1)} copy(bf16[2,8,128,512]{3,1,0,2:T(8,128)(2,1)S(1)} %all-to-all-done.1) | data formatting | bytes 4194304 | tf_op jit(solution)/shard_map/all_to_all | solution.py:269
  96.5 6.7 %shard_map.48.refs_4_ = f32[4,256,128]{2,1,0:T(8,128)} custom-call(bf16[2,8,128,512]{3,2,1,0:T(8,128)(2,1)} %copy.40.refs_0_, bf16[4,512,512]{2,1,0:T(8,128)(2,1)} %maximum_maximum_fusion.refs_1_, f32[4,256,1]{2,1,0:T(8,128)} %get-tuple-element.6.refs_2_, f32[4,256,1]{2,1,0:T(8,128)} %get-tuple-element.5.refs_3_), custom_call_target="tpu_custom_call" | custom-call | flops 1073741824 | bytes 4194304 | tf_op jit(solution)/shard_map/pallas_call | solution.py:254
  103.2 12.9 %all-to-all-done = bf16[2,8,128,512]{3,1,0,2:T(8,128)(2,1)} async-done(((bf16[2,8,128,512]{3,1,0,2:T(8,128)(2,1)}), bf16[2,8,128,512]{3,1,0,2:T(8,128)(2,1)}, u32[]{:S(2)}, u32[]{:S(2)}) %all-to-all-start) | async-done | bytes 2097184 | tf_op jit(solution)/shard_map/all_to_all | solution.py:269
  116.1 4.1 %copy.41.refs_0_ = bf16[2,8,128,512]{3,2,1,0:T(8,128)(2,1)} copy(bf16[2,8,128,512]{3,1,0,2:T(8,128)(2,1)} %all-to-all-done) | data formatting | bytes 4194304 | tf_op jit(solution)/shard_map/all_to_all | solution.py:269
  120.2 7.2 %shard_map.49 = f32[4,64,256]{2,1,0:T(8,128)} custom-call(bf16[2,8,128,512]{3,2,1,0:T(8,128)(2,1)} %copy.41.refs_0_, bf16[4,512,512]{2,1,0:T(8,128)(2,1)} %maximum_maximum_fusion.refs_1_, f32[4,256,1]{2,1,0:T(8,128)} %get-tuple-element.6.refs_2_, f32[4,256,1]{2,1,0:T(8,128)} %get-tuple-element.5.refs_3_, f32[4,256,128]{2,1,0:T(8,128)} %shard_map.48.refs_4_), custom_call_target="tpu_custom_call" | custom-call | flops 1073741824 | bytes 4194304 | tf_op jit(solution)/shard_map/pallas_call | solution.py:254
  127.4 9.6 %all_to_all.15 = f32[4,64,256]{2,1,0:T(8,128)S(1)} all-to-all(f32[4,64,256]{2,1,0:T(8,128)} %shard_map.49), channel_id=1, replica_groups=mesh['freq'=32,'dish'=4] {'dish'}, dimensions={0} | all-to-all | bytes 524288 | tf_op jit(solution)/shard_map/all_to_all | solution.py:275
  (36 shorter events, 5.9 us)
Async XLA Ops:
  0.0 0.7 copy-start
  0.0 5.6 %copy-start.1 = (bf16[8,1,2,8192]{3,2,1,0:T(2,128)(2,1)S(1)}, bf16[8,1,2,8192]{3,2,1,0:T(2,128)(2,1)}, u32[]{:S(2)}) copy-start(bf16[8,1,2,8192]{3,2,1,0:T(2,128)(2,1)} %param.5) | copy-start | bytes 786436
  39.3 41.4 %all-to-all-start.1 = ((bf16[2,8,128,512]{3,1,0,2:T(8,128)(2,1)}), bf16[2,8,128,512]{3,1,0,2:T(8,128)(2,1)S(1)}, u32[]{:S(2)}, u32[]{:S(2)}) async-start(bf16[2,8,128,512]{3,1,0,2:T(8,128)(2,1)} %copy.39), calls=%async_computation.1 | async-start | bytes 4194304 | tf_op jit(solution)/shard_map/all_to_all | solution.py:269
  69.4 17.1 %copy-start.2 = (s32[4,256]{1,0:T(4,128)S(1)}, s32[4,256]{1,0:T(4,128)}, u32[]{:S(2)}) copy-start(s32[4,256]{1,0:T(4,128)} %param.7) | copy-start | bytes 12292
  80.7 35.4 %all-to-all-start = ((bf16[2,8,128,512]{3,1,0,2:T(8,128)(2,1)}), bf16[2,8,128,512]{3,1,0,2:T(8,128)(2,1)}, u32[]{:S(2)}, u32[]{:S(2)}) async-start(bf16[2,8,128,512]{3,1,0,2:T(8,128)(2,1)} %copy.34), calls=%async_computation | async-start | bytes 4194304 | tf_op jit(solution)/shard_map/all_to_all | solution.py:269

commit v2 on v1

--- a/solution.py
+++ b/solution.py
@@ -3,6 +3,8 @@
 
 import jax
 import jax.numpy as jnp
+import ml_dtypes
+import numpy as np
 from jax import lax
 from jax.experimental import pallas as pl
 from jax.experimental.pallas import tpu as pltpu
@@ -16,6 +18,32 @@
 
 
 full_turn = 2.0 * math.pi
+
+
+def table_constant(row_count, col_count, modulus, scaling):
+    rows = np.arange(row_count, dtype=np.int64)[:, None]
+    cols = np.arange(col_count, dtype=np.int64)[None, :]
+    angles = np.float32(full_turn / modulus) * (rows * cols % modulus).astype(np.float32)
+    cosine = (np.cos(angles.astype(np.float64)) * scaling).astype(ml_dtypes.bfloat16)
+    sine = (np.sin(angles.astype(np.float64)) * scaling).astype(ml_dtypes.bfloat16)
+    return cosine, sine
+
+
+def window_constant():
+    sample_index = np.arange(TAPS * NCHAN, dtype=np.float64)
+    centred = (sample_index - TAPS * NCHAN / 2 + 0.5) / NCHAN
+    taper_curve = 0.5 - 0.5 * np.cos(full_turn * (sample_index + 0.5) / (TAPS * NCHAN))
+    shaped_window = (np.sinc(centred) * taper_curve).reshape(TAPS, NCHAN)
+    energy = np.mean(np.sum(shaped_window * shaped_window, axis=0))
+    return (shaped_window / np.sqrt(energy)).astype(np.float32)
+
+
+def rotation_constant(row_count, col_count, modulus):
+    rows = np.arange(row_count, dtype=np.int64)[:, None]
+    cols = np.arange(col_count, dtype=np.int64)[None, :]
+    angles = np.float32(-(full_turn / modulus)) * (rows * cols % modulus).astype(np.float32)
+    angles = angles.astype(np.float64)
+    return np.cos(angles).astype(np.float32), np.sin(angles).astype(np.float32)
 
 
 def fourier_table(row_index, col_index, modulus, scaling):
@@ -39,11 +67,9 @@
 
 def beam_tables(grid_rows, grid_len, rows_per_device):
     positions = jnp.arange(grid_len, dtype=jnp.int32)
-    phases = positions[:, None] * positions[None, :] % grid_len
-    angles = full_turn / grid_len * phases.astype(jnp.float32)
-    scaling = 1.0 / math.sqrt(grid_len)
-    cosine_base = (jnp.cos(angles) * scaling).astype(jnp.bfloat16)
-    sine_base = (jnp.sin(angles) * scaling).astype(jnp.bfloat16)
+    cosine_base, sine_base = table_constant(grid_len, grid_len, grid_len, 1.0 / math.sqrt(grid_len))
+    cosine_base = jnp.asarray(cosine_base)
+    sine_base = jnp.asarray(sine_base)
     devices = grid_len // rows_per_device
     ordered_rows = jnp.transpose(
         grid_rows.reshape(grid_rows.shape[0], devices, rows_per_device), (0, 2, 1)
@@ -73,7 +99,7 @@
     def one_frame(frame):
         acc = None
         for tap in range(TAPS):
-            start = pl.multiple_of((frame + tap) * CHA, CHA)
+            start = pl.multiple_of((frame - 2 * first_pair + tap) * CHA, CHA)
             piece = v_ref[0, :, pl.ds(start, CHA), :].astype(jnp.float32)
             term = w_ref[tap][None] * piece
             acc = term if acc is None else acc + term
@@ -184,19 +210,17 @@
     dest_block = jnp.take(block_assign, dest % block_count)
     dest_e = dest_block * dish_count + dest_quarter
 
-    volts = voltages[:, 0].reshape(dish_rows, 2, samples // CHB, CHB)
-    window = filter_window().reshape(TAPS, CHA, CHB)
-    first_index = jnp.arange(CHA, dtype=jnp.int32)
-    second_index = jnp.arange(CHB, dtype=jnp.int32)
-    first_table = fourier_table(first_index, first_index, CHA, 1.0 / math.sqrt(CHA))
-    first_table = jnp.transpose(first_table, (2, 3, 0, 1)).reshape(2 * CHA, 2 * CHA)
-    angles = -(full_turn / NCHAN) * (first_index[:, None] * second_index[None, :] % NCHAN).astype(
-        jnp.float32
+    window = jnp.asarray(window_constant().reshape(TAPS, CHA, CHB))
+    first_cos, first_sin = table_constant(CHA, CHA, CHA, 1.0 / math.sqrt(CHA))
+    first_table = np.block([[first_cos, first_sin], [-first_sin, first_cos]])
+    first_table = jnp.asarray(first_table)
+    twiddle = jnp.asarray(np.stack(rotation_constant(CHA, CHB, NCHAN), axis=0))
+    second_cos, second_sin = table_constant(CHB, CHB, CHB, 1.0 / math.sqrt(CHB))
+    second_table = np.stack(
+        [np.stack([second_cos, -second_sin], axis=0), np.stack([second_sin, second_cos], axis=0)],
+        axis=0,
     )
-    twiddle = jnp.stack([jnp.cos(angles), jnp.sin(angles)], axis=0)
-    second_table = fourier_table(second_index, second_index, CHB, 1.0 / math.sqrt(CHB))
-    second_table = jnp.transpose(second_table, (0, 2, 3, 1))
-    second_table = jnp.take(second_table, dest_e, axis=2).reshape(2, 2 * dests, CHB)
+    second_table = jnp.take(jnp.asarray(second_table), dest_e, axis=2).reshape(2, 2 * dests, CHB)
     gains = feed_gains[:, 0].reshape(dish_rows, 2, CHB, CHA).astype(jnp.float32)
     gains = jnp.take(gains, dest_e, axis=2)
     gains = jnp.concatenate([gains, gains], axis=3)
@@ -207,19 +231,21 @@
     tables = beam_tables(grid_rows, grid_len, dish_rows)
     feed_index = jnp.arange(dish_count, dtype=jnp.int32)
     positions = jnp.arange(grid_len, dtype=jnp.int32)
-    twist_angles = -(full_turn / total_dishes) * (
-        feed_index[:, None] * positions[None, :] % total_dishes
-    ).astype(jnp.float32)
-    twist_cos = jnp.cos(twist_angles)[:, :, None]
-    twist_sin = jnp.sin(twist_angles)[:, :, None]
+    twist_cos, twist_sin = rotation_constant(dish_count, grid_len, total_dishes)
+    twist_cos = jnp.asarray(twist_cos[:, :, None])
+    twist_sin = jnp.asarray(twist_sin[:, :, None])
     lane_block = 2 * quarter
 
+    span = (2 * pairs + TAPS - 1) * CHA
+
     def channelize_chunk(chunk):
+        first = chunk * 2 * pairs * NCHAN
+        volts = voltages[:, 0, :, first : first + span * CHB].reshape(dish_rows, 2, span, CHB)
         return pl.pallas_call(
             functools.partial(channelize_kernel, chunk * pairs, pairs),
             grid=(dish_rows,),
             in_specs=[
-                pl.BlockSpec((1, 2, samples // CHB, CHB), lambda r: (r, 0, 0, 0)),
+                pl.BlockSpec((1, 2, span, CHB), lambda r: (r, 0, 0, 0)),
                 pl.BlockSpec((TAPS, CHA, CHB), lambda r: (0, 0, 0)),
                 pl.BlockSpec((2 * CHA, 2 * CHA), lambda r: (0, 0)),
                 pl.BlockSpec((2, CHA, CHB), lambda r: (0, 0, 0)),
@@ -272,7 +298,15 @@
         carried = beamform_chunk(arrived[c], carried, c == chunks - 1)
     powers = carried
 
-    received = lax.all_to_all(powers, "dish", 0, 0, tiled=True)
+    me = lax.axis_index("dish")
+    pieces = [lax.dynamic_index_in_dim(powers, me, 0, keepdims=False)]
+    for shift in range(1, dish_count):
+        outgoing = lax.dynamic_index_in_dim(powers, me ^ shift, 0, keepdims=False)
+        pairs_list = [(i, i ^ shift) for i in range(dish_count)]
+        pieces.append(lax.ppermute(outgoing, "dish", pairs_list))
+    stacked = jnp.stack(pieces, axis=0)
+    order = jnp.arange(dish_count, dtype=jnp.int32) ^ me
+    received = jnp.take(stacked, order, axis=0)
     return received.reshape(block_width, grid_len)
 
 

time: 138 us -> 137 us (level)
  local copies, waits for them, and re-layouts: 29.1 us -> 40.9 us
  blocking collectives: 9.59 us -> 0 us
  other arithmetic: 10.9 us -> 4.91 us
  starting transfers between devices: 17.2 us -> 19.7 us
  waiting for transfers between devices: 24.2 us -> 26.3 us
  matrix products: 2.82 us -> 0.87 us
    all_to_all x1 -> x0, blocking collectives: 9.59 us -> none  [body(): received = lax.all_to_all(powers, 'dish', 0, 0, tiled=True)]
    slice x0 -> x1, local copies, waits for them, and re-layouts: none -> 7.57 us  [channelize_chunk(): voltages[:, 0, :, first:first + span * CHB].reshape(dish_rows, 2, span, CHB)]
    ppermute x0 -> x3, waiting for transfers between devices: none -> 3.5 us  [body(): pieces.append(lax.ppermute(outgoing, 'dish', pairs_list))]
    ppermute x0 -> x3, starting transfers between devices: none -> 3.03 us  [body(): pieces.append(lax.ppermute(outgoing, 'dish', pairs_list))]
    another operation x1 -> x2, local copies, waits for them, and re-layouts: 8.38 us -> 11.2 us  [channelize_chunk(): voltages[:, 0, :, first:first + span * CHB].reshape(dish_rows, 2, span, CHB)]
    sin x2 -> x0, other arithmetic: 2.83 us -> none  [the longest x1 2.68 us: body(): twist_sin = jnp.sin(twist_angles)[:, :, None]]
  transfers between devices with their start and end apart: 2 -> 5, of which waited for: 2 -> 4; matrix products, arithmetic and copies ran while one was open for 10% -> 11% of each run, Pallas kernels for 15% -> 16%
where the time goes in v2:
time: 137 us; the launch traced here: 136 us
  Pallas kernels  42.9 us (31%)
  local copies, waits for them, and re-layouts  40.9 us (30%)
  waiting for transfers between devices  26.3 us (19%)
  starting transfers between devices  19.7 us (14%)
  other arithmetic  4.91 us (4%)
    pallas_call x2, Pallas kernels, channelize_chunk(): pl.pallas_call(functools.partial(channelize_kernel, chunk * pairs, pairs)...  28.9 us
    all_to_all x2, waiting for transfers between devices, body(): lax.all_to_all(s, ('dish', 'freq'), 2, 2, tiled=True)  22.8 us
    all_to_all x2, starting transfers between devices, body(): lax.all_to_all(s, ('dish', 'freq'), 2, 2, tiled=True)  16.6 us
    pallas_call x2, Pallas kernels, beamform_chunk(): pl.pallas_call(functools.partial(beam_kernel, dish_count, carry_in, finis...  14 us
    another operation x2, local copies, waits for them, and re-layouts, channelize_chunk(): voltages[:, 0, :, first:first + span * CHB].reshape(dish_rows, 2, span, CHB)  11.2 us
    pallas_call x2, local copies, waits for them, and re-layouts, channelize_chunk(): pl.pallas_call(functools.partial(channelize_kernel, chunk * pairs, pairs)...  8.21 us
    slice x1, local copies, waits for them, and re-layouts, channelize_chunk(): voltages[:, 0, :, first:first + span * CHB].reshape(dish_rows, 2, span, CHB)  7.57 us
    all_to_all x2, local copies, waits for them, and re-layouts, body(): lax.all_to_all(s, ('dish', 'freq'), 2, 2, tiled=True)  6.64 us
  transfers between devices with their start and end apart: 5, of which 4 were waited for; matrix products, arithmetic and copies ran while one was open for 11% of the time, Pallas kernels for 16%

profile of v2, /device:TPU:1, one launch (start us, length us, event | category | flops | bytes accessed | tf_op | source)
XLA Modules:
  0.0 135.8 jit_solution(2175866981681202642)
XLA Ops:
  0.7 1.2 gather_fusion
  1.9 1.3 reshape.170
  5.0 1.3 pad_maximum_fusion.g_ref
  7.2 7.6 %fusion.10 = (bf16[8,1,2,90112]{3,2,1,0:T(2,128)(2,1)}, bf16[8,1,2,90112]{3,2,1,0:T(2,128)(2,1)S(1)}) fusion(bf16[8,1,2,155648]{3,2,1,0:T(2,128)(2,1)} %param.12), kind=kLoop, calls=%fused_computation.51 | loop fusion | bytes 11534336 | tf_op jit(solution)/shard_map/slice | solution.py:243
  14.8 6.9 %reshape_squeeze.8.v_ref = bf16[8,2,704,128]{3,2,1,0:T(8,128)(2,1)} reshape(bf16[8,1,2,90112]{3,2,1,0:T(2,128)(2,1)} %get-tuple-element.5) | data formatting | bytes 5767168 | tf_op jit(solution)/shard_map/reshape;squeeze | solution.py:243
  22.4 14.4 %shard_map.119 = bf16[2,8,128,512]{3,2,1,0:T(8,128)(2,1)} custom-call(bf16[8,2,704,128]{3,2,1,0:T(8,128)(2,1)} %reshape_squeeze.8.v_ref, f32[4,64,128]{2,1,0:T(8,128)} %constant.126.clone.w_ref, bf16[128,128]{1,0:T(8,128)(2,1)} %constant.127.clone.t1_ref, f32[2,64,128]{2,1,0:T(8,128)} %constant.128.clone.tw_ref, ...), custom_call_target="tpu_custom_call" | custom-call | flops 805306368 | bytes 7077888 | tf_op jit(solution)/shard_map/pallas_call | solution.py:244
  36.8 4.1 %copy.30 = bf16[2,8,128,512]{3,1,0,2:T(8,128)(2,1)} copy(bf16[2,8,128,512]{3,2,1,0:T(8,128)(2,1)} %shard_map.119) | data formatting | bytes 4194304 | tf_op jit(solution)/shard_map/pallas_call | solution.py:244
  40.9 12.0 %all-to-all-start.1 = ((bf16[2,8,128,512]{3,1,0,2:T(8,128)(2,1)}), bf16[2,8,128,512]{3,1,0,2:T(8,128)(2,1)}, u32[]{:S(2)}, u32[]{:S(2)}) async-start(bf16[2,8,128,512]{3,1,0,2:T(8,128)(2,1)} %copy.30), calls=%async_computation.1 | async-start | bytes 4194304 | tf_op jit(solution)/shard_map/all_to_all | solution.py:295
  52.9 4.4 %reshape_squeeze.7.v_ref = bf16[8,2,704,128]{3,2,1,0:T(8,128)(2,1)} reshape(bf16[8,1,2,90112]{3,2,1,0:T(2,128)(2,1)S(1)} %get-tuple-element.6) | data formatting | bytes 5767168 | tf_op jit(solution)/shard_map/reshape;squeeze | solution.py:243
  57.3 14.5 %shard_map.118 = bf16[2,8,128,512]{3,2,1,0:T(8,128)(2,1)} custom-call(bf16[8,2,704,128]{3,2,1,0:T(8,128)(2,1)} %reshape_squeeze.7.v_ref, f32[4,64,128]{2,1,0:T(8,128)} %constant.126.clone.w_ref, bf16[128,128]{1,0:T(8,128)(2,1)} %constant.127.clone.t1_ref, f32[2,64,128]{2,1,0:T(8,128)} %constant.128.clone.tw_ref, ...), custom_call_target="tpu_custom_call" | custom-call | flops 805306368 | bytes 7077888 | tf_op jit(solution)/shard_map/pallas_call | solution.py:244
  71.7 4.1 %copy.26 = bf16[2,8,128,512]{3,1,0,2:T(8,128)(2,1)} copy(bf16[2,8,128,512]{3,2,1,0:T(8,128)(2,1)} %shard_map.118) | data formatting | bytes 4194304 | tf_op jit(solution)/shard_map/pallas_call | solution.py:244
  75.8 6.6 %all-to-all-done.1 = bf16[2,8,128,512]{3,1,0,2:T(8,128)(2,1)} async-done(((bf16[2,8,128,512]{3,1,0,2:T(8,128)(2,1)}), bf16[2,8,128,512]{3,1,0,2:T(8,128)(2,1)}, u32[]{:S(2)}, u32[]{:S(2)}) %all-to-all-start.1) | async-done | bytes 2097184 | tf_op jit(solution)/shard_map/all_to_all | solution.py:295
  82.4 4.7 %all-to-all-start = ((bf16[2,8,128,512]{3,1,0,2:T(8,128)(2,1)}), bf16[2,8,128,512]{3,1,0,2:T(8,128)(2,1)S(1)}, u32[]{:S(2)}, u32[]{:S(2)}) async-start(bf16[2,8,128,512]{3,1,0,2:T(8,128)(2,1)} %copy.26), calls=%async_computation | async-start | bytes 4194304 | tf_op jit(solution)/shard_map/all_to_all | solution.py:295
  88.5 1.5 %maximum_maximum_fusion.refs_1_ = bf16[4,512,512]{2,1,0:T(8,128)(2,1)} fusion(bf16[4,256,256]{2,1,0:T(8,128)(2,1)S(1)} %fusion, bf16[4,256,256]{2,1,0:T(8,128)(2,1)S(1)} %get-tuple-element.11, bf16[4,256,256]{2,1,0:T(8,128)(2,1)S(1)} %get-tuple-element.12), kind=kLoop, calls=%fused_computation.4 | loop fusion | flops 8388608 | bytes 3670016 | tf_op jit(solution)/shard_map/concatenate | solution.py:86
  90.0 4.1 %copy.31.refs_0_ = bf16[2,8,128,512]{3,2,1,0:T(8,128)(2,1)} copy(bf16[2,8,128,512]{3,1,0,2:T(8,128)(2,1)} %all-to-all-done.1) | data formatting | bytes 4194304 | tf_op jit(solution)/shard_map/all_to_all | solution.py:295
  94.2 6.8 %shard_map.120.refs_4_ = f32[4,256,128]{2,1,0:T(8,128)} custom-call(bf16[2,8,128,512]{3,2,1,0:T(8,128)(2,1)} %copy.31.refs_0_, bf16[4,512,512]{2,1,0:T(8,128)(2,1)} %maximum_maximum_fusion.refs_1_, f32[4,256,1]{2,1,0:T(8,128)} %constant.132.clone.refs_2_, f32[4,256,1]{2,1,0:T(8,128)} %constant.133.clone.refs_3_), custom_call_target="tpu_custom_call" | custom-call | flops 1073741824 | bytes 4194304 | tf_op jit(solution)/shard_map/pallas_call | solution.py:280
  100.9 16.2 %all-to-all-done = bf16[2,8,128,512]{3,1,0,2:T(8,128)(2,1)S(1)} async-done(((bf16[2,8,128,512]{3,1,0,2:T(8,128)(2,1)}), bf16[2,8,128,512]{3,1,0,2:T(8,128)(2,1)S(1)}, u32[]{:S(2)}, u32[]{:S(2)}) %all-to-all-start) | async-done | bytes 2097184 | tf_op jit(solution)/shard_map/all_to_all | solution.py:295
  117.2 2.5 %copy.32.refs_0_ = bf16[2,8,128,512]{3,2,1,0:T(8,128)(2,1)} copy(bf16[2,8,128,512]{3,1,0,2:T(8,128)(2,1)S(1)} %all-to-all-done) | data formatting | bytes 4194304 | tf_op jit(solution)/shard_map/all_to_all | solution.py:295
  119.7 7.2 %shard_map.121 = f32[4,64,256]{2,1,0:T(8,128)} custom-call(bf16[2,8,128,512]{3,2,1,0:T(8,128)(2,1)} %copy.32.refs_0_, bf16[4,512,512]{2,1,0:T(8,128)(2,1)} %maximum_maximum_fusion.refs_1_, f32[4,256,1]{2,1,0:T(8,128)} %constant.132.clone.refs_2_, f32[4,256,1]{2,1,0:T(8,128)} %constant.133.clone.refs_3_, f32[4,256,128]{2,1,0:T(8,128)} %shard_map.120.refs_4_), custom_call_target="tpu_custom_call" | custom-call | flops 1073741824 | bytes 4194304 | tf_op jit(solution)/shard_map/pallas_call | solution.py:280
  126.9 1.0 constant_dynamic-slice_fusion
  127.8 1.3 collective-permute-start
  129.5 1.4 %collective-permute-start.2 = (f32[64,256]{1,0:T(8,128)S(1)}, f32[64,256]{1,0:T(8,128)S(1)}, u32[]{:S(2)}, u32[]{:S(2)}) collective-permute-start(f32[64,256]{1,0:T(8,128)S(1)} %get-tuple-element.8), channel_id=1, source_target_pairs={{0,3},{1,2},{2,1},{3,0},{4,7},{5,6},{6,5},{7,4},{8,11},{9,10},{10,... | collective-permute-start | bytes 196616 | tf_op jit(solution)/shard_map/ppermute | solution.py:306
  130.9 1.9 %collective-permute-done.1 = f32[64,256]{1,0:T(8,128)S(1)} collective-permute-done((f32[64,256]{1,0:T(8,128)S(1)}, f32[64,256]{1,0:T(8,128)S(1)}, u32[]{:S(2)}, u32[]{:S(2)}) %collective-permute-start.1) | collective-permute-done | bytes 65568 | tf_op jit(solution)/shard_map/ppermute | solution.py:306
  132.8 1.6 %collective-permute-done.2 = f32[64,256]{1,0:T(8,128)S(1)} collective-permute-done((f32[64,256]{1,0:T(8,128)S(1)}, f32[64,256]{1,0:T(8,128)S(1)}, u32[]{:S(2)}, u32[]{:S(2)}) %collective-permute-start.2) | collective-permute-done | bytes 65568 | tf_op jit(solution)/shard_map/ppermute | solution.py:306
  (37 shorter events, 7.1 us)
Async XLA Ops:
  0.0 0.7 copy-start
  3.8 2.4 %copy-start.2 = (bf16[2,2,128,128]{3,1,2,0:T(2,128)(2,1)S(1)}, bf16[2,2,128,128]{3,1,2,0:T(2,128)(2,1)}, u32[]{:S(2)}) copy-start(bf16[2,2,128,128]{3,1,2,0:T(2,128)(2,1)} %constant.129.clone) | copy-start | bytes 393220
  40.9 41.5 %all-to-all-start.1 = ((bf16[2,8,128,512]{3,1,0,2:T(8,128)(2,1)}), bf16[2,8,128,512]{3,1,0,2:T(8,128)(2,1)}, u32[]{:S(2)}, u32[]{:S(2)}) async-start(bf16[2,8,128,512]{3,1,0,2:T(8,128)(2,1)} %copy.30), calls=%async_computation.1 | async-start | bytes 4194304 | tf_op jit(solution)/shard_map/all_to_all | solution.py:295
  75.8 11.3 %copy-start.3 = (s32[4,256]{1,0:T(4,128)S(1)}, s32[4,256]{1,0:T(4,128)}, u32[]{:S(2)}) copy-start(s32[4,256]{1,0:T(4,128)} %param.15) | copy-start | bytes 12292
  75.8 11.8 %copy-start.4 = (bf16[256,256,1]{1,0,2:T(8,128)(2,1)S(1)}, bf16[256,256,1]{1,0,2:T(8,128)(2,1)}, u32[]{:S(2)}) copy-start(bf16[256,256,1]{1,0,2:T(8,128)(2,1)} %constant.136) | copy-start | bytes 393220
  75.8 12.2 %copy-start.1 = (bf16[256,256,1]{1,0,2:T(8,128)(2,1)S(1)}, bf16[256,256,1]{1,0,2:T(8,128)(2,1)}, u32[]{:S(2)}) copy-start(bf16[256,256,1]{1,0,2:T(8,128)(2,1)} %constant.137) | copy-start | bytes 393220
  82.4 34.7 %all-to-all-start = ((bf16[2,8,128,512]{3,1,0,2:T(8,128)(2,1)}), bf16[2,8,128,512]{3,1,0,2:T(8,128)(2,1)S(1)}, u32[]{:S(2)}, u32[]{:S(2)}) async-start(bf16[2,8,128,512]{3,1,0,2:T(8,128)(2,1)} %copy.26), calls=%async_computation | async-start | bytes 4194304 | tf_op jit(solution)/shard_map/all_to_all | solution.py:295
  127.8 3.0 %collective-permute-start = (f32[64,256]{1,0:T(8,128)S(1)}, f32[64,256]{1,0:T(8,128)S(1)}, u32[]{:S(2)}, u32[]{:S(2)}) collective-permute-start(f32[64,256]{1,0:T(8,128)S(1)} %get-tuple-element.10), channel_id=1, source_target_pairs={{0,1},{1,0},{2,3},{3,2},{4,5},{5,4},{6,7},{7,6},{8,9},{9,8},{10,11... | collective-permute-start | bytes 196616 | tf_op jit(solution)/shard_map/ppermute | solution.py:306
  129.1 3.6 %collective-permute-start.1 = (f32[64,256]{1,0:T(8,128)S(1)}, f32[64,256]{1,0:T(8,128)S(1)}, u32[]{:S(2)}, u32[]{:S(2)}) collective-permute-start(f32[64,256]{1,0:T(8,128)S(1)} %get-tuple-element.9), channel_id=1, source_target_pairs={{0,2},{1,3},{2,0},{3,1},{4,6},{5,7},{6,4},{7,5},{8,10},{9,11},{10,... | collective-permute-start | bytes 196616 | tf_op jit(solution)/shard_map/ppermute | solution.py:306
  129.5 4.9 %collective-permute-start.2 = (f32[64,256]{1,0:T(8,128)S(1)}, f32[64,256]{1,0:T(8,128)S(1)}, u32[]{:S(2)}, u32[]{:S(2)}) collective-permute-start(f32[64,256]{1,0:T(8,128)S(1)} %get-tuple-element.8), channel_id=1, source_target_pairs={{0,3},{1,2},{2,1},{3,0},{4,7},{5,6},{6,5},{7,4},{8,11},{9,10},{10,... | collective-permute-start | bytes 196616 | tf_op jit(solution)/shard_map/ppermute | solution.py:306

commit v3 on v2

--- a/solution.py
+++ b/solution.py
@@ -99,7 +99,7 @@
     def one_frame(frame):
         acc = None
         for tap in range(TAPS):
-            start = pl.multiple_of((frame - 2 * first_pair + tap) * CHA, CHA)
+            start = pl.multiple_of((frame + tap) * CHA, CHA)
             piece = v_ref[0, :, pl.ds(start, CHA), :].astype(jnp.float32)
             term = w_ref[tap][None] * piece
             acc = term if acc is None else acc + term
@@ -236,16 +236,14 @@
     twist_sin = jnp.asarray(twist_sin[:, :, None])
     lane_block = 2 * quarter
 
-    span = (2 * pairs + TAPS - 1) * CHA
+    volts = voltages[:, 0].reshape(dish_rows, 2, samples // CHB, CHB)
 
     def channelize_chunk(chunk):
-        first = chunk * 2 * pairs * NCHAN
-        volts = voltages[:, 0, :, first : first + span * CHB].reshape(dish_rows, 2, span, CHB)
         return pl.pallas_call(
             functools.partial(channelize_kernel, chunk * pairs, pairs),
             grid=(dish_rows,),
             in_specs=[
-                pl.BlockSpec((1, 2, span, CHB), lambda r: (r, 0, 0, 0)),
+                pl.BlockSpec((1, 2, samples // CHB, CHB), lambda r: (r, 0, 0, 0)),
                 pl.BlockSpec((TAPS, CHA, CHB), lambda r: (0, 0, 0)),
                 pl.BlockSpec((2 * CHA, 2 * CHA), lambda r: (0, 0)),
                 pl.BlockSpec((2, CHA, CHB), lambda r: (0, 0, 0)),

time: 137 us -> 133 us (0.971)
  local copies, waits for them, and re-layouts: 40.9 us -> 30.5 us
  waiting for transfers between devices: 26.3 us -> 32.3 us
    slice x1 -> x0, local copies, waits for them, and re-layouts: 7.57 us -> none  [channelize_chunk(): voltages[:, 0, :, first:first + span * CHB].reshape(dish_rows, 2, span, CHB)]
    all_to_all x2, waiting for transfers between devices: 22.8 us -> 28.8 us  [body(): lax.all_to_all(s, ('dish', 'freq'), 2, 2, tiled=True)]
    another operation x2 -> x1, local copies, waits for them, and re-layouts: 11.2 us -> 8.4 us  [body(): volts = voltages[:, 0].reshape(dish_rows, 2, samples // CHB, CHB)]
  transfers between devices with their start and end apart: 5 -> 5, of which waited for: 4 -> 4; matrix products, arithmetic and copies ran while one was open for 11% -> 7% of each run, Pallas kernels for 16% -> 16%
where the time goes in v3:
time: 133 us; the launch traced here: 132 us
  Pallas kernels  43 us (32%)
  waiting for transfers between devices  32.3 us (24%)
  local copies, waits for them, and re-layouts  30.5 us (23%)
  starting transfers between devices  20.3 us (15%)
  other arithmetic  4.87 us (4%)
    pallas_call x2, Pallas kernels, channelize_chunk(): pl.pallas_call(functools.partial(channelize_kernel, chunk * pairs, pairs)...  29 us
    all_to_all x2, waiting for transfers between devices, body(): lax.all_to_all(s, ('dish', 'freq'), 2, 2, tiled=True)  28.8 us
    all_to_all x2, starting transfers between devices, body(): lax.all_to_all(s, ('dish', 'freq'), 2, 2, tiled=True)  17.2 us
    pallas_call x2, Pallas kernels, beamform_chunk(): pl.pallas_call(functools.partial(beam_kernel, dish_count, carry_in, finis...  14 us
    another operation x1, local copies, waits for them, and re-layouts, body(): volts = voltages[:, 0].reshape(dish_rows, 2, samples // CHB, CHB)  8.4 us
    pallas_call x2, local copies, waits for them, and re-layouts, channelize_chunk(): pl.pallas_call(functools.partial(channelize_kernel, chunk * pairs, pairs)...  8.19 us
    all_to_all x2, local copies, waits for them, and re-layouts, body(): lax.all_to_all(s, ('dish', 'freq'), 2, 2, tiled=True)  6.58 us
    ppermute x3, waiting for transfers between devices, body(): pieces.append(lax.ppermute(outgoing, 'dish', pairs_list))  3.5 us
  transfers between devices with their start and end apart: 5, of which 4 were waited for; matrix products, arithmetic and copies ran while one was open for 7% of the time, Pallas kernels for 16%

profile of v3, /device:TPU:1, one launch (start us, length us, event | category | flops | bytes accessed | tf_op | source)
XLA Modules:
  0.0 132.0 jit_solution(5284506297338978138)
XLA Ops:
  0.7 1.2 gather_fusion
  1.9 1.3 reshape.170
  5.0 1.3 pad_maximum_fusion.g_ref
  6.3 0.9 gather_fusion.1
  7.2 8.4 %reshape_squeeze.4.v_ref = bf16[8,2,1216,128]{3,2,1,0:T(8,128)(2,1)} reshape(bf16[8,1,2,155648]{3,2,1,0:T(2,128)(2,1)} %param.12) | data formatting | bytes 9961472 | tf_op jit(solution)/shard_map/reshape;squeeze | solution.py:239
  16.4 14.5 %shard_map.119 = bf16[2,8,128,512]{3,2,1,0:T(8,128)(2,1)} custom-call(bf16[8,2,1216,128]{3,2,1,0:T(8,128)(2,1)} %reshape_squeeze.4.v_ref, f32[4,64,128]{2,1,0:T(8,128)} %constant.126.clone.w_ref, bf16[128,128]{1,0:T(8,128)(2,1)} %constant.127.clone.t1_ref, f32[2,64,128]{2,1,0:T(8,128)} %constant.128.clone.tw_ref, ...), custom_call_target="tpu_custom_call" | custom-call | flops 805306368 | bytes 7077888 | tf_op jit(solution)/shard_map/pallas_call | solution.py:242
  30.9 4.1 %copy.30 = bf16[2,8,128,512]{3,1,0,2:T(8,128)(2,1)} copy(bf16[2,8,128,512]{3,2,1,0:T(8,128)(2,1)} %shard_map.119) | data formatting | bytes 4194304 | tf_op jit(solution)/shard_map/pallas_call | solution.py:242
  35.0 11.5 %all-to-all-start.1 = ((bf16[2,8,128,512]{3,1,0,2:T(8,128)(2,1)}), bf16[2,8,128,512]{3,1,0,2:T(8,128)(2,1)S(1)}, u32[]{:S(2)}, u32[]{:S(2)}) async-start(bf16[2,8,128,512]{3,1,0,2:T(8,128)(2,1)} %copy.30), calls=%async_computation.1 | async-start | bytes 4194304 | tf_op jit(solution)/shard_map/all_to_all | solution.py:293
  46.5 14.5 %shard_map.118 = bf16[2,8,128,512]{3,2,1,0:T(8,128)(2,1)} custom-call(bf16[8,2,1216,128]{3,2,1,0:T(8,128)(2,1)} %reshape_squeeze.4.v_ref, f32[4,64,128]{2,1,0:T(8,128)} %constant.126.clone.w_ref, bf16[128,128]{1,0:T(8,128)(2,1)} %constant.127.clone.t1_ref, f32[2,64,128]{2,1,0:T(8,128)} %constant.128.clone.tw_ref, ...), custom_call_target="tpu_custom_call" | custom-call | flops 805306368 | bytes 7077888 | tf_op jit(solution)/shard_map/pallas_call | solution.py:242
  61.0 4.1 %copy.26 = bf16[2,8,128,512]{3,1,0,2:T(8,128)(2,1)} copy(bf16[2,8,128,512]{3,2,1,0:T(8,128)(2,1)} %shard_map.118) | data formatting | bytes 4194304 | tf_op jit(solution)/shard_map/pallas_call | solution.py:242
  65.1 11.3 %all-to-all-done.1 = bf16[2,8,128,512]{3,1,0,2:T(8,128)(2,1)S(1)} async-done(((bf16[2,8,128,512]{3,1,0,2:T(8,128)(2,1)}), bf16[2,8,128,512]{3,1,0,2:T(8,128)(2,1)S(1)}, u32[]{:S(2)}, u32[]{:S(2)}) %all-to-all-start.1) | async-done | bytes 2097184 | tf_op jit(solution)/shard_map/all_to_all | solution.py:293
  76.4 5.7 %all-to-all-start = ((bf16[2,8,128,512]{3,1,0,2:T(8,128)(2,1)}), bf16[2,8,128,512]{3,1,0,2:T(8,128)(2,1)}, u32[]{:S(2)}, u32[]{:S(2)}) async-start(bf16[2,8,128,512]{3,1,0,2:T(8,128)(2,1)} %copy.26), calls=%async_computation | async-start | bytes 4194304 | tf_op jit(solution)/shard_map/all_to_all | solution.py:293
  83.5 1.5 %maximum_maximum_fusion.refs_1_ = bf16[4,512,512]{2,1,0:T(8,128)(2,1)} fusion(bf16[4,256,256]{2,1,0:T(8,128)(2,1)S(1)} %fusion, bf16[4,256,256]{2,1,0:T(8,128)(2,1)S(1)} %get-tuple-element.9, bf16[4,256,256]{2,1,0:T(8,128)(2,1)S(1)} %get-tuple-element.10), kind=kLoop, calls=%fused_computation.4 | loop fusion | flops 8388608 | bytes 3670016 | tf_op jit(solution)/shard_map/concatenate | solution.py:86
  85.0 2.5 %copy.31.refs_0_ = bf16[2,8,128,512]{3,2,1,0:T(8,128)(2,1)} copy(bf16[2,8,128,512]{3,1,0,2:T(8,128)(2,1)S(1)} %all-to-all-done.1) | data formatting | bytes 4194304 | tf_op jit(solution)/shard_map/all_to_all | solution.py:293
  87.5 6.8 %shard_map.120.refs_4_ = f32[4,256,128]{2,1,0:T(8,128)} custom-call(bf16[2,8,128,512]{3,2,1,0:T(8,128)(2,1)} %copy.31.refs_0_, bf16[4,512,512]{2,1,0:T(8,128)(2,1)} %maximum_maximum_fusion.refs_1_, f32[4,256,1]{2,1,0:T(8,128)} %constant.132.clone.refs_2_, f32[4,256,1]{2,1,0:T(8,128)} %constant.133.clone.refs_3_), custom_call_target="tpu_custom_call" | custom-call | flops 1073741824 | bytes 4194304 | tf_op jit(solution)/shard_map/pallas_call | solution.py:278
  94.3 17.5 %all-to-all-done = bf16[2,8,128,512]{3,1,0,2:T(8,128)(2,1)} async-done(((bf16[2,8,128,512]{3,1,0,2:T(8,128)(2,1)}), bf16[2,8,128,512]{3,1,0,2:T(8,128)(2,1)}, u32[]{:S(2)}, u32[]{:S(2)}) %all-to-all-start) | async-done | bytes 2097184 | tf_op jit(solution)/shard_map/all_to_all | solution.py:293
  111.8 4.1 %copy.32.refs_0_ = bf16[2,8,128,512]{3,2,1,0:T(8,128)(2,1)} copy(bf16[2,8,128,512]{3,1,0,2:T(8,128)(2,1)} %all-to-all-done) | data formatting | bytes 4194304 | tf_op jit(solution)/shard_map/all_to_all | solution.py:293
  115.9 7.2 %shard_map.121 = f32[4,64,256]{2,1,0:T(8,128)} custom-call(bf16[2,8,128,512]{3,2,1,0:T(8,128)(2,1)} %copy.32.refs_0_, bf16[4,512,512]{2,1,0:T(8,128)(2,1)} %maximum_maximum_fusion.refs_1_, f32[4,256,1]{2,1,0:T(8,128)} %constant.132.clone.refs_2_, f32[4,256,1]{2,1,0:T(8,128)} %constant.133.clone.refs_3_, f32[4,256,128]{2,1,0:T(8,128)} %shard_map.120.refs_4_), custom_call_target="tpu_custom_call" | custom-call | flops 1073741824 | bytes 4194304 | tf_op jit(solution)/shard_map/pallas_call | solution.py:278
  123.1 1.0 constant_dynamic-slice_fusion
  124.0 1.3 collective-permute-start
  125.7 1.4 %collective-permute-start.2 = (f32[64,256]{1,0:T(8,128)S(1)}, f32[64,256]{1,0:T(8,128)S(1)}, u32[]{:S(2)}, u32[]{:S(2)}) collective-permute-start(f32[64,256]{1,0:T(8,128)S(1)} %get-tuple-element.6), channel_id=1, source_target_pairs={{0,3},{1,2},{2,1},{3,0},{4,7},{5,6},{6,5},{7,4},{8,11},{9,10},{10,... | collective-permute-start | bytes 196616 | tf_op jit(solution)/shard_map/ppermute | solution.py:304
  127.1 1.9 %collective-permute-done.1 = f32[64,256]{1,0:T(8,128)S(1)} collective-permute-done((f32[64,256]{1,0:T(8,128)S(1)}, f32[64,256]{1,0:T(8,128)S(1)}, u32[]{:S(2)}, u32[]{:S(2)}) %collective-permute-start.1) | collective-permute-done | bytes 65568 | tf_op jit(solution)/shard_map/ppermute | solution.py:304
  129.0 1.6 %collective-permute-done.2 = f32[64,256]{1,0:T(8,128)S(1)} collective-permute-done((f32[64,256]{1,0:T(8,128)S(1)}, f32[64,256]{1,0:T(8,128)S(1)}, u32[]{:S(2)}, u32[]{:S(2)}) %collective-permute-start.2) | collective-permute-done | bytes 65568 | tf_op jit(solution)/shard_map/ppermute | solution.py:304
  131.2 0.8 bitcast_select_fusion
  (35 shorter events, 5.4 us)
Async XLA Ops:
  0.0 0.7 copy-start
  4.5 1.7 %copy-start.2 = (bf16[2,2,128,128]{3,1,2,0:T(2,128)(2,1)S(1)}, bf16[2,2,128,128]{3,1,2,0:T(2,128)(2,1)}, u32[]{:S(2)}) copy-start(bf16[2,2,128,128]{3,1,2,0:T(2,128)(2,1)} %constant.129.clone) | copy-start | bytes 393220
  35.0 41.4 %all-to-all-start.1 = ((bf16[2,8,128,512]{3,1,0,2:T(8,128)(2,1)}), bf16[2,8,128,512]{3,1,0,2:T(8,128)(2,1)S(1)}, u32[]{:S(2)}, u32[]{:S(2)}) async-start(bf16[2,8,128,512]{3,1,0,2:T(8,128)(2,1)} %copy.30), calls=%async_computation.1 | async-start | bytes 4194304 | tf_op jit(solution)/shard_map/all_to_all | solution.py:293
  65.1 17.1 %copy-start.3 = (s32[4,256]{1,0:T(4,128)S(1)}, s32[4,256]{1,0:T(4,128)}, u32[]{:S(2)}) copy-start(s32[4,256]{1,0:T(4,128)} %param.15) | copy-start | bytes 12292
  65.1 17.5 %copy-start.4 = (bf16[256,256,1]{1,0,2:T(8,128)(2,1)S(1)}, bf16[256,256,1]{1,0,2:T(8,128)(2,1)}, u32[]{:S(2)}) copy-start(bf16[256,256,1]{1,0,2:T(8,128)(2,1)} %constant.136) | copy-start | bytes 393220
  65.1 18.0 %copy-start.1 = (bf16[256,256,1]{1,0,2:T(8,128)(2,1)S(1)}, bf16[256,256,1]{1,0,2:T(8,128)(2,1)}, u32[]{:S(2)}) copy-start(bf16[256,256,1]{1,0,2:T(8,128)(2,1)} %constant.137) | copy-start | bytes 393220
  76.4 35.4 %all-to-all-start = ((bf16[2,8,128,512]{3,1,0,2:T(8,128)(2,1)}), bf16[2,8,128,512]{3,1,0,2:T(8,128)(2,1)}, u32[]{:S(2)}, u32[]{:S(2)}) async-start(bf16[2,8,128,512]{3,1,0,2:T(8,128)(2,1)} %copy.26), calls=%async_computation | async-start | bytes 4194304 | tf_op jit(solution)/shard_map/all_to_all | solution.py:293
  124.0 3.0 %collective-permute-start = (f32[64,256]{1,0:T(8,128)S(1)}, f32[64,256]{1,0:T(8,128)S(1)}, u32[]{:S(2)}, u32[]{:S(2)}) collective-permute-start(f32[64,256]{1,0:T(8,128)S(1)} %get-tuple-element.8), channel_id=1, source_target_pairs={{0,1},{1,0},{2,3},{3,2},{4,5},{5,4},{6,7},{7,6},{8,9},{9,8},{10,11... | collective-permute-start | bytes 196616 | tf_op jit(solution)/shard_map/ppermute | solution.py:304
  125.4 3.6 %collective-permute-start.1 = (f32[64,256]{1,0:T(8,128)S(1)}, f32[64,256]{1,0:T(8,128)S(1)}, u32[]{:S(2)}, u32[]{:S(2)}) collective-permute-start(f32[64,256]{1,0:T(8,128)S(1)} %get-tuple-element.7), channel_id=1, source_target_pairs={{0,2},{1,3},{2,0},{3,1},{4,6},{5,7},{6,4},{7,5},{8,10},{9,11},{10,... | collective-permute-start | bytes 196616 | tf_op jit(solution)/shard_map/ppermute | solution.py:304
  125.7 4.9 %collective-permute-start.2 = (f32[64,256]{1,0:T(8,128)S(1)}, f32[64,256]{1,0:T(8,128)S(1)}, u32[]{:S(2)}, u32[]{:S(2)}) collective-permute-start(f32[64,256]{1,0:T(8,128)S(1)} %get-tuple-element.6), channel_id=1, source_target_pairs={{0,3},{1,2},{2,1},{3,0},{4,7},{5,6},{6,5},{7,4},{8,11},{9,10},{10,... | collective-permute-start | bytes 196616 | tf_op jit(solution)/shard_map/ppermute | solution.py:304

commit v4 on v3

--- a/solution.py
+++ b/solution.py
@@ -225,9 +225,8 @@
     gains = jnp.take(gains, dest_e, axis=2)
     gains = jnp.concatenate([gains, gains], axis=3)
 
-    chunks = 2
-    pairs = FRAMES // 2 // chunks
-    chunk_lanes = pairs * 2 * quarter
+    chunk_pairs = [2, 3, 3]
+    chunk_starts = [sum(chunk_pairs[:c]) for c in range(len(chunk_pairs))]
     tables = beam_tables(grid_rows, grid_len, dish_rows)
     feed_index = jnp.arange(dish_count, dtype=jnp.int32)
     positions = jnp.arange(grid_len, dtype=jnp.int32)
@@ -239,8 +238,10 @@
     volts = voltages[:, 0].reshape(dish_rows, 2, samples // CHB, CHB)
 
     def channelize_chunk(chunk):
+        pairs = chunk_pairs[chunk]
+        chunk_lanes = pairs * 2 * quarter
         return pl.pallas_call(
-            functools.partial(channelize_kernel, chunk * pairs, pairs),
+            functools.partial(channelize_kernel, chunk_starts[chunk], pairs),
             grid=(dish_rows,),
             in_specs=[
                 pl.BlockSpec((1, 2, samples // CHB, CHB), lambda r: (r, 0, 0, 0)),
@@ -261,6 +262,7 @@
 
     def beamform_chunk(received, carried, finish):
         carry_in = carried is not None
+        chunk_lanes = received.shape[3]
         in_specs = [
             pl.BlockSpec((2, dish_rows, dests, lane_block), lambda f: (0, 0, 0, f)),
             pl.BlockSpec((dish_count, 2 * grid_len, 2 * grid_len), lambda f: (0, 0, 0)),
@@ -289,6 +291,7 @@
             ),
         )(*operands)
 
+    chunks = len(chunk_pairs)
     sent = [channelize_chunk(c) for c in range(chunks)]
     arrived = [lax.all_to_all(s, ("dish", "freq"), 2, 2, tiled=True) for s in sent]
     carried = None

time: 133 us -> 138 us (1.038)
  waiting for transfers between devices: 32.3 us -> 24.2 us
  Pallas kernels: 43 us -> 49.3 us
  starting transfers between devices: 20.3 us -> 25.1 us
    all_to_all x2 -> x3, waiting for transfers between devices: 28.8 us -> 21 us  [body(): lax.all_to_all(s, ('dish', 'freq'), 2, 2, tiled=True)]
    all_to_all x2 -> x3, starting transfers between devices: 17.2 us -> 22.3 us  [body(): lax.all_to_all(s, ('dish', 'freq'), 2, 2, tiled=True)]
    pallas_call x2 -> x3, Pallas kernels: 29 us -> 32.5 us  [channelize_chunk(): pl.pallas_call(functools.partial(channelize_kernel, chunk_starts[chunk],...]
    pallas_call x2 -> x3, Pallas kernels: 14 us -> 16.8 us  [beamform_chunk(): pl.pallas_call(functools.partial(beam_kernel, dish_count, carry_in, finis...]
    all_to_all x2 -> x3, local copies, waits for them, and re-layouts: 6.58 us -> 4.37 us  [body(): lax.all_to_all(s, ('dish', 'freq'), 2, 2, tiled=True)]
    pallas_call x2 -> x3, local copies, waits for them, and re-layouts: 8.19 us -> 9.79 us  [channelize_chunk(): pl.pallas_call(functools.partial(channelize_kernel, chunk_starts[chunk],...]
  transfers between devices with their start and end apart: 5 -> 6, of which waited for: 4 -> 5; matrix products, arithmetic and copies ran while one was open for 7% -> 9% of each run, Pallas kernels for 16% -> 25%
where the time goes in v4:
time: 138 us; the launch traced here: 136 us
  Pallas kernels  49.3 us (36%)
  local copies, waits for them, and re-layouts  31.7 us (23%)
  starting transfers between devices  25.1 us (18%)
  waiting for transfers between devices  24.2 us (18%)
  other arithmetic  4.97 us (4%)
    pallas_call x3, Pallas kernels, channelize_chunk(): pl.pallas_call(functools.partial(channelize_kernel, chunk_starts[chunk],...  32.5 us
    all_to_all x3, starting transfers between devices, body(): lax.all_to_all(s, ('dish', 'freq'), 2, 2, tiled=True)  22.3 us
    all_to_all x3, waiting for transfers between devices, body(): lax.all_to_all(s, ('dish', 'freq'), 2, 2, tiled=True)  21 us
    pallas_call x3, Pallas kernels, beamform_chunk(): pl.pallas_call(functools.partial(beam_kernel, dish_count, carry_in, finis...  16.8 us
    pallas_call x3, local copies, waits for them, and re-layouts, channelize_chunk(): pl.pallas_call(functools.partial(channelize_kernel, chunk_starts[chunk],...  9.79 us
    another operation x1, local copies, waits for them, and re-layouts, body(): volts = voltages[:, 0].reshape(dish_rows, 2, samples // CHB, CHB)  8.41 us
    all_to_all x3, local copies, waits for them, and re-layouts, body(): lax.all_to_all(s, ('dish', 'freq'), 2, 2, tiled=True)  4.37 us
    ppermute x3, waiting for transfers between devices, body(): pieces.append(lax.ppermute(outgoing, 'dish', pairs_list))  3.25 us
  transfers between devices with their start and end apart: 6, of which 5 were waited for; matrix products, arithmetic and copies ran while one was open for 9% of the time, Pallas kernels for 25%

profile of v4, /device:TPU:1, one launch (start us, length us, event | category | flops | bytes accessed | tf_op | source)
XLA Modules:
  0.0 136.4 jit_solution(12932200010296284783)
XLA Ops:
  1.9 1.8 %gather_fusion.1 = bf16[128,2,2,128]{3,2,1,0:T(2,128)(2,1)S(1)} fusion(bf16[2,2,128,128]{3,1,2,0:T(2,128)(2,1)} %constant.129.clone, s32[1024]{0:T(1024)S(1)} %pad_clamp_fusion.1), kind=kCustom, calls=%fused_computation.1 | custom fusion | bytes 262656 | tf_op jit(solution)/shard_map/jit(_take)/gather | solution.py:223
  6.8 1.4 %pad_maximum_fusion.g_ref = f32[8,2,128,128]{3,2,1,0:T(8,128)} fusion(f32[8,2,128,64]{3,2,1,0:T(8,128)S(1)} %fusion.2), kind=kLoop, calls=%fused_computation.9 | loop fusion | flops 262144 | bytes 1572864 | tf_op jit(solution)/shard_map/concatenate | solution.py:226
  8.2 8.4 %reshape_squeeze.4.v_ref = bf16[8,2,1216,128]{3,2,1,0:T(8,128)(2,1)} reshape(bf16[8,1,2,155648]{3,2,1,0:T(2,128)(2,1)} %param.12) | data formatting | bytes 9961472 | tf_op jit(solution)/shard_map/reshape;squeeze | solution.py:238
  17.4 9.5 %shard_map.120 = bf16[2,8,128,256]{3,2,1,0:T(8,128)(2,1)} custom-call(bf16[8,2,1216,128]{3,2,1,0:T(8,128)(2,1)} %reshape_squeeze.4.v_ref, f32[4,64,128]{2,1,0:T(8,128)} %constant.126.clone.w_ref, bf16[128,128]{1,0:T(8,128)(2,1)} %constant.127.clone.t1_ref, f32[2,64,128]{2,1,0:T(8,128)} %constant.128.clone.tw_ref, ...), custom_call_target="tpu_custom_call" | custom-call | flops 402653184 | bytes 6029312 | tf_op jit(solution)/shard_map/pallas_call | solution.py:243
  26.8 2.8 %copy.31 = bf16[2,8,128,256]{3,1,0,2:T(8,128)(2,1)} copy(bf16[2,8,128,256]{3,2,1,0:T(8,128)(2,1)} %shard_map.120) | data formatting | bytes 2097152 | tf_op jit(solution)/shard_map/pallas_call | solution.py:243
  29.6 11.5 %all-to-all-start.2 = ((bf16[2,8,128,256]{3,1,0,2:T(8,128)(2,1)}), bf16[2,8,128,256]{3,1,0,2:T(8,128)(2,1)S(1)}, u32[]{:S(2)}, u32[]{:S(2)}) async-start(bf16[2,8,128,256]{3,1,0,2:T(8,128)(2,1)} %copy.31), calls=%async_computation.2 | async-start | bytes 2097152 | tf_op jit(solution)/shard_map/all_to_all | solution.py:296
  41.1 11.5 %shard_map.119 = bf16[2,8,128,384]{3,2,1,0:T(8,128)(2,1)} custom-call(bf16[8,2,1216,128]{3,2,1,0:T(8,128)(2,1)} %reshape_squeeze.4.v_ref, f32[4,64,128]{2,1,0:T(8,128)} %constant.126.clone.w_ref, bf16[128,128]{1,0:T(8,128)(2,1)} %constant.127.clone.t1_ref, f32[2,64,128]{2,1,0:T(8,128)} %constant.128.clone.tw_ref, ...), custom_call_target="tpu_custom_call" | custom-call | flops 603979776 | bytes 6553600 | tf_op jit(solution)/shard_map/pallas_call | solution.py:243
  52.6 3.5 %copy.30 = bf16[2,8,128,384]{3,1,0,2:T(8,128)(2,1)} copy(bf16[2,8,128,384]{3,2,1,0:T(8,128)(2,1)} %shard_map.119) | data formatting | bytes 3145728 | tf_op jit(solution)/shard_map/pallas_call | solution.py:243
  56.1 3.8 %all-to-all-done.2 = bf16[2,8,128,256]{3,1,0,2:T(8,128)(2,1)S(1)} async-done(((bf16[2,8,128,256]{3,1,0,2:T(8,128)(2,1)}), bf16[2,8,128,256]{3,1,0,2:T(8,128)(2,1)S(1)}, u32[]{:S(2)}, u32[]{:S(2)}) %all-to-all-start.2) | async-done | bytes 1048608 | tf_op jit(solution)/shard_map/all_to_all | solution.py:296
  60.9 6.0 %all-to-all-start.1 = ((bf16[2,8,128,384]{3,1,0,2:T(8,128)(2,1)}), bf16[2,8,128,384]{3,1,0,2:T(8,128)(2,1)S(1)}, u32[]{:S(2)}, u32[]{:S(2)}) async-start(bf16[2,8,128,384]{3,1,0,2:T(8,128)(2,1)} %copy.30), calls=%async_computation.1 | async-start | bytes 3145728 | tf_op jit(solution)/shard_map/all_to_all | solution.py:296
  66.9 11.5 %shard_map.118 = bf16[2,8,128,384]{3,2,1,0:T(8,128)(2,1)} custom-call(bf16[8,2,1216,128]{3,2,1,0:T(8,128)(2,1)} %reshape_squeeze.4.v_ref, f32[4,64,128]{2,1,0:T(8,128)} %constant.126.clone.w_ref, bf16[128,128]{1,0:T(8,128)(2,1)} %constant.127.clone.t1_ref, f32[2,64,128]{2,1,0:T(8,128)} %constant.128.clone.tw_ref, ...), custom_call_target="tpu_custom_call" | custom-call | flops 603979776 | bytes 6553600 | tf_op jit(solution)/shard_map/pallas_call | solution.py:243
  78.4 3.5 %copy.26 = bf16[2,8,128,384]{3,1,0,2:T(8,128)(2,1)} copy(bf16[2,8,128,384]{3,2,1,0:T(8,128)(2,1)} %shard_map.118) | data formatting | bytes 3145728 | tf_op jit(solution)/shard_map/pallas_call | solution.py:243
  81.9 9.3 %all-to-all-done.1 = bf16[2,8,128,384]{3,1,0,2:T(8,128)(2,1)S(1)} async-done(((bf16[2,8,128,384]{3,1,0,2:T(8,128)(2,1)}), bf16[2,8,128,384]{3,1,0,2:T(8,128)(2,1)S(1)}, u32[]{:S(2)}, u32[]{:S(2)}) %all-to-all-start.1) | async-done | bytes 1572896 | tf_op jit(solution)/shard_map/all_to_all | solution.py:296
  91.1 4.8 %all-to-all-start = ((bf16[2,8,128,384]{3,1,0,2:T(8,128)(2,1)}), bf16[2,8,128,384]{3,1,0,2:T(8,128)(2,1)S(1)}, u32[]{:S(2)}, u32[]{:S(2)}) async-start(bf16[2,8,128,384]{3,1,0,2:T(8,128)(2,1)} %copy.26), calls=%async_computation | async-start | bytes 3145728 | tf_op jit(solution)/shard_map/all_to_all | solution.py:296
  97.3 1.5 %maximum_maximum_fusion.refs_1_ = bf16[4,512,512]{2,1,0:T(8,128)(2,1)} fusion(bf16[4,256,256]{2,1,0:T(8,128)(2,1)S(1)} %fusion, bf16[4,256,256]{2,1,0:T(8,128)(2,1)S(1)} %get-tuple-element.9, bf16[4,256,256]{2,1,0:T(8,128)(2,1)S(1)} %get-tuple-element.10), kind=kLoop, calls=%fused_computation.4 | loop fusion | flops 8388608 | bytes 3670016 | tf_op jit(solution)/shard_map/concatenate | solution.py:86
  100.1 4.7 %shard_map.121.refs_4_ = f32[4,256,128]{2,1,0:T(8,128)} custom-call(bf16[2,8,128,256]{3,2,1,0:T(8,128)(2,1)} %copy.32.refs_0_, bf16[4,512,512]{2,1,0:T(8,128)(2,1)} %maximum_maximum_fusion.refs_1_, f32[4,256,1]{2,1,0:T(8,128)} %constant.132.clone.refs_2_, f32[4,256,1]{2,1,0:T(8,128)} %constant.133.clone.refs_3_), custom_call_target="tpu_custom_call" | custom-call | flops 536870912 | bytes 3145728 | tf_op jit(solution)/shard_map/pallas_call | solution.py:280
  104.9 1.5 %copy.33.refs_0_ = bf16[2,8,128,384]{3,2,1,0:T(8,128)(2,1)} copy(bf16[2,8,128,384]{3,1,0,2:T(8,128)(2,1)S(1)} %all-to-all-done.1) | data formatting | bytes 3145728 | tf_op jit(solution)/shard_map/all_to_all | solution.py:296
  106.4 5.9 %shard_map.122.refs_4_ = f32[4,256,128]{2,1,0:T(8,128)} custom-call(bf16[2,8,128,384]{3,2,1,0:T(8,128)(2,1)} %copy.33.refs_0_, bf16[4,512,512]{2,1,0:T(8,128)(2,1)} %maximum_maximum_fusion.refs_1_, f32[4,256,1]{2,1,0:T(8,128)} %constant.132.clone.refs_2_, f32[4,256,1]{2,1,0:T(8,128)} %constant.133.clone.refs_3_, f32[4,256,128]{2,1,0:T(8,128)} %shard_map.121.refs_4_), custom_call_target="tpu_custom_call" | custom-call | flops 805306368 | bytes 3670016 | tf_op jit(solution)/shard_map/pallas_call | solution.py:280
  112.3 8.0 %all-to-all-done = bf16[2,8,128,384]{3,1,0,2:T(8,128)(2,1)S(1)} async-done(((bf16[2,8,128,384]{3,1,0,2:T(8,128)(2,1)}), bf16[2,8,128,384]{3,1,0,2:T(8,128)(2,1)S(1)}, u32[]{:S(2)}, u32[]{:S(2)}) %all-to-all-start) | async-done | bytes 1572896 | tf_op jit(solution)/shard_map/all_to_all | solution.py:296
  120.3 1.5 %copy.34.refs_0_ = bf16[2,8,128,384]{3,2,1,0:T(8,128)(2,1)} copy(bf16[2,8,128,384]{3,1,0,2:T(8,128)(2,1)S(1)} %all-to-all-done) | data formatting | bytes 3145728 | tf_op jit(solution)/shard_map/all_to_all | solution.py:296
  121.8 6.1 %shard_map.123 = f32[4,64,256]{2,1,0:T(8,128)} custom-call(bf16[2,8,128,384]{3,2,1,0:T(8,128)(2,1)} %copy.34.refs_0_, bf16[4,512,512]{2,1,0:T(8,128)(2,1)} %maximum_maximum_fusion.refs_1_, f32[4,256,1]{2,1,0:T(8,128)} %constant.132.clone.refs_2_, f32[4,256,1]{2,1,0:T(8,128)} %constant.133.clone.refs_3_, f32[4,256,128]{2,1,0:T(8,128)} %shard_map.122.refs_4_), custom_call_target="tpu_custom_call" | custom-call | flops 805306368 | bytes 3670016 | tf_op jit(solution)/shard_map/pallas_call | solution.py:280
  128.9 1.6 %collective-permute-start.2 = (f32[64,256]{1,0:T(8,128)S(1)}, f32[64,256]{1,0:T(8,128)S(1)}, u32[]{:S(2)}, u32[]{:S(2)}) collective-permute-start(f32[64,256]{1,0:T(8,128)S(1)} %get-tuple-element.6), channel_id=1, source_target_pairs={{0,3},{1,2},{2,1},{3,0},{4,7},{5,6},{6,5},{7,4},{8,11},{9,10},{10,... | collective-permute-start | bytes 196616 | tf_op jit(solution)/shard_map/ppermute | solution.py:307
  131.7 1.4 collective-permute-done.2
  133.1 1.9 %collective-permute-done.1 = f32[64,256]{1,0:T(8,128)S(1)} collective-permute-done((f32[64,256]{1,0:T(8,128)S(1)}, f32[64,256]{1,0:T(8,128)S(1)}, u32[]{:S(2)}, u32[]{:S(2)}) %collective-permute-start.1) | collective-permute-done | bytes 65568 | tf_op jit(solution)/shard_map/ppermute | solution.py:307
  (43 shorter events, 12.8 us)
Async XLA Ops:
  0.0 0.7 copy-start
  29.6 30.3 %all-to-all-start.2 = ((bf16[2,8,128,256]{3,1,0,2:T(8,128)(2,1)}), bf16[2,8,128,256]{3,1,0,2:T(8,128)(2,1)S(1)}, u32[]{:S(2)}, u32[]{:S(2)}) async-start(bf16[2,8,128,256]{3,1,0,2:T(8,128)(2,1)} %copy.31), calls=%async_computation.2 | async-start | bytes 2097152 | tf_op jit(solution)/shard_map/all_to_all | solution.py:296
  59.9 1.0 copy-start.1
  60.9 30.3 %all-to-all-start.1 = ((bf16[2,8,128,384]{3,1,0,2:T(8,128)(2,1)}), bf16[2,8,128,384]{3,1,0,2:T(8,128)(2,1)S(1)}, u32[]{:S(2)}, u32[]{:S(2)}) async-start(bf16[2,8,128,384]{3,1,0,2:T(8,128)(2,1)} %copy.30), calls=%async_computation.1 | async-start | bytes 3145728 | tf_op jit(solution)/shard_map/all_to_all | solution.py:296
  81.9 14.3 %copy-start.4 = (s32[4,256]{1,0:T(4,128)S(1)}, s32[4,256]{1,0:T(4,128)}, u32[]{:S(2)}) copy-start(s32[4,256]{1,0:T(4,128)} %param.15) | copy-start | bytes 12292
  81.9 14.5 %copy-start.5 = (bf16[256,256,1]{1,0,2:T(8,128)(2,1)S(1)}, bf16[256,256,1]{1,0,2:T(8,128)(2,1)}, u32[]{:S(2)}) copy-start(bf16[256,256,1]{1,0,2:T(8,128)(2,1)} %constant.136) | copy-start | bytes 393220
  81.9 15.0 %copy-start.3 = (bf16[256,256,1]{1,0,2:T(8,128)(2,1)S(1)}, bf16[256,256,1]{1,0,2:T(8,128)(2,1)}, u32[]{:S(2)}) copy-start(bf16[256,256,1]{1,0,2:T(8,128)(2,1)} %constant.137) | copy-start | bytes 393220
  91.1 29.2 %all-to-all-start = ((bf16[2,8,128,384]{3,1,0,2:T(8,128)(2,1)}), bf16[2,8,128,384]{3,1,0,2:T(8,128)(2,1)S(1)}, u32[]{:S(2)}, u32[]{:S(2)}) async-start(bf16[2,8,128,384]{3,1,0,2:T(8,128)(2,1)} %copy.26), calls=%async_computation | async-start | bytes 3145728 | tf_op jit(solution)/shard_map/all_to_all | solution.py:296
  97.3 1.5 %copy-start.2 = (bf16[2,8,128,256]{3,1,0,2:T(8,128)(2,1)S(1)}, bf16[2,8,128,256]{3,1,0,2:T(8,128)(2,1)}, u32[]{:S(2)}) copy-start(bf16[2,8,128,256]{3,1,0,2:T(8,128)(2,1)} %copy-done.1) | copy-start | bytes 3145732
  128.9 4.2 %collective-permute-start.2 = (f32[64,256]{1,0:T(8,128)S(1)}, f32[64,256]{1,0:T(8,128)S(1)}, u32[]{:S(2)}, u32[]{:S(2)}) collective-permute-start(f32[64,256]{1,0:T(8,128)S(1)} %get-tuple-element.6), channel_id=1, source_target_pairs={{0,3},{1,2},{2,1},{3,0},{4,7},{5,6},{6,5},{7,4},{8,11},{9,10},{10,... | collective-permute-start | bytes 196616 | tf_op jit(solution)/shard_map/ppermute | solution.py:307
  130.5 4.4 %collective-permute-start.1 = (f32[64,256]{1,0:T(8,128)S(1)}, f32[64,256]{1,0:T(8,128)S(1)}, u32[]{:S(2)}, u32[]{:S(2)}) collective-permute-start(f32[64,256]{1,0:T(8,128)S(1)} %get-tuple-element.7), channel_id=1, source_target_pairs={{0,2},{1,3},{2,0},{3,1},{4,6},{5,7},{6,4},{7,5},{8,10},{9,11},{10,... | collective-permute-start | bytes 196616 | tf_op jit(solution)/shard_map/ppermute | solution.py:307
  131.7 3.3 %collective-permute-start = (f32[64,256]{1,0:T(8,128)S(1)}, f32[64,256]{1,0:T(8,128)S(1)}, u32[]{:S(2)}, u32[]{:S(2)}) collective-permute-start(f32[64,256]{1,0:T(8,128)S(1)} %get-tuple-element.8), channel_id=1, source_target_pairs={{0,1},{1,0},{2,3},{3,2},{4,5},{5,4},{6,7},{7,6},{8,9},{9,8},{10,11... | collective-permute-start | bytes 196616 | tf_op jit(solution)/shard_map/ppermute | solution.py:307

commit v5 on v3

--- a/solution.py
+++ b/solution.py
@@ -99,7 +99,7 @@
     def one_frame(frame):
         acc = None
         for tap in range(TAPS):
-            start = pl.multiple_of((frame + tap) * CHA, CHA)
+            start = pl.multiple_of((frame - 2 * first_pair + tap) * CHA, CHA)
             piece = v_ref[0, :, pl.ds(start, CHA), :].astype(jnp.float32)
             term = w_ref[tap][None] * piece
             acc = term if acc is None else acc + term
@@ -207,8 +207,9 @@
 
     dest = jnp.arange(dests, dtype=jnp.int32)
     dest_quarter = dest // block_count
-    dest_block = jnp.take(block_assign, dest % block_count)
+    dest_block = jnp.tile(block_assign, dish_count)
     dest_e = dest_block * dish_count + dest_quarter
+    picks_e = (dest_e[:, None] == jnp.arange(dests, dtype=jnp.int32)[None, :]).astype(jnp.bfloat16)
 
     window = jnp.asarray(window_constant().reshape(TAPS, CHA, CHB))
     first_cos, first_sin = table_constant(CHA, CHA, CHA, 1.0 / math.sqrt(CHA))
@@ -220,9 +221,11 @@
         [np.stack([second_cos, -second_sin], axis=0), np.stack([second_sin, second_cos], axis=0)],
         axis=0,
     )
-    second_table = jnp.take(jnp.asarray(second_table), dest_e, axis=2).reshape(2, 2 * dests, CHB)
-    gains = feed_gains[:, 0].reshape(dish_rows, 2, CHB, CHA).astype(jnp.float32)
-    gains = jnp.take(gains, dest_e, axis=2)
+    second_table = jnp.einsum(
+        "je,qseb->qsjb", picks_e, jnp.asarray(second_table), preferred_element_type=jnp.float32
+    ).astype(jnp.bfloat16).reshape(2, 2 * dests, CHB)
+    gains = feed_gains[:, 0].reshape(dish_rows, 2, CHB, CHA)
+    gains = jnp.einsum("je,rpec->rpjc", picks_e, gains, preferred_element_type=jnp.float32)
     gains = jnp.concatenate([gains, gains], axis=3)
 
     chunks = 2
@@ -238,12 +241,18 @@
 
     volts = voltages[:, 0].reshape(dish_rows, 2, samples // CHB, CHB)
 
+    span = (2 * pairs + TAPS - 1) * CHA
+
     def channelize_chunk(chunk):
+        first_row = 2 * chunk * pairs * CHA
         return pl.pallas_call(
             functools.partial(channelize_kernel, chunk * pairs, pairs),
             grid=(dish_rows,),
             in_specs=[
-                pl.BlockSpec((1, 2, samples // CHB, CHB), lambda r: (r, 0, 0, 0)),
+                pl.BlockSpec(
+                    (pl.Element(1), pl.Element(2), pl.Element(span), pl.Element(CHB)),
+                    lambda r: (r, 0, first_row, 0),
+                ),
                 pl.BlockSpec((TAPS, CHA, CHB), lambda r: (0, 0, 0)),
                 pl.BlockSpec((2 * CHA, 2 * CHA), lambda r: (0, 0)),
                 pl.BlockSpec((2, CHA, CHB), lambda r: (0, 0, 0)),

time: 133 us -> 127 us (0.955)
  local copies, waits for them, and re-layouts: 30.5 us -> 25.6 us
    gather x4 -> x0, local copies, waits for them, and re-layouts: 2.83 us -> none  [the longest x1 1.22 us: body(): dest_block = jnp.take(block_assign, dest % block_count)]
    convert_element_type x2 -> x0, local copies, waits for them, and re-layouts: 1.88 us -> none  [body(): gains = feed_gains[:, 0].reshape(dish_rows, 2, CHB, CHA).astype(jnp.float32)]
  transfers between devices with their start and end apart: 5 -> 5, of which waited for: 4 -> 4; matrix products, arithmetic and copies ran while one was open for 7% -> 7% of each run, Pallas kernels for 16% -> 17%
where the time goes in v5:
time: 127 us; the launch traced here: 126 us
  Pallas kernels  42.9 us (34%)
  waiting for transfers between devices  32.1 us (25%)
  local copies, waits for them, and re-layouts  25.6 us (20%)
  starting transfers between devices  19.9 us (16%)
  other arithmetic  3.69 us (3%)
  matrix products  2.09 us (2%)
    pallas_call x2, Pallas kernels, channelize_chunk(): pl.pallas_call(functools.partial(channelize_kernel, chunk * pairs, pairs)...  28.9 us
    all_to_all x2, waiting for transfers between devices, body(): lax.all_to_all(s, ('dish', 'freq'), 2, 2, tiled=True)  28.9 us
    all_to_all x2, starting transfers between devices, body(): lax.all_to_all(s, ('dish', 'freq'), 2, 2, tiled=True)  17.2 us
    pallas_call x2, Pallas kernels, beamform_chunk(): pl.pallas_call(functools.partial(beam_kernel, dish_count, carry_in, finis...  14 us
    another operation x1, local copies, waits for them, and re-layouts, body(): volts = voltages[:, 0].reshape(dish_rows, 2, samples // CHB, CHB)  8.46 us
    pallas_call x2, local copies, waits for them, and re-layouts, channelize_chunk(): pl.pallas_call(functools.partial(channelize_kernel, chunk * pairs, pairs)...  8.21 us
    all_to_all x2, local copies, waits for them, and re-layouts, body(): lax.all_to_all(s, ('dish', 'freq'), 2, 2, tiled=True)  6.59 us
    ppermute x3, waiting for transfers between devices, body(): pieces.append(lax.ppermute(outgoing, 'dish', pairs_list))  3.25 us
  transfers between devices with their start and end apart: 5, of which 4 were waited for; matrix products, arithmetic and copies ran while one was open for 7% of the time, Pallas kernels for 17%

profile of v5, /device:TPU:1, one launch (start us, length us, event | category | flops | bytes accessed | tf_op | source)
XLA Modules:
  0.0 126.5 jit_solution(13426791769914089486)
XLA Ops:
  0.0 8.5 %reshape_squeeze.6.v_ref = bf16[8,2,1216,128]{3,2,1,0:T(8,128)(2,1)} reshape(bf16[8,1,2,155648]{3,2,1,0:T(2,128)(2,1)} %param.12) | data formatting | bytes 9961472 | tf_op jit(solution)/shard_map/reshape;squeeze | solution.py:242
  8.9 0.9 convolution_convert_fusion.2
  10.2 1.3 %pad_maximum_fusion.g_ref = f32[8,2,128,128]{3,2,1,0:T(8,128)} fusion(f32[8,2,128,64]{3,2,1,0:T(8,128)S(1)} %convolution_bitcast_fusion), kind=kLoop, calls=%fused_computation.8 | loop fusion | flops 262144 | bytes 1572864 | tf_op jit(solution)/shard_map/concatenate | solution.py:229
  11.5 14.4 %shard_map.119 = bf16[2,8,128,512]{3,2,1,0:T(8,128)(2,1)} custom-call(bf16[8,2,1216,128]{3,2,1,0:T(8,128)(2,1)} %reshape_squeeze.6.v_ref, f32[4,64,128]{2,1,0:T(8,128)} %constant.68.clone.w_ref, bf16[128,128]{1,0:T(8,128)(2,1)} %constant.69.clone.t1_ref, f32[2,64,128]{2,1,0:T(8,128)} %constant.70.clone.tw_ref, bf16[2,256,128]{2,1,0:T(8,128)(2,1)} %bitcast.35, ...), custom_call_target="tpu_custom_call" | custom-call | flops 805306368 | bytes 7077888 | tf_op jit(solution)/shard_map/pallas_call | solution.py:248
  25.9 4.1 %copy.30 = bf16[2,8,128,512]{3,1,0,2:T(8,128)(2,1)} copy(bf16[2,8,128,512]{3,2,1,0:T(8,128)(2,1)} %shard_map.119) | data formatting | bytes 4194304 | tf_op jit(solution)/shard_map/pallas_call | solution.py:248
  30.1 11.5 %all-to-all-start.1 = ((bf16[2,8,128,512]{3,1,0,2:T(8,128)(2,1)}), bf16[2,8,128,512]{3,1,0,2:T(8,128)(2,1)S(1)}, u32[]{:S(2)}, u32[]{:S(2)}) async-start(bf16[2,8,128,512]{3,1,0,2:T(8,128)(2,1)} %copy.30), calls=%async_computation.1 | async-start | bytes 4194304 | tf_op jit(solution)/shard_map/all_to_all | solution.py:302
  41.6 14.5 %shard_map.118 = bf16[2,8,128,512]{3,2,1,0:T(8,128)(2,1)} custom-call(bf16[8,2,1216,128]{3,2,1,0:T(8,128)(2,1)} %reshape_squeeze.6.v_ref, f32[4,64,128]{2,1,0:T(8,128)} %constant.68.clone.w_ref, bf16[128,128]{1,0:T(8,128)(2,1)} %constant.69.clone.t1_ref, f32[2,64,128]{2,1,0:T(8,128)} %constant.70.clone.tw_ref, bf16[2,256,128]{2,1,0:T(8,128)(2,1)} %bitcast.36, ...), custom_call_target="tpu_custom_call" | custom-call | flops 805306368 | bytes 7077888 | tf_op jit(solution)/shard_map/pallas_call | solution.py:248
  56.0 4.1 %copy.26 = bf16[2,8,128,512]{3,1,0,2:T(8,128)(2,1)} copy(bf16[2,8,128,512]{3,2,1,0:T(8,128)(2,1)} %shard_map.118) | data formatting | bytes 4194304 | tf_op jit(solution)/shard_map/pallas_call | solution.py:248
  60.1 11.3 %all-to-all-done.1 = bf16[2,8,128,512]{3,1,0,2:T(8,128)(2,1)S(1)} async-done(((bf16[2,8,128,512]{3,1,0,2:T(8,128)(2,1)}), bf16[2,8,128,512]{3,1,0,2:T(8,128)(2,1)S(1)}, u32[]{:S(2)}, u32[]{:S(2)}) %all-to-all-start.1) | async-done | bytes 2097184 | tf_op jit(solution)/shard_map/all_to_all | solution.py:302
  71.5 5.7 %all-to-all-start = ((bf16[2,8,128,512]{3,1,0,2:T(8,128)(2,1)}), bf16[2,8,128,512]{3,1,0,2:T(8,128)(2,1)}, u32[]{:S(2)}, u32[]{:S(2)}) async-start(bf16[2,8,128,512]{3,1,0,2:T(8,128)(2,1)} %copy.26), calls=%async_computation | async-start | bytes 4194304 | tf_op jit(solution)/shard_map/all_to_all | solution.py:302
  77.7 0.4 fusion
  78.5 1.5 %maximum_maximum_fusion.refs_1_ = bf16[4,512,512]{2,1,0:T(8,128)(2,1)} fusion(bf16[4,256,256]{2,1,0:T(8,128)(2,1)S(1)} %fusion, bf16[4,256,256]{2,1,0:T(8,128)(2,1)S(1)} %get-tuple-element.9, bf16[4,256,256]{2,1,0:T(8,128)(2,1)S(1)} %get-tuple-element.10), kind=kLoop, calls=%fused_computation.1 | loop fusion | flops 8388608 | bytes 3670016 | tf_op jit(solution)/shard_map/concatenate | solution.py:86
  80.1 2.5 %copy.31.refs_0_ = bf16[2,8,128,512]{3,2,1,0:T(8,128)(2,1)} copy(bf16[2,8,128,512]{3,1,0,2:T(8,128)(2,1)S(1)} %all-to-all-done.1) | data formatting | bytes 4194304 | tf_op jit(solution)/shard_map/all_to_all | solution.py:302
  82.6 6.8 %shard_map.120.refs_4_ = f32[4,256,128]{2,1,0:T(8,128)} custom-call(bf16[2,8,128,512]{3,2,1,0:T(8,128)(2,1)} %copy.31.refs_0_, bf16[4,512,512]{2,1,0:T(8,128)(2,1)} %maximum_maximum_fusion.refs_1_, f32[4,256,1]{2,1,0:T(8,128)} %constant.74.clone.refs_2_, f32[4,256,1]{2,1,0:T(8,128)} %constant.75.clone.refs_3_), custom_call_target="tpu_custom_call" | custom-call | flops 1073741824 | bytes 4194304 | tf_op jit(solution)/shard_map/pallas_call | solution.py:287
  89.3 17.5 %all-to-all-done = bf16[2,8,128,512]{3,1,0,2:T(8,128)(2,1)} async-done(((bf16[2,8,128,512]{3,1,0,2:T(8,128)(2,1)}), bf16[2,8,128,512]{3,1,0,2:T(8,128)(2,1)}, u32[]{:S(2)}, u32[]{:S(2)}) %all-to-all-start) | async-done | bytes 2097184 | tf_op jit(solution)/shard_map/all_to_all | solution.py:302
  106.9 4.1 %copy.32.refs_0_ = bf16[2,8,128,512]{3,2,1,0:T(8,128)(2,1)} copy(bf16[2,8,128,512]{3,1,0,2:T(8,128)(2,1)} %all-to-all-done) | data formatting | bytes 4194304 | tf_op jit(solution)/shard_map/all_to_all | solution.py:302
  111.0 7.2 %shard_map.121 = f32[4,64,256]{2,1,0:T(8,128)} custom-call(bf16[2,8,128,512]{3,2,1,0:T(8,128)(2,1)} %copy.32.refs_0_, bf16[4,512,512]{2,1,0:T(8,128)(2,1)} %maximum_maximum_fusion.refs_1_, f32[4,256,1]{2,1,0:T(8,128)} %constant.74.clone.refs_2_, f32[4,256,1]{2,1,0:T(8,128)} %constant.75.clone.refs_3_, f32[4,256,128]{2,1,0:T(8,128)} %shard_map.120.refs_4_), custom_call_target="tpu_custom_call" | custom-call | flops 1073741824 | bytes 4194304 | tf_op jit(solution)/shard_map/pallas_call | solution.py:287
  118.2 1.0 constant_dynamic-slice_fusion
  119.1 1.5 %collective-permute-start.2 = (f32[64,256]{1,0:T(8,128)S(1)}, f32[64,256]{1,0:T(8,128)S(1)}, u32[]{:S(2)}, u32[]{:S(2)}) collective-permute-start(f32[64,256]{1,0:T(8,128)S(1)} %get-tuple-element.6), channel_id=1, source_target_pairs={{0,3},{1,2},{2,1},{3,0},{4,7},{5,6},{6,5},{7,4},{8,11},{9,10},{10,... | collective-permute-start | bytes 196616 | tf_op jit(solution)/shard_map/ppermute | solution.py:313
  120.6 1.2 collective-permute-start.1
  121.8 1.6 %collective-permute-done.2 = f32[64,256]{1,0:T(8,128)S(1)} collective-permute-done((f32[64,256]{1,0:T(8,128)S(1)}, f32[64,256]{1,0:T(8,128)S(1)}, u32[]{:S(2)}, u32[]{:S(2)}) %collective-permute-start.2) | collective-permute-done | bytes 65568 | tf_op jit(solution)/shard_map/ppermute | solution.py:313
  123.4 1.6 %collective-permute-done.1 = f32[64,256]{1,0:T(8,128)S(1)} collective-permute-done((f32[64,256]{1,0:T(8,128)S(1)}, f32[64,256]{1,0:T(8,128)S(1)}, u32[]{:S(2)}, u32[]{:S(2)}) %collective-permute-start.1) | collective-permute-done | bytes 65568 | tf_op jit(solution)/shard_map/ppermute | solution.py:313
  125.1 0.6 gather_fusion
  125.7 0.8 bitcast_select_fusion
  (30 shorter events, 1.7 us)
Async XLA Ops:
  0.0 8.9 %copy-start.2 = (bf16[2,2,128,128]{3,2,1,0:T(8,128)(2,1)S(1)}, bf16[2,2,128,128]{3,2,1,0:T(8,128)(2,1)}, u32[]{:S(2)}) copy-start(bf16[2,2,128,128]{3,2,1,0:T(8,128)(2,1)} %constant.71.clone) | copy-start | bytes 393220
  0.0 8.5 %copy-start.4 = (s32[32]{0:T(128)S(1)}, s32[32]{0:T(128)}, u32[]{:S(2)}) copy-start(s32[32]{0:T(128)} %param.14) | copy-start | bytes 388
  0.0 8.6 %copy-start = (bf16[8,1,2,8192]{3,2,1,0:T(2,128)(2,1)S(1)}, bf16[8,1,2,8192]{3,2,1,0:T(2,128)(2,1)}, u32[]{:S(2)}) copy-start(bf16[8,1,2,8192]{3,2,1,0:T(2,128)(2,1)} %param.13) | copy-start | bytes 786436
  30.1 41.4 %all-to-all-start.1 = ((bf16[2,8,128,512]{3,1,0,2:T(8,128)(2,1)}), bf16[2,8,128,512]{3,1,0,2:T(8,128)(2,1)S(1)}, u32[]{:S(2)}, u32[]{:S(2)}) async-start(bf16[2,8,128,512]{3,1,0,2:T(8,128)(2,1)} %copy.30), calls=%async_computation.1 | async-start | bytes 4194304 | tf_op jit(solution)/shard_map/all_to_all | solution.py:302
  60.1 17.1 %copy-start.3 = (s32[4,256]{1,0:T(4,128)S(1)}, s32[4,256]{1,0:T(4,128)}, u32[]{:S(2)}) copy-start(s32[4,256]{1,0:T(4,128)} %param.15) | copy-start | bytes 12292
  60.1 17.5 %copy-start.5 = (bf16[256,256,1]{1,0,2:T(8,128)(2,1)S(1)}, bf16[256,256,1]{1,0,2:T(8,128)(2,1)}, u32[]{:S(2)}) copy-start(bf16[256,256,1]{1,0,2:T(8,128)(2,1)} %constant.78) | copy-start | bytes 393220
  60.1 18.0 %copy-start.1 = (bf16[256,256,1]{1,0,2:T(8,128)(2,1)S(1)}, bf16[256,256,1]{1,0,2:T(8,128)(2,1)}, u32[]{:S(2)}) copy-start(bf16[256,256,1]{1,0,2:T(8,128)(2,1)} %constant.79) | copy-start | bytes 393220
  71.5 35.4 %all-to-all-start = ((bf16[2,8,128,512]{3,1,0,2:T(8,128)(2,1)}), bf16[2,8,128,512]{3,1,0,2:T(8,128)(2,1)}, u32[]{:S(2)}, u32[]{:S(2)}) async-start(bf16[2,8,128,512]{3,1,0,2:T(8,128)(2,1)} %copy.26), calls=%async_computation | async-start | bytes 4194304 | tf_op jit(solution)/shard_map/all_to_all | solution.py:302
  119.1 4.3 %collective-permute-start.2 = (f32[64,256]{1,0:T(8,128)S(1)}, f32[64,256]{1,0:T(8,128)S(1)}, u32[]{:S(2)}, u32[]{:S(2)}) collective-permute-start(f32[64,256]{1,0:T(8,128)S(1)} %get-tuple-element.6), channel_id=1, source_target_pairs={{0,3},{1,2},{2,1},{3,0},{4,7},{5,6},{6,5},{7,4},{8,11},{9,10},{10,... | collective-permute-start | bytes 196616 | tf_op jit(solution)/shard_map/ppermute | solution.py:313
  120.6 4.4 %collective-permute-start.1 = (f32[64,256]{1,0:T(8,128)S(1)}, f32[64,256]{1,0:T(8,128)S(1)}, u32[]{:S(2)}, u32[]{:S(2)}) collective-permute-start(f32[64,256]{1,0:T(8,128)S(1)} %get-tuple-element.7), channel_id=1, source_target_pairs={{0,2},{1,3},{2,0},{3,1},{4,6},{5,7},{6,4},{7,5},{8,10},{9,11},{10,... | collective-permute-start | bytes 196616 | tf_op jit(solution)/shard_map/ppermute | solution.py:313
  121.8 3.3 %collective-permute-start = (f32[64,256]{1,0:T(8,128)S(1)}, f32[64,256]{1,0:T(8,128)S(1)}, u32[]{:S(2)}, u32[]{:S(2)}) collective-permute-start(f32[64,256]{1,0:T(8,128)S(1)} %get-tuple-element.8), channel_id=1, source_target_pairs={{0,1},{1,0},{2,3},{3,2},{4,5},{5,4},{6,7},{7,6},{8,9},{9,8},{10,11... | collective-permute-start | bytes 196616 | tf_op jit(solution)/shard_map/ppermute | solution.py:313

commit v6 on v5

--- a/solution.py
+++ b/solution.py
@@ -71,19 +71,20 @@
     cosine_base = jnp.asarray(cosine_base)
     sine_base = jnp.asarray(sine_base)
     devices = grid_len // rows_per_device
-    ordered_rows = jnp.transpose(
-        grid_rows.reshape(grid_rows.shape[0], devices, rows_per_device), (0, 2, 1)
-    ).reshape(grid_rows.shape[0], grid_len)
-    picks = (positions[None, :, None] == ordered_rows[:, None, :]).astype(jnp.bfloat16)
+    picks = (positions[None, :, None] == grid_rows[:, None, :]).astype(jnp.bfloat16)
     cosine_table = jnp.einsum(
         "jg,dgm->djm", cosine_base, picks, preferred_element_type=jnp.float32
     ).astype(jnp.bfloat16)
     sine_table = jnp.einsum(
         "jg,dgm->djm", sine_base, picks, preferred_element_type=jnp.float32
     ).astype(jnp.bfloat16)
-    real_rows = jnp.concatenate([cosine_table, sine_table], axis=2)
-    imag_rows = jnp.concatenate([-sine_table, cosine_table], axis=2)
-    return jnp.concatenate([real_rows, imag_rows], axis=1)
+    shape = (grid_rows.shape[0], grid_len, devices, 1, rows_per_device)
+    cosine_table = cosine_table.reshape(shape)
+    sine_table = sine_table.reshape(shape)
+    real_rows = jnp.concatenate([cosine_table, sine_table], axis=3)
+    imag_rows = jnp.concatenate([-sine_table, cosine_table], axis=3)
+    rows = jnp.concatenate([real_rows, imag_rows], axis=1)
+    return rows.reshape(grid_rows.shape[0], 2 * grid_len, 2 * grid_len)
 
 
 def channelize_kernel(first_pair, pairs, v_ref, w_ref, t1_ref, tw_ref, t2_ref, g_ref, o_ref):
@@ -138,8 +139,8 @@
     else:
         x_ref, t_ref, c_ref, s_ref, o_ref, acc_ref = refs
     step = pl.program_id(0)
-    rows = x_ref.shape[1]
-    devices = x_ref.shape[2] // dish_count
+    devices = x_ref.shape[0] // dish_count
+    rows = x_ref.shape[2]
     grid_len = t_ref.shape[1] // 2
     lanes = x_ref.shape[3]
 
@@ -152,7 +153,7 @@
 
     parts = []
     for d in range(dish_count):
-        block = x_ref[:, :, pl.ds(d * devices, devices), :].reshape(2 * rows * devices, lanes)
+        block = x_ref[pl.ds(d * devices, devices)].reshape(2 * rows * devices, lanes)
         sums = jnp.dot(t_ref[d], block, preferred_element_type=jnp.float32)
         sum_real = sums[:grid_len]
         sum_imag = sums[grid_len:]
@@ -271,7 +272,7 @@
     def beamform_chunk(received, carried, finish):
         carry_in = carried is not None
         in_specs = [
-            pl.BlockSpec((2, dish_rows, dests, lane_block), lambda f: (0, 0, 0, f)),
+            pl.BlockSpec((dests, 2, dish_rows, lane_block), lambda f: (0, 0, 0, f)),
             pl.BlockSpec((dish_count, 2 * grid_len, 2 * grid_len), lambda f: (0, 0, 0)),
             pl.BlockSpec((dish_count, grid_len, 1), lambda f: (0, 0, 0)),
             pl.BlockSpec((dish_count, grid_len, 1), lambda f: (0, 0, 0)),
@@ -299,7 +300,10 @@
         )(*operands)
 
     sent = [channelize_chunk(c) for c in range(chunks)]
-    arrived = [lax.all_to_all(s, ("dish", "freq"), 2, 2, tiled=True) for s in sent]
+    arrived = [
+        jnp.transpose(lax.all_to_all(s, ("dish", "freq"), 2, 2, tiled=True), (2, 0, 1, 3))
+        for s in sent
+    ]
     carried = None
     for c in range(chunks):
         carried = beamform_chunk(arrived[c], carried, c == chunks - 1)

time: 127 us -> 125 us (0.984)
    all_to_all x2 -> x0, local copies, waits for them, and re-layouts: 6.59 us -> none  [body(): lax.all_to_all(s, ('dish', 'freq'), 2, 2, tiled=True)]
    reshape x1, local copies, waits for them, and re-layouts: 0.09 us -> 4.17 us  [beam_tables(): return rows.reshape(grid_rows.shape[0], 2 * grid_len, 2 * grid_len)]
    unnamed x12 -> x16, local copies, waits for them, and re-layouts: 0.02 us -> 2.71 us
  transfers between devices with their start and end apart: 5 -> 5, of which waited for: 4 -> 4; matrix products, arithmetic and copies ran while one was open for 7% -> 9% of each run, Pallas kernels for 17% -> 17%
where the time goes in v6:
time: 125 us; the launch traced here: 124 us
  Pallas kernels  42.9 us (34%)
  waiting for transfers between devices  31.1 us (25%)
  local copies, waits for them, and re-layouts  25.7 us (21%)
  starting transfers between devices  18.8 us (15%)
  other arithmetic  3.81 us (3%)
  matrix products  1.93 us (2%)
    pallas_call x2, Pallas kernels, channelize_chunk(): pl.pallas_call(functools.partial(channelize_kernel, chunk * pairs, pairs)...  28.9 us
    all_to_all x2, waiting for transfers between devices, body(): lax.all_to_all(s, ('dish', 'freq'), 2, 2, tiled=True)  27.8 us
    all_to_all x2, starting transfers between devices, body(): lax.all_to_all(s, ('dish', 'freq'), 2, 2, tiled=True)  16.2 us
    pallas_call x2, Pallas kernels, beamform_chunk(): pl.pallas_call(functools.partial(beam_kernel, dish_count, carry_in, finis...  14 us
    another operation x1, local copies, waits for them, and re-layouts, body(): volts = voltages[:, 0].reshape(dish_rows, 2, samples // CHB, CHB)  8.46 us
    pallas_call x2, local copies, waits for them, and re-layouts, channelize_chunk(): pl.pallas_call(functools.partial(channelize_kernel, chunk * pairs, pairs)...  8.19 us
    reshape x1, local copies, waits for them, and re-layouts, beam_tables(): return rows.reshape(grid_rows.shape[0], 2 * grid_len, 2 * grid_len)  4.17 us
    ppermute x3, waiting for transfers between devices, body(): pieces.append(lax.ppermute(outgoing, 'dish', pairs_list))  3.25 us
  transfers between devices with their start and end apart: 5, of which 4 were waited for; matrix products, arithmetic and copies ran while one was open for 9% of the time, Pallas kernels for 17%

profile of v6, /device:TPU:1, one launch (start us, length us, event | category | flops | bytes accessed | tf_op | source)
XLA Modules:
  0.0 124.4 jit_solution(17934590536021419617)
XLA Ops:
  0.0 8.5 %reshape_squeeze.6.v_ref = bf16[8,2,1216,128]{3,2,1,0:T(8,128)(2,1)} reshape(bf16[8,1,2,155648]{3,2,1,0:T(2,128)(2,1)} %param.12) | data formatting | bytes 9961472 | tf_op jit(solution)/shard_map/reshape;squeeze | solution.py:243
  8.9 0.9 convolution_convert_fusion.2
  10.2 1.3 %pad_maximum_fusion.g_ref = f32[8,2,128,128]{3,2,1,0:T(8,128)} fusion(f32[8,2,128,64]{3,2,1,0:T(8,128)S(1)} %convolution_bitcast_fusion), kind=kLoop, calls=%fused_computation.8 | loop fusion | flops 262144 | bytes 1572864 | tf_op jit(solution)/shard_map/concatenate | solution.py:230
  11.5 14.4 %shard_map.119 = bf16[2,8,128,512]{3,2,1,0:T(8,128)(2,1)} custom-call(bf16[8,2,1216,128]{3,2,1,0:T(8,128)(2,1)} %reshape_squeeze.6.v_ref, f32[4,64,128]{2,1,0:T(8,128)} %constant.68.clone.w_ref, bf16[128,128]{1,0:T(8,128)(2,1)} %constant.69.clone.t1_ref, f32[2,64,128]{2,1,0:T(8,128)} %constant.70.clone.tw_ref, bf16[2,256,128]{2,1,0:T(8,128)(2,1)} %bitcast.50, ...), custom_call_target="tpu_custom_call" | custom-call | flops 805306368 | bytes 7077888 | tf_op jit(solution)/shard_map/pallas_call | solution.py:249
  25.9 4.1 %copy.29 = bf16[2,8,128,512]{3,1,0,2:T(8,128)(2,1)} copy(bf16[2,8,128,512]{3,2,1,0:T(8,128)(2,1)} %shard_map.119) | data formatting | bytes 4194304 | tf_op jit(solution)/shard_map/pallas_call | solution.py:249
  30.0 11.5 %all-to-all-start.1 = ((bf16[2,8,128,512]{3,1,0,2:T(8,128)(2,1)}), bf16[2,8,128,512]{3,1,0,2:T(8,128)(2,1)S(1)}, u32[]{:S(2)}, u32[]{:S(2)}) async-start(bf16[2,8,128,512]{3,1,0,2:T(8,128)(2,1)} %copy.29), calls=%async_computation.1 | async-start | bytes 4194304 | tf_op jit(solution)/shard_map/all_to_all | solution.py:304
  41.6 14.5 %shard_map.118 = bf16[2,8,128,512]{3,2,1,0:T(8,128)(2,1)} custom-call(bf16[8,2,1216,128]{3,2,1,0:T(8,128)(2,1)} %reshape_squeeze.6.v_ref, f32[4,64,128]{2,1,0:T(8,128)} %constant.68.clone.w_ref, bf16[128,128]{1,0:T(8,128)(2,1)} %constant.69.clone.t1_ref, f32[2,64,128]{2,1,0:T(8,128)} %constant.70.clone.tw_ref, bf16[2,256,128]{2,1,0:T(8,128)(2,1)} %bitcast.51, ...), custom_call_target="tpu_custom_call" | custom-call | flops 805306368 | bytes 7077888 | tf_op jit(solution)/shard_map/pallas_call | solution.py:249
  56.0 4.1 %copy.24 = bf16[2,8,128,512]{3,1,0,2:T(8,128)(2,1)} copy(bf16[2,8,128,512]{3,2,1,0:T(8,128)(2,1)} %shard_map.118) | data formatting | bytes 4194304 | tf_op jit(solution)/shard_map/pallas_call | solution.py:249
  60.1 11.3 %all-to-all-done.1 = bf16[2,8,128,512]{3,1,0,2:T(8,128)(2,1)S(1)} async-done(((bf16[2,8,128,512]{3,1,0,2:T(8,128)(2,1)}), bf16[2,8,128,512]{3,1,0,2:T(8,128)(2,1)S(1)}, u32[]{:S(2)}, u32[]{:S(2)}) %all-to-all-start.1) | async-done | bytes 2097184 | tf_op jit(solution)/shard_map/all_to_all | solution.py:304
  71.5 1.4 %copy-done.1 = bf16[2,8,128,512]{3,1,0,2:T(8,128)(2,1)} copy-done((bf16[2,8,128,512]{3,1,0,2:T(8,128)(2,1)}, bf16[2,8,128,512]{3,1,0,2:T(8,128)(2,1)S(1)}, u32[]{:S(2)}) %copy-start.1) | copy-done | bytes 2097176
  72.8 4.7 %all-to-all-start = ((bf16[2,8,128,512]{3,1,0,2:T(8,128)(2,1)}), bf16[2,8,128,512]{3,1,0,2:T(8,128)(2,1)S(1)}, u32[]{:S(2)}, u32[]{:S(2)}) async-start(bf16[2,8,128,512]{3,1,0,2:T(8,128)(2,1)} %copy.24), calls=%async_computation | async-start | bytes 4194304 | tf_op jit(solution)/shard_map/all_to_all | solution.py:304
  78.3 1.6 %maximum_maximum_fusion = bf16[4,512,32,2,8]{1,4,3,2,0:T(8,128)(2,1)} fusion(bf16[4,256,32,1,8]{1,4,3,2,0:T(8,128)(2,1)S(1)} %fusion, bf16[4,256,32,1,8]{1,4,3,2,0:T(8,128)(2,1)S(1)} %get-tuple-element.9, bf16[4,256,32,1,8]{1,4,3,2,0:T(8,128)(2,1)S(1)} %get-tuple-element.10), kind=kLoop, calls=%fused_computation.1 | loop fusion | flops 8388608 | bytes 3670016 | tf_op jit(solution)/shard_map/concatenate | solution.py:86
  79.9 4.2 %copy.31.refs_1_ = bf16[4,512,512]{2,1,0:T(8,128)(2,1)} copy(bf16[4,512,512]{1,2,0:T(8,128)(2,1)} %bitcast.48) | data formatting | bytes 4194304 | tf_op jit(solution)/shard_map/reshape | solution.py:87
  84.3 6.8 %shard_map.120.refs_4_ = f32[4,256,128]{2,1,0:T(8,128)} custom-call(bf16[128,2,8,512]{3,2,1,0:T(8,128)(2,1)} %bitcast.49, bf16[4,512,512]{2,1,0:T(8,128)(2,1)} %copy.31.refs_1_, f32[4,256,1]{2,1,0:T(8,128)} %constant.74.clone.refs_2_, f32[4,256,1]{2,1,0:T(8,128)} %constant.75.clone.refs_3_), custom_call_target="tpu_custom_call" | custom-call | flops 1073741824 | bytes 4194304 | tf_op jit(solution)/shard_map/pallas_call | solution.py:288
  91.0 16.5 %all-to-all-done = bf16[2,8,128,512]{3,1,0,2:T(8,128)(2,1)S(1)} async-done(((bf16[2,8,128,512]{3,1,0,2:T(8,128)(2,1)}), bf16[2,8,128,512]{3,1,0,2:T(8,128)(2,1)S(1)}, u32[]{:S(2)}, u32[]{:S(2)}) %all-to-all-start) | async-done | bytes 2097184 | tf_op jit(solution)/shard_map/all_to_all | solution.py:304
  107.5 1.3 %copy-done = bf16[2,8,128,512]{3,1,0,2:T(8,128)(2,1)} copy-done((bf16[2,8,128,512]{3,1,0,2:T(8,128)(2,1)}, bf16[2,8,128,512]{3,1,0,2:T(8,128)(2,1)S(1)}, u32[]{:S(2)}) %copy-start) | copy-done | bytes 2097176
  108.9 7.2 %shard_map.121 = f32[4,64,256]{2,1,0:T(8,128)} custom-call(bf16[128,2,8,512]{3,2,1,0:T(8,128)(2,1)} %bitcast.47, bf16[4,512,512]{2,1,0:T(8,128)(2,1)} %copy.31.refs_1_, f32[4,256,1]{2,1,0:T(8,128)} %constant.74.clone.refs_2_, f32[4,256,1]{2,1,0:T(8,128)} %constant.75.clone.refs_3_, f32[4,256,128]{2,1,0:T(8,128)} %shard_map.120.refs_4_), custom_call_target="tpu_custom_call" | custom-call | flops 1073741824 | bytes 4194304 | tf_op jit(solution)/shard_map/pallas_call | solution.py:288
  116.1 1.0 constant_dynamic-slice_fusion
  117.0 1.5 %collective-permute-start.2 = (f32[64,256]{1,0:T(8,128)S(1)}, f32[64,256]{1,0:T(8,128)S(1)}, u32[]{:S(2)}, u32[]{:S(2)}) collective-permute-start(f32[64,256]{1,0:T(8,128)S(1)} %get-tuple-element.6), channel_id=1, source_target_pairs={{0,3},{1,2},{2,1},{3,0},{4,7},{5,6},{6,5},{7,4},{8,11},{9,10},{10,... | collective-permute-start | bytes 196616 | tf_op jit(solution)/shard_map/ppermute | solution.py:317
  118.5 1.2 collective-permute-start.1
  119.7 1.6 %collective-permute-done.2 = f32[64,256]{1,0:T(8,128)S(1)} collective-permute-done((f32[64,256]{1,0:T(8,128)S(1)}, f32[64,256]{1,0:T(8,128)S(1)}, u32[]{:S(2)}, u32[]{:S(2)}) %collective-permute-start.2) | collective-permute-done | bytes 65568 | tf_op jit(solution)/shard_map/ppermute | solution.py:317
  121.3 1.6 %collective-permute-done.1 = f32[64,256]{1,0:T(8,128)S(1)} collective-permute-done((f32[64,256]{1,0:T(8,128)S(1)}, f32[64,256]{1,0:T(8,128)S(1)}, u32[]{:S(2)}, u32[]{:S(2)}) %collective-permute-start.1) | collective-permute-done | bytes 65568 | tf_op jit(solution)/shard_map/ppermute | solution.py:317
  123.0 0.6 gather_fusion
  123.5 0.8 bitcast_select_fusion
  (30 shorter events, 1.7 us)
Async XLA Ops:
  0.0 8.9 %copy-start.5 = (bf16[2,2,128,128]{3,2,1,0:T(8,128)(2,1)S(1)}, bf16[2,2,128,128]{3,2,1,0:T(8,128)(2,1)}, u32[]{:S(2)}) copy-start(bf16[2,2,128,128]{3,2,1,0:T(8,128)(2,1)} %constant.71.clone) | copy-start | bytes 393220
  0.0 8.5 %copy-start.7 = (s32[32]{0:T(128)S(1)}, s32[32]{0:T(128)}, u32[]{:S(2)}) copy-start(s32[32]{0:T(128)} %param.14) | copy-start | bytes 388
  0.0 8.6 %copy-start.2 = (bf16[8,1,2,8192]{3,2,1,0:T(2,128)(2,1)S(1)}, bf16[8,1,2,8192]{3,2,1,0:T(2,128)(2,1)}, u32[]{:S(2)}) copy-start(bf16[8,1,2,8192]{3,2,1,0:T(2,128)(2,1)} %param.13) | copy-start | bytes 786436
  30.0 41.4 %all-to-all-start.1 = ((bf16[2,8,128,512]{3,1,0,2:T(8,128)(2,1)}), bf16[2,8,128,512]{3,1,0,2:T(8,128)(2,1)S(1)}, u32[]{:S(2)}, u32[]{:S(2)}) async-start(bf16[2,8,128,512]{3,1,0,2:T(8,128)(2,1)} %copy.29), calls=%async_computation.1 | async-start | bytes 4194304 | tf_op jit(solution)/shard_map/all_to_all | solution.py:304
  60.1 17.4 %copy-start.4 = (bf16[256,256,1]{1,0,2:T(8,128)(2,1)S(1)}, bf16[256,256,1]{1,0,2:T(8,128)(2,1)}, u32[]{:S(2)}) copy-start(bf16[256,256,1]{1,0,2:T(8,128)(2,1)} %constant.78) | copy-start | bytes 393220
  60.1 17.4 %copy-start.6 = (s32[4,256]{1,0:T(4,128)S(1)}, s32[4,256]{1,0:T(4,128)}, u32[]{:S(2)}) copy-start(s32[4,256]{1,0:T(4,128)} %param.15) | copy-start | bytes 12292
  60.1 17.8 %copy-start.3 = (bf16[256,256,1]{1,0,2:T(8,128)(2,1)S(1)}, bf16[256,256,1]{1,0,2:T(8,128)(2,1)}, u32[]{:S(2)}) copy-start(bf16[256,256,1]{1,0,2:T(8,128)(2,1)} %constant.79) | copy-start | bytes 393220
  71.5 1.4 %copy-start.1 = (bf16[2,8,128,512]{3,1,0,2:T(8,128)(2,1)}, bf16[2,8,128,512]{3,1,0,2:T(8,128)(2,1)S(1)}, u32[]{:S(2)}) copy-start(bf16[2,8,128,512]{3,1,0,2:T(8,128)(2,1)S(1)} %all-to-all-done.1) | copy-start | bytes 6291460
  72.8 34.7 %all-to-all-start = ((bf16[2,8,128,512]{3,1,0,2:T(8,128)(2,1)}), bf16[2,8,128,512]{3,1,0,2:T(8,128)(2,1)S(1)}, u32[]{:S(2)}, u32[]{:S(2)}) async-start(bf16[2,8,128,512]{3,1,0,2:T(8,128)(2,1)} %copy.24), calls=%async_computation | async-start | bytes 4194304 | tf_op jit(solution)/shard_map/all_to_all | solution.py:304
  107.5 1.3 %copy-start = (bf16[2,8,128,512]{3,1,0,2:T(8,128)(2,1)}, bf16[2,8,128,512]{3,1,0,2:T(8,128)(2,1)S(1)}, u32[]{:S(2)}) copy-start(bf16[2,8,128,512]{3,1,0,2:T(8,128)(2,1)S(1)} %all-to-all-done) | copy-start | bytes 6291460
  117.0 4.3 %collective-permute-start.2 = (f32[64,256]{1,0:T(8,128)S(1)}, f32[64,256]{1,0:T(8,128)S(1)}, u32[]{:S(2)}, u32[]{:S(2)}) collective-permute-start(f32[64,256]{1,0:T(8,128)S(1)} %get-tuple-element.6), channel_id=1, source_target_pairs={{0,3},{1,2},{2,1},{3,0},{4,7},{5,6},{6,5},{7,4},{8,11},{9,10},{10,... | collective-permute-start | bytes 196616 | tf_op jit(solution)/shard_map/ppermute | solution.py:317
  118.5 4.4 %collective-permute-start.1 = (f32[64,256]{1,0:T(8,128)S(1)}, f32[64,256]{1,0:T(8,128)S(1)}, u32[]{:S(2)}, u32[]{:S(2)}) collective-permute-start(f32[64,256]{1,0:T(8,128)S(1)} %get-tuple-element.7), channel_id=1, source_target_pairs={{0,2},{1,3},{2,0},{3,1},{4,6},{5,7},{6,4},{7,5},{8,10},{9,11},{10,... | collective-permute-start | bytes 196616 | tf_op jit(solution)/shard_map/ppermute | solution.py:317
  119.7 3.3 %collective-permute-start = (f32[64,256]{1,0:T(8,128)S(1)}, f32[64,256]{1,0:T(8,128)S(1)}, u32[]{:S(2)}, u32[]{:S(2)}) collective-permute-start(f32[64,256]{1,0:T(8,128)S(1)} %get-tuple-element.8), channel_id=1, source_target_pairs={{0,1},{1,0},{2,3},{3,2},{4,5},{5,4},{6,7},{7,6},{8,9},{9,8},{10,11... | collective-permute-start | bytes 196616 | tf_op jit(solution)/shard_map/ppermute | solution.py:317

commit v7 on v6

--- a/solution.py
+++ b/solution.py
@@ -97,12 +97,10 @@
     g_imag = g_ref[0, 1]
     half = t2_real.shape[0] // 2
 
-    def one_frame(frame):
+    def one_frame(pieces):
         acc = None
         for tap in range(TAPS):
-            start = pl.multiple_of((frame - 2 * first_pair + tap) * CHA, CHA)
-            piece = v_ref[0, :, pl.ds(start, CHA), :].astype(jnp.float32)
-            term = w_ref[tap][None] * piece
+            term = w_ref[tap][None] * pieces[tap]
             acc = term if acc is None else acc + term
         block = acc.astype(jnp.bfloat16).reshape(2 * CHA, CHB)
         section = jnp.dot(t1, block, preferred_element_type=jnp.float32)
@@ -113,8 +111,12 @@
         return turned_real.astype(jnp.bfloat16), turned_imag.astype(jnp.bfloat16)
 
     def pair(step, carry):
-        first_real, first_imag = one_frame(2 * step)
-        second_real, second_imag = one_frame(2 * step + 1)
+        pieces = []
+        for offset in range(TAPS + 1):
+            start = pl.multiple_of((2 * (step - first_pair) + offset) * CHA, CHA)
+            pieces.append(v_ref[0, :, pl.ds(start, CHA), :].astype(jnp.float32))
+        first_real, first_imag = one_frame(pieces[:TAPS])
+        second_real, second_imag = one_frame(pieces[1:])
         both_real = jnp.concatenate([first_real, second_real], axis=0)
         both_imag = jnp.concatenate([first_imag, second_imag], axis=0)
         dims = (((1,), (1,)), ((), ()))
@@ -130,7 +132,7 @@
         o_ref[1, 0, :, lanes] = out_imag.astype(o_ref.dtype)
         return carry
 
-    lax.fori_loop(first_pair, first_pair + pairs, pair, 0)
+    lax.fori_loop(first_pair, first_pair + pairs, pair, 0, unroll=True)
 
 
 def beam_kernel(dish_count, carry_in, finish, *refs):

time: 125 us -> 120 us (0.960)
  Pallas kernels: 42.9 us -> 31.6 us
  waiting for transfers between devices: 31.1 us -> 36.7 us
    pallas_call x2, Pallas kernels: 28.9 us -> 17.6 us  [channelize_chunk(): pl.pallas_call(functools.partial(channelize_kernel, chunk * pairs, pairs)...]
    all_to_all x2, waiting for transfers between devices: 27.8 us -> 33.5 us  [body(): lax.all_to_all(s, ('dish', 'freq'), 2, 2, tiled=True)]
  transfers between devices with their start and end apart: 5 -> 5, of which waited for: 4 -> 4; matrix products, arithmetic and copies ran while one was open for 9% -> 9% of each run, Pallas kernels for 17% -> 13%
where the time goes in v7:
time: 120 us; the launch traced here: 119 us
  waiting for transfers between devices  36.7 us (31%)
  Pallas kernels  31.6 us (26%)
  local copies, waits for them, and re-layouts  25.7 us (21%)
  starting transfers between devices  18.8 us (16%)
  other arithmetic  3.81 us (3%)
  matrix products  1.94 us (2%)
    all_to_all x2, waiting for transfers between devices, body(): lax.all_to_all(s, ('dish', 'freq'), 2, 2, tiled=True)  33.5 us
    pallas_call x2, Pallas kernels, channelize_chunk(): pl.pallas_call(functools.partial(channelize_kernel, chunk * pairs, pairs)...  17.6 us
    all_to_all x2, starting transfers between devices, body(): lax.all_to_all(s, ('dish', 'freq'), 2, 2, tiled=True)  16.2 us
    pallas_call x2, Pallas kernels, beamform_chunk(): pl.pallas_call(functools.partial(beam_kernel, dish_count, carry_in, finis...  14 us
    another operation x1, local copies, waits for them, and re-layouts, body(): volts = voltages[:, 0].reshape(dish_rows, 2, samples // CHB, CHB)  8.46 us
    pallas_call x2, local copies, waits for them, and re-layouts, channelize_chunk(): pl.pallas_call(functools.partial(channelize_kernel, chunk * pairs, pairs)...  8.19 us
    reshape x1, local copies, waits for them, and re-layouts, beam_tables(): return rows.reshape(grid_rows.shape[0], 2 * grid_len, 2 * grid_len)  4.17 us
    ppermute x3, waiting for transfers between devices, body(): pieces.append(lax.ppermute(outgoing, 'dish', pairs_list))  3.25 us
  transfers between devices with their start and end apart: 5, of which 4 were waited for; matrix products, arithmetic and copies ran while one was open for 9% of the time, Pallas kernels for 13%

profile of v7, /device:TPU:1, one launch (start us, length us, event | category | flops | bytes accessed | tf_op | source)
XLA Modules:
  0.0 118.7 jit_solution(11192809503417809129)
XLA Ops:
  0.0 8.5 %reshape_squeeze.6.v_ref = bf16[8,2,1216,128]{3,2,1,0:T(8,128)(2,1)} reshape(bf16[8,1,2,155648]{3,2,1,0:T(2,128)(2,1)} %param.12) | data formatting | bytes 9961472 | tf_op jit(solution)/shard_map/reshape;squeeze | solution.py:245
  8.9 0.9 convolution_convert_fusion.2
  10.2 1.3 %pad_maximum_fusion.g_ref = f32[8,2,128,128]{3,2,1,0:T(8,128)} fusion(f32[8,2,128,64]{3,2,1,0:T(8,128)S(1)} %convolution_bitcast_fusion), kind=kLoop, calls=%fused_computation.8 | loop fusion | flops 262144 | bytes 1572864 | tf_op jit(solution)/shard_map/concatenate | solution.py:232
  11.5 8.8 %shard_map.119 = bf16[2,8,128,512]{3,2,1,0:T(8,128)(2,1)} custom-call(bf16[8,2,1216,128]{3,2,1,0:T(8,128)(2,1)} %reshape_squeeze.6.v_ref, f32[4,64,128]{2,1,0:T(8,128)} %constant.68.clone.w_ref, bf16[128,128]{1,0:T(8,128)(2,1)} %constant.69.clone.t1_ref, f32[2,64,128]{2,1,0:T(8,128)} %constant.70.clone.tw_ref, bf16[2,256,128]{2,1,0:T(8,128)(2,1)} %bitcast.50, ...), custom_call_target="tpu_custom_call" | custom-call | flops 805306368 | bytes 7077888 | tf_op jit(solution)/shard_map/pallas_call | solution.py:251
  20.3 4.1 %copy.29 = bf16[2,8,128,512]{3,1,0,2:T(8,128)(2,1)} copy(bf16[2,8,128,512]{3,2,1,0:T(8,128)(2,1)} %shard_map.119) | data formatting | bytes 4194304 | tf_op jit(solution)/shard_map/pallas_call | solution.py:251
  24.4 11.5 %all-to-all-start.1 = ((bf16[2,8,128,512]{3,1,0,2:T(8,128)(2,1)}), bf16[2,8,128,512]{3,1,0,2:T(8,128)(2,1)S(1)}, u32[]{:S(2)}, u32[]{:S(2)}) async-start(bf16[2,8,128,512]{3,1,0,2:T(8,128)(2,1)} %copy.29), calls=%async_computation.1 | async-start | bytes 4194304 | tf_op jit(solution)/shard_map/all_to_all | solution.py:306
  35.9 8.8 %shard_map.118 = bf16[2,8,128,512]{3,2,1,0:T(8,128)(2,1)} custom-call(bf16[8,2,1216,128]{3,2,1,0:T(8,128)(2,1)} %reshape_squeeze.6.v_ref, f32[4,64,128]{2,1,0:T(8,128)} %constant.68.clone.w_ref, bf16[128,128]{1,0:T(8,128)(2,1)} %constant.69.clone.t1_ref, f32[2,64,128]{2,1,0:T(8,128)} %constant.70.clone.tw_ref, bf16[2,256,128]{2,1,0:T(8,128)(2,1)} %bitcast.51, ...), custom_call_target="tpu_custom_call" | custom-call | flops 805306368 | bytes 7077888 | tf_op jit(solution)/shard_map/pallas_call | solution.py:251
  44.7 4.1 %copy.24 = bf16[2,8,128,512]{3,1,0,2:T(8,128)(2,1)} copy(bf16[2,8,128,512]{3,2,1,0:T(8,128)(2,1)} %shard_map.118) | data formatting | bytes 4194304 | tf_op jit(solution)/shard_map/pallas_call | solution.py:251
  48.8 17.0 %all-to-all-done.1 = bf16[2,8,128,512]{3,1,0,2:T(8,128)(2,1)S(1)} async-done(((bf16[2,8,128,512]{3,1,0,2:T(8,128)(2,1)}), bf16[2,8,128,512]{3,1,0,2:T(8,128)(2,1)S(1)}, u32[]{:S(2)}, u32[]{:S(2)}) %all-to-all-start.1) | async-done | bytes 2097184 | tf_op jit(solution)/shard_map/all_to_all | solution.py:306
  65.8 1.4 %copy-done.1 = bf16[2,8,128,512]{3,1,0,2:T(8,128)(2,1)} copy-done((bf16[2,8,128,512]{3,1,0,2:T(8,128)(2,1)}, bf16[2,8,128,512]{3,1,0,2:T(8,128)(2,1)S(1)}, u32[]{:S(2)}) %copy-start.1) | copy-done | bytes 2097176
  67.1 4.7 %all-to-all-start = ((bf16[2,8,128,512]{3,1,0,2:T(8,128)(2,1)}), bf16[2,8,128,512]{3,1,0,2:T(8,128)(2,1)S(1)}, u32[]{:S(2)}, u32[]{:S(2)}) async-start(bf16[2,8,128,512]{3,1,0,2:T(8,128)(2,1)} %copy.24), calls=%async_computation | async-start | bytes 4194304 | tf_op jit(solution)/shard_map/all_to_all | solution.py:306
  72.6 1.6 %maximum_maximum_fusion = bf16[4,512,32,2,8]{1,4,3,2,0:T(8,128)(2,1)} fusion(bf16[4,256,32,1,8]{1,4,3,2,0:T(8,128)(2,1)S(1)} %fusion, bf16[4,256,32,1,8]{1,4,3,2,0:T(8,128)(2,1)S(1)} %get-tuple-element.9, bf16[4,256,32,1,8]{1,4,3,2,0:T(8,128)(2,1)S(1)} %get-tuple-element.10), kind=kLoop, calls=%fused_computation.1 | loop fusion | flops 8388608 | bytes 3670016 | tf_op jit(solution)/shard_map/concatenate | solution.py:86
  74.2 4.2 %copy.31.refs_1_ = bf16[4,512,512]{2,1,0:T(8,128)(2,1)} copy(bf16[4,512,512]{1,2,0:T(8,128)(2,1)} %bitcast.48) | data formatting | bytes 4194304 | tf_op jit(solution)/shard_map/reshape | solution.py:87
  78.6 6.8 %shard_map.120.refs_4_ = f32[4,256,128]{2,1,0:T(8,128)} custom-call(bf16[128,2,8,512]{3,2,1,0:T(8,128)(2,1)} %bitcast.49, bf16[4,512,512]{2,1,0:T(8,128)(2,1)} %copy.31.refs_1_, f32[4,256,1]{2,1,0:T(8,128)} %constant.74.clone.refs_2_, f32[4,256,1]{2,1,0:T(8,128)} %constant.75.clone.refs_3_), custom_call_target="tpu_custom_call" | custom-call | flops 1073741824 | bytes 4194304 | tf_op jit(solution)/shard_map/pallas_call | solution.py:290
  85.4 16.5 %all-to-all-done = bf16[2,8,128,512]{3,1,0,2:T(8,128)(2,1)S(1)} async-done(((bf16[2,8,128,512]{3,1,0,2:T(8,128)(2,1)}), bf16[2,8,128,512]{3,1,0,2:T(8,128)(2,1)S(1)}, u32[]{:S(2)}, u32[]{:S(2)}) %all-to-all-start) | async-done | bytes 2097184 | tf_op jit(solution)/shard_map/all_to_all | solution.py:306
  101.9 1.3 %copy-done = bf16[2,8,128,512]{3,1,0,2:T(8,128)(2,1)} copy-done((bf16[2,8,128,512]{3,1,0,2:T(8,128)(2,1)}, bf16[2,8,128,512]{3,1,0,2:T(8,128)(2,1)S(1)}, u32[]{:S(2)}) %copy-start) | copy-done | bytes 2097176
  103.2 7.2 %shard_map.121 = f32[4,64,256]{2,1,0:T(8,128)} custom-call(bf16[128,2,8,512]{3,2,1,0:T(8,128)(2,1)} %bitcast.47, bf16[4,512,512]{2,1,0:T(8,128)(2,1)} %copy.31.refs_1_, f32[4,256,1]{2,1,0:T(8,128)} %constant.74.clone.refs_2_, f32[4,256,1]{2,1,0:T(8,128)} %constant.75.clone.refs_3_, f32[4,256,128]{2,1,0:T(8,128)} %shard_map.120.refs_4_), custom_call_target="tpu_custom_call" | custom-call | flops 1073741824 | bytes 4194304 | tf_op jit(solution)/shard_map/pallas_call | solution.py:290
  110.4 1.0 constant_dynamic-slice_fusion
  111.4 1.5 %collective-permute-start.2 = (f32[64,256]{1,0:T(8,128)S(1)}, f32[64,256]{1,0:T(8,128)S(1)}, u32[]{:S(2)}, u32[]{:S(2)}) collective-permute-start(f32[64,256]{1,0:T(8,128)S(1)} %get-tuple-element.6), channel_id=1, source_target_pairs={{0,3},{1,2},{2,1},{3,0},{4,7},{5,6},{6,5},{7,4},{8,11},{9,10},{10,... | collective-permute-start | bytes 196616 | tf_op jit(solution)/shard_map/ppermute | solution.py:319
  112.9 1.2 collective-permute-start.1
  114.0 1.6 %collective-permute-done.2 = f32[64,256]{1,0:T(8,128)S(1)} collective-permute-done((f32[64,256]{1,0:T(8,128)S(1)}, f32[64,256]{1,0:T(8,128)S(1)}, u32[]{:S(2)}, u32[]{:S(2)}) %collective-permute-start.2) | collective-permute-done | bytes 65568 | tf_op jit(solution)/shard_map/ppermute | solution.py:319
  115.6 1.6 %collective-permute-done.1 = f32[64,256]{1,0:T(8,128)S(1)} collective-permute-done((f32[64,256]{1,0:T(8,128)S(1)}, f32[64,256]{1,0:T(8,128)S(1)}, u32[]{:S(2)}, u32[]{:S(2)}) %collective-permute-start.1) | collective-permute-done | bytes 65568 | tf_op jit(solution)/shard_map/ppermute | solution.py:319
  117.3 0.6 gather_fusion
  117.9 0.8 bitcast_select_fusion
  (30 shorter events, 1.7 us)
Async XLA Ops:
  0.0 8.9 %copy-start.5 = (bf16[2,2,128,128]{3,2,1,0:T(8,128)(2,1)S(1)}, bf16[2,2,128,128]{3,2,1,0:T(8,128)(2,1)}, u32[]{:S(2)}) copy-start(bf16[2,2,128,128]{3,2,1,0:T(8,128)(2,1)} %constant.71.clone) | copy-start | bytes 393220
  0.0 8.5 %copy-start.7 = (s32[32]{0:T(128)S(1)}, s32[32]{0:T(128)}, u32[]{:S(2)}) copy-start(s32[32]{0:T(128)} %param.14) | copy-start | bytes 388
  0.0 8.6 %copy-start.2 = (bf16[8,1,2,8192]{3,2,1,0:T(2,128)(2,1)S(1)}, bf16[8,1,2,8192]{3,2,1,0:T(2,128)(2,1)}, u32[]{:S(2)}) copy-start(bf16[8,1,2,8192]{3,2,1,0:T(2,128)(2,1)} %param.13) | copy-start | bytes 786436
  24.4 41.4 %all-to-all-start.1 = ((bf16[2,8,128,512]{3,1,0,2:T(8,128)(2,1)}), bf16[2,8,128,512]{3,1,0,2:T(8,128)(2,1)S(1)}, u32[]{:S(2)}, u32[]{:S(2)}) async-start(bf16[2,8,128,512]{3,1,0,2:T(8,128)(2,1)} %copy.29), calls=%async_computation.1 | async-start | bytes 4194304 | tf_op jit(solution)/shard_map/all_to_all | solution.py:306
  48.8 23.0 %copy-start.4 = (bf16[256,256,1]{1,0,2:T(8,128)(2,1)S(1)}, bf16[256,256,1]{1,0,2:T(8,128)(2,1)}, u32[]{:S(2)}) copy-start(bf16[256,256,1]{1,0,2:T(8,128)(2,1)} %constant.78) | copy-start | bytes 393220
  48.8 23.1 %copy-start.6 = (s32[4,256]{1,0:T(4,128)S(1)}, s32[4,256]{1,0:T(4,128)}, u32[]{:S(2)}) copy-start(s32[4,256]{1,0:T(4,128)} %param.15) | copy-start | bytes 12292
  48.8 23.4 %copy-start.3 = (bf16[256,256,1]{1,0,2:T(8,128)(2,1)S(1)}, bf16[256,256,1]{1,0,2:T(8,128)(2,1)}, u32[]{:S(2)}) copy-start(bf16[256,256,1]{1,0,2:T(8,128)(2,1)} %constant.79) | copy-start | bytes 393220
  65.8 1.4 %copy-start.1 = (bf16[2,8,128,512]{3,1,0,2:T(8,128)(2,1)}, bf16[2,8,128,512]{3,1,0,2:T(8,128)(2,1)S(1)}, u32[]{:S(2)}) copy-start(bf16[2,8,128,512]{3,1,0,2:T(8,128)(2,1)S(1)} %all-to-all-done.1) | copy-start | bytes 6291460
  67.1 34.7 %all-to-all-start = ((bf16[2,8,128,512]{3,1,0,2:T(8,128)(2,1)}), bf16[2,8,128,512]{3,1,0,2:T(8,128)(2,1)S(1)}, u32[]{:S(2)}, u32[]{:S(2)}) async-start(bf16[2,8,128,512]{3,1,0,2:T(8,128)(2,1)} %copy.24), calls=%async_computation | async-start | bytes 4194304 | tf_op jit(solution)/shard_map/all_to_all | solution.py:306
  101.9 1.3 %copy-start = (bf16[2,8,128,512]{3,1,0,2:T(8,128)(2,1)}, bf16[2,8,128,512]{3,1,0,2:T(8,128)(2,1)S(1)}, u32[]{:S(2)}) copy-start(bf16[2,8,128,512]{3,1,0,2:T(8,128)(2,1)S(1)} %all-to-all-done) | copy-start | bytes 6291460
  111.4 4.3 %collective-permute-start.2 = (f32[64,256]{1,0:T(8,128)S(1)}, f32[64,256]{1,0:T(8,128)S(1)}, u32[]{:S(2)}, u32[]{:S(2)}) collective-permute-start(f32[64,256]{1,0:T(8,128)S(1)} %get-tuple-element.6), channel_id=1, source_target_pairs={{0,3},{1,2},{2,1},{3,0},{4,7},{5,6},{6,5},{7,4},{8,11},{9,10},{10,... | collective-permute-start | bytes 196616 | tf_op jit(solution)/shard_map/ppermute | solution.py:319
  112.9 4.4 %collective-permute-start.1 = (f32[64,256]{1,0:T(8,128)S(1)}, f32[64,256]{1,0:T(8,128)S(1)}, u32[]{:S(2)}, u32[]{:S(2)}) collective-permute-start(f32[64,256]{1,0:T(8,128)S(1)} %get-tuple-element.7), channel_id=1, source_target_pairs={{0,2},{1,3},{2,0},{3,1},{4,6},{5,7},{6,4},{7,5},{8,10},{9,11},{10,... | collective-permute-start | bytes 196616 | tf_op jit(solution)/shard_map/ppermute | solution.py:319
  114.0 3.3 %collective-permute-start = (f32[64,256]{1,0:T(8,128)S(1)}, f32[64,256]{1,0:T(8,128)S(1)}, u32[]{:S(2)}, u32[]{:S(2)}) collective-permute-start(f32[64,256]{1,0:T(8,128)S(1)} %get-tuple-element.8), channel_id=1, source_target_pairs={{0,1},{1,0},{2,3},{3,2},{4,5},{5,4},{6,7},{7,6},{8,9},{9,8},{10,11... | collective-permute-start | bytes 196616 | tf_op jit(solution)/shard_map/ppermute | solution.py:319

commit v8 on v7

--- a/solution.py
+++ b/solution.py
@@ -185,16 +185,20 @@
         if not finish:
             o_ref[...] = acc_ref[...]
             return
-        reversal = [
-            int(format(s, "0%db" % (dish_count.bit_length() - 1))[::-1], 2)
-            for s in range(dish_count)
-        ]
+        me = lax.axis_index("dish")
         width = o_ref.shape[1]
-        for s in range(dish_count):
-            total = acc_ref[reversal[s]]
-            total = total + pltpu.roll(total, width, 1)
-            flipped = jnp.transpose(total, (1, 0))
-            o_ref[s] = flipped[:width] * (0.25 / FRAMES)
+        for shift in range(dish_count):
+            target = jnp.bitwise_xor(me, shift)
+            beam_index = jnp.bitwise_or(
+                jnp.left_shift(jnp.bitwise_and(target, 1), 1), jnp.right_shift(target, 1)
+            )
+            total = acc_ref[beam_index]
+            folded = total[:, :CHB]
+            for k in range(1, lanes // CHB):
+                folded = folded + total[:, k * CHB : (k + 1) * CHB]
+            folded = folded + pltpu.roll(folded, width, 1)
+            flipped = jnp.transpose(folded, (1, 0))
+            o_ref[shift] = flipped[:width] * (0.25 / FRAMES)
 
 
 def body(voltages, feed_gains, block_assign, grid_rows):
@@ -240,7 +244,7 @@
     twist_cos, twist_sin = rotation_constant(dish_count, grid_len, total_dishes)
     twist_cos = jnp.asarray(twist_cos[:, :, None])
     twist_sin = jnp.asarray(twist_sin[:, :, None])
-    lane_block = 2 * quarter
+    lane_block = 4 * quarter
 
     volts = voltages[:, 0].reshape(dish_rows, 2, samples // CHB, CHB)
 
@@ -312,9 +316,9 @@
     powers = carried
 
     me = lax.axis_index("dish")
-    pieces = [lax.dynamic_index_in_dim(powers, me, 0, keepdims=False)]
+    pieces = [powers[0]]
     for shift in range(1, dish_count):
-        outgoing = lax.dynamic_index_in_dim(powers, me ^ shift, 0, keepdims=False)
+        outgoing = powers[shift]
         pairs_list = [(i, i ^ shift) for i in range(dish_count)]
         pieces.append(lax.ppermute(outgoing, "dish", pairs_list))
     stacked = jnp.stack(pieces, axis=0)

time: 120 us -> 120 us (level)
  waiting for transfers between devices: 36.7 us -> 40.8 us
  local copies, waits for them, and re-layouts: 25.7 us -> 23.4 us
  Pallas kernels: 31.6 us -> 29.6 us
  starting transfers between devices: 18.8 us -> 20.3 us
    all_to_all x2, waiting for transfers between devices: 33.5 us -> 37.3 us  [body(): lax.all_to_all(s, ('dish', 'freq'), 2, 2, tiled=True)]
    pallas_call x2, Pallas kernels: 14 us -> 12 us  [beamform_chunk(): pl.pallas_call(functools.partial(beam_kernel, dish_count, carry_in, finis...]
    reshape x1, local copies, waits for them, and re-layouts: 4.17 us -> 2.37 us  [beam_tables(): return rows.reshape(grid_rows.shape[0], 2 * grid_len, 2 * grid_len)]
    concatenate x1, other arithmetic: 1.65 us -> 0.28 us  [beam_tables(): rows = jnp.concatenate([real_rows, imag_rows], axis=1)]
    unnamed x16 -> x10, local copies, waits for them, and re-layouts: 2.71 us -> 1.36 us
  transfers between devices with their start and end apart: 5 -> 5, of which waited for: 4 -> 4; matrix products, arithmetic and copies ran while one was open for 9% -> 6% of each run, Pallas kernels for 13% -> 12%
where the time goes in v8:
time: 120 us; the launch traced here: 119 us
  waiting for transfers between devices  40.8 us (34%)
  Pallas kernels  29.6 us (25%)
  local copies, waits for them, and re-layouts  23.4 us (20%)
  starting transfers between devices  20.3 us (17%)
  other arithmetic  3.1 us (3%)
  matrix products  1.94 us (2%)
    all_to_all x2, waiting for transfers between devices, body(): lax.all_to_all(s, ('dish', 'freq'), 2, 2, tiled=True)  37.3 us
    pallas_call x2, Pallas kernels, channelize_chunk(): pl.pallas_call(functools.partial(channelize_kernel, chunk * pairs, pairs)...  17.5 us
    all_to_all x2, starting transfers between devices, body(): lax.all_to_all(s, ('dish', 'freq'), 2, 2, tiled=True)  17.2 us
    pallas_call x2, Pallas kernels, beamform_chunk(): pl.pallas_call(functools.partial(beam_kernel, dish_count, carry_in, finis...  12 us
    another operation x1, local copies, waits for them, and re-layouts, body(): volts = voltages[:, 0].reshape(dish_rows, 2, samples // CHB, CHB)  8.4 us
    pallas_call x2, local copies, waits for them, and re-layouts, channelize_chunk(): pl.pallas_call(functools.partial(channelize_kernel, chunk * pairs, pairs)...  8.19 us
    ppermute x3, waiting for transfers between devices, body(): pieces.append(lax.ppermute(outgoing, 'dish', pairs_list))  3.5 us
    ppermute x3, starting transfers between devices, body(): pieces.append(lax.ppermute(outgoing, 'dish', pairs_list))  3.03 us
  transfers between devices with their start and end apart: 5, of which 4 were waited for; matrix products, arithmetic and copies ran while one was open for 6% of the time, Pallas kernels for 12%

profile of v8, /device:TPU:1, one launch (start us, length us, event | category | flops | bytes accessed | tf_op | source)
XLA Modules:
  0.0 119.2 jit_solution(11597280803674685776)
XLA Ops:
  0.0 0.7 broadcast_multiply_fusion
  0.8 1.4 %reshape.86 = bf16[8,2,128,64]{3,2,1,0:T(8,128)(2,1)S(1)} reshape(bf16[8,1,2,8192]{3,2,1,0:T(2,128)(2,1)} %param.13) | data formatting | bytes 524288 | tf_op jit(solution)/shard_map/reshape;squeeze | solution.py:234
  2.5 1.3 %pad_maximum_fusion.g_ref = f32[8,2,128,128]{3,2,1,0:T(8,128)} fusion(f32[8,2,128,64]{3,2,1,0:T(8,128)S(1)} %convolution_bitcast_fusion), kind=kLoop, calls=%fused_computation.8 | loop fusion | flops 262144 | bytes 1572864 | tf_op jit(solution)/shard_map/concatenate | solution.py:236
  3.8 0.9 convolution_convert_fusion.2
  4.7 8.4 %reshape_squeeze.6.v_ref = bf16[8,2,1216,128]{3,2,1,0:T(8,128)(2,1)} reshape(bf16[8,1,2,155648]{3,2,1,0:T(2,128)(2,1)} %param.12) | data formatting | bytes 9961472 | tf_op jit(solution)/shard_map/reshape;squeeze | solution.py:249
  13.1 8.8 %shard_map.119 = bf16[2,8,128,512]{3,2,1,0:T(8,128)(2,1)} custom-call(bf16[8,2,1216,128]{3,2,1,0:T(8,128)(2,1)} %reshape_squeeze.6.v_ref, f32[4,64,128]{2,1,0:T(8,128)} %constant.54.clone.w_ref, bf16[128,128]{1,0:T(8,128)(2,1)} %constant.55.clone.t1_ref, f32[2,64,128]{2,1,0:T(8,128)} %constant.56.clone.tw_ref, bf16[2,256,128]{2,1,0:T(8,128)(2,1)} %bitcast.49, ...), custom_call_target="tpu_custom_call" | custom-call | flops 805306368 | bytes 7077888 | tf_op jit(solution)/shard_map/pallas_call | solution.py:255
  21.8 4.1 %copy.29 = bf16[2,8,128,512]{3,1,0,2:T(8,128)(2,1)} copy(bf16[2,8,128,512]{3,2,1,0:T(8,128)(2,1)} %shard_map.119) | data formatting | bytes 4194304 | tf_op jit(solution)/shard_map/pallas_call | solution.py:255
  25.9 11.5 %all-to-all-start.1 = ((bf16[2,8,128,512]{3,1,0,2:T(8,128)(2,1)}), bf16[2,8,128,512]{3,1,0,2:T(8,128)(2,1)S(1)}, u32[]{:S(2)}, u32[]{:S(2)}) async-start(bf16[2,8,128,512]{3,1,0,2:T(8,128)(2,1)} %copy.29), calls=%async_computation.1 | async-start | bytes 4194304 | tf_op jit(solution)/shard_map/all_to_all | solution.py:310
  37.4 8.8 %shard_map.118 = bf16[2,8,128,512]{3,2,1,0:T(8,128)(2,1)} custom-call(bf16[8,2,1216,128]{3,2,1,0:T(8,128)(2,1)} %reshape_squeeze.6.v_ref, f32[4,64,128]{2,1,0:T(8,128)} %constant.54.clone.w_ref, bf16[128,128]{1,0:T(8,128)(2,1)} %constant.55.clone.t1_ref, f32[2,64,128]{2,1,0:T(8,128)} %constant.56.clone.tw_ref, bf16[2,256,128]{2,1,0:T(8,128)(2,1)} %bitcast.50, ...), custom_call_target="tpu_custom_call" | custom-call | flops 805306368 | bytes 7077888 | tf_op jit(solution)/shard_map/pallas_call | solution.py:255
  46.2 4.1 %copy.24 = bf16[2,8,128,512]{3,1,0,2:T(8,128)(2,1)} copy(bf16[2,8,128,512]{3,2,1,0:T(8,128)(2,1)} %shard_map.118) | data formatting | bytes 4194304 | tf_op jit(solution)/shard_map/pallas_call | solution.py:255
  50.3 17.0 %all-to-all-done.1 = bf16[2,8,128,512]{3,1,0,2:T(8,128)(2,1)S(1)} async-done(((bf16[2,8,128,512]{3,1,0,2:T(8,128)(2,1)}), bf16[2,8,128,512]{3,1,0,2:T(8,128)(2,1)S(1)}, u32[]{:S(2)}, u32[]{:S(2)}) %all-to-all-start.1) | async-done | bytes 2097184 | tf_op jit(solution)/shard_map/all_to_all | solution.py:310
  67.3 1.3 %copy-done = bf16[2,8,128,512]{3,1,0,2:T(8,128)(2,1)} copy-done((bf16[2,8,128,512]{3,1,0,2:T(8,128)(2,1)}, bf16[2,8,128,512]{3,1,0,2:T(8,128)(2,1)S(1)}, u32[]{:S(2)}) %copy-start) | copy-done | bytes 2097176
  68.7 5.7 %all-to-all-start = ((bf16[2,8,128,512]{3,1,0,2:T(8,128)(2,1)}), bf16[2,8,128,512]{3,1,0,2:T(8,128)(2,1)}, u32[]{:S(2)}, u32[]{:S(2)}) async-start(bf16[2,8,128,512]{3,1,0,2:T(8,128)(2,1)} %copy.24), calls=%async_computation | async-start | bytes 4194304 | tf_op jit(solution)/shard_map/all_to_all | solution.py:310
  75.5 2.4 %copy.31.refs_1_ = bf16[4,512,512]{2,1,0:T(8,128)(2,1)} copy(bf16[4,512,512]{1,2,0:T(8,128)(2,1)S(1)} %bitcast.48) | data formatting | bytes 4194304 | tf_op jit(solution)/shard_map/reshape | solution.py:87
  78.0 5.9 %shard_map.120.refs_4_ = f32[4,256,256]{2,1,0:T(8,128)} custom-call(bf16[128,2,8,512]{3,2,1,0:T(8,128)(2,1)} %bitcast.47, bf16[4,512,512]{2,1,0:T(8,128)(2,1)} %copy.31.refs_1_, f32[4,256,1]{2,1,0:T(8,128)} %constant.60.clone.refs_2_, f32[4,256,1]{2,1,0:T(8,128)} %constant.61.clone.refs_3_), custom_call_target="tpu_custom_call" | custom-call | flops 1073741824 | bytes 4194304 | tf_op jit(solution)/shard_map/pallas_call | solution.py:294
  83.9 20.2 %all-to-all-done = bf16[2,8,128,512]{3,1,0,2:T(8,128)(2,1)} async-done(((bf16[2,8,128,512]{3,1,0,2:T(8,128)(2,1)}), bf16[2,8,128,512]{3,1,0,2:T(8,128)(2,1)}, u32[]{:S(2)}, u32[]{:S(2)}) %all-to-all-start) | async-done | bytes 2097184 | tf_op jit(solution)/shard_map/all_to_all | solution.py:310
  104.1 6.2 %shard_map.121 = f32[4,64,256]{2,1,0:T(8,128)} custom-call(bf16[128,2,8,512]{3,2,1,0:T(8,128)(2,1)} %bitcast.6.refs_0_, bf16[4,512,512]{2,1,0:T(8,128)(2,1)} %copy.31.refs_1_, f32[4,256,1]{2,1,0:T(8,128)} %constant.60.clone.refs_2_, f32[4,256,1]{2,1,0:T(8,128)} %constant.61.clone.refs_3_, f32[4,256,256]{2,1,0:T(8,128)} %shard_map.120.refs_4_), custom_call_target="tpu_custom_call" | custom-call | flops 1073741824 | bytes 4194304 | tf_op jit(solution)/shard_map/pallas_call | solution.py:294
  110.3 1.0 fusion.11
  111.2 1.3 %collective-permute-start = (f32[64,256]{1,0:T(8,128)S(1)}, f32[64,256]{1,0:T(8,128)S(1)}, u32[]{:S(2)}, u32[]{:S(2)}) collective-permute-start(f32[64,256]{1,0:T(8,128)S(1)} %get-tuple-element.8), channel_id=1, source_target_pairs={{0,1},{1,0},{2,3},{3,2},{4,5},{5,4},{6,7},{7,6},{8,9},{9,8},{10,11... | collective-permute-start | bytes 196616 | tf_op jit(solution)/shard_map/ppermute | solution.py:323
  112.9 1.4 %collective-permute-start.2 = (f32[64,256]{1,0:T(8,128)S(1)}, f32[64,256]{1,0:T(8,128)S(1)}, u32[]{:S(2)}, u32[]{:S(2)}) collective-permute-start(f32[64,256]{1,0:T(8,128)S(1)} %get-tuple-element.6), channel_id=1, source_target_pairs={{0,3},{1,2},{2,1},{3,0},{4,7},{5,6},{6,5},{7,4},{8,11},{9,10},{10,... | collective-permute-start | bytes 196616 | tf_op jit(solution)/shard_map/ppermute | solution.py:323
  114.3 1.9 %collective-permute-done.1 = f32[64,256]{1,0:T(8,128)S(1)} collective-permute-done((f32[64,256]{1,0:T(8,128)S(1)}, f32[64,256]{1,0:T(8,128)S(1)}, u32[]{:S(2)}, u32[]{:S(2)}) %collective-permute-start.1) | collective-permute-done | bytes 65568 | tf_op jit(solution)/shard_map/ppermute | solution.py:323
  116.2 1.6 %collective-permute-done.2 = f32[64,256]{1,0:T(8,128)S(1)} collective-permute-done((f32[64,256]{1,0:T(8,128)S(1)}, f32[64,256]{1,0:T(8,128)S(1)}, u32[]{:S(2)}, u32[]{:S(2)}) %collective-permute-start.2) | collective-permute-done | bytes 65568 | tf_op jit(solution)/shard_map/ppermute | solution.py:323
  117.8 0.6 gather_fusion
  118.4 0.8 bitcast_select_fusion
  (24 shorter events, 2.0 us)
Async XLA Ops:
  0.8 3.0 %copy-start.3 = (bf16[2,2,128,128]{3,2,1,0:T(8,128)(2,1)S(1)}, bf16[2,2,128,128]{3,2,1,0:T(8,128)(2,1)}, u32[]{:S(2)}) copy-start(bf16[2,2,128,128]{3,2,1,0:T(8,128)(2,1)} %constant.57.clone) | copy-start | bytes 393220
  25.9 41.4 %all-to-all-start.1 = ((bf16[2,8,128,512]{3,1,0,2:T(8,128)(2,1)}), bf16[2,8,128,512]{3,1,0,2:T(8,128)(2,1)S(1)}, u32[]{:S(2)}, u32[]{:S(2)}) async-start(bf16[2,8,128,512]{3,1,0,2:T(8,128)(2,1)} %copy.29), calls=%async_computation.1 | async-start | bytes 4194304 | tf_op jit(solution)/shard_map/all_to_all | solution.py:310
  50.3 24.1 %copy-start.2 = (bf16[256,256,1]{1,0,2:T(8,128)(2,1)S(1)}, bf16[256,256,1]{1,0,2:T(8,128)(2,1)}, u32[]{:S(2)}) copy-start(bf16[256,256,1]{1,0,2:T(8,128)(2,1)} %constant.64) | copy-start | bytes 393220
  50.3 24.1 %copy-start.4 = (s32[4,256]{1,0:T(4,128)S(1)}, s32[4,256]{1,0:T(4,128)}, u32[]{:S(2)}) copy-start(s32[4,256]{1,0:T(4,128)} %param.15) | copy-start | bytes 12292
  50.3 24.5 %copy-start.1 = (bf16[256,256,1]{1,0,2:T(8,128)(2,1)S(1)}, bf16[256,256,1]{1,0,2:T(8,128)(2,1)}, u32[]{:S(2)}) copy-start(bf16[256,256,1]{1,0,2:T(8,128)(2,1)} %constant.65) | copy-start | bytes 393220
  67.3 1.3 %copy-start = (bf16[2,8,128,512]{3,1,0,2:T(8,128)(2,1)}, bf16[2,8,128,512]{3,1,0,2:T(8,128)(2,1)S(1)}, u32[]{:S(2)}) copy-start(bf16[2,8,128,512]{3,1,0,2:T(8,128)(2,1)S(1)} %all-to-all-done.1) | copy-start | bytes 6291460
  68.7 35.4 %all-to-all-start = ((bf16[2,8,128,512]{3,1,0,2:T(8,128)(2,1)}), bf16[2,8,128,512]{3,1,0,2:T(8,128)(2,1)}, u32[]{:S(2)}, u32[]{:S(2)}) async-start(bf16[2,8,128,512]{3,1,0,2:T(8,128)(2,1)} %copy.24), calls=%async_computation | async-start | bytes 4194304 | tf_op jit(solution)/shard_map/all_to_all | solution.py:310
  111.2 3.0 %collective-permute-start = (f32[64,256]{1,0:T(8,128)S(1)}, f32[64,256]{1,0:T(8,128)S(1)}, u32[]{:S(2)}, u32[]{:S(2)}) collective-permute-start(f32[64,256]{1,0:T(8,128)S(1)} %get-tuple-element.8), channel_id=1, source_target_pairs={{0,1},{1,0},{2,3},{3,2},{4,5},{5,4},{6,7},{7,6},{8,9},{9,8},{10,11... | collective-permute-start | bytes 196616 | tf_op jit(solution)/shard_map/ppermute | solution.py:323
  112.6 3.6 %collective-permute-start.1 = (f32[64,256]{1,0:T(8,128)S(1)}, f32[64,256]{1,0:T(8,128)S(1)}, u32[]{:S(2)}, u32[]{:S(2)}) collective-permute-start(f32[64,256]{1,0:T(8,128)S(1)} %get-tuple-element.7), channel_id=1, source_target_pairs={{0,2},{1,3},{2,0},{3,1},{4,6},{5,7},{6,4},{7,5},{8,10},{9,11},{10,... | collective-permute-start | bytes 196616 | tf_op jit(solution)/shard_map/ppermute | solution.py:323
  112.9 4.9 %collective-permute-start.2 = (f32[64,256]{1,0:T(8,128)S(1)}, f32[64,256]{1,0:T(8,128)S(1)}, u32[]{:S(2)}, u32[]{:S(2)}) collective-permute-start(f32[64,256]{1,0:T(8,128)S(1)} %get-tuple-element.6), channel_id=1, source_target_pairs={{0,3},{1,2},{2,1},{3,0},{4,7},{5,6},{6,5},{7,4},{8,11},{9,10},{10,... | collective-permute-start | bytes 196616 | tf_op jit(solution)/shard_map/ppermute | solution.py:323

commit v9 on v8

--- a/solution.py
+++ b/solution.py
@@ -235,9 +235,8 @@
     gains = jnp.einsum("je,rpec->rpjc", picks_e, gains, preferred_element_type=jnp.float32)
     gains = jnp.concatenate([gains, gains], axis=3)
 
-    chunks = 2
-    pairs = FRAMES // 2 // chunks
-    chunk_lanes = pairs * 2 * quarter
+    chunk_pairs = [2, 6]
+    chunks = len(chunk_pairs)
     tables = beam_tables(grid_rows, grid_len, dish_rows)
     feed_index = jnp.arange(dish_count, dtype=jnp.int32)
     positions = jnp.arange(grid_len, dtype=jnp.int32)
@@ -248,12 +247,14 @@
 
     volts = voltages[:, 0].reshape(dish_rows, 2, samples // CHB, CHB)
 
-    span = (2 * pairs + TAPS - 1) * CHA
-
     def channelize_chunk(chunk):
-        first_row = 2 * chunk * pairs * CHA
+        pairs = chunk_pairs[chunk]
+        first_pair = sum(chunk_pairs[:chunk])
+        chunk_lanes = pairs * 2 * quarter
+        span = (2 * pairs + TAPS - 1) * CHA
+        first_row = 2 * first_pair * CHA
         return pl.pallas_call(
-            functools.partial(channelize_kernel, chunk * pairs, pairs),
+            functools.partial(channelize_kernel, first_pair, pairs),
             grid=(dish_rows,),
             in_specs=[
                 pl.BlockSpec(
@@ -277,6 +278,7 @@
 
     def beamform_chunk(received, carried, finish):
         carry_in = carried is not None
+        chunk_lanes = received.shape[3]
         in_specs = [
             pl.BlockSpec((dests, 2, dish_rows, lane_block), lambda f: (0, 0, 0, f)),
             pl.BlockSpec((dish_count, 2 * grid_len, 2 * grid_len), lambda f: (0, 0, 0)),

time: 120 us -> 121 us (level)
  waiting for transfers between devices: 40.8 us -> 36.4 us
  local copies, waits for them, and re-layouts: 23.4 us -> 26.4 us
  other arithmetic: 3.1 us -> 4.53 us
    all_to_all x2, waiting for transfers between devices: 37.3 us -> 32.9 us  [body(): lax.all_to_all(s, ('dish', 'freq'), 2, 2, tiled=True)]
    reshape x1, local copies, waits for them, and re-layouts: 2.37 us -> 4.15 us  [beam_tables(): return rows.reshape(grid_rows.shape[0], 2 * grid_len, 2 * grid_len)]
    concatenate x1, other arithmetic: 0.28 us -> 1.67 us  [beam_tables(): rows = jnp.concatenate([real_rows, imag_rows], axis=1)]
    unnamed x10 -> x12, local copies, waits for them, and re-layouts: 1.36 us -> 2.66 us
  transfers between devices with their start and end apart: 5 -> 5, of which waited for: 4 -> 4; matrix products, arithmetic and copies ran while one was open for 6% -> 10% of each run, Pallas kernels for 12% -> 12%
where the time goes in v9:
time: 121 us; the launch traced here: 120 us
  waiting for transfers between devices  36.4 us (30%)
  Pallas kernels  29.8 us (25%)
  local copies, waits for them, and re-layouts  26.4 us (22%)
  starting transfers between devices  21.1 us (17%)
  other arithmetic  4.53 us (4%)
  matrix products  1.94 us (2%)
    all_to_all x2, waiting for transfers between devices, body(): lax.all_to_all(s, ('dish', 'freq'), 2, 2, tiled=True)  32.9 us
    all_to_all x2, starting transfers between devices, body(): lax.all_to_all(s, ('dish', 'freq'), 2, 2, tiled=True)  18.1 us
    pallas_call x2, Pallas kernels, channelize_chunk(): pl.pallas_call(functools.partial(channelize_kernel, first_pair, pairs), g...  18 us
    pallas_call x2, Pallas kernels, beamform_chunk(): pl.pallas_call(functools.partial(beam_kernel, dish_count, carry_in, finis...  11.8 us
    another operation x1, local copies, waits for them, and re-layouts, body(): volts = voltages[:, 0].reshape(dish_rows, 2, samples // CHB, CHB)  8.4 us
    pallas_call x2, local copies, waits for them, and re-layouts, channelize_chunk(): pl.pallas_call(functools.partial(channelize_kernel, first_pair, pairs), g...  8.14 us
    reshape x1, local copies, waits for them, and re-layouts, beam_tables(): return rows.reshape(grid_rows.shape[0], 2 * grid_len, 2 * grid_len)  4.15 us
    ppermute x3, waiting for transfers between devices, body(): pieces.append(lax.ppermute(outgoing, 'dish', pairs_list))  3.5 us
  transfers between devices with their start and end apart: 5, of which 4 were waited for; matrix products, arithmetic and copies ran while one was open for 10% of the time, Pallas kernels for 12%

profile of v9, /device:TPU:1, one launch (start us, length us, event | category | flops | bytes accessed | tf_op | source)
XLA Modules:
  0.0 120.4 jit_solution(14595246384870290146)
XLA Ops:
  0.8 1.3 %reshape.86 = bf16[8,2,128,64]{3,2,1,0:T(8,128)(2,1)S(1)} reshape(bf16[8,1,2,8192]{3,2,1,0:T(2,128)(2,1)} %param.13) | data formatting | bytes 524288 | tf_op jit(solution)/shard_map/reshape;squeeze | solution.py:234
  2.5 1.3 %pad_maximum_fusion.g_ref = f32[8,2,128,128]{3,2,1,0:T(8,128)} fusion(f32[8,2,128,64]{3,2,1,0:T(8,128)S(1)} %convolution_bitcast_fusion), kind=kLoop, calls=%fused_computation.8 | loop fusion | flops 262144 | bytes 1572864 | tf_op jit(solution)/shard_map/concatenate | solution.py:236
  3.8 0.9 convolution_convert_fusion.2
  4.7 8.4 %reshape_squeeze.6.v_ref = bf16[8,2,1216,128]{3,2,1,0:T(8,128)(2,1)} reshape(bf16[8,1,2,155648]{3,2,1,0:T(2,128)(2,1)} %param.12) | data formatting | bytes 9961472 | tf_op jit(solution)/shard_map/reshape;squeeze | solution.py:248
  13.1 7.6 %shard_map.119 = bf16[2,8,128,256]{3,2,1,0:T(8,128)(2,1)} custom-call(bf16[8,2,1216,128]{3,2,1,0:T(8,128)(2,1)} %reshape_squeeze.6.v_ref, f32[4,64,128]{2,1,0:T(8,128)} %constant.54.clone.w_ref, bf16[128,128]{1,0:T(8,128)(2,1)} %constant.55.clone.t1_ref, f32[2,64,128]{2,1,0:T(8,128)} %constant.56.clone.tw_ref, bf16[2,256,128]{2,1,0:T(8,128)(2,1)} %bitcast.50, ...), custom_call_target="tpu_custom_call" | custom-call | flops 402653184 | bytes 6029312 | tf_op jit(solution)/shard_map/pallas_call | solution.py:256
  20.7 2.9 %copy.29 = bf16[2,8,128,256]{3,1,0,2:T(8,128)(2,1)} copy(bf16[2,8,128,256]{3,2,1,0:T(8,128)(2,1)} %shard_map.119) | data formatting | bytes 2097152 | tf_op jit(solution)/shard_map/pallas_call | solution.py:256
  23.6 11.5 %all-to-all-start.1 = ((bf16[2,8,128,256]{3,1,0,2:T(8,128)(2,1)}), bf16[2,8,128,256]{3,1,0,2:T(8,128)(2,1)S(1)}, u32[]{:S(2)}, u32[]{:S(2)}) async-start(bf16[2,8,128,256]{3,1,0,2:T(8,128)(2,1)} %copy.29), calls=%async_computation.1 | async-start | bytes 2097152 | tf_op jit(solution)/shard_map/all_to_all | solution.py:312
  35.1 10.4 %shard_map.118 = bf16[2,8,128,768]{3,2,1,0:T(8,128)(2,1)} custom-call(bf16[8,2,1216,128]{3,2,1,0:T(8,128)(2,1)} %reshape_squeeze.6.v_ref, f32[4,64,128]{2,1,0:T(8,128)} %constant.54.clone.w_ref, bf16[128,128]{1,0:T(8,128)(2,1)} %constant.55.clone.t1_ref, f32[2,64,128]{2,1,0:T(8,128)} %constant.56.clone.tw_ref, bf16[2,256,128]{2,1,0:T(8,128)(2,1)} %bitcast.51, ...), custom_call_target="tpu_custom_call" | custom-call | flops 1207959552 | bytes 8126464 | tf_op jit(solution)/shard_map/pallas_call | solution.py:256
  45.5 5.3 %copy.24 = bf16[2,8,128,768]{3,1,0,2:T(8,128)(2,1)} copy(bf16[2,8,128,768]{3,2,1,0:T(8,128)(2,1)} %shard_map.118) | data formatting | bytes 6291456 | tf_op jit(solution)/shard_map/pallas_call | solution.py:256
  50.8 3.1 %all-to-all-done.1 = bf16[2,8,128,256]{3,1,0,2:T(8,128)(2,1)S(1)} async-done(((bf16[2,8,128,256]{3,1,0,2:T(8,128)(2,1)}), bf16[2,8,128,256]{3,1,0,2:T(8,128)(2,1)S(1)}, u32[]{:S(2)}, u32[]{:S(2)}) %all-to-all-start.1) | async-done | bytes 1048608 | tf_op jit(solution)/shard_map/all_to_all | solution.py:312
  53.9 1.0 copy-done.1
  54.9 6.6 %all-to-all-start = ((bf16[2,8,128,768]{3,1,0,2:T(8,128)(2,1)}), bf16[2,8,128,768]{3,1,0,2:T(8,128)(2,1)S(1)}, u32[]{:S(2)}, u32[]{:S(2)}) async-start(bf16[2,8,128,768]{3,1,0,2:T(8,128)(2,1)} %copy.24), calls=%async_computation | async-start | bytes 6291456 | tf_op jit(solution)/shard_map/all_to_all | solution.py:312
  62.3 1.7 %maximum_maximum_fusion = bf16[4,512,32,2,8]{1,4,3,2,0:T(8,128)(2,1)} fusion(bf16[4,256,32,1,8]{1,4,3,2,0:T(8,128)(2,1)S(1)} %fusion, bf16[4,256,32,1,8]{1,4,3,2,0:T(8,128)(2,1)S(1)} %get-tuple-element.9, bf16[4,256,32,1,8]{1,4,3,2,0:T(8,128)(2,1)S(1)} %get-tuple-element.10), kind=kLoop, calls=%fused_computation.1 | loop fusion | flops 8388608 | bytes 3670016 | tf_op jit(solution)/shard_map/concatenate | solution.py:86
  64.0 4.1 %copy.31.refs_1_ = bf16[4,512,512]{2,1,0:T(8,128)(2,1)} copy(bf16[4,512,512]{1,2,0:T(8,128)(2,1)} %bitcast.48) | data formatting | bytes 4194304 | tf_op jit(solution)/shard_map/reshape | solution.py:87
  68.3 4.4 %shard_map.120.refs_4_ = f32[4,256,256]{2,1,0:T(8,128)} custom-call(bf16[128,2,8,256]{3,2,1,0:T(8,128)(2,1)} %bitcast.49, bf16[4,512,512]{2,1,0:T(8,128)(2,1)} %copy.31.refs_1_, f32[4,256,1]{2,1,0:T(8,128)} %constant.60.clone.refs_2_, f32[4,256,1]{2,1,0:T(8,128)} %constant.61.clone.refs_3_), custom_call_target="tpu_custom_call" | custom-call | flops 536870912 | bytes 3145728 | tf_op jit(solution)/shard_map/pallas_call | solution.py:296
  72.7 29.8 %all-to-all-done = bf16[2,8,128,768]{3,1,0,2:T(8,128)(2,1)S(1)} async-done(((bf16[2,8,128,768]{3,1,0,2:T(8,128)(2,1)}), bf16[2,8,128,768]{3,1,0,2:T(8,128)(2,1)S(1)}, u32[]{:S(2)}, u32[]{:S(2)}) %all-to-all-start) | async-done | bytes 3145760 | tf_op jit(solution)/shard_map/all_to_all | solution.py:312
  102.4 1.6 %copy-done = bf16[2,8,128,768]{3,1,0,2:T(8,128)(2,1)} copy-done((bf16[2,8,128,768]{3,1,0,2:T(8,128)(2,1)}, bf16[2,8,128,768]{3,1,0,2:T(8,128)(2,1)S(1)}, u32[]{:S(2)}) %copy-start) | copy-done | bytes 3145752
  104.1 7.5 %shard_map.121 = f32[4,64,256]{2,1,0:T(8,128)} custom-call(bf16[128,2,8,768]{3,2,1,0:T(8,128)(2,1)} %bitcast.47, bf16[4,512,512]{2,1,0:T(8,128)(2,1)} %copy.31.refs_1_, f32[4,256,1]{2,1,0:T(8,128)} %constant.60.clone.refs_2_, f32[4,256,1]{2,1,0:T(8,128)} %constant.61.clone.refs_3_, f32[4,256,256]{2,1,0:T(8,128)} %shard_map.120.refs_4_), custom_call_target="tpu_custom_call" | custom-call | flops 1610612736 | bytes 5242880 | tf_op jit(solution)/shard_map/pallas_call | solution.py:296
  111.5 1.0 fusion.11
  112.5 1.3 %collective-permute-start = (f32[64,256]{1,0:T(8,128)S(1)}, f32[64,256]{1,0:T(8,128)S(1)}, u32[]{:S(2)}, u32[]{:S(2)}) collective-permute-start(f32[64,256]{1,0:T(8,128)S(1)} %get-tuple-element.8), channel_id=1, source_target_pairs={{0,1},{1,0},{2,3},{3,2},{4,5},{5,4},{6,7},{7,6},{8,9},{9,8},{10,11... | collective-permute-start | bytes 196616 | tf_op jit(solution)/shard_map/ppermute | solution.py:325
  114.3 1.2 %collective-permute-start.2 = (f32[64,256]{1,0:T(8,128)S(1)}, f32[64,256]{1,0:T(8,128)S(1)}, u32[]{:S(2)}, u32[]{:S(2)}) collective-permute-start(f32[64,256]{1,0:T(8,128)S(1)} %get-tuple-element.6), channel_id=1, source_target_pairs={{0,3},{1,2},{2,1},{3,0},{4,7},{5,6},{6,5},{7,4},{8,11},{9,10},{10,... | collective-permute-start | bytes 196616 | tf_op jit(solution)/shard_map/ppermute | solution.py:325
  115.5 1.9 %collective-permute-done.1 = f32[64,256]{1,0:T(8,128)S(1)} collective-permute-done((f32[64,256]{1,0:T(8,128)S(1)}, f32[64,256]{1,0:T(8,128)S(1)}, u32[]{:S(2)}, u32[]{:S(2)}) %collective-permute-start.1) | collective-permute-done | bytes 65568 | tf_op jit(solution)/shard_map/ppermute | solution.py:325
  117.4 1.6 %collective-permute-done.2 = f32[64,256]{1,0:T(8,128)S(1)} collective-permute-done((f32[64,256]{1,0:T(8,128)S(1)}, f32[64,256]{1,0:T(8,128)S(1)}, u32[]{:S(2)}, u32[]{:S(2)}) %collective-permute-start.2) | collective-permute-done | bytes 65568 | tf_op jit(solution)/shard_map/ppermute | solution.py:325
  119.6 0.8 bitcast_select_fusion
  (26 shorter events, 3.1 us)
Async XLA Ops:
  0.0 3.8 %copy-start.4 = (bf16[2,2,128,128]{3,2,1,0:T(8,128)(2,1)S(1)}, bf16[2,2,128,128]{3,2,1,0:T(8,128)(2,1)}, u32[]{:S(2)}) copy-start(bf16[2,2,128,128]{3,2,1,0:T(8,128)(2,1)} %constant.57.clone) | copy-start | bytes 393220
  23.6 30.3 %all-to-all-start.1 = ((bf16[2,8,128,256]{3,1,0,2:T(8,128)(2,1)}), bf16[2,8,128,256]{3,1,0,2:T(8,128)(2,1)S(1)}, u32[]{:S(2)}, u32[]{:S(2)}) async-start(bf16[2,8,128,256]{3,1,0,2:T(8,128)(2,1)} %copy.29), calls=%async_computation.1 | async-start | bytes 2097152 | tf_op jit(solution)/shard_map/all_to_all | solution.py:312
  50.7 10.8 %copy-start.3 = (bf16[256,256,1]{1,0,2:T(8,128)(2,1)S(1)}, bf16[256,256,1]{1,0,2:T(8,128)(2,1)}, u32[]{:S(2)}) copy-start(bf16[256,256,1]{1,0,2:T(8,128)(2,1)} %constant.64) | copy-start | bytes 393220
  50.7 10.8 %copy-start.5 = (s32[4,256]{1,0:T(4,128)S(1)}, s32[4,256]{1,0:T(4,128)}, u32[]{:S(2)}) copy-start(s32[4,256]{1,0:T(4,128)} %param.15) | copy-start | bytes 12292
  50.8 11.2 %copy-start.2 = (bf16[256,256,1]{1,0,2:T(8,128)(2,1)S(1)}, bf16[256,256,1]{1,0,2:T(8,128)(2,1)}, u32[]{:S(2)}) copy-start(bf16[256,256,1]{1,0,2:T(8,128)(2,1)} %constant.65) | copy-start | bytes 393220
  53.9 1.0 copy-start.1
  54.9 47.5 %all-to-all-start = ((bf16[2,8,128,768]{3,1,0,2:T(8,128)(2,1)}), bf16[2,8,128,768]{3,1,0,2:T(8,128)(2,1)S(1)}, u32[]{:S(2)}, u32[]{:S(2)}) async-start(bf16[2,8,128,768]{3,1,0,2:T(8,128)(2,1)} %copy.24), calls=%async_computation | async-start | bytes 6291456 | tf_op jit(solution)/shard_map/all_to_all | solution.py:312
  102.4 1.6 %copy-start = (bf16[2,8,128,768]{3,1,0,2:T(8,128)(2,1)}, bf16[2,8,128,768]{3,1,0,2:T(8,128)(2,1)S(1)}, u32[]{:S(2)}) copy-start(bf16[2,8,128,768]{3,1,0,2:T(8,128)(2,1)S(1)} %all-to-all-done) | copy-start | bytes 9437188
  112.5 3.0 %collective-permute-start = (f32[64,256]{1,0:T(8,128)S(1)}, f32[64,256]{1,0:T(8,128)S(1)}, u32[]{:S(2)}, u32[]{:S(2)}) collective-permute-start(f32[64,256]{1,0:T(8,128)S(1)} %get-tuple-element.8), channel_id=1, source_target_pairs={{0,1},{1,0},{2,3},{3,2},{4,5},{5,4},{6,7},{7,6},{8,9},{9,8},{10,11... | collective-permute-start | bytes 196616 | tf_op jit(solution)/shard_map/ppermute | solution.py:325
  113.8 3.6 %collective-permute-start.1 = (f32[64,256]{1,0:T(8,128)S(1)}, f32[64,256]{1,0:T(8,128)S(1)}, u32[]{:S(2)}, u32[]{:S(2)}) collective-permute-start(f32[64,256]{1,0:T(8,128)S(1)} %get-tuple-element.7), channel_id=1, source_target_pairs={{0,2},{1,3},{2,0},{3,1},{4,6},{5,7},{6,4},{7,5},{8,10},{9,11},{10,... | collective-permute-start | bytes 196616 | tf_op jit(solution)/shard_map/ppermute | solution.py:325
  114.3 4.8 %collective-permute-start.2 = (f32[64,256]{1,0:T(8,128)S(1)}, f32[64,256]{1,0:T(8,128)S(1)}, u32[]{:S(2)}, u32[]{:S(2)}) collective-permute-start(f32[64,256]{1,0:T(8,128)S(1)} %get-tuple-element.6), channel_id=1, source_target_pairs={{0,3},{1,2},{2,1},{3,0},{4,7},{5,6},{6,5},{7,4},{8,11},{9,10},{10,... | collective-permute-start | bytes 196616 | tf_op jit(solution)/shard_map/ppermute | solution.py:325

commit v10 on v9

--- a/solution.py
+++ b/solution.py
@@ -15,6 +15,7 @@
 CHB = 128
 TAPS = 4
 FRAMES = 16
+FEEDS_PER_STEP = 2
 
 
 full_turn = 2.0 * math.pi
@@ -93,9 +94,8 @@
     t1 = t1_ref[...]
     t2_real = t2_ref[0]
     t2_imag = t2_ref[1]
-    g_real = g_ref[0, 0]
-    g_imag = g_ref[0, 1]
     half = t2_real.shape[0] // 2
+    feeds = v_ref.shape[0]
 
     def one_frame(pieces):
         acc = None
@@ -110,11 +110,13 @@
         turned_imag = sec_real * sin_tw + sec_imag * cos_tw
         return turned_real.astype(jnp.bfloat16), turned_imag.astype(jnp.bfloat16)
 
-    def pair(step, carry):
+    def pair(feed, step):
+        g_real = g_ref[feed, 0].astype(jnp.float32)
+        g_imag = g_ref[feed, 1].astype(jnp.float32)
         pieces = []
         for offset in range(TAPS + 1):
             start = pl.multiple_of((2 * (step - first_pair) + offset) * CHA, CHA)
-            pieces.append(v_ref[0, :, pl.ds(start, CHA), :].astype(jnp.float32))
+            pieces.append(v_ref[feed, :, pl.ds(start, CHA), :].astype(jnp.float32))
         first_real, first_imag = one_frame(pieces[:TAPS])
         second_real, second_imag = one_frame(pieces[1:])
         both_real = jnp.concatenate([first_real, second_real], axis=0)
@@ -128,11 +130,12 @@
         out_real = spec_real * g_real - spec_imag * g_imag
         out_imag = spec_real * g_imag + spec_imag * g_real
         lanes = pl.ds(pl.multiple_of((step - first_pair) * 2 * CHA, 2 * CHA), 2 * CHA)
-        o_ref[0, 0, :, lanes] = out_real.astype(o_ref.dtype)
-        o_ref[1, 0, :, lanes] = out_imag.astype(o_ref.dtype)
-        return carry
-
-    lax.fori_loop(first_pair, first_pair + pairs, pair, 0, unroll=True)
+        o_ref[0, feed, :, lanes] = out_real.astype(o_ref.dtype)
+        o_ref[1, feed, :, lanes] = out_imag.astype(o_ref.dtype)
+
+    for feed in range(feeds):
+        for step in range(first_pair, first_pair + pairs):
+            pair(feed, step)
 
 
 def beam_kernel(dish_count, carry_in, finish, *refs):
@@ -233,9 +236,9 @@
     ).astype(jnp.bfloat16).reshape(2, 2 * dests, CHB)
     gains = feed_gains[:, 0].reshape(dish_rows, 2, CHB, CHA)
     gains = jnp.einsum("je,rpec->rpjc", picks_e, gains, preferred_element_type=jnp.float32)
-    gains = jnp.concatenate([gains, gains], axis=3)
-
-    chunk_pairs = [2, 6]
+    gains = jnp.concatenate([gains, gains], axis=3).astype(jnp.bfloat16)
+
+    chunk_pairs = [4, 4]
     chunks = len(chunk_pairs)
     tables = beam_tables(grid_rows, grid_len, dish_rows)
     feed_index = jnp.arange(dish_count, dtype=jnp.int32)
@@ -255,19 +258,19 @@
         first_row = 2 * first_pair * CHA
         return pl.pallas_call(
             functools.partial(channelize_kernel, first_pair, pairs),
-            grid=(dish_rows,),
+            grid=(dish_rows // FEEDS_PER_STEP,),
             in_specs=[
                 pl.BlockSpec(
-                    (pl.Element(1), pl.Element(2), pl.Element(span), pl.Element(CHB)),
-                    lambda r: (r, 0, first_row, 0),
+                    (pl.Element(FEEDS_PER_STEP), pl.Element(2), pl.Element(span), pl.Element(CHB)),
+                    lambda r: (r * FEEDS_PER_STEP, 0, first_row, 0),
                 ),
                 pl.BlockSpec((TAPS, CHA, CHB), lambda r: (0, 0, 0)),
                 pl.BlockSpec((2 * CHA, 2 * CHA), lambda r: (0, 0)),
                 pl.BlockSpec((2, CHA, CHB), lambda r: (0, 0, 0)),
                 pl.BlockSpec((2, 2 * dests, CHB), lambda r: (0, 0, 0)),
-                pl.BlockSpec((1, 2, dests, 2 * CHA), lambda r: (r, 0, 0, 0)),
+                pl.BlockSpec((FEEDS_PER_STEP, 2, dests, 2 * CHA), lambda r: (r, 0, 0, 0)),
             ],
-            out_specs=pl.BlockSpec((2, 1, dests, chunk_lanes), lambda r: (0, r, 0, 0)),
+            out_specs=pl.BlockSpec((2, FEEDS_PER_STEP, dests, chunk_lanes), lambda r: (0, r, 0, 0)),
             out_shape=jax.ShapeDtypeStruct((2, dish_rows, dests, chunk_lanes), jnp.bfloat16),
             cost_estimate=pl.CostEstimate(
                 flops=int(dish_rows * pairs * 2 * 2 * 128 * 128 * 128 * 3),

time: 121 us -> 118 us (0.975)
  waiting for transfers between devices: 36.4 us -> 42.5 us
  Pallas kernels: 29.8 us -> 26 us
  local copies, waits for them, and re-layouts: 26.4 us -> 23.7 us
  other arithmetic: 4.53 us -> 2.91 us
    all_to_all x2, waiting for transfers between devices: 32.9 us -> 39 us  [body(): lax.all_to_all(s, ('dish', 'freq'), 2, 2, tiled=True)]
    pallas_call x2, Pallas kernels: 18 us -> 14 us  [channelize_chunk(): pl.pallas_call(functools.partial(channelize_kernel, first_pair, pairs), g...]
    reshape x1, local copies, waits for them, and re-layouts: 4.15 us -> 2.37 us  [beam_tables(): return rows.reshape(grid_rows.shape[0], 2 * grid_len, 2 * grid_len)]
    concatenate x1, other arithmetic: 1.67 us -> 0.28 us  [beam_tables(): rows = jnp.concatenate([real_rows, imag_rows], axis=1)]
    unnamed x12 -> x10, local copies, waits for them, and re-layouts: 2.66 us -> 1.36 us
  transfers between devices with their start and end apart: 5 -> 5, of which waited for: 4 -> 4; matrix products, arithmetic and copies ran while one was open for 10% -> 6% of each run, Pallas kernels for 12% -> 11%
where the time goes in v10:
time: 118 us; the launch traced here: 117 us
  waiting for transfers between devices  42.5 us (36%)
  Pallas kernels  26 us (22%)
  local copies, waits for them, and re-layouts  23.7 us (20%)
  starting transfers between devices  20.3 us (17%)
  other arithmetic  2.91 us (2%)
  matrix products  1.93 us (2%)
    all_to_all x2, waiting for transfers between devices, body(): lax.all_to_all(s, ('dish', 'freq'), 2, 2, tiled=True)  39 us
    all_to_all x2, starting transfers between devices, body(): lax.all_to_all(s, ('dish', 'freq'), 2, 2, tiled=True)  17.2 us
    pallas_call x2, Pallas kernels, channelize_chunk(): pl.pallas_call(functools.partial(channelize_kernel, first_pair, pairs), g...  14 us
    pallas_call x2, Pallas kernels, beamform_chunk(): pl.pallas_call(functools.partial(beam_kernel, dish_count, carry_in, finis...  12 us
    another operation x1, local copies, waits for them, and re-layouts, body(): volts = voltages[:, 0].reshape(dish_rows, 2, samples // CHB, CHB)  8.4 us
    pallas_call x2, local copies, waits for them, and re-layouts, channelize_chunk(): pl.pallas_call(functools.partial(channelize_kernel, first_pair, pairs), g...  8.19 us
    ppermute x3, waiting for transfers between devices, body(): pieces.append(lax.ppermute(outgoing, 'dish', pairs_list))  3.5 us
    ppermute x3, starting transfers between devices, body(): pieces.append(lax.ppermute(outgoing, 'dish', pairs_list))  3.03 us
  transfers between devices with their start and end apart: 5, of which 4 were waited for; matrix products, arithmetic and copies ran while one was open for 6% of the time, Pallas kernels for 11%

profile of v10, /device:TPU:1, one launch (start us, length us, event | category | flops | bytes accessed | tf_op | source)
XLA Modules:
  0.0 117.5 jit_solution(16462161963601411236)
XLA Ops:
  0.0 0.7 broadcast_multiply_fusion
  0.8 1.3 %reshape.86 = bf16[8,2,128,64]{3,2,1,0:T(8,128)(2,1)S(1)} reshape(bf16[8,1,2,8192]{3,2,1,0:T(2,128)(2,1)} %param.13) | data formatting | bytes 524288 | tf_op jit(solution)/shard_map/reshape;squeeze | solution.py:237
  2.8 1.1 pad_maximum_fusion.g_ref
  3.9 0.9 convolution_convert_fusion.3
  4.7 8.4 %reshape_squeeze.6.v_ref = bf16[8,2,1216,128]{3,2,1,0:T(8,128)(2,1)} reshape(bf16[8,1,2,155648]{3,2,1,0:T(2,128)(2,1)} %param.12) | data formatting | bytes 9961472 | tf_op jit(solution)/shard_map/reshape;squeeze | solution.py:251
  13.1 7.0 %shard_map.119 = bf16[2,8,128,512]{3,2,1,0:T(8,128)(2,1)} custom-call(bf16[8,2,1216,128]{3,2,1,0:T(8,128)(2,1)} %reshape_squeeze.6.v_ref, f32[4,64,128]{2,1,0:T(8,128)} %constant.54.clone.w_ref, bf16[128,128]{1,0:T(8,128)(2,1)} %constant.55.clone.t1_ref, f32[2,64,128]{2,1,0:T(8,128)} %constant.56.clone.tw_ref, bf16[2,256,128]{2,1,0:T(8,128)(2,1)} %bitcast.49, ...), custom_call_target="tpu_custom_call" | custom-call | flops 805306368 | bytes 7077888 | tf_op jit(solution)/shard_map/pallas_call | solution.py:259
  20.1 4.1 %copy.40 = bf16[2,8,128,512]{3,1,0,2:T(8,128)(2,1)} copy(bf16[2,8,128,512]{3,2,1,0:T(8,128)(2,1)} %shard_map.119) | data formatting | bytes 4194304 | tf_op jit(solution)/shard_map/pallas_call | solution.py:259
  24.2 11.5 %all-to-all-start.1 = ((bf16[2,8,128,512]{3,1,0,2:T(8,128)(2,1)}), bf16[2,8,128,512]{3,1,0,2:T(8,128)(2,1)S(1)}, u32[]{:S(2)}, u32[]{:S(2)}) async-start(bf16[2,8,128,512]{3,1,0,2:T(8,128)(2,1)} %copy.40), calls=%async_computation.1 | async-start | bytes 4194304 | tf_op jit(solution)/shard_map/all_to_all | solution.py:315
  35.7 7.0 %shard_map.118 = bf16[2,8,128,512]{3,2,1,0:T(8,128)(2,1)} custom-call(bf16[8,2,1216,128]{3,2,1,0:T(8,128)(2,1)} %reshape_squeeze.6.v_ref, f32[4,64,128]{2,1,0:T(8,128)} %constant.54.clone.w_ref, bf16[128,128]{1,0:T(8,128)(2,1)} %constant.55.clone.t1_ref, f32[2,64,128]{2,1,0:T(8,128)} %constant.56.clone.tw_ref, bf16[2,256,128]{2,1,0:T(8,128)(2,1)} %bitcast.50, ...), custom_call_target="tpu_custom_call" | custom-call | flops 805306368 | bytes 7077888 | tf_op jit(solution)/shard_map/pallas_call | solution.py:259
  42.7 4.1 %copy.35 = bf16[2,8,128,512]{3,1,0,2:T(8,128)(2,1)} copy(bf16[2,8,128,512]{3,2,1,0:T(8,128)(2,1)} %shard_map.118) | data formatting | bytes 4194304 | tf_op jit(solution)/shard_map/pallas_call | solution.py:259
  46.8 18.8 %all-to-all-done.1 = bf16[2,8,128,512]{3,1,0,2:T(8,128)(2,1)S(1)} async-done(((bf16[2,8,128,512]{3,1,0,2:T(8,128)(2,1)}), bf16[2,8,128,512]{3,1,0,2:T(8,128)(2,1)S(1)}, u32[]{:S(2)}, u32[]{:S(2)}) %all-to-all-start.1) | async-done | bytes 2097184 | tf_op jit(solution)/shard_map/all_to_all | solution.py:315
  65.6 1.3 %copy-done = bf16[2,8,128,512]{3,1,0,2:T(8,128)(2,1)} copy-done((bf16[2,8,128,512]{3,1,0,2:T(8,128)(2,1)}, bf16[2,8,128,512]{3,1,0,2:T(8,128)(2,1)S(1)}, u32[]{:S(2)}) %copy-start) | copy-done | bytes 2097176
  67.0 5.7 %all-to-all-start = ((bf16[2,8,128,512]{3,1,0,2:T(8,128)(2,1)}), bf16[2,8,128,512]{3,1,0,2:T(8,128)(2,1)}, u32[]{:S(2)}, u32[]{:S(2)}) async-start(bf16[2,8,128,512]{3,1,0,2:T(8,128)(2,1)} %copy.35), calls=%async_computation | async-start | bytes 4194304 | tf_op jit(solution)/shard_map/all_to_all | solution.py:315
  73.8 2.4 %copy.42.refs_1_ = bf16[4,512,512]{2,1,0:T(8,128)(2,1)} copy(bf16[4,512,512]{1,2,0:T(8,128)(2,1)S(1)} %bitcast.47) | data formatting | bytes 4194304 | tf_op jit(solution)/shard_map/reshape | solution.py:88
  76.3 5.9 %shard_map.120.refs_4_ = f32[4,256,256]{2,1,0:T(8,128)} custom-call(bf16[128,2,8,512]{3,2,1,0:T(8,128)(2,1)} %bitcast.46, bf16[4,512,512]{2,1,0:T(8,128)(2,1)} %copy.42.refs_1_, f32[4,256,1]{2,1,0:T(8,128)} %constant.60.clone.refs_2_, f32[4,256,1]{2,1,0:T(8,128)} %constant.61.clone.refs_3_), custom_call_target="tpu_custom_call" | custom-call | flops 1073741824 | bytes 4194304 | tf_op jit(solution)/shard_map/pallas_call | solution.py:299
  82.2 20.2 %all-to-all-done = bf16[2,8,128,512]{3,1,0,2:T(8,128)(2,1)} async-done(((bf16[2,8,128,512]{3,1,0,2:T(8,128)(2,1)}), bf16[2,8,128,512]{3,1,0,2:T(8,128)(2,1)}, u32[]{:S(2)}, u32[]{:S(2)}) %all-to-all-start) | async-done | bytes 2097184 | tf_op jit(solution)/shard_map/all_to_all | solution.py:315
  102.4 6.2 %shard_map.121 = f32[4,64,256]{2,1,0:T(8,128)} custom-call(bf16[128,2,8,512]{3,2,1,0:T(8,128)(2,1)} %bitcast.6.refs_0_, bf16[4,512,512]{2,1,0:T(8,128)(2,1)} %copy.42.refs_1_, f32[4,256,1]{2,1,0:T(8,128)} %constant.60.clone.refs_2_, f32[4,256,1]{2,1,0:T(8,128)} %constant.61.clone.refs_3_, f32[4,256,256]{2,1,0:T(8,128)} %shard_map.120.refs_4_), custom_call_target="tpu_custom_call" | custom-call | flops 1073741824 | bytes 4194304 | tf_op jit(solution)/shard_map/pallas_call | solution.py:299
  108.6 1.0 fusion.11
  109.5 1.3 %collective-permute-start = (f32[64,256]{1,0:T(8,128)S(1)}, f32[64,256]{1,0:T(8,128)S(1)}, u32[]{:S(2)}, u32[]{:S(2)}) collective-permute-start(f32[64,256]{1,0:T(8,128)S(1)} %get-tuple-element.8), channel_id=1, source_target_pairs={{0,1},{1,0},{2,3},{3,2},{4,5},{5,4},{6,7},{7,6},{8,9},{9,8},{10,11... | collective-permute-start | bytes 196616 | tf_op jit(solution)/shard_map/ppermute | solution.py:328
  111.1 1.4 %collective-permute-start.2 = (f32[64,256]{1,0:T(8,128)S(1)}, f32[64,256]{1,0:T(8,128)S(1)}, u32[]{:S(2)}, u32[]{:S(2)}) collective-permute-start(f32[64,256]{1,0:T(8,128)S(1)} %get-tuple-element.6), channel_id=1, source_target_pairs={{0,3},{1,2},{2,1},{3,0},{4,7},{5,6},{6,5},{7,4},{8,11},{9,10},{10,... | collective-permute-start | bytes 196616 | tf_op jit(solution)/shard_map/ppermute | solution.py:328
  112.6 1.9 %collective-permute-done.1 = f32[64,256]{1,0:T(8,128)S(1)} collective-permute-done((f32[64,256]{1,0:T(8,128)S(1)}, f32[64,256]{1,0:T(8,128)S(1)}, u32[]{:S(2)}, u32[]{:S(2)}) %collective-permute-start.1) | collective-permute-done | bytes 65568 | tf_op jit(solution)/shard_map/ppermute | solution.py:328
  114.5 1.6 %collective-permute-done.2 = f32[64,256]{1,0:T(8,128)S(1)} collective-permute-done((f32[64,256]{1,0:T(8,128)S(1)}, f32[64,256]{1,0:T(8,128)S(1)}, u32[]{:S(2)}, u32[]{:S(2)}) %collective-permute-start.2) | collective-permute-done | bytes 65568 | tf_op jit(solution)/shard_map/ppermute | solution.py:328
  116.1 0.6 gather_fusion
  116.7 0.8 bitcast_select_fusion
  (25 shorter events, 2.2 us)
Async XLA Ops:
  0.0 3.9 %copy-start.3 = (bf16[2,2,128,128]{3,2,1,0:T(8,128)(2,1)S(1)}, bf16[2,2,128,128]{3,2,1,0:T(8,128)(2,1)}, u32[]{:S(2)}) copy-start(bf16[2,2,128,128]{3,2,1,0:T(8,128)(2,1)} %constant.57.clone) | copy-start | bytes 393220
  24.2 41.4 %all-to-all-start.1 = ((bf16[2,8,128,512]{3,1,0,2:T(8,128)(2,1)}), bf16[2,8,128,512]{3,1,0,2:T(8,128)(2,1)S(1)}, u32[]{:S(2)}, u32[]{:S(2)}) async-start(bf16[2,8,128,512]{3,1,0,2:T(8,128)(2,1)} %copy.40), calls=%async_computation.1 | async-start | bytes 4194304 | tf_op jit(solution)/shard_map/all_to_all | solution.py:315
  46.8 25.9 %copy-start.2 = (bf16[256,256,1]{1,0,2:T(8,128)(2,1)S(1)}, bf16[256,256,1]{1,0,2:T(8,128)(2,1)}, u32[]{:S(2)}) copy-start(bf16[256,256,1]{1,0,2:T(8,128)(2,1)} %constant.64) | copy-start | bytes 393220
  46.8 25.9 %copy-start.4 = (s32[4,256]{1,0:T(4,128)S(1)}, s32[4,256]{1,0:T(4,128)}, u32[]{:S(2)}) copy-start(s32[4,256]{1,0:T(4,128)} %param.15) | copy-start | bytes 12292
  46.8 26.3 %copy-start.1 = (bf16[256,256,1]{1,0,2:T(8,128)(2,1)S(1)}, bf16[256,256,1]{1,0,2:T(8,128)(2,1)}, u32[]{:S(2)}) copy-start(bf16[256,256,1]{1,0,2:T(8,128)(2,1)} %constant.65) | copy-start | bytes 393220
  65.6 1.3 %copy-start = (bf16[2,8,128,512]{3,1,0,2:T(8,128)(2,1)}, bf16[2,8,128,512]{3,1,0,2:T(8,128)(2,1)S(1)}, u32[]{:S(2)}) copy-start(bf16[2,8,128,512]{3,1,0,2:T(8,128)(2,1)S(1)} %all-to-all-done.1) | copy-start | bytes 6291460
  67.0 35.4 %all-to-all-start = ((bf16[2,8,128,512]{3,1,0,2:T(8,128)(2,1)}), bf16[2,8,128,512]{3,1,0,2:T(8,128)(2,1)}, u32[]{:S(2)}, u32[]{:S(2)}) async-start(bf16[2,8,128,512]{3,1,0,2:T(8,128)(2,1)} %copy.35), calls=%async_computation | async-start | bytes 4194304 | tf_op jit(solution)/shard_map/all_to_all | solution.py:315
  109.5 3.0 %collective-permute-start = (f32[64,256]{1,0:T(8,128)S(1)}, f32[64,256]{1,0:T(8,128)S(1)}, u32[]{:S(2)}, u32[]{:S(2)}) collective-permute-start(f32[64,256]{1,0:T(8,128)S(1)} %get-tuple-element.8), channel_id=1, source_target_pairs={{0,1},{1,0},{2,3},{3,2},{4,5},{5,4},{6,7},{7,6},{8,9},{9,8},{10,11... | collective-permute-start | bytes 196616 | tf_op jit(solution)/shard_map/ppermute | solution.py:328
  110.8 3.6 %collective-permute-start.1 = (f32[64,256]{1,0:T(8,128)S(1)}, f32[64,256]{1,0:T(8,128)S(1)}, u32[]{:S(2)}, u32[]{:S(2)}) collective-permute-start(f32[64,256]{1,0:T(8,128)S(1)} %get-tuple-element.7), channel_id=1, source_target_pairs={{0,2},{1,3},{2,0},{3,1},{4,6},{5,7},{6,4},{7,5},{8,10},{9,11},{10,... | collective-permute-start | bytes 196616 | tf_op jit(solution)/shard_map/ppermute | solution.py:328
  111.1 4.9 %collective-permute-start.2 = (f32[64,256]{1,0:T(8,128)S(1)}, f32[64,256]{1,0:T(8,128)S(1)}, u32[]{:S(2)}, u32[]{:S(2)}) collective-permute-start(f32[64,256]{1,0:T(8,128)S(1)} %get-tuple-element.6), channel_id=1, source_target_pairs={{0,3},{1,2},{2,1},{3,0},{4,7},{5,6},{6,5},{7,4},{8,11},{9,10},{10,... | collective-permute-start | bytes 196616 | tf_op jit(solution)/shard_map/ppermute | solution.py:328

commit v11 on v10

--- a/solution.py
+++ b/solution.py
@@ -15,7 +15,7 @@
 CHB = 128
 TAPS = 4
 FRAMES = 16
-FEEDS_PER_STEP = 2
+FEEDS_PER_STEP = 4
 
 
 full_turn = 2.0 * math.pi

time: 118 us -> 118 us (level)
  no operation moved by 1% of the time
where the time goes in v11:
time: 118 us; the launch traced here: 117 us
  waiting for transfers between devices  42.6 us (36%)
  Pallas kernels  25.9 us (22%)
  local copies, waits for them, and re-layouts  23.7 us (20%)
  starting transfers between devices  20.3 us (17%)
  other arithmetic  2.91 us (2%)
  matrix products  1.92 us (2%)
    all_to_all x2, waiting for transfers between devices, body(): lax.all_to_all(s, ('dish', 'freq'), 2, 2, tiled=True)  39.1 us
    all_to_all x2, starting transfers between devices, body(): lax.all_to_all(s, ('dish', 'freq'), 2, 2, tiled=True)  17.2 us
    pallas_call x2, Pallas kernels, channelize_chunk(): pl.pallas_call(functools.partial(channelize_kernel, first_pair, pairs), g...  13.9 us
    pallas_call x2, Pallas kernels, beamform_chunk(): pl.pallas_call(functools.partial(beam_kernel, dish_count, carry_in, finis...  12 us
    another operation x1, local copies, waits for them, and re-layouts, body(): volts = voltages[:, 0].reshape(dish_rows, 2, samples // CHB, CHB)  8.4 us
    pallas_call x2, local copies, waits for them, and re-layouts, channelize_chunk(): pl.pallas_call(functools.partial(channelize_kernel, first_pair, pairs), g...  8.19 us
    ppermute x3, waiting for transfers between devices, body(): pieces.append(lax.ppermute(outgoing, 'dish', pairs_list))  3.5 us
    ppermute x3, starting transfers between devices, body(): pieces.append(lax.ppermute(outgoing, 'dish', pairs_list))  3.03 us
  transfers between devices with their start and end apart: 5, of which 4 were waited for; matrix products, arithmetic and copies ran while one was open for 6% of the time, Pallas kernels for 11%

profile of v11, /device:TPU:1, one launch (start us, length us, event | category | flops | bytes accessed | tf_op | source)
XLA Modules:
  0.0 117.4 jit_solution(14295333120948228002)
XLA Ops:
  0.0 0.7 broadcast_multiply_fusion
  0.8 1.3 %reshape.86 = bf16[8,2,128,64]{3,2,1,0:T(8,128)(2,1)S(1)} reshape(bf16[8,1,2,8192]{3,2,1,0:T(2,128)(2,1)} %param.13) | data formatting | bytes 524288 | tf_op jit(solution)/shard_map/reshape;squeeze | solution.py:237
  2.8 1.1 pad_maximum_fusion.g_ref
  3.9 0.9 convolution_convert_fusion.3
  4.7 8.4 %reshape_squeeze.6.v_ref = bf16[8,2,1216,128]{3,2,1,0:T(8,128)(2,1)} reshape(bf16[8,1,2,155648]{3,2,1,0:T(2,128)(2,1)} %param.12) | data formatting | bytes 9961472 | tf_op jit(solution)/shard_map/reshape;squeeze | solution.py:251
  13.1 6.9 %shard_map.119 = bf16[2,8,128,512]{3,2,1,0:T(8,128)(2,1)} custom-call(bf16[8,2,1216,128]{3,2,1,0:T(8,128)(2,1)} %reshape_squeeze.6.v_ref, f32[4,64,128]{2,1,0:T(8,128)} %constant.54.clone.w_ref, bf16[128,128]{1,0:T(8,128)(2,1)} %constant.55.clone.t1_ref, f32[2,64,128]{2,1,0:T(8,128)} %constant.56.clone.tw_ref, bf16[2,256,128]{2,1,0:T(8,128)(2,1)} %bitcast.49, ...), custom_call_target="tpu_custom_call" | custom-call | flops 805306368 | bytes 7077888 | tf_op jit(solution)/shard_map/pallas_call | solution.py:259
  20.1 4.1 %copy.40 = bf16[2,8,128,512]{3,1,0,2:T(8,128)(2,1)} copy(bf16[2,8,128,512]{3,2,1,0:T(8,128)(2,1)} %shard_map.119) | data formatting | bytes 4194304 | tf_op jit(solution)/shard_map/pallas_call | solution.py:259
  24.2 11.5 %all-to-all-start.1 = ((bf16[2,8,128,512]{3,1,0,2:T(8,128)(2,1)}), bf16[2,8,128,512]{3,1,0,2:T(8,128)(2,1)S(1)}, u32[]{:S(2)}, u32[]{:S(2)}) async-start(bf16[2,8,128,512]{3,1,0,2:T(8,128)(2,1)} %copy.40), calls=%async_computation.1 | async-start | bytes 4194304 | tf_op jit(solution)/shard_map/all_to_all | solution.py:315
  35.7 7.0 %shard_map.118 = bf16[2,8,128,512]{3,2,1,0:T(8,128)(2,1)} custom-call(bf16[8,2,1216,128]{3,2,1,0:T(8,128)(2,1)} %reshape_squeeze.6.v_ref, f32[4,64,128]{2,1,0:T(8,128)} %constant.54.clone.w_ref, bf16[128,128]{1,0:T(8,128)(2,1)} %constant.55.clone.t1_ref, f32[2,64,128]{2,1,0:T(8,128)} %constant.56.clone.tw_ref, bf16[2,256,128]{2,1,0:T(8,128)(2,1)} %bitcast.50, ...), custom_call_target="tpu_custom_call" | custom-call | flops 805306368 | bytes 7077888 | tf_op jit(solution)/shard_map/pallas_call | solution.py:259
  42.6 4.1 %copy.35 = bf16[2,8,128,512]{3,1,0,2:T(8,128)(2,1)} copy(bf16[2,8,128,512]{3,2,1,0:T(8,128)(2,1)} %shard_map.118) | data formatting | bytes 4194304 | tf_op jit(solution)/shard_map/pallas_call | solution.py:259
  46.7 18.9 %all-to-all-done.1 = bf16[2,8,128,512]{3,1,0,2:T(8,128)(2,1)S(1)} async-done(((bf16[2,8,128,512]{3,1,0,2:T(8,128)(2,1)}), bf16[2,8,128,512]{3,1,0,2:T(8,128)(2,1)S(1)}, u32[]{:S(2)}, u32[]{:S(2)}) %all-to-all-start.1) | async-done | bytes 2097184 | tf_op jit(solution)/shard_map/all_to_all | solution.py:315
  65.6 1.3 %copy-done = bf16[2,8,128,512]{3,1,0,2:T(8,128)(2,1)} copy-done((bf16[2,8,128,512]{3,1,0,2:T(8,128)(2,1)}, bf16[2,8,128,512]{3,1,0,2:T(8,128)(2,1)S(1)}, u32[]{:S(2)}) %copy-start) | copy-done | bytes 2097176
  66.9 5.7 %all-to-all-start = ((bf16[2,8,128,512]{3,1,0,2:T(8,128)(2,1)}), bf16[2,8,128,512]{3,1,0,2:T(8,128)(2,1)}, u32[]{:S(2)}, u32[]{:S(2)}) async-start(bf16[2,8,128,512]{3,1,0,2:T(8,128)(2,1)} %copy.35), calls=%async_computation | async-start | bytes 4194304 | tf_op jit(solution)/shard_map/all_to_all | solution.py:315
  73.7 2.4 %copy.42.refs_1_ = bf16[4,512,512]{2,1,0:T(8,128)(2,1)} copy(bf16[4,512,512]{1,2,0:T(8,128)(2,1)S(1)} %bitcast.47) | data formatting | bytes 4194304 | tf_op jit(solution)/shard_map/reshape | solution.py:88
  76.3 5.9 %shard_map.120.refs_4_ = f32[4,256,256]{2,1,0:T(8,128)} custom-call(bf16[128,2,8,512]{3,2,1,0:T(8,128)(2,1)} %bitcast.46, bf16[4,512,512]{2,1,0:T(8,128)(2,1)} %copy.42.refs_1_, f32[4,256,1]{2,1,0:T(8,128)} %constant.60.clone.refs_2_, f32[4,256,1]{2,1,0:T(8,128)} %constant.61.clone.refs_3_), custom_call_target="tpu_custom_call" | custom-call | flops 1073741824 | bytes 4194304 | tf_op jit(solution)/shard_map/pallas_call | solution.py:299
  82.1 20.2 %all-to-all-done = bf16[2,8,128,512]{3,1,0,2:T(8,128)(2,1)} async-done(((bf16[2,8,128,512]{3,1,0,2:T(8,128)(2,1)}), bf16[2,8,128,512]{3,1,0,2:T(8,128)(2,1)}, u32[]{:S(2)}, u32[]{:S(2)}) %all-to-all-start) | async-done | bytes 2097184 | tf_op jit(solution)/shard_map/all_to_all | solution.py:315
  102.3 6.2 %shard_map.121 = f32[4,64,256]{2,1,0:T(8,128)} custom-call(bf16[128,2,8,512]{3,2,1,0:T(8,128)(2,1)} %bitcast.6.refs_0_, bf16[4,512,512]{2,1,0:T(8,128)(2,1)} %copy.42.refs_1_, f32[4,256,1]{2,1,0:T(8,128)} %constant.60.clone.refs_2_, f32[4,256,1]{2,1,0:T(8,128)} %constant.61.clone.refs_3_, f32[4,256,256]{2,1,0:T(8,128)} %shard_map.120.refs_4_), custom_call_target="tpu_custom_call" | custom-call | flops 1073741824 | bytes 4194304 | tf_op jit(solution)/shard_map/pallas_call | solution.py:299
  108.5 1.0 fusion.11
  109.5 1.3 %collective-permute-start = (f32[64,256]{1,0:T(8,128)S(1)}, f32[64,256]{1,0:T(8,128)S(1)}, u32[]{:S(2)}, u32[]{:S(2)}) collective-permute-start(f32[64,256]{1,0:T(8,128)S(1)} %get-tuple-element.8), channel_id=1, source_target_pairs={{0,1},{1,0},{2,3},{3,2},{4,5},{5,4},{6,7},{7,6},{8,9},{9,8},{10,11... | collective-permute-start | bytes 196616 | tf_op jit(solution)/shard_map/ppermute | solution.py:328
  111.1 1.4 %collective-permute-start.2 = (f32[64,256]{1,0:T(8,128)S(1)}, f32[64,256]{1,0:T(8,128)S(1)}, u32[]{:S(2)}, u32[]{:S(2)}) collective-permute-start(f32[64,256]{1,0:T(8,128)S(1)} %get-tuple-element.6), channel_id=1, source_target_pairs={{0,3},{1,2},{2,1},{3,0},{4,7},{5,6},{6,5},{7,4},{8,11},{9,10},{10,... | collective-permute-start | bytes 196616 | tf_op jit(solution)/shard_map/ppermute | solution.py:328
  112.5 1.9 %collective-permute-done.1 = f32[64,256]{1,0:T(8,128)S(1)} collective-permute-done((f32[64,256]{1,0:T(8,128)S(1)}, f32[64,256]{1,0:T(8,128)S(1)}, u32[]{:S(2)}, u32[]{:S(2)}) %collective-permute-start.1) | collective-permute-done | bytes 65568 | tf_op jit(solution)/shard_map/ppermute | solution.py:328
  114.4 1.6 %collective-permute-done.2 = f32[64,256]{1,0:T(8,128)S(1)} collective-permute-done((f32[64,256]{1,0:T(8,128)S(1)}, f32[64,256]{1,0:T(8,128)S(1)}, u32[]{:S(2)}, u32[]{:S(2)}) %collective-permute-start.2) | collective-permute-done | bytes 65568 | tf_op jit(solution)/shard_map/ppermute | solution.py:328
  116.0 0.6 gather_fusion
  116.6 0.8 bitcast_select_fusion
  (25 shorter events, 2.2 us)
Async XLA Ops:
  0.0 3.9 %copy-start.3 = (bf16[2,2,128,128]{3,2,1,0:T(8,128)(2,1)S(1)}, bf16[2,2,128,128]{3,2,1,0:T(8,128)(2,1)}, u32[]{:S(2)}) copy-start(bf16[2,2,128,128]{3,2,1,0:T(8,128)(2,1)} %constant.57.clone) | copy-start | bytes 393220
  24.2 41.4 %all-to-all-start.1 = ((bf16[2,8,128,512]{3,1,0,2:T(8,128)(2,1)}), bf16[2,8,128,512]{3,1,0,2:T(8,128)(2,1)S(1)}, u32[]{:S(2)}, u32[]{:S(2)}) async-start(bf16[2,8,128,512]{3,1,0,2:T(8,128)(2,1)} %copy.40), calls=%async_computation.1 | async-start | bytes 4194304 | tf_op jit(solution)/shard_map/all_to_all | solution.py:315
  46.7 26.0 %copy-start.2 = (bf16[256,256,1]{1,0,2:T(8,128)(2,1)S(1)}, bf16[256,256,1]{1,0,2:T(8,128)(2,1)}, u32[]{:S(2)}) copy-start(bf16[256,256,1]{1,0,2:T(8,128)(2,1)} %constant.64) | copy-start | bytes 393220
  46.7 26.0 %copy-start.4 = (s32[4,256]{1,0:T(4,128)S(1)}, s32[4,256]{1,0:T(4,128)}, u32[]{:S(2)}) copy-start(s32[4,256]{1,0:T(4,128)} %param.15) | copy-start | bytes 12292
  46.7 26.4 %copy-start.1 = (bf16[256,256,1]{1,0,2:T(8,128)(2,1)S(1)}, bf16[256,256,1]{1,0,2:T(8,128)(2,1)}, u32[]{:S(2)}) copy-start(bf16[256,256,1]{1,0,2:T(8,128)(2,1)} %constant.65) | copy-start | bytes 393220
  65.6 1.3 %copy-start = (bf16[2,8,128,512]{3,1,0,2:T(8,128)(2,1)}, bf16[2,8,128,512]{3,1,0,2:T(8,128)(2,1)S(1)}, u32[]{:S(2)}) copy-start(bf16[2,8,128,512]{3,1,0,2:T(8,128)(2,1)S(1)} %all-to-all-done.1) | copy-start | bytes 6291460
  66.9 35.4 %all-to-all-start = ((bf16[2,8,128,512]{3,1,0,2:T(8,128)(2,1)}), bf16[2,8,128,512]{3,1,0,2:T(8,128)(2,1)}, u32[]{:S(2)}, u32[]{:S(2)}) async-start(bf16[2,8,128,512]{3,1,0,2:T(8,128)(2,1)} %copy.35), calls=%async_computation | async-start | bytes 4194304 | tf_op jit(solution)/shard_map/all_to_all | solution.py:315
  109.5 3.0 %collective-permute-start = (f32[64,256]{1,0:T(8,128)S(1)}, f32[64,256]{1,0:T(8,128)S(1)}, u32[]{:S(2)}, u32[]{:S(2)}) collective-permute-start(f32[64,256]{1,0:T(8,128)S(1)} %get-tuple-element.8), channel_id=1, source_target_pairs={{0,1},{1,0},{2,3},{3,2},{4,5},{5,4},{6,7},{7,6},{8,9},{9,8},{10,11... | collective-permute-start | bytes 196616 | tf_op jit(solution)/shard_map/ppermute | solution.py:328
  110.8 3.6 %collective-permute-start.1 = (f32[64,256]{1,0:T(8,128)S(1)}, f32[64,256]{1,0:T(8,128)S(1)}, u32[]{:S(2)}, u32[]{:S(2)}) collective-permute-start(f32[64,256]{1,0:T(8,128)S(1)} %get-tuple-element.7), channel_id=1, source_target_pairs={{0,2},{1,3},{2,0},{3,1},{4,6},{5,7},{6,4},{7,5},{8,10},{9,11},{10,... | collective-permute-start | bytes 196616 | tf_op jit(solution)/shard_map/ppermute | solution.py:328
  111.1 4.9 %collective-permute-start.2 = (f32[64,256]{1,0:T(8,128)S(1)}, f32[64,256]{1,0:T(8,128)S(1)}, u32[]{:S(2)}, u32[]{:S(2)}) collective-permute-start(f32[64,256]{1,0:T(8,128)S(1)} %get-tuple-element.6), channel_id=1, source_target_pairs={{0,3},{1,2},{2,1},{3,0},{4,7},{5,6},{6,5},{7,4},{8,11},{9,10},{10,... | collective-permute-start | bytes 196616 | tf_op jit(solution)/shard_map/ppermute | solution.py:328

commit v12 on v11

--- a/solution.py
+++ b/solution.py
@@ -138,16 +138,16 @@
             pair(feed, step)
 
 
-def beam_kernel(dish_count, carry_in, finish, *refs):
-    if carry_in:
-        x_ref, t_ref, c_ref, s_ref, init_ref, o_ref, acc_ref = refs
-    else:
-        x_ref, t_ref, c_ref, s_ref, o_ref, acc_ref = refs
+def beam_kernel(dish_count, carry_in, finish, lanes, *refs):
+    x_ref, t_ref, c_ref, s_ref = refs[:4]
+    init_ref = refs[4] if carry_in else None
+    out_refs = refs[4 + carry_in : -1]
+    acc_ref = refs[-1]
     step = pl.program_id(0)
     devices = x_ref.shape[0] // dish_count
     rows = x_ref.shape[2]
     grid_len = t_ref.shape[1] // 2
-    lanes = x_ref.shape[3]
+    lane_window = slice(None)
 
     @pl.when(step == 0)
     def _():
@@ -158,7 +158,9 @@
 
     parts = []
     for d in range(dish_count):
-        block = x_ref[pl.ds(d * devices, devices)].reshape(2 * rows * devices, lanes)
+        block = x_ref[pl.ds(d * devices, devices), :, :, lane_window].reshape(
+            2 * rows * devices, lanes
+        )
         sums = jnp.dot(t_ref[d], block, preferred_element_type=jnp.float32)
         sum_real = sums[:grid_len]
         sum_imag = sums[grid_len:]
@@ -186,10 +188,10 @@
     @pl.when(step == pl.num_programs(0) - 1)
     def _():
         if not finish:
-            o_ref[...] = acc_ref[...]
+            out_refs[0][...] = acc_ref[...]
             return
         me = lax.axis_index("dish")
-        width = o_ref.shape[1]
+        width = out_refs[0].shape[0]
         for shift in range(dish_count):
             target = jnp.bitwise_xor(me, shift)
             beam_index = jnp.bitwise_or(
@@ -201,7 +203,7 @@
                 folded = folded + total[:, k * CHB : (k + 1) * CHB]
             folded = folded + pltpu.roll(folded, width, 1)
             flipped = jnp.transpose(folded, (1, 0))
-            o_ref[shift] = flipped[:width] * (0.25 / FRAMES)
+            out_refs[shift][...] = flipped[:width] * (0.25 / FRAMES)
 
 
 def body(voltages, feed_gains, block_assign, grid_rows):
@@ -285,23 +287,24 @@
         in_specs = [
             pl.BlockSpec((dests, 2, dish_rows, lane_block), lambda f: (0, 0, 0, f)),
             pl.BlockSpec((dish_count, 2 * grid_len, 2 * grid_len), lambda f: (0, 0, 0)),
-            pl.BlockSpec((dish_count, grid_len, 1), lambda f: (0, 0, 0)),
-            pl.BlockSpec((dish_count, grid_len, 1), lambda f: (0, 0, 0)),
         ]
+        in_specs += [pl.BlockSpec((dish_count, grid_len, 1), lambda f: (0, 0, 0))] * 2
         operands = [received, tables, twist_cos, twist_sin]
         if carry_in:
             in_specs.append(pl.BlockSpec((dish_count, grid_len, lane_block), lambda f: (0, 0, 0)))
             operands.append(carried)
         if finish:
-            out_shape = (dish_count, quarter, grid_len)
+            out_specs = [pl.BlockSpec((quarter, grid_len), lambda f: (0, 0))] * dish_count
+            out_shape = [jax.ShapeDtypeStruct((quarter, grid_len), jnp.float32)] * dish_count
         else:
-            out_shape = (dish_count, grid_len, lane_block)
+            out_specs = pl.BlockSpec((dish_count, grid_len, lane_block), lambda f: (0, 0, 0))
+            out_shape = jax.ShapeDtypeStruct((dish_count, grid_len, lane_block), jnp.float32)
         return pl.pallas_call(
-            functools.partial(beam_kernel, dish_count, carry_in, finish),
+            functools.partial(beam_kernel, dish_count, carry_in, finish, lane_block),
             grid=(chunk_lanes // lane_block,),
             in_specs=in_specs,
-            out_specs=pl.BlockSpec(out_shape, lambda f: (0, 0, 0)),
-            out_shape=jax.ShapeDtypeStruct(out_shape, jnp.float32),
+            out_specs=out_specs,
+            out_shape=out_shape,
             scratch_shapes=[pltpu.VMEM((dish_count, grid_len, lane_block), jnp.float32)],
             cost_estimate=pl.CostEstimate(
                 flops=int(dish_count * 2 * 512 * 512 * chunk_lanes),

time: 118 us -> 118 us (level)
  no operation moved by 1% of the time
where the time goes in v12:
time: 118 us; the launch traced here: 117 us
  waiting for transfers between devices  42.8 us (36%)
  Pallas kernels  25.9 us (22%)
  local copies, waits for them, and re-layouts  22.7 us (19%)
  starting transfers between devices  20.2 us (17%)
  other arithmetic  3.75 us (3%)
  matrix products  1.93 us (2%)
    all_to_all x2, waiting for transfers between devices, body(): lax.all_to_all(s, ('dish', 'freq'), 2, 2, tiled=True)  39.1 us
    all_to_all x2, starting transfers between devices, body(): lax.all_to_all(s, ('dish', 'freq'), 2, 2, tiled=True)  17.2 us
    pallas_call x2, Pallas kernels, channelize_chunk(): pl.pallas_call(functools.partial(channelize_kernel, first_pair, pairs), g...  13.9 us
    pallas_call x2, Pallas kernels, beamform_chunk(): pl.pallas_call(functools.partial(beam_kernel, dish_count, carry_in, finis...  12 us
    another operation x1, local copies, waits for them, and re-layouts, body(): volts = voltages[:, 0].reshape(dish_rows, 2, samples // CHB, CHB)  8.4 us
    pallas_call x2, local copies, waits for them, and re-layouts, channelize_chunk(): pl.pallas_call(functools.partial(channelize_kernel, first_pair, pairs), g...  8.17 us
    ppermute x3, waiting for transfers between devices, body(): pieces.append(lax.ppermute(outgoing, 'dish', pairs_list))  3.72 us
    ppermute x3, starting transfers between devices, body(): pieces.append(lax.ppermute(outgoing, 'dish', pairs_list))  2.93 us
  transfers between devices with their start and end apart: 5, of which 4 were waited for; matrix products, arithmetic and copies ran while one was open for 6% of the time, Pallas kernels for 11%

profile of v12, /device:TPU:1, one launch (start us, length us, event | category | flops | bytes accessed | tf_op | source)
XLA Modules:
  0.0 117.4 jit_solution(2239146312015073388)
XLA Ops:
  0.0 0.7 broadcast_multiply_fusion
  0.8 1.3 %reshape.86 = bf16[8,2,128,64]{3,2,1,0:T(8,128)(2,1)S(1)} reshape(bf16[8,1,2,8192]{3,2,1,0:T(2,128)(2,1)} %param.13) | data formatting | bytes 524288 | tf_op jit(solution)/shard_map/reshape;squeeze | solution.py:239
  2.8 1.1 pad_maximum_fusion.g_ref
  3.9 0.9 convolution_convert_fusion.3
  4.7 8.4 %reshape_squeeze.6.v_ref = bf16[8,2,1216,128]{3,2,1,0:T(8,128)(2,1)} reshape(bf16[8,1,2,155648]{3,2,1,0:T(2,128)(2,1)} %param.12) | data formatting | bytes 9961472 | tf_op jit(solution)/shard_map/reshape;squeeze | solution.py:253
  13.1 6.9 %shard_map.119 = bf16[2,8,128,512]{3,2,1,0:T(8,128)(2,1)} custom-call(bf16[8,2,1216,128]{3,2,1,0:T(8,128)(2,1)} %reshape_squeeze.6.v_ref, f32[4,64,128]{2,1,0:T(8,128)} %constant.54.clone.w_ref, bf16[128,128]{1,0:T(8,128)(2,1)} %constant.55.clone.t1_ref, f32[2,64,128]{2,1,0:T(8,128)} %constant.56.clone.tw_ref, bf16[2,256,128]{2,1,0:T(8,128)(2,1)} %bitcast.44, ...), custom_call_target="tpu_custom_call" | custom-call | flops 805306368 | bytes 7077888 | tf_op jit(solution)/shard_map/pallas_call | solution.py:261
  20.1 4.1 %copy.40 = bf16[2,8,128,512]{3,1,0,2:T(8,128)(2,1)} copy(bf16[2,8,128,512]{3,2,1,0:T(8,128)(2,1)} %shard_map.119) | data formatting | bytes 4194304 | tf_op jit(solution)/shard_map/pallas_call | solution.py:261
  24.2 11.5 %all-to-all-start.1 = ((bf16[2,8,128,512]{3,1,0,2:T(8,128)(2,1)}), bf16[2,8,128,512]{3,1,0,2:T(8,128)(2,1)S(1)}, u32[]{:S(2)}, u32[]{:S(2)}) async-start(bf16[2,8,128,512]{3,1,0,2:T(8,128)(2,1)} %copy.40), calls=%async_computation.1 | async-start | bytes 4194304 | tf_op jit(solution)/shard_map/all_to_all | solution.py:318
  35.7 7.0 %shard_map.118 = bf16[2,8,128,512]{3,2,1,0:T(8,128)(2,1)} custom-call(bf16[8,2,1216,128]{3,2,1,0:T(8,128)(2,1)} %reshape_squeeze.6.v_ref, f32[4,64,128]{2,1,0:T(8,128)} %constant.54.clone.w_ref, bf16[128,128]{1,0:T(8,128)(2,1)} %constant.55.clone.t1_ref, f32[2,64,128]{2,1,0:T(8,128)} %constant.56.clone.tw_ref, bf16[2,256,128]{2,1,0:T(8,128)(2,1)} %bitcast.45, ...), custom_call_target="tpu_custom_call" | custom-call | flops 805306368 | bytes 7077888 | tf_op jit(solution)/shard_map/pallas_call | solution.py:261
  42.6 4.1 %copy.35 = bf16[2,8,128,512]{3,1,0,2:T(8,128)(2,1)} copy(bf16[2,8,128,512]{3,2,1,0:T(8,128)(2,1)} %shard_map.118) | data formatting | bytes 4194304 | tf_op jit(solution)/shard_map/pallas_call | solution.py:261
  46.7 18.9 %all-to-all-done.1 = bf16[2,8,128,512]{3,1,0,2:T(8,128)(2,1)S(1)} async-done(((bf16[2,8,128,512]{3,1,0,2:T(8,128)(2,1)}), bf16[2,8,128,512]{3,1,0,2:T(8,128)(2,1)S(1)}, u32[]{:S(2)}, u32[]{:S(2)}) %all-to-all-start.1) | async-done | bytes 2097184 | tf_op jit(solution)/shard_map/all_to_all | solution.py:318
  65.6 1.3 %copy-done = bf16[2,8,128,512]{3,1,0,2:T(8,128)(2,1)} copy-done((bf16[2,8,128,512]{3,1,0,2:T(8,128)(2,1)}, bf16[2,8,128,512]{3,1,0,2:T(8,128)(2,1)S(1)}, u32[]{:S(2)}) %copy-start) | copy-done | bytes 2097176
  66.9 5.7 %all-to-all-start = ((bf16[2,8,128,512]{3,1,0,2:T(8,128)(2,1)}), bf16[2,8,128,512]{3,1,0,2:T(8,128)(2,1)}, u32[]{:S(2)}, u32[]{:S(2)}) async-start(bf16[2,8,128,512]{3,1,0,2:T(8,128)(2,1)} %copy.35), calls=%async_computation | async-start | bytes 4194304 | tf_op jit(solution)/shard_map/all_to_all | solution.py:318
  73.7 2.4 %copy.42.refs_1_ = bf16[4,512,512]{2,1,0:T(8,128)(2,1)} copy(bf16[4,512,512]{1,2,0:T(8,128)(2,1)S(1)} %bitcast.42) | data formatting | bytes 4194304 | tf_op jit(solution)/shard_map/reshape | solution.py:88
  76.3 5.9 %shard_map.120.refs_4_ = f32[4,256,256]{2,1,0:T(8,128)} custom-call(bf16[128,2,8,512]{3,2,1,0:T(8,128)(2,1)} %bitcast.41, bf16[4,512,512]{2,1,0:T(8,128)(2,1)} %copy.42.refs_1_, f32[4,256,1]{2,1,0:T(8,128)} %constant.60.clone.refs_2_, f32[4,256,1]{2,1,0:T(8,128)} %constant.61.clone.refs_3_), custom_call_target="tpu_custom_call" | custom-call | flops 1073741824 | bytes 4194304 | tf_op jit(solution)/shard_map/pallas_call | solution.py:302
  82.1 20.2 %all-to-all-done = bf16[2,8,128,512]{3,1,0,2:T(8,128)(2,1)} async-done(((bf16[2,8,128,512]{3,1,0,2:T(8,128)(2,1)}), bf16[2,8,128,512]{3,1,0,2:T(8,128)(2,1)}, u32[]{:S(2)}, u32[]{:S(2)}) %all-to-all-start) | async-done | bytes 2097184 | tf_op jit(solution)/shard_map/all_to_all | solution.py:318
  102.3 6.2 %shard_map.121 = (f32[64,256]{1,0:T(8,128)}, f32[64,256]{1,0:T(8,128)}, f32[64,256]{1,0:T(8,128)}, f32[64,256]{1,0:T(8,128)}) custom-call(bf16[128,2,8,512]{3,2,1,0:T(8,128)(2,1)} %bitcast.6.refs_0_, bf16[4,512,512]{2,1,0:T(8,128)(2,1)} %copy.42.refs_1_, f32[4,256,1]{2,1,0:T(8,128)} %constant.60.clone.refs_2_, f32[4,256,1]{2,1,0:T(8,128)} %constant.61.clone.refs_3_, ...), custom_call_target="tpu_custom_call" | custom-call | flops 1073741824 | bytes 4194304 | tf_op jit(solution)/shard_map/pallas_call | solution.py:302
  108.5 1.2 %collective-permute-start = (f32[64,256]{1,0:T(8,128)}, f32[64,256]{1,0:T(8,128)S(1)}, u32[]{:S(2)}, u32[]{:S(2)}) collective-permute-start(f32[64,256]{1,0:T(8,128)} %get-tuple-element.10), channel_id=1, source_target_pairs={{0,1},{1,0},{2,3},{3,2},{4,5},{5,4},{6,7},{7,6},{8,9},{9,8},{10,11... | collective-permute-start | bytes 196616 | tf_op jit(solution)/shard_map/ppermute | solution.py:331
  110.0 1.4 %collective-permute-start.2 = (f32[64,256]{1,0:T(8,128)}, f32[64,256]{1,0:T(8,128)S(1)}, u32[]{:S(2)}, u32[]{:S(2)}) collective-permute-start(f32[64,256]{1,0:T(8,128)} %get-tuple-element.12), channel_id=1, source_target_pairs={{0,3},{1,2},{2,1},{3,0},{4,7},{5,6},{6,5},{7,4},{8,11},{9,10},{10,... | collective-permute-start | bytes 196616 | tf_op jit(solution)/shard_map/ppermute | solution.py:331
  111.4 2.1 %collective-permute-done.1 = f32[64,256]{1,0:T(8,128)S(1)} collective-permute-done((f32[64,256]{1,0:T(8,128)}, f32[64,256]{1,0:T(8,128)S(1)}, u32[]{:S(2)}, u32[]{:S(2)}) %collective-permute-start.1) | collective-permute-done | bytes 65568 | tf_op jit(solution)/shard_map/ppermute | solution.py:331
  113.6 1.6 %collective-permute-done.2 = f32[64,256]{1,0:T(8,128)S(1)} collective-permute-done((f32[64,256]{1,0:T(8,128)}, f32[64,256]{1,0:T(8,128)S(1)}, u32[]{:S(2)}, u32[]{:S(2)}) %collective-permute-start.2) | collective-permute-done | bytes 65568 | tf_op jit(solution)/shard_map/ppermute | solution.py:331
  115.2 0.9 pad_maximum_fusion.1
  116.0 0.6 gather_fusion
  116.6 0.8 bitcast_select_fusion
  (24 shorter events, 2.2 us)
Async XLA Ops:
  0.0 3.9 %copy-start.3 = (bf16[2,2,128,128]{3,2,1,0:T(8,128)(2,1)S(1)}, bf16[2,2,128,128]{3,2,1,0:T(8,128)(2,1)}, u32[]{:S(2)}) copy-start(bf16[2,2,128,128]{3,2,1,0:T(8,128)(2,1)} %constant.57.clone) | copy-start | bytes 393220
  24.2 41.4 %all-to-all-start.1 = ((bf16[2,8,128,512]{3,1,0,2:T(8,128)(2,1)}), bf16[2,8,128,512]{3,1,0,2:T(8,128)(2,1)S(1)}, u32[]{:S(2)}, u32[]{:S(2)}) async-start(bf16[2,8,128,512]{3,1,0,2:T(8,128)(2,1)} %copy.40), calls=%async_computation.1 | async-start | bytes 4194304 | tf_op jit(solution)/shard_map/all_to_all | solution.py:318
  46.7 26.0 %copy-start.2 = (bf16[256,256,1]{1,0,2:T(8,128)(2,1)S(1)}, bf16[256,256,1]{1,0,2:T(8,128)(2,1)}, u32[]{:S(2)}) copy-start(bf16[256,256,1]{1,0,2:T(8,128)(2,1)} %constant.64) | copy-start | bytes 393220
  46.7 26.0 %copy-start.4 = (s32[4,256]{1,0:T(4,128)S(1)}, s32[4,256]{1,0:T(4,128)}, u32[]{:S(2)}) copy-start(s32[4,256]{1,0:T(4,128)} %param.15) | copy-start | bytes 12292
  46.7 26.4 %copy-start.1 = (bf16[256,256,1]{1,0,2:T(8,128)(2,1)S(1)}, bf16[256,256,1]{1,0,2:T(8,128)(2,1)}, u32[]{:S(2)}) copy-start(bf16[256,256,1]{1,0,2:T(8,128)(2,1)} %constant.65) | copy-start | bytes 393220
  65.6 1.3 %copy-start = (bf16[2,8,128,512]{3,1,0,2:T(8,128)(2,1)}, bf16[2,8,128,512]{3,1,0,2:T(8,128)(2,1)S(1)}, u32[]{:S(2)}) copy-start(bf16[2,8,128,512]{3,1,0,2:T(8,128)(2,1)S(1)} %all-to-all-done.1) | copy-start | bytes 6291460
  66.9 35.4 %all-to-all-start = ((bf16[2,8,128,512]{3,1,0,2:T(8,128)(2,1)}), bf16[2,8,128,512]{3,1,0,2:T(8,128)(2,1)}, u32[]{:S(2)}, u32[]{:S(2)}) async-start(bf16[2,8,128,512]{3,1,0,2:T(8,128)(2,1)} %copy.35), calls=%async_computation | async-start | bytes 4194304 | tf_op jit(solution)/shard_map/all_to_all | solution.py:318
  108.5 2.9 %collective-permute-start = (f32[64,256]{1,0:T(8,128)}, f32[64,256]{1,0:T(8,128)S(1)}, u32[]{:S(2)}, u32[]{:S(2)}) collective-permute-start(f32[64,256]{1,0:T(8,128)} %get-tuple-element.10), channel_id=1, source_target_pairs={{0,1},{1,0},{2,3},{3,2},{4,5},{5,4},{6,7},{7,6},{8,9},{9,8},{10,11... | collective-permute-start | bytes 196616 | tf_op jit(solution)/shard_map/ppermute | solution.py:331
  109.7 3.9 %collective-permute-start.1 = (f32[64,256]{1,0:T(8,128)}, f32[64,256]{1,0:T(8,128)S(1)}, u32[]{:S(2)}, u32[]{:S(2)}) collective-permute-start(f32[64,256]{1,0:T(8,128)} %get-tuple-element.11), channel_id=1, source_target_pairs={{0,2},{1,3},{2,0},{3,1},{4,6},{5,7},{6,4},{7,5},{8,10},{9,11},{10,... | collective-permute-start | bytes 196616 | tf_op jit(solution)/shard_map/ppermute | solution.py:331
  110.0 5.1 %collective-permute-start.2 = (f32[64,256]{1,0:T(8,128)}, f32[64,256]{1,0:T(8,128)S(1)}, u32[]{:S(2)}, u32[]{:S(2)}) collective-permute-start(f32[64,256]{1,0:T(8,128)} %get-tuple-element.12), channel_id=1, source_target_pairs={{0,3},{1,2},{2,1},{3,0},{4,7},{5,6},{6,5},{7,4},{8,11},{9,10},{10,... | collective-permute-start | bytes 196616 | tf_op jit(solution)/shard_map/ppermute | solution.py:331

commit v13 on v12

--- a/solution.py
+++ b/solution.py
@@ -329,10 +329,14 @@
         outgoing = powers[shift]
         pairs_list = [(i, i ^ shift) for i in range(dish_count)]
         pieces.append(lax.ppermute(outgoing, "dish", pairs_list))
-    stacked = jnp.stack(pieces, axis=0)
-    order = jnp.arange(dish_count, dtype=jnp.int32) ^ me
-    received = jnp.take(stacked, order, axis=0)
-    return received.reshape(block_width, grid_len)
+    blocks = []
+    for source in range(dish_count):
+        shift_of = jnp.bitwise_xor(me, source)
+        chosen = pieces[dish_count - 1]
+        for shift in range(dish_count - 2, -1, -1):
+            chosen = jnp.where(shift_of == shift, pieces[shift], chosen)
+        blocks.append(chosen)
+    return jnp.concatenate(blocks, axis=0)
 
 
 def solution(mesh):

time: 118 us -> 117 us (level)
  no operation moved by 1% of the time
where the time goes in v13:
time: 117 us
  waiting for transfers between devices  43 us (37%)
  Pallas kernels  25.9 us (22%)
  local copies, waits for them, and re-layouts  22 us (19%)
  starting transfers between devices  20.2 us (17%)
  other arithmetic  3.67 us (3%)
  matrix products  1.93 us (2%)
    all_to_all x2, waiting for transfers between devices, body(): lax.all_to_all(s, ('dish', 'freq'), 2, 2, tiled=True)  39.2 us
    all_to_all x2, starting transfers between devices, body(): lax.all_to_all(s, ('dish', 'freq'), 2, 2, tiled=True)  17.2 us
    pallas_call x2, Pallas kernels, channelize_chunk(): pl.pallas_call(functools.partial(channelize_kernel, first_pair, pairs), g...  13.9 us
    pallas_call x2, Pallas kernels, beamform_chunk(): pl.pallas_call(functools.partial(beam_kernel, dish_count, carry_in, finis...  12 us
    another operation x1, local copies, waits for them, and re-layouts, body(): volts = voltages[:, 0].reshape(dish_rows, 2, samples // CHB, CHB)  8.4 us
    pallas_call x2, local copies, waits for them, and re-layouts, channelize_chunk(): pl.pallas_call(functools.partial(channelize_kernel, first_pair, pairs), g...  8.19 us
    ppermute x3, waiting for transfers between devices, body(): pieces.append(lax.ppermute(outgoing, 'dish', pairs_list))  3.73 us
    ppermute x3, starting transfers between devices, body(): pieces.append(lax.ppermute(outgoing, 'dish', pairs_list))  2.92 us
  transfers between devices with their start and end apart: 5, of which 4 were waited for; matrix products, arithmetic and copies ran while one was open for 6% of the time, Pallas kernels for 11%

profile of v13, /device:TPU:1, one launch (start us, length us, event | category | flops | bytes accessed | tf_op | source)
XLA Modules:
  0.0 116.8 jit_solution(7739907069397053051)
XLA Ops:
  0.0 0.7 broadcast_multiply_fusion
  0.8 1.3 %reshape.54 = bf16[8,2,128,64]{3,2,1,0:T(8,128)(2,1)S(1)} reshape(bf16[8,1,2,8192]{3,2,1,0:T(2,128)(2,1)} %param.13) | data formatting | bytes 524288 | tf_op jit(solution)/shard_map/reshape;squeeze | solution.py:239
  2.8 1.1 pad_maximum_fusion.g_ref
  3.9 0.9 convolution_convert_fusion.3
  4.7 8.4 %reshape_squeeze.6.v_ref = bf16[8,2,1216,128]{3,2,1,0:T(8,128)(2,1)} reshape(bf16[8,1,2,155648]{3,2,1,0:T(2,128)(2,1)} %param.12) | data formatting | bytes 9961472 | tf_op jit(solution)/shard_map/reshape;squeeze | solution.py:253
  13.1 6.9 %shard_map.119 = bf16[2,8,128,512]{3,2,1,0:T(8,128)(2,1)} custom-call(bf16[8,2,1216,128]{3,2,1,0:T(8,128)(2,1)} %reshape_squeeze.6.v_ref, f32[4,64,128]{2,1,0:T(8,128)} %constant.46.clone.w_ref, bf16[128,128]{1,0:T(8,128)(2,1)} %constant.47.clone.t1_ref, f32[2,64,128]{2,1,0:T(8,128)} %constant.48.clone.tw_ref, bf16[2,256,128]{2,1,0:T(8,128)(2,1)} %bitcast.36, ...), custom_call_target="tpu_custom_call" | custom-call | flops 805306368 | bytes 7077888 | tf_op jit(solution)/shard_map/pallas_call | solution.py:261
  20.1 4.1 %copy.40 = bf16[2,8,128,512]{3,1,0,2:T(8,128)(2,1)} copy(bf16[2,8,128,512]{3,2,1,0:T(8,128)(2,1)} %shard_map.119) | data formatting | bytes 4194304 | tf_op jit(solution)/shard_map/pallas_call | solution.py:261
  24.2 11.5 %all-to-all-start.1 = ((bf16[2,8,128,512]{3,1,0,2:T(8,128)(2,1)}), bf16[2,8,128,512]{3,1,0,2:T(8,128)(2,1)S(1)}, u32[]{:S(2)}, u32[]{:S(2)}) async-start(bf16[2,8,128,512]{3,1,0,2:T(8,128)(2,1)} %copy.40), calls=%async_computation.1 | async-start | bytes 4194304 | tf_op jit(solution)/shard_map/all_to_all | solution.py:318
  35.7 7.0 %shard_map.118 = bf16[2,8,128,512]{3,2,1,0:T(8,128)(2,1)} custom-call(bf16[8,2,1216,128]{3,2,1,0:T(8,128)(2,1)} %reshape_squeeze.6.v_ref, f32[4,64,128]{2,1,0:T(8,128)} %constant.46.clone.w_ref, bf16[128,128]{1,0:T(8,128)(2,1)} %constant.47.clone.t1_ref, f32[2,64,128]{2,1,0:T(8,128)} %constant.48.clone.tw_ref, bf16[2,256,128]{2,1,0:T(8,128)(2,1)} %bitcast.37, ...), custom_call_target="tpu_custom_call" | custom-call | flops 805306368 | bytes 7077888 | tf_op jit(solution)/shard_map/pallas_call | solution.py:261
  42.7 4.1 %copy.35 = bf16[2,8,128,512]{3,1,0,2:T(8,128)(2,1)} copy(bf16[2,8,128,512]{3,2,1,0:T(8,128)(2,1)} %shard_map.118) | data formatting | bytes 4194304 | tf_op jit(solution)/shard_map/pallas_call | solution.py:261
  46.8 18.8 %all-to-all-done.1 = bf16[2,8,128,512]{3,1,0,2:T(8,128)(2,1)S(1)} async-done(((bf16[2,8,128,512]{3,1,0,2:T(8,128)(2,1)}), bf16[2,8,128,512]{3,1,0,2:T(8,128)(2,1)S(1)}, u32[]{:S(2)}, u32[]{:S(2)}) %all-to-all-start.1) | async-done | bytes 2097184 | tf_op jit(solution)/shard_map/all_to_all | solution.py:318
  65.6 1.3 %copy-done = bf16[2,8,128,512]{3,1,0,2:T(8,128)(2,1)} copy-done((bf16[2,8,128,512]{3,1,0,2:T(8,128)(2,1)}, bf16[2,8,128,512]{3,1,0,2:T(8,128)(2,1)S(1)}, u32[]{:S(2)}) %copy-start) | copy-done | bytes 2097176
  66.9 5.7 %all-to-all-start = ((bf16[2,8,128,512]{3,1,0,2:T(8,128)(2,1)}), bf16[2,8,128,512]{3,1,0,2:T(8,128)(2,1)}, u32[]{:S(2)}, u32[]{:S(2)}) async-start(bf16[2,8,128,512]{3,1,0,2:T(8,128)(2,1)} %copy.35), calls=%async_computation | async-start | bytes 4194304 | tf_op jit(solution)/shard_map/all_to_all | solution.py:318
  73.1 0.4 fusion.10
  73.7 2.4 %copy.42.refs_1_ = bf16[4,512,512]{2,1,0:T(8,128)(2,1)} copy(bf16[4,512,512]{1,2,0:T(8,128)(2,1)S(1)} %bitcast.34) | data formatting | bytes 4194304 | tf_op jit(solution)/shard_map/reshape | solution.py:88
  76.1 5.8 %shard_map.120.refs_4_ = f32[4,256,256]{2,1,0:T(8,128)} custom-call(bf16[128,2,8,512]{3,2,1,0:T(8,128)(2,1)} %bitcast.33, bf16[4,512,512]{2,1,0:T(8,128)(2,1)} %copy.42.refs_1_, f32[4,256,1]{2,1,0:T(8,128)} %constant.52.clone.refs_2_, f32[4,256,1]{2,1,0:T(8,128)} %constant.53.clone.refs_3_), custom_call_target="tpu_custom_call" | custom-call | flops 1073741824 | bytes 4194304 | tf_op jit(solution)/shard_map/pallas_call | solution.py:302
  82.0 20.4 %all-to-all-done = bf16[2,8,128,512]{3,1,0,2:T(8,128)(2,1)} async-done(((bf16[2,8,128,512]{3,1,0,2:T(8,128)(2,1)}), bf16[2,8,128,512]{3,1,0,2:T(8,128)(2,1)}, u32[]{:S(2)}, u32[]{:S(2)}) %all-to-all-start) | async-done | bytes 2097184 | tf_op jit(solution)/shard_map/all_to_all | solution.py:318
  102.4 6.2 %shard_map.121 = (f32[64,256]{1,0:T(8,128)}, f32[64,256]{1,0:T(8,128)}, f32[64,256]{1,0:T(8,128)}, f32[64,256]{1,0:T(8,128)}) custom-call(bf16[128,2,8,512]{3,2,1,0:T(8,128)(2,1)} %bitcast.6.refs_0_, bf16[4,512,512]{2,1,0:T(8,128)(2,1)} %copy.42.refs_1_, f32[4,256,1]{2,1,0:T(8,128)} %constant.52.clone.refs_2_, f32[4,256,1]{2,1,0:T(8,128)} %constant.53.clone.refs_3_, ...), custom_call_target="tpu_custom_call" | custom-call | flops 1073741824 | bytes 4194304 | tf_op jit(solution)/shard_map/pallas_call | solution.py:302
  108.5 1.2 %collective-permute-start = (f32[64,256]{1,0:T(8,128)}, f32[64,256]{1,0:T(8,128)S(1)}, u32[]{:S(2)}, u32[]{:S(2)}) collective-permute-start(f32[64,256]{1,0:T(8,128)} %get-tuple-element.10), channel_id=1, source_target_pairs={{0,1},{1,0},{2,3},{3,2},{4,5},{5,4},{6,7},{7,6},{8,9},{9,8},{10,11... | collective-permute-start | bytes 196616 | tf_op jit(solution)/shard_map/ppermute | solution.py:331
  110.1 1.4 %collective-permute-start.2 = (f32[64,256]{1,0:T(8,128)}, f32[64,256]{1,0:T(8,128)S(1)}, u32[]{:S(2)}, u32[]{:S(2)}) collective-permute-start(f32[64,256]{1,0:T(8,128)} %get-tuple-element.12), channel_id=1, source_target_pairs={{0,3},{1,2},{2,1},{3,0},{4,7},{5,6},{6,5},{7,4},{8,11},{9,10},{10,... | collective-permute-start | bytes 196616 | tf_op jit(solution)/shard_map/ppermute | solution.py:331
  111.5 2.2 %collective-permute-done.1 = f32[64,256]{1,0:T(8,128)S(1)} collective-permute-done((f32[64,256]{1,0:T(8,128)}, f32[64,256]{1,0:T(8,128)S(1)}, u32[]{:S(2)}, u32[]{:S(2)}) %collective-permute-start.1) | collective-permute-done | bytes 65568 | tf_op jit(solution)/shard_map/ppermute | solution.py:331
  113.6 1.6 %collective-permute-done.2 = f32[64,256]{1,0:T(8,128)S(1)} collective-permute-done((f32[64,256]{1,0:T(8,128)}, f32[64,256]{1,0:T(8,128)S(1)}, u32[]{:S(2)}, u32[]{:S(2)}) %collective-permute-start.2) | collective-permute-done | bytes 65568 | tf_op jit(solution)/shard_map/ppermute | solution.py:331
  115.2 0.9 select_select_fusion.3
  116.1 0.7 pad_maximum_fusion.1
  (18 shorter events, 1.7 us)
Async XLA Ops:
  0.0 3.9 %copy-start.3 = (bf16[2,2,128,128]{3,2,1,0:T(8,128)(2,1)S(1)}, bf16[2,2,128,128]{3,2,1,0:T(8,128)(2,1)}, u32[]{:S(2)}) copy-start(bf16[2,2,128,128]{3,2,1,0:T(8,128)(2,1)} %constant.49.clone) | copy-start | bytes 393220
  24.2 41.4 %all-to-all-start.1 = ((bf16[2,8,128,512]{3,1,0,2:T(8,128)(2,1)}), bf16[2,8,128,512]{3,1,0,2:T(8,128)(2,1)S(1)}, u32[]{:S(2)}, u32[]{:S(2)}) async-start(bf16[2,8,128,512]{3,1,0,2:T(8,128)(2,1)} %copy.40), calls=%async_computation.1 | async-start | bytes 4194304 | tf_op jit(solution)/shard_map/all_to_all | solution.py:318
  46.8 25.9 %copy-start.2 = (bf16[256,256,1]{1,0,2:T(8,128)(2,1)S(1)}, bf16[256,256,1]{1,0,2:T(8,128)(2,1)}, u32[]{:S(2)}) copy-start(bf16[256,256,1]{1,0,2:T(8,128)(2,1)} %constant.56) | copy-start | bytes 393220
  46.8 25.9 %copy-start.4 = (s32[4,256]{1,0:T(4,128)S(1)}, s32[4,256]{1,0:T(4,128)}, u32[]{:S(2)}) copy-start(s32[4,256]{1,0:T(4,128)} %param.15) | copy-start | bytes 12292
  46.8 26.3 %copy-start.1 = (bf16[256,256,1]{1,0,2:T(8,128)(2,1)S(1)}, bf16[256,256,1]{1,0,2:T(8,128)(2,1)}, u32[]{:S(2)}) copy-start(bf16[256,256,1]{1,0,2:T(8,128)(2,1)} %constant.57) | copy-start | bytes 393220
  65.6 1.3 %copy-start = (bf16[2,8,128,512]{3,1,0,2:T(8,128)(2,1)}, bf16[2,8,128,512]{3,1,0,2:T(8,128)(2,1)S(1)}, u32[]{:S(2)}) copy-start(bf16[2,8,128,512]{3,1,0,2:T(8,128)(2,1)S(1)} %all-to-all-done.1) | copy-start | bytes 6291460
  66.9 35.4 %all-to-all-start = ((bf16[2,8,128,512]{3,1,0,2:T(8,128)(2,1)}), bf16[2,8,128,512]{3,1,0,2:T(8,128)(2,1)}, u32[]{:S(2)}, u32[]{:S(2)}) async-start(bf16[2,8,128,512]{3,1,0,2:T(8,128)(2,1)} %copy.35), calls=%async_computation | async-start | bytes 4194304 | tf_op jit(solution)/shard_map/all_to_all | solution.py:318
  108.5 2.9 %collective-permute-start = (f32[64,256]{1,0:T(8,128)}, f32[64,256]{1,0:T(8,128)S(1)}, u32[]{:S(2)}, u32[]{:S(2)}) collective-permute-start(f32[64,256]{1,0:T(8,128)} %get-tuple-element.10), channel_id=1, source_target_pairs={{0,1},{1,0},{2,3},{3,2},{4,5},{5,4},{6,7},{7,6},{8,9},{9,8},{10,11... | collective-permute-start | bytes 196616 | tf_op jit(solution)/shard_map/ppermute | solution.py:331
  109.8 3.9 %collective-permute-start.1 = (f32[64,256]{1,0:T(8,128)}, f32[64,256]{1,0:T(8,128)S(1)}, u32[]{:S(2)}, u32[]{:S(2)}) collective-permute-start(f32[64,256]{1,0:T(8,128)} %get-tuple-element.11), channel_id=1, source_target_pairs={{0,2},{1,3},{2,0},{3,1},{4,6},{5,7},{6,4},{7,5},{8,10},{9,11},{10,... | collective-permute-start | bytes 196616 | tf_op jit(solution)/shard_map/ppermute | solution.py:331
  110.1 5.1 %collective-permute-start.2 = (f32[64,256]{1,0:T(8,128)}, f32[64,256]{1,0:T(8,128)S(1)}, u32[]{:S(2)}, u32[]{:S(2)}) collective-permute-start(f32[64,256]{1,0:T(8,128)} %get-tuple-element.12), channel_id=1, source_target_pairs={{0,3},{1,2},{2,1},{3,0},{4,7},{5,6},{6,5},{7,4},{8,11},{9,10},{10,... | collective-permute-start | bytes 196616 | tf_op jit(solution)/shard_map/ppermute | solution.py:331

commit v14 on v13

--- a/solution.py
+++ b/solution.py
@@ -250,7 +250,7 @@
     twist_sin = jnp.asarray(twist_sin[:, :, None])
     lane_block = 4 * quarter
 
-    volts = voltages[:, 0].reshape(dish_rows, 2, samples // CHB, CHB)
+    volts = voltages[:, 0].astype(jnp.float32).reshape(dish_rows, 2, samples // CHB, CHB)
 
     def channelize_chunk(chunk):
         pairs = chunk_pairs[chunk]

time: 117 us -> 118 us (level)
    convert_element_type x0 -> x1, local copies, waits for them, and re-layouts: none -> 9.05 us  [body(): voltages[:, 0].astype(jnp.float32)]
    another operation x2 -> x1, local copies, waits for them, and re-layouts: 8.69 us -> 0.28 us  [the longest x1 8.4 us: body(): volts = voltages[:, 0].reshape(dish_rows, 2, samples // CHB, CHB)]
where the time goes in v14:
time: 118 us
  waiting for transfers between devices  42.6 us (36%)
  Pallas kernels  26.7 us (23%)
  local copies, waits for them, and re-layouts  22.6 us (19%)
  starting transfers between devices  20.2 us (17%)
  other arithmetic  3.67 us (3%)
  matrix products  1.93 us (2%)
    all_to_all x2, waiting for transfers between devices, body(): lax.all_to_all(s, ('dish', 'freq'), 2, 2, tiled=True)  38.9 us
    all_to_all x2, starting transfers between devices, body(): lax.all_to_all(s, ('dish', 'freq'), 2, 2, tiled=True)  17.2 us
    pallas_call x2, Pallas kernels, channelize_chunk(): pl.pallas_call(functools.partial(channelize_kernel, first_pair, pairs), g...  14.7 us
    pallas_call x2, Pallas kernels, beamform_chunk(): pl.pallas_call(functools.partial(beam_kernel, dish_count, carry_in, finis...  12 us
    convert_element_type x1, local copies, waits for them, and re-layouts, body(): voltages[:, 0].astype(jnp.float32)  9.05 us
    pallas_call x2, local copies, waits for them, and re-layouts, channelize_chunk(): pl.pallas_call(functools.partial(channelize_kernel, first_pair, pairs), g...  8.14 us
    ppermute x3, waiting for transfers between devices, body(): pieces.append(lax.ppermute(outgoing, 'dish', pairs_list))  3.73 us
    ppermute x3, starting transfers between devices, body(): pieces.append(lax.ppermute(outgoing, 'dish', pairs_list))  2.92 us
  transfers between devices with their start and end apart: 5, of which 4 were waited for; matrix products, arithmetic and copies ran while one was open for 6% of the time, Pallas kernels for 11%

profile of v14, /device:TPU:1, one launch (start us, length us, event | category | flops | bytes accessed | tf_op | source)
XLA Modules:
  0.0 117.8 jit_solution(16712972066491386418)
XLA Ops:
  0.0 0.7 broadcast_multiply_fusion
  0.8 1.3 %reshape.59 = bf16[8,2,128,64]{3,2,1,0:T(8,128)(2,1)S(1)} reshape(bf16[8,1,2,8192]{3,2,1,0:T(2,128)(2,1)} %param.13) | data formatting | bytes 524288 | tf_op jit(solution)/shard_map/reshape;squeeze | solution.py:239
  2.8 1.1 pad_maximum_fusion.g_ref
  3.9 0.9 convolution_convert_fusion.3
  4.7 9.1 %reshape.55.v_ref = f32[8,2,1216,128]{3,2,1,0:T(8,128)} reshape(bf16[8,1,2,155648]{3,2,1,0:T(2,128)(2,1)} %param.12) | data formatting | bytes 14942208 | tf_op jit(solution)/shard_map/convert_element_type | solution.py:253
  13.8 7.3 %shard_map.119 = bf16[2,8,128,512]{3,2,1,0:T(8,128)(2,1)} custom-call(f32[8,2,1216,128]{3,2,1,0:T(8,128)} %reshape.55.v_ref, f32[4,64,128]{2,1,0:T(8,128)} %constant.46.clone.w_ref, bf16[128,128]{1,0:T(8,128)(2,1)} %constant.47.clone.t1_ref, f32[2,64,128]{2,1,0:T(8,128)} %constant.48.clone.tw_ref, bf16[2,256,128]{2,1,0:T(8,128)(2,1)} %bitcast.36, ...), custom_call_target="tpu_custom_call" | custom-call | flops 805306368 | bytes 7077888 | tf_op jit(solution)/shard_map/pallas_call | solution.py:261
  21.1 4.1 %copy.40 = bf16[2,8,128,512]{3,1,0,2:T(8,128)(2,1)} copy(bf16[2,8,128,512]{3,2,1,0:T(8,128)(2,1)} %shard_map.119) | data formatting | bytes 4194304 | tf_op jit(solution)/shard_map/pallas_call | solution.py:261
  25.2 11.5 %all-to-all-start.1 = ((bf16[2,8,128,512]{3,1,0,2:T(8,128)(2,1)}), bf16[2,8,128,512]{3,1,0,2:T(8,128)(2,1)S(1)}, u32[]{:S(2)}, u32[]{:S(2)}) async-start(bf16[2,8,128,512]{3,1,0,2:T(8,128)(2,1)} %copy.40), calls=%async_computation.1 | async-start | bytes 4194304 | tf_op jit(solution)/shard_map/all_to_all | solution.py:318
  36.7 7.4 %shard_map.118 = bf16[2,8,128,512]{3,2,1,0:T(8,128)(2,1)} custom-call(f32[8,2,1216,128]{3,2,1,0:T(8,128)} %reshape.55.v_ref, f32[4,64,128]{2,1,0:T(8,128)} %constant.46.clone.w_ref, bf16[128,128]{1,0:T(8,128)(2,1)} %constant.47.clone.t1_ref, f32[2,64,128]{2,1,0:T(8,128)} %constant.48.clone.tw_ref, bf16[2,256,128]{2,1,0:T(8,128)(2,1)} %bitcast.37, ...), custom_call_target="tpu_custom_call" | custom-call | flops 805306368 | bytes 7077888 | tf_op jit(solution)/shard_map/pallas_call | solution.py:261
  44.0 4.1 %copy.35 = bf16[2,8,128,512]{3,1,0,2:T(8,128)(2,1)} copy(bf16[2,8,128,512]{3,2,1,0:T(8,128)(2,1)} %shard_map.118) | data formatting | bytes 4194304 | tf_op jit(solution)/shard_map/pallas_call | solution.py:261
  48.1 18.5 %all-to-all-done.1 = bf16[2,8,128,512]{3,1,0,2:T(8,128)(2,1)S(1)} async-done(((bf16[2,8,128,512]{3,1,0,2:T(8,128)(2,1)}), bf16[2,8,128,512]{3,1,0,2:T(8,128)(2,1)S(1)}, u32[]{:S(2)}, u32[]{:S(2)}) %all-to-all-start.1) | async-done | bytes 2097184 | tf_op jit(solution)/shard_map/all_to_all | solution.py:318
  66.6 1.3 %copy-done = bf16[2,8,128,512]{3,1,0,2:T(8,128)(2,1)} copy-done((bf16[2,8,128,512]{3,1,0,2:T(8,128)(2,1)}, bf16[2,8,128,512]{3,1,0,2:T(8,128)(2,1)S(1)}, u32[]{:S(2)}) %copy-start) | copy-done | bytes 2097176
  67.9 5.7 %all-to-all-start = ((bf16[2,8,128,512]{3,1,0,2:T(8,128)(2,1)}), bf16[2,8,128,512]{3,1,0,2:T(8,128)(2,1)}, u32[]{:S(2)}, u32[]{:S(2)}) async-start(bf16[2,8,128,512]{3,1,0,2:T(8,128)(2,1)} %copy.35), calls=%async_computation | async-start | bytes 4194304 | tf_op jit(solution)/shard_map/all_to_all | solution.py:318
  74.1 0.4 fusion.10
  74.7 2.4 %copy.42.refs_1_ = bf16[4,512,512]{2,1,0:T(8,128)(2,1)} copy(bf16[4,512,512]{1,2,0:T(8,128)(2,1)S(1)} %bitcast.34) | data formatting | bytes 4194304 | tf_op jit(solution)/shard_map/reshape | solution.py:88
  77.1 5.8 %shard_map.120.refs_4_ = f32[4,256,256]{2,1,0:T(8,128)} custom-call(bf16[128,2,8,512]{3,2,1,0:T(8,128)(2,1)} %bitcast.33, bf16[4,512,512]{2,1,0:T(8,128)(2,1)} %copy.42.refs_1_, f32[4,256,1]{2,1,0:T(8,128)} %constant.52.clone.refs_2_, f32[4,256,1]{2,1,0:T(8,128)} %constant.53.clone.refs_3_), custom_call_target="tpu_custom_call" | custom-call | flops 1073741824 | bytes 4194304 | tf_op jit(solution)/shard_map/pallas_call | solution.py:302
  83.0 20.4 %all-to-all-done = bf16[2,8,128,512]{3,1,0,2:T(8,128)(2,1)} async-done(((bf16[2,8,128,512]{3,1,0,2:T(8,128)(2,1)}), bf16[2,8,128,512]{3,1,0,2:T(8,128)(2,1)}, u32[]{:S(2)}, u32[]{:S(2)}) %all-to-all-start) | async-done | bytes 2097184 | tf_op jit(solution)/shard_map/all_to_all | solution.py:318
  103.3 6.2 %shard_map.121 = (f32[64,256]{1,0:T(8,128)}, f32[64,256]{1,0:T(8,128)}, f32[64,256]{1,0:T(8,128)}, f32[64,256]{1,0:T(8,128)}) custom-call(bf16[128,2,8,512]{3,2,1,0:T(8,128)(2,1)} %bitcast.6.refs_0_, bf16[4,512,512]{2,1,0:T(8,128)(2,1)} %copy.42.refs_1_, f32[4,256,1]{2,1,0:T(8,128)} %constant.52.clone.refs_2_, f32[4,256,1]{2,1,0:T(8,128)} %constant.53.clone.refs_3_, ...), custom_call_target="tpu_custom_call" | custom-call | flops 1073741824 | bytes 4194304 | tf_op jit(solution)/shard_map/pallas_call | solution.py:302
  109.5 1.2 %collective-permute-start = (f32[64,256]{1,0:T(8,128)}, f32[64,256]{1,0:T(8,128)S(1)}, u32[]{:S(2)}, u32[]{:S(2)}) collective-permute-start(f32[64,256]{1,0:T(8,128)} %get-tuple-element.10), channel_id=1, source_target_pairs={{0,1},{1,0},{2,3},{3,2},{4,5},{5,4},{6,7},{7,6},{8,9},{9,8},{10,11... | collective-permute-start | bytes 196616 | tf_op jit(solution)/shard_map/ppermute | solution.py:331
  111.0 1.4 %collective-permute-start.2 = (f32[64,256]{1,0:T(8,128)}, f32[64,256]{1,0:T(8,128)S(1)}, u32[]{:S(2)}, u32[]{:S(2)}) collective-permute-start(f32[64,256]{1,0:T(8,128)} %get-tuple-element.12), channel_id=1, source_target_pairs={{0,3},{1,2},{2,1},{3,0},{4,7},{5,6},{6,5},{7,4},{8,11},{9,10},{10,... | collective-permute-start | bytes 196616 | tf_op jit(solution)/shard_map/ppermute | solution.py:331
  112.4 2.2 %collective-permute-done.1 = f32[64,256]{1,0:T(8,128)S(1)} collective-permute-done((f32[64,256]{1,0:T(8,128)}, f32[64,256]{1,0:T(8,128)S(1)}, u32[]{:S(2)}, u32[]{:S(2)}) %collective-permute-start.1) | collective-permute-done | bytes 65568 | tf_op jit(solution)/shard_map/ppermute | solution.py:331
  114.6 1.6 %collective-permute-done.2 = f32[64,256]{1,0:T(8,128)S(1)} collective-permute-done((f32[64,256]{1,0:T(8,128)}, f32[64,256]{1,0:T(8,128)S(1)}, u32[]{:S(2)}, u32[]{:S(2)}) %collective-permute-start.2) | collective-permute-done | bytes 65568 | tf_op jit(solution)/shard_map/ppermute | solution.py:331
  116.2 0.9 select_select_fusion.3
  117.0 0.7 pad_maximum_fusion.1
  (18 shorter events, 1.7 us)
Async XLA Ops:
  0.0 3.9 %copy-start.3 = (bf16[2,2,128,128]{3,2,1,0:T(8,128)(2,1)S(1)}, bf16[2,2,128,128]{3,2,1,0:T(8,128)(2,1)}, u32[]{:S(2)}) copy-start(bf16[2,2,128,128]{3,2,1,0:T(8,128)(2,1)} %constant.49.clone) | copy-start | bytes 393220
  25.2 41.4 %all-to-all-start.1 = ((bf16[2,8,128,512]{3,1,0,2:T(8,128)(2,1)}), bf16[2,8,128,512]{3,1,0,2:T(8,128)(2,1)S(1)}, u32[]{:S(2)}, u32[]{:S(2)}) async-start(bf16[2,8,128,512]{3,1,0,2:T(8,128)(2,1)} %copy.40), calls=%async_computation.1 | async-start | bytes 4194304 | tf_op jit(solution)/shard_map/all_to_all | solution.py:318
  48.1 25.6 %copy-start.2 = (bf16[256,256,1]{1,0,2:T(8,128)(2,1)S(1)}, bf16[256,256,1]{1,0,2:T(8,128)(2,1)}, u32[]{:S(2)}) copy-start(bf16[256,256,1]{1,0,2:T(8,128)(2,1)} %constant.56) | copy-start | bytes 393220
  48.1 25.6 %copy-start.4 = (s32[4,256]{1,0:T(4,128)S(1)}, s32[4,256]{1,0:T(4,128)}, u32[]{:S(2)}) copy-start(s32[4,256]{1,0:T(4,128)} %param.15) | copy-start | bytes 12292
  48.1 25.9 %copy-start.1 = (bf16[256,256,1]{1,0,2:T(8,128)(2,1)S(1)}, bf16[256,256,1]{1,0,2:T(8,128)(2,1)}, u32[]{:S(2)}) copy-start(bf16[256,256,1]{1,0,2:T(8,128)(2,1)} %constant.57) | copy-start | bytes 393220
  66.6 1.3 %copy-start = (bf16[2,8,128,512]{3,1,0,2:T(8,128)(2,1)}, bf16[2,8,128,512]{3,1,0,2:T(8,128)(2,1)S(1)}, u32[]{:S(2)}) copy-start(bf16[2,8,128,512]{3,1,0,2:T(8,128)(2,1)S(1)} %all-to-all-done.1) | copy-start | bytes 6291460
  67.9 35.4 %all-to-all-start = ((bf16[2,8,128,512]{3,1,0,2:T(8,128)(2,1)}), bf16[2,8,128,512]{3,1,0,2:T(8,128)(2,1)}, u32[]{:S(2)}, u32[]{:S(2)}) async-start(bf16[2,8,128,512]{3,1,0,2:T(8,128)(2,1)} %copy.35), calls=%async_computation | async-start | bytes 4194304 | tf_op jit(solution)/shard_map/all_to_all | solution.py:318
  109.5 2.9 %collective-permute-start = (f32[64,256]{1,0:T(8,128)}, f32[64,256]{1,0:T(8,128)S(1)}, u32[]{:S(2)}, u32[]{:S(2)}) collective-permute-start(f32[64,256]{1,0:T(8,128)} %get-tuple-element.10), channel_id=1, source_target_pairs={{0,1},{1,0},{2,3},{3,2},{4,5},{5,4},{6,7},{7,6},{8,9},{9,8},{10,11... | collective-permute-start | bytes 196616 | tf_op jit(solution)/shard_map/ppermute | solution.py:331
  110.7 3.9 %collective-permute-start.1 = (f32[64,256]{1,0:T(8,128)}, f32[64,256]{1,0:T(8,128)S(1)}, u32[]{:S(2)}, u32[]{:S(2)}) collective-permute-start(f32[64,256]{1,0:T(8,128)} %get-tuple-element.11), channel_id=1, source_target_pairs={{0,2},{1,3},{2,0},{3,1},{4,6},{5,7},{6,4},{7,5},{8,10},{9,11},{10,... | collective-permute-start | bytes 196616 | tf_op jit(solution)/shard_map/ppermute | solution.py:331
  111.0 5.1 %collective-permute-start.2 = (f32[64,256]{1,0:T(8,128)}, f32[64,256]{1,0:T(8,128)S(1)}, u32[]{:S(2)}, u32[]{:S(2)}) collective-permute-start(f32[64,256]{1,0:T(8,128)} %get-tuple-element.12), channel_id=1, source_target_pairs={{0,3},{1,2},{2,1},{3,0},{4,7},{5,6},{6,5},{7,4},{8,11},{9,10},{10,... | collective-permute-start | bytes 196616 | tf_op jit(solution)/shard_map/ppermute | solution.py:331

commit v15 on v13

--- a/solution.py
+++ b/solution.py
@@ -88,7 +88,9 @@
     return rows.reshape(grid_rows.shape[0], 2 * grid_len, 2 * grid_len)
 
 
-def channelize_kernel(first_pair, pairs, v_ref, w_ref, t1_ref, tw_ref, t2_ref, g_ref, o_ref):
+def channelize_kernel(
+    first_pair, pairs, v_ref, w_ref, t1_ref, tw_ref, t2_ref, g_ref, pe_ref, dup_ref, o_ref
+):
     cos_tw = tw_ref[0]
     sin_tw = tw_ref[1]
     t1 = t1_ref[...]
@@ -110,9 +112,11 @@
         turned_imag = sec_real * sin_tw + sec_imag * cos_tw
         return turned_real.astype(jnp.bfloat16), turned_imag.astype(jnp.bfloat16)
 
-    def pair(feed, step):
-        g_real = g_ref[feed, 0].astype(jnp.float32)
-        g_imag = g_ref[feed, 1].astype(jnp.float32)
+    def feed_gains(feed, part):
+        picked = jnp.dot(pe_ref[...], g_ref[feed, part], preferred_element_type=jnp.float32)
+        return jnp.dot(picked.astype(jnp.bfloat16), dup_ref[...], preferred_element_type=jnp.float32)
+
+    def pair(feed, step, g_real, g_imag):
         pieces = []
         for offset in range(TAPS + 1):
             start = pl.multiple_of((2 * (step - first_pair) + offset) * CHA, CHA)
@@ -134,8 +138,10 @@
         o_ref[1, feed, :, lanes] = out_imag.astype(o_ref.dtype)
 
     for feed in range(feeds):
+        g_real = feed_gains(feed, 0)
+        g_imag = feed_gains(feed, 1)
         for step in range(first_pair, first_pair + pairs):
-            pair(feed, step)
+            pair(feed, step, g_real, g_imag)
 
 
 def beam_kernel(dish_count, carry_in, finish, lanes, *refs):
@@ -237,8 +243,8 @@
         "je,qseb->qsjb", picks_e, jnp.asarray(second_table), preferred_element_type=jnp.float32
     ).astype(jnp.bfloat16).reshape(2, 2 * dests, CHB)
     gains = feed_gains[:, 0].reshape(dish_rows, 2, CHB, CHA)
-    gains = jnp.einsum("je,rpec->rpjc", picks_e, gains, preferred_element_type=jnp.float32)
-    gains = jnp.concatenate([gains, gains], axis=3).astype(jnp.bfloat16)
+    lane_pick = np.arange(2 * CHA)[None, :] % CHA == np.arange(CHA)[:, None]
+    duplicate = jnp.asarray(lane_pick.astype(ml_dtypes.bfloat16))
 
     chunk_pairs = [4, 4]
     chunks = len(chunk_pairs)
@@ -270,7 +276,9 @@
                 pl.BlockSpec((2 * CHA, 2 * CHA), lambda r: (0, 0)),
                 pl.BlockSpec((2, CHA, CHB), lambda r: (0, 0, 0)),
                 pl.BlockSpec((2, 2 * dests, CHB), lambda r: (0, 0, 0)),
-                pl.BlockSpec((FEEDS_PER_STEP, 2, dests, 2 * CHA), lambda r: (r, 0, 0, 0)),
+                pl.BlockSpec((FEEDS_PER_STEP, 2, dests, CHA), lambda r: (r, 0, 0, 0)),
+                pl.BlockSpec((dests, dests), lambda r: (0, 0)),
+                pl.BlockSpec((CHA, 2 * CHA), lambda r: (0, 0)),
             ],
             out_specs=pl.BlockSpec((2, FEEDS_PER_STEP, dests, chunk_lanes), lambda r: (0, r, 0, 0)),
             out_shape=jax.ShapeDtypeStruct((2, dish_rows, dests, chunk_lanes), jnp.bfloat16),
@@ -279,7 +287,7 @@
                 bytes_accessed=int(voltages.size * 2 + 2 * dish_rows * dests * chunk_lanes * 2),
                 transcendentals=0,
             ),
-        )(volts, window, first_table, twiddle, second_table, gains)
+        )(volts, window, first_table, twiddle, second_table, gains, picks_e, duplicate)
 
     def beamform_chunk(received, carried, finish):
         carry_in = carried is not None

time: 117 us -> 119 us (1.017)
  Pallas kernels: 25.9 us -> 29.9 us
  waiting for transfers between devices: 43 us -> 41 us
    pallas_call x2, Pallas kernels: 13.9 us -> 17.9 us  [channelize_chunk(): pl.pallas_call(functools.partial(channelize_kernel, first_pair, pairs), g...]
    all_to_all x2, waiting for transfers between devices: 39.2 us -> 37.2 us  [body(): lax.all_to_all(s, ('dish', 'freq'), 2, 2, tiled=True)]
  transfers between devices with their start and end apart: 5 -> 5, of which waited for: 4 -> 4; matrix products, arithmetic and copies ran while one was open for 6% -> 6% of each run, Pallas kernels for 11% -> 13%
where the time goes in v15:
time: 119 us; the launch traced here: 118 us
  waiting for transfers between devices  41 us (34%)
  Pallas kernels  29.9 us (25%)
  local copies, waits for them, and re-layouts  21.6 us (18%)
  starting transfers between devices  20.2 us (17%)
  other arithmetic  3.23 us (3%)
  matrix products  2.5 us (2%)
    all_to_all x2, waiting for transfers between devices, body(): lax.all_to_all(s, ('dish', 'freq'), 2, 2, tiled=True)  37.2 us
    pallas_call x2, Pallas kernels, channelize_chunk(): pl.pallas_call(functools.partial(channelize_kernel, first_pair, pairs), g...  17.9 us
    all_to_all x2, starting transfers between devices, body(): lax.all_to_all(s, ('dish', 'freq'), 2, 2, tiled=True)  17.2 us
    pallas_call x2, Pallas kernels, beamform_chunk(): pl.pallas_call(functools.partial(beam_kernel, dish_count, carry_in, finis...  12 us
    another operation x1, local copies, waits for them, and re-layouts, body(): volts = voltages[:, 0].reshape(dish_rows, 2, samples // CHB, CHB)  8.45 us
    pallas_call x2, local copies, waits for them, and re-layouts, channelize_chunk(): pl.pallas_call(functools.partial(channelize_kernel, first_pair, pairs), g...  8.19 us
    ppermute x3, waiting for transfers between devices, body(): pieces.append(lax.ppermute(outgoing, 'dish', pairs_list))  3.73 us
    ppermute x3, starting transfers between devices, body(): pieces.append(lax.ppermute(outgoing, 'dish', pairs_list))  2.93 us
  transfers between devices with their start and end apart: 5, of which 4 were waited for; matrix products, arithmetic and copies ran while one was open for 6% of the time, Pallas kernels for 13%

profile of v15, /device:TPU:1, one launch (start us, length us, event | category | flops | bytes accessed | tf_op | source)
XLA Modules:
  0.0 118.5 jit_solution(1665347887524431177)
XLA Ops:
  0.0 0.7 broadcast_multiply_fusion
  0.8 0.7 fusion.4.pe_ref
  1.4 1.8 %convolution_convert_fusion.2 = bf16[128,2,2,128]{3,0,2,1:T(8,128)(2,1)} fusion(bf16[2,2,128,128]{3,2,1,0:T(8,128)(2,1)} %constant.51.clone, s32[128]{0:T(128)S(1)} %fusion.8), kind=kOutput, calls=%fused_computation.5 | convolution fusion | flops 16859136 | bytes 262656 | tf_op jit(solution)/shard_map/je,qseb->qsjb/dot_general | solution.py:242
  3.2 8.4 %reshape_squeeze.6.v_ref = bf16[8,2,1216,128]{3,2,1,0:T(8,128)(2,1)} reshape(bf16[8,1,2,155648]{3,2,1,0:T(2,128)(2,1)} %param.13) | data formatting | bytes 9961472 | tf_op jit(solution)/shard_map/reshape;squeeze | solution.py:259
  11.7 1.2 reshape.54.g_ref
  12.8 8.9 %shard_map.128 = bf16[2,8,128,512]{3,2,1,0:T(8,128)(2,1)} custom-call(bf16[8,2,1216,128]{3,2,1,0:T(8,128)(2,1)} %reshape_squeeze.6.v_ref, f32[4,64,128]{2,1,0:T(8,128)} %constant.48.clone.w_ref, bf16[128,128]{1,0:T(8,128)(2,1)} %constant.49.clone.t1_ref, f32[2,64,128]{2,1,0:T(8,128)} %constant.50.clone.tw_ref, bf16[2,256,128]{2,1,0:T(8,128)(2,1)} %bitcast.32, ...), custom_call_target="tpu_custom_call" | custom-call | flops 805306368 | bytes 7077888 | tf_op jit(solution)/shard_map/pallas_call | solution.py:267
  21.8 4.1 %copy.28 = bf16[2,8,128,512]{3,1,0,2:T(8,128)(2,1)} copy(bf16[2,8,128,512]{3,2,1,0:T(8,128)(2,1)} %shard_map.128) | data formatting | bytes 4194304 | tf_op jit(solution)/shard_map/pallas_call | solution.py:267
  25.9 11.5 %all-to-all-start.1 = ((bf16[2,8,128,512]{3,1,0,2:T(8,128)(2,1)}), bf16[2,8,128,512]{3,1,0,2:T(8,128)(2,1)S(1)}, u32[]{:S(2)}, u32[]{:S(2)}) async-start(bf16[2,8,128,512]{3,1,0,2:T(8,128)(2,1)} %copy.28), calls=%async_computation.1 | async-start | bytes 4194304 | tf_op jit(solution)/shard_map/all_to_all | solution.py:326
  37.4 9.0 %shard_map.127 = bf16[2,8,128,512]{3,2,1,0:T(8,128)(2,1)} custom-call(bf16[8,2,1216,128]{3,2,1,0:T(8,128)(2,1)} %reshape_squeeze.6.v_ref, f32[4,64,128]{2,1,0:T(8,128)} %constant.48.clone.w_ref, bf16[128,128]{1,0:T(8,128)(2,1)} %constant.49.clone.t1_ref, f32[2,64,128]{2,1,0:T(8,128)} %constant.50.clone.tw_ref, bf16[2,256,128]{2,1,0:T(8,128)(2,1)} %bitcast.33, ...), custom_call_target="tpu_custom_call" | custom-call | flops 805306368 | bytes 7077888 | tf_op jit(solution)/shard_map/pallas_call | solution.py:267
  46.4 4.1 %copy.22 = bf16[2,8,128,512]{3,1,0,2:T(8,128)(2,1)} copy(bf16[2,8,128,512]{3,2,1,0:T(8,128)(2,1)} %shard_map.127) | data formatting | bytes 4194304 | tf_op jit(solution)/shard_map/pallas_call | solution.py:267
  50.4 16.8 %all-to-all-done.1 = bf16[2,8,128,512]{3,1,0,2:T(8,128)(2,1)S(1)} async-done(((bf16[2,8,128,512]{3,1,0,2:T(8,128)(2,1)}), bf16[2,8,128,512]{3,1,0,2:T(8,128)(2,1)S(1)}, u32[]{:S(2)}, u32[]{:S(2)}) %all-to-all-start.1) | async-done | bytes 2097184 | tf_op jit(solution)/shard_map/all_to_all | solution.py:326
  67.3 1.3 %copy-done = bf16[2,8,128,512]{3,1,0,2:T(8,128)(2,1)} copy-done((bf16[2,8,128,512]{3,1,0,2:T(8,128)(2,1)}, bf16[2,8,128,512]{3,1,0,2:T(8,128)(2,1)S(1)}, u32[]{:S(2)}) %copy-start) | copy-done | bytes 2097176
  68.6 5.7 %all-to-all-start = ((bf16[2,8,128,512]{3,1,0,2:T(8,128)(2,1)}), bf16[2,8,128,512]{3,1,0,2:T(8,128)(2,1)}, u32[]{:S(2)}, u32[]{:S(2)}) async-start(bf16[2,8,128,512]{3,1,0,2:T(8,128)(2,1)} %copy.22), calls=%async_computation | async-start | bytes 4194304 | tf_op jit(solution)/shard_map/all_to_all | solution.py:326
  74.8 0.4 fusion.9
  75.4 2.4 %copy.30.refs_1_ = bf16[4,512,512]{2,1,0:T(8,128)(2,1)} copy(bf16[4,512,512]{1,2,0:T(8,128)(2,1)S(1)} %bitcast.31) | data formatting | bytes 4194304 | tf_op jit(solution)/shard_map/reshape | solution.py:88
  77.8 5.8 %shard_map.129.refs_4_ = f32[4,256,256]{2,1,0:T(8,128)} custom-call(bf16[128,2,8,512]{3,2,1,0:T(8,128)(2,1)} %bitcast.30, bf16[4,512,512]{2,1,0:T(8,128)(2,1)} %copy.30.refs_1_, f32[4,256,1]{2,1,0:T(8,128)} %constant.55.clone.refs_2_, f32[4,256,1]{2,1,0:T(8,128)} %constant.56.clone.refs_3_), custom_call_target="tpu_custom_call" | custom-call | flops 1073741824 | bytes 4194304 | tf_op jit(solution)/shard_map/pallas_call | solution.py:310
  83.6 20.4 %all-to-all-done = bf16[2,8,128,512]{3,1,0,2:T(8,128)(2,1)} async-done(((bf16[2,8,128,512]{3,1,0,2:T(8,128)(2,1)}), bf16[2,8,128,512]{3,1,0,2:T(8,128)(2,1)}, u32[]{:S(2)}, u32[]{:S(2)}) %all-to-all-start) | async-done | bytes 2097184 | tf_op jit(solution)/shard_map/all_to_all | solution.py:326
  104.0 6.2 %shard_map.130 = (f32[64,256]{1,0:T(8,128)}, f32[64,256]{1,0:T(8,128)}, f32[64,256]{1,0:T(8,128)}, f32[64,256]{1,0:T(8,128)}) custom-call(bf16[128,2,8,512]{3,2,1,0:T(8,128)(2,1)} %bitcast.4.refs_0_, bf16[4,512,512]{2,1,0:T(8,128)(2,1)} %copy.30.refs_1_, f32[4,256,1]{2,1,0:T(8,128)} %constant.55.clone.refs_2_, f32[4,256,1]{2,1,0:T(8,128)} %constant.56.clone.refs_3_, ...), custom_call_target="tpu_custom_call" | custom-call | flops 1073741824 | bytes 4194304 | tf_op jit(solution)/shard_map/pallas_call | solution.py:310
  110.2 1.2 %collective-permute-start = (f32[64,256]{1,0:T(8,128)}, f32[64,256]{1,0:T(8,128)S(1)}, u32[]{:S(2)}, u32[]{:S(2)}) collective-permute-start(f32[64,256]{1,0:T(8,128)} %get-tuple-element.10), channel_id=1, source_target_pairs={{0,1},{1,0},{2,3},{3,2},{4,5},{5,4},{6,7},{7,6},{8,9},{9,8},{10,11... | collective-permute-start | bytes 196616 | tf_op jit(solution)/shard_map/ppermute | solution.py:339
  111.7 1.4 %collective-permute-start.2 = (f32[64,256]{1,0:T(8,128)}, f32[64,256]{1,0:T(8,128)S(1)}, u32[]{:S(2)}, u32[]{:S(2)}) collective-permute-start(f32[64,256]{1,0:T(8,128)} %get-tuple-element.12), channel_id=1, source_target_pairs={{0,3},{1,2},{2,1},{3,0},{4,7},{5,6},{6,5},{7,4},{8,11},{9,10},{10,... | collective-permute-start | bytes 196616 | tf_op jit(solution)/shard_map/ppermute | solution.py:339
  113.1 2.2 %collective-permute-done.1 = f32[64,256]{1,0:T(8,128)S(1)} collective-permute-done((f32[64,256]{1,0:T(8,128)}, f32[64,256]{1,0:T(8,128)S(1)}, u32[]{:S(2)}, u32[]{:S(2)}) %collective-permute-start.1) | collective-permute-done | bytes 65568 | tf_op jit(solution)/shard_map/ppermute | solution.py:339
  115.3 1.6 %collective-permute-done.2 = f32[64,256]{1,0:T(8,128)S(1)} collective-permute-done((f32[64,256]{1,0:T(8,128)}, f32[64,256]{1,0:T(8,128)S(1)}, u32[]{:S(2)}, u32[]{:S(2)}) %collective-permute-start.2) | collective-permute-done | bytes 65568 | tf_op jit(solution)/shard_map/ppermute | solution.py:339
  116.9 0.9 select_select_fusion.3
  117.7 0.7 pad_maximum_fusion
  (16 shorter events, 1.0 us)
Async XLA Ops:
  3.2 8.4 %copy-start.1 = (bf16[8,1,2,8192]{3,2,1,0:T(2,128)(2,1)S(1)}, bf16[8,1,2,8192]{3,2,1,0:T(2,128)(2,1)}, u32[]{:S(2)}) copy-start(bf16[8,1,2,8192]{3,2,1,0:T(2,128)(2,1)} %param.14) | copy-start | bytes 786436
  25.9 41.4 %all-to-all-start.1 = ((bf16[2,8,128,512]{3,1,0,2:T(8,128)(2,1)}), bf16[2,8,128,512]{3,1,0,2:T(8,128)(2,1)S(1)}, u32[]{:S(2)}, u32[]{:S(2)}) async-start(bf16[2,8,128,512]{3,1,0,2:T(8,128)(2,1)} %copy.28), calls=%async_computation.1 | async-start | bytes 4194304 | tf_op jit(solution)/shard_map/all_to_all | solution.py:326
  50.4 23.9 %copy-start.3 = (bf16[256,256,1]{1,0,2:T(8,128)(2,1)S(1)}, bf16[256,256,1]{1,0,2:T(8,128)(2,1)}, u32[]{:S(2)}) copy-start(bf16[256,256,1]{1,0,2:T(8,128)(2,1)} %constant.59) | copy-start | bytes 393220
  50.4 24.0 %copy-start.4 = (s32[4,256]{1,0:T(4,128)S(1)}, s32[4,256]{1,0:T(4,128)}, u32[]{:S(2)}) copy-start(s32[4,256]{1,0:T(4,128)} %param.16) | copy-start | bytes 12292
  50.4 24.3 %copy-start.2 = (bf16[256,256,1]{1,0,2:T(8,128)(2,1)S(1)}, bf16[256,256,1]{1,0,2:T(8,128)(2,1)}, u32[]{:S(2)}) copy-start(bf16[256,256,1]{1,0,2:T(8,128)(2,1)} %constant.60) | copy-start | bytes 393220
  67.3 1.3 %copy-start = (bf16[2,8,128,512]{3,1,0,2:T(8,128)(2,1)}, bf16[2,8,128,512]{3,1,0,2:T(8,128)(2,1)S(1)}, u32[]{:S(2)}) copy-start(bf16[2,8,128,512]{3,1,0,2:T(8,128)(2,1)S(1)} %all-to-all-done.1) | copy-start | bytes 6291460
  68.6 35.4 %all-to-all-start = ((bf16[2,8,128,512]{3,1,0,2:T(8,128)(2,1)}), bf16[2,8,128,512]{3,1,0,2:T(8,128)(2,1)}, u32[]{:S(2)}, u32[]{:S(2)}) async-start(bf16[2,8,128,512]{3,1,0,2:T(8,128)(2,1)} %copy.22), calls=%async_computation | async-start | bytes 4194304 | tf_op jit(solution)/shard_map/all_to_all | solution.py:326
  110.2 2.9 %collective-permute-start = (f32[64,256]{1,0:T(8,128)}, f32[64,256]{1,0:T(8,128)S(1)}, u32[]{:S(2)}, u32[]{:S(2)}) collective-permute-start(f32[64,256]{1,0:T(8,128)} %get-tuple-element.10), channel_id=1, source_target_pairs={{0,1},{1,0},{2,3},{3,2},{4,5},{5,4},{6,7},{7,6},{8,9},{9,8},{10,11... | collective-permute-start | bytes 196616 | tf_op jit(solution)/shard_map/ppermute | solution.py:339
  111.4 3.9 %collective-permute-start.1 = (f32[64,256]{1,0:T(8,128)}, f32[64,256]{1,0:T(8,128)S(1)}, u32[]{:S(2)}, u32[]{:S(2)}) collective-permute-start(f32[64,256]{1,0:T(8,128)} %get-tuple-element.11), channel_id=1, source_target_pairs={{0,2},{1,3},{2,0},{3,1},{4,6},{5,7},{6,4},{7,5},{8,10},{9,11},{10,... | collective-permute-start | bytes 196616 | tf_op jit(solution)/shard_map/ppermute | solution.py:339
  111.7 5.1 %collective-permute-start.2 = (f32[64,256]{1,0:T(8,128)}, f32[64,256]{1,0:T(8,128)S(1)}, u32[]{:S(2)}, u32[]{:S(2)}) collective-permute-start(f32[64,256]{1,0:T(8,128)} %get-tuple-element.12), channel_id=1, source_target_pairs={{0,3},{1,2},{2,1},{3,0},{4,7},{5,6},{6,5},{7,4},{8,11},{9,10},{10,... | collective-permute-start | bytes 196616 | tf_op jit(solution)/shard_map/ppermute | solution.py:339

commit v16 on v13

--- a/solution.py
+++ b/solution.py
@@ -240,7 +240,7 @@
     gains = jnp.einsum("je,rpec->rpjc", picks_e, gains, preferred_element_type=jnp.float32)
     gains = jnp.concatenate([gains, gains], axis=3).astype(jnp.bfloat16)
 
-    chunk_pairs = [4, 4]
+    chunk_pairs = [8]
     chunks = len(chunk_pairs)
     tables = beam_tables(grid_rows, grid_len, dish_rows)
     feed_index = jnp.arange(dish_count, dtype=jnp.int32)

time: 117 us -> 113 us (0.966)
  waiting for transfers between devices: 43 us -> 52.4 us
  Pallas kernels: 25.9 us -> 19.9 us
  starting transfers between devices: 20.2 us -> 14.9 us
  local copies, waits for them, and re-layouts: 22 us -> 19.1 us
    all_to_all x2 -> x1, waiting for transfers between devices: 39.2 us -> 48.6 us  [body(): lax.all_to_all(s, ('dish', 'freq'), 2, 2, tiled=True)]
    all_to_all x2 -> x1, starting transfers between devices: 17.2 us -> 12 us  [body(): lax.all_to_all(s, ('dish', 'freq'), 2, 2, tiled=True)]
    pallas_call x2 -> x1, Pallas kernels: 12 us -> 8.31 us  [beamform_chunk(): pl.pallas_call(functools.partial(beam_kernel, dish_count, carry_in, finis...]
    pallas_call x2 -> x1, Pallas kernels: 13.9 us -> 11.6 us  [channelize_chunk(): pl.pallas_call(functools.partial(channelize_kernel, first_pair, pairs), g...]
    pallas_call x2 -> x1, local copies, waits for them, and re-layouts: 8.19 us -> 6.52 us  [channelize_chunk(): pl.pallas_call(functools.partial(channelize_kernel, first_pair, pairs), g...]
    unnamed x10 -> x6, local copies, waits for them, and re-layouts: 1.36 us -> 0.01 us
  transfers between devices with their start and end apart: 5 -> 4, of which waited for: 4 -> 3; matrix products, arithmetic and copies ran while one was open for 6% -> 3% of each run, Pallas kernels for 11% -> 0%
where the time goes in v16:
time: 113 us
  waiting for transfers between devices  52.4 us (46%)
  Pallas kernels  19.9 us (18%)
  local copies, waits for them, and re-layouts  19.1 us (17%)
  starting transfers between devices  14.9 us (13%)
  other arithmetic  3.64 us (3%)
  matrix products  2.83 us (3%)
    all_to_all x1, waiting for transfers between devices, body(): lax.all_to_all(s, ('dish', 'freq'), 2, 2, tiled=True)  48.6 us
    all_to_all x1, starting transfers between devices, body(): lax.all_to_all(s, ('dish', 'freq'), 2, 2, tiled=True)  12 us
    pallas_call x1, Pallas kernels, channelize_chunk(): pl.pallas_call(functools.partial(channelize_kernel, first_pair, pairs), g...  11.6 us
    another operation x1, local copies, waits for them, and re-layouts, body(): volts = voltages[:, 0].reshape(dish_rows, 2, samples // CHB, CHB)  8.46 us
    pallas_call x1, Pallas kernels, beamform_chunk(): pl.pallas_call(functools.partial(beam_kernel, dish_count, carry_in, finis...  8.31 us
    pallas_call x1, local copies, waits for them, and re-layouts, channelize_chunk(): pl.pallas_call(functools.partial(channelize_kernel, first_pair, pairs), g...  6.52 us
    ppermute x3, waiting for transfers between devices, body(): pieces.append(lax.ppermute(outgoing, 'dish', pairs_list))  3.87 us
    ppermute x3, starting transfers between devices, body(): pieces.append(lax.ppermute(outgoing, 'dish', pairs_list))  2.95 us
  transfers between devices with their start and end apart: 4, of which 3 were waited for; matrix products, arithmetic and copies ran while one was open for 3% of the time, Pallas kernels for 0%

profile of v16, /device:TPU:1, one launch (start us, length us, event | category | flops | bytes accessed | tf_op | source)
XLA Modules:
  0.0 112.9 jit_solution(716993284784504229)
XLA Ops:
  0.0 0.7 broadcast_multiply_fusion
  0.7 0.1 mul.16
  0.8 1.3 %reshape.54 = bf16[8,2,128,64]{3,2,1,0:T(8,128)(2,1)S(1)} reshape(bf16[8,1,2,8192]{3,2,1,0:T(2,128)(2,1)} %param.13) | data formatting | bytes 524288 | tf_op jit(solution)/shard_map/reshape;squeeze | solution.py:239
  2.1 0.3 convolution_convert_fusion.2
  2.4 0.3 copy.31
  2.7 1.1 pad_maximum_fusion.g_ref
  3.8 1.8 %convolution_convert_fusion.3 = bf16[128,2,2,128]{3,0,2,1:T(8,128)(2,1)} fusion(bf16[2,2,128,128]{3,2,1,0:T(8,128)(2,1)} %constant.49.clone, s32[128]{0:T(128)S(1)} %fusion.9), kind=kOutput, calls=%fused_computation.6 | convolution fusion | flops 16859136 | bytes 262656 | tf_op jit(solution)/shard_map/je,qseb->qsjb/dot_general | solution.py:236
  5.6 8.5 %reshape_squeeze.6.v_ref = bf16[8,2,1216,128]{3,2,1,0:T(8,128)(2,1)} reshape(bf16[8,1,2,155648]{3,2,1,0:T(2,128)(2,1)} %param.12) | data formatting | bytes 9961472 | tf_op jit(solution)/shard_map/reshape;squeeze | solution.py:253
  14.1 11.6 %shard_map.118 = bf16[2,8,128,1024]{3,2,1,0:T(8,128)(2,1)} custom-call(bf16[8,2,1216,128]{3,2,1,0:T(8,128)(2,1)} %reshape_squeeze.6.v_ref, f32[4,64,128]{2,1,0:T(8,128)} %constant.46.clone.w_ref, bf16[128,128]{1,0:T(8,128)(2,1)} %constant.47.clone.t1_ref, f32[2,64,128]{2,1,0:T(8,128)} %constant.48.clone.tw_ref, bf16[2,256,128]{2,1,0:T(8,128)(2,1)} %bitcast.34, ...), custom_call_target="tpu_custom_call" | custom-call | flops 1610612736 | bytes 9175040 | tf_op jit(solution)/shard_map/pallas_call | solution.py:261
  25.7 6.5 %copy.32 = bf16[2,8,128,1024]{3,1,0,2:T(8,128)(2,1)} copy(bf16[2,8,128,1024]{3,2,1,0:T(8,128)(2,1)} %shard_map.118) | data formatting | bytes 8388608 | tf_op jit(solution)/shard_map/pallas_call | solution.py:261
  32.2 12.0 %all-to-all-start = ((bf16[2,8,128,1024]{3,1,0,2:T(8,128)(2,1)}), bf16[2,8,128,1024]{3,1,0,2:T(8,128)(2,1)}, u32[]{:S(2)}, u32[]{:S(2)}) async-start(bf16[2,8,128,1024]{3,1,0,2:T(8,128)(2,1)} %copy.32), calls=%async_computation | async-start | bytes 8388608 | tf_op jit(solution)/shard_map/all_to_all | solution.py:318
  44.2 0.4 fusion
  44.6 0.4 fusion.10
  44.9 0.3 maximum_maximum_fusion
  45.2 2.4 %copy.37.refs_1_ = bf16[4,512,512]{2,1,0:T(8,128)(2,1)} copy(bf16[4,512,512]{1,2,0:T(8,128)(2,1)S(1)} %bitcast.32) | data formatting | bytes 4194304 | tf_op jit(solution)/shard_map/reshape | solution.py:88
  47.6 48.6 %all-to-all-done = bf16[2,8,128,1024]{3,1,0,2:T(8,128)(2,1)} async-done(((bf16[2,8,128,1024]{3,1,0,2:T(8,128)(2,1)}), bf16[2,8,128,1024]{3,1,0,2:T(8,128)(2,1)}, u32[]{:S(2)}, u32[]{:S(2)}) %all-to-all-start) | async-done | bytes 4194336 | tf_op jit(solution)/shard_map/all_to_all | solution.py:318
  96.2 8.3 %shard_map.119 = (f32[64,256]{1,0:T(8,128)}, f32[64,256]{1,0:T(8,128)}, f32[64,256]{1,0:T(8,128)}, f32[64,256]{1,0:T(8,128)}) custom-call(bf16[128,2,8,1024]{3,2,1,0:T(8,128)(2,1)} %bitcast.6.refs_0_, bf16[4,512,512]{2,1,0:T(8,128)(2,1)} %copy.37.refs_1_, f32[4,256,1]{2,1,0:T(8,128)} %constant.52.clone.refs_2_, f32[4,256,1]{2,1,0:T(8,128)} %constant.53.clone.refs_3_), custom_call_target="tpu_custom_call" | custom-call | flops 2147483648 | bytes 6291456 | tf_op jit(solution)/shard_map/pallas_call | solution.py:302
  104.5 1.3 %collective-permute-start = (f32[64,256]{1,0:T(8,128)}, f32[64,256]{1,0:T(8,128)S(1)}, u32[]{:S(2)}, u32[]{:S(2)}) collective-permute-start(f32[64,256]{1,0:T(8,128)} %get-tuple-element.10), channel_id=1, source_target_pairs={{0,1},{1,0},{2,3},{3,2},{4,5},{5,4},{6,7},{7,6},{8,9},{9,8},{10,11... | collective-permute-start | bytes 196616 | tf_op jit(solution)/shard_map/ppermute | solution.py:331
  105.7 1.3 %collective-permute-start.1 = (f32[64,256]{1,0:T(8,128)}, f32[64,256]{1,0:T(8,128)S(1)}, u32[]{:S(2)}, u32[]{:S(2)}) collective-permute-start(f32[64,256]{1,0:T(8,128)} %get-tuple-element.11), channel_id=1, source_target_pairs={{0,2},{1,3},{2,0},{3,1},{4,6},{5,7},{6,4},{7,5},{8,10},{9,11},{10,... | collective-permute-start | bytes 196616 | tf_op jit(solution)/shard_map/ppermute | solution.py:331
  107.0 0.4 collective-permute-start.2
  107.4 2.2 %collective-permute-done.1 = f32[64,256]{1,0:T(8,128)S(1)} collective-permute-done((f32[64,256]{1,0:T(8,128)}, f32[64,256]{1,0:T(8,128)S(1)}, u32[]{:S(2)}, u32[]{:S(2)}) %collective-permute-start.1) | collective-permute-done | bytes 65568 | tf_op jit(solution)/shard_map/ppermute | solution.py:331
  109.6 1.7 %collective-permute-done.2 = f32[64,256]{1,0:T(8,128)S(1)} collective-permute-done((f32[64,256]{1,0:T(8,128)}, f32[64,256]{1,0:T(8,128)S(1)}, u32[]{:S(2)}, u32[]{:S(2)}) %collective-permute-start.2) | collective-permute-done | bytes 65568 | tf_op jit(solution)/shard_map/ppermute | solution.py:331
  111.3 0.9 select_select_fusion.3
  112.2 0.7 pad_maximum_fusion.1
  (9 shorter events, 0.0 us)
Async XLA Ops:
  32.2 12.0 %copy-start.1 = (bf16[256,256,1]{1,0,2:T(8,128)(2,1)S(1)}, bf16[256,256,1]{1,0,2:T(8,128)(2,1)}, u32[]{:S(2)}) copy-start(bf16[256,256,1]{1,0,2:T(8,128)(2,1)} %constant.56) | copy-start | bytes 393220
  32.2 12.0 %copy-start.2 = (s32[4,256]{1,0:T(4,128)S(1)}, s32[4,256]{1,0:T(4,128)}, u32[]{:S(2)}) copy-start(s32[4,256]{1,0:T(4,128)} %param.15) | copy-start | bytes 12292
  32.2 12.3 %copy-start = (bf16[256,256,1]{1,0,2:T(8,128)(2,1)S(1)}, bf16[256,256,1]{1,0,2:T(8,128)(2,1)}, u32[]{:S(2)}) copy-start(bf16[256,256,1]{1,0,2:T(8,128)(2,1)} %constant.57) | copy-start | bytes 393220
  32.2 63.9 %all-to-all-start = ((bf16[2,8,128,1024]{3,1,0,2:T(8,128)(2,1)}), bf16[2,8,128,1024]{3,1,0,2:T(8,128)(2,1)}, u32[]{:S(2)}, u32[]{:S(2)}) async-start(bf16[2,8,128,1024]{3,1,0,2:T(8,128)(2,1)} %copy.32), calls=%async_computation | async-start | bytes 8388608 | tf_op jit(solution)/shard_map/all_to_all | solution.py:318
  104.5 3.0 %collective-permute-start = (f32[64,256]{1,0:T(8,128)}, f32[64,256]{1,0:T(8,128)S(1)}, u32[]{:S(2)}, u32[]{:S(2)}) collective-permute-start(f32[64,256]{1,0:T(8,128)} %get-tuple-element.10), channel_id=1, source_target_pairs={{0,1},{1,0},{2,3},{3,2},{4,5},{5,4},{6,7},{7,6},{8,9},{9,8},{10,11... | collective-permute-start | bytes 196616 | tf_op jit(solution)/shard_map/ppermute | solution.py:331
  105.7 3.9 %collective-permute-start.1 = (f32[64,256]{1,0:T(8,128)}, f32[64,256]{1,0:T(8,128)S(1)}, u32[]{:S(2)}, u32[]{:S(2)}) collective-permute-start(f32[64,256]{1,0:T(8,128)} %get-tuple-element.11), channel_id=1, source_target_pairs={{0,2},{1,3},{2,0},{3,1},{4,6},{5,7},{6,4},{7,5},{8,10},{9,11},{10,... | collective-permute-start | bytes 196616 | tf_op jit(solution)/shard_map/ppermute | solution.py:331
  107.0 4.3 %collective-permute-start.2 = (f32[64,256]{1,0:T(8,128)}, f32[64,256]{1,0:T(8,128)S(1)}, u32[]{:S(2)}, u32[]{:S(2)}) collective-permute-start(f32[64,256]{1,0:T(8,128)} %get-tuple-element.12), channel_id=1, source_target_pairs={{0,3},{1,2},{2,1},{3,0},{4,7},{5,6},{6,5},{7,4},{8,11},{9,10},{10,... | collective-permute-start | bytes 196616 | tf_op jit(solution)/shard_map/ppermute | solution.py:331

commit v17 on v16

--- a/solution.py
+++ b/solution.py
@@ -110,9 +110,7 @@
         turned_imag = sec_real * sin_tw + sec_imag * cos_tw
         return turned_real.astype(jnp.bfloat16), turned_imag.astype(jnp.bfloat16)
 
-    def pair(feed, step):
-        g_real = g_ref[feed, 0].astype(jnp.float32)
-        g_imag = g_ref[feed, 1].astype(jnp.float32)
+    def pair(feed, step, g_real, g_imag):
         pieces = []
         for offset in range(TAPS + 1):
             start = pl.multiple_of((2 * (step - first_pair) + offset) * CHA, CHA)
@@ -134,8 +132,12 @@
         o_ref[1, feed, :, lanes] = out_imag.astype(o_ref.dtype)
 
     for feed in range(feeds):
+        g_half_real = g_ref[feed, 0].astype(jnp.float32)
+        g_half_imag = g_ref[feed, 1].astype(jnp.float32)
+        g_real = jnp.concatenate([g_half_real, g_half_real], axis=1)
+        g_imag = jnp.concatenate([g_half_imag, g_half_imag], axis=1)
         for step in range(first_pair, first_pair + pairs):
-            pair(feed, step)
+            pair(feed, step, g_real, g_imag)
 
 
 def beam_kernel(dish_count, carry_in, finish, lanes, *refs):
@@ -238,7 +240,7 @@
     ).astype(jnp.bfloat16).reshape(2, 2 * dests, CHB)
     gains = feed_gains[:, 0].reshape(dish_rows, 2, CHB, CHA)
     gains = jnp.einsum("je,rpec->rpjc", picks_e, gains, preferred_element_type=jnp.float32)
-    gains = jnp.concatenate([gains, gains], axis=3).astype(jnp.bfloat16)
+    gains = gains.astype(jnp.bfloat16)
 
     chunk_pairs = [8]
     chunks = len(chunk_pairs)
@@ -270,7 +272,7 @@
                 pl.BlockSpec((2 * CHA, 2 * CHA), lambda r: (0, 0)),
                 pl.BlockSpec((2, CHA, CHB), lambda r: (0, 0, 0)),
                 pl.BlockSpec((2, 2 * dests, CHB), lambda r: (0, 0, 0)),
-                pl.BlockSpec((FEEDS_PER_STEP, 2, dests, 2 * CHA), lambda r: (r, 0, 0, 0)),
+                pl.BlockSpec((FEEDS_PER_STEP, 2, dests, CHA), lambda r: (r, 0, 0, 0)),
             ],
             out_specs=pl.BlockSpec((2, FEEDS_PER_STEP, dests, chunk_lanes), lambda r: (0, r, 0, 0)),
             out_shape=jax.ShapeDtypeStruct((2, dish_rows, dests, chunk_lanes), jnp.bfloat16),

time: 113 us -> 113 us (level)
  no operation moved by 1% of the time
where the time goes in v17:
time: 113 us; the launch traced here: 112 us
  waiting for transfers between devices  52.4 us (46%)
  Pallas kernels  19.9 us (18%)
  local copies, waits for them, and re-layouts  19.8 us (18%)
  starting transfers between devices  14.9 us (13%)
  matrix products  2.83 us (3%)
  other arithmetic  2.54 us (2%)
    all_to_all x1, waiting for transfers between devices, body(): lax.all_to_all(s, ('dish', 'freq'), 2, 2, tiled=True)  48.6 us
    all_to_all x1, starting transfers between devices, body(): lax.all_to_all(s, ('dish', 'freq'), 2, 2, tiled=True)  12 us
    pallas_call x1, Pallas kernels, channelize_chunk(): pl.pallas_call(functools.partial(channelize_kernel, first_pair, pairs), g...  11.6 us
    another operation x1, local copies, waits for them, and re-layouts, body(): volts = voltages[:, 0].reshape(dish_rows, 2, samples // CHB, CHB)  8.46 us
    pallas_call x1, Pallas kernels, beamform_chunk(): pl.pallas_call(functools.partial(beam_kernel, dish_count, carry_in, finis...  8.31 us
    pallas_call x1, local copies, waits for them, and re-layouts, channelize_chunk(): pl.pallas_call(functools.partial(channelize_kernel, first_pair, pairs), g...  6.52 us
    ppermute x3, waiting for transfers between devices, body(): pieces.append(lax.ppermute(outgoing, 'dish', pairs_list))  3.87 us
    ppermute x3, starting transfers between devices, body(): pieces.append(lax.ppermute(outgoing, 'dish', pairs_list))  2.95 us
  transfers between devices with their start and end apart: 4, of which 3 were waited for; matrix products, arithmetic and copies ran while one was open for 3% of the time, Pallas kernels for 0%

profile of v17, /device:TPU:1, one launch (start us, length us, event | category | flops | bytes accessed | tf_op | source)
XLA Modules:
  0.0 112.5 jit_solution(2274905276344426209)
XLA Ops:
  0.0 0.7 broadcast_multiply_fusion
  0.7 0.1 mul.16
  0.8 1.3 %reshape.54 = bf16[8,2,128,64]{3,2,1,0:T(8,128)(2,1)S(1)} reshape(bf16[8,1,2,8192]{3,2,1,0:T(2,128)(2,1)} %param.13) | data formatting | bytes 524288 | tf_op jit(solution)/shard_map/reshape;squeeze | solution.py:241
  2.1 0.3 convolution_convert_fusion.2
  2.4 1.0 copy.31
  3.5 1.8 %convolution_convert_fusion.3 = bf16[128,2,2,128]{3,0,2,1:T(8,128)(2,1)} fusion(bf16[2,2,128,128]{3,2,1,0:T(8,128)(2,1)} %constant.49.clone, s32[128]{0:T(128)S(1)} %fusion.9), kind=kOutput, calls=%fused_computation.6 | convolution fusion | flops 16859136 | bytes 262656 | tf_op jit(solution)/shard_map/je,qseb->qsjb/dot_general | solution.py:238
  5.2 8.5 %reshape_squeeze.6.v_ref = bf16[8,2,1216,128]{3,2,1,0:T(8,128)(2,1)} reshape(bf16[8,1,2,155648]{3,2,1,0:T(2,128)(2,1)} %param.12) | data formatting | bytes 9961472 | tf_op jit(solution)/shard_map/reshape;squeeze | solution.py:255
  13.7 11.6 %shard_map.118 = bf16[2,8,128,1024]{3,2,1,0:T(8,128)(2,1)} custom-call(bf16[8,2,1216,128]{3,2,1,0:T(8,128)(2,1)} %reshape_squeeze.6.v_ref, f32[4,64,128]{2,1,0:T(8,128)} %constant.46.clone.w_ref, bf16[128,128]{1,0:T(8,128)(2,1)} %constant.47.clone.t1_ref, f32[2,64,128]{2,1,0:T(8,128)} %constant.48.clone.tw_ref, bf16[2,256,128]{2,1,0:T(8,128)(2,1)} %bitcast.34, ...), custom_call_target="tpu_custom_call" | custom-call | flops 1610612736 | bytes 9175040 | tf_op jit(solution)/shard_map/pallas_call | solution.py:263
  25.3 6.5 %copy.32 = bf16[2,8,128,1024]{3,1,0,2:T(8,128)(2,1)} copy(bf16[2,8,128,1024]{3,2,1,0:T(8,128)(2,1)} %shard_map.118) | data formatting | bytes 8388608 | tf_op jit(solution)/shard_map/pallas_call | solution.py:263
  31.8 12.0 %all-to-all-start = ((bf16[2,8,128,1024]{3,1,0,2:T(8,128)(2,1)}), bf16[2,8,128,1024]{3,1,0,2:T(8,128)(2,1)}, u32[]{:S(2)}, u32[]{:S(2)}) async-start(bf16[2,8,128,1024]{3,1,0,2:T(8,128)(2,1)} %copy.32), calls=%async_computation | async-start | bytes 8388608 | tf_op jit(solution)/shard_map/all_to_all | solution.py:320
  43.8 0.4 fusion
  44.2 0.4 fusion.10
  44.5 0.3 maximum_maximum_fusion
  44.8 2.4 %copy.37.refs_1_ = bf16[4,512,512]{2,1,0:T(8,128)(2,1)} copy(bf16[4,512,512]{1,2,0:T(8,128)(2,1)S(1)} %bitcast.32) | data formatting | bytes 4194304 | tf_op jit(solution)/shard_map/reshape | solution.py:88
  47.2 48.6 %all-to-all-done = bf16[2,8,128,1024]{3,1,0,2:T(8,128)(2,1)} async-done(((bf16[2,8,128,1024]{3,1,0,2:T(8,128)(2,1)}), bf16[2,8,128,1024]{3,1,0,2:T(8,128)(2,1)}, u32[]{:S(2)}, u32[]{:S(2)}) %all-to-all-start) | async-done | bytes 4194336 | tf_op jit(solution)/shard_map/all_to_all | solution.py:320
  95.7 8.3 %shard_map.119 = (f32[64,256]{1,0:T(8,128)}, f32[64,256]{1,0:T(8,128)}, f32[64,256]{1,0:T(8,128)}, f32[64,256]{1,0:T(8,128)}) custom-call(bf16[128,2,8,1024]{3,2,1,0:T(8,128)(2,1)} %bitcast.6.refs_0_, bf16[4,512,512]{2,1,0:T(8,128)(2,1)} %copy.37.refs_1_, f32[4,256,1]{2,1,0:T(8,128)} %constant.52.clone.refs_2_, f32[4,256,1]{2,1,0:T(8,128)} %constant.53.clone.refs_3_), custom_call_target="tpu_custom_call" | custom-call | flops 2147483648 | bytes 6291456 | tf_op jit(solution)/shard_map/pallas_call | solution.py:304
  104.1 1.3 %collective-permute-start = (f32[64,256]{1,0:T(8,128)}, f32[64,256]{1,0:T(8,128)S(1)}, u32[]{:S(2)}, u32[]{:S(2)}) collective-permute-start(f32[64,256]{1,0:T(8,128)} %get-tuple-element.10), channel_id=1, source_target_pairs={{0,1},{1,0},{2,3},{3,2},{4,5},{5,4},{6,7},{7,6},{8,9},{9,8},{10,11... | collective-permute-start | bytes 196616 | tf_op jit(solution)/shard_map/ppermute | solution.py:333
  105.3 1.3 %collective-permute-start.1 = (f32[64,256]{1,0:T(8,128)}, f32[64,256]{1,0:T(8,128)S(1)}, u32[]{:S(2)}, u32[]{:S(2)}) collective-permute-start(f32[64,256]{1,0:T(8,128)} %get-tuple-element.11), channel_id=1, source_target_pairs={{0,2},{1,3},{2,0},{3,1},{4,6},{5,7},{6,4},{7,5},{8,10},{9,11},{10,... | collective-permute-start | bytes 196616 | tf_op jit(solution)/shard_map/ppermute | solution.py:333
  106.6 0.4 collective-permute-start.2
  107.0 0.0 collective-permute-done
  107.0 2.2 %collective-permute-done.1 = f32[64,256]{1,0:T(8,128)S(1)} collective-permute-done((f32[64,256]{1,0:T(8,128)}, f32[64,256]{1,0:T(8,128)S(1)}, u32[]{:S(2)}, u32[]{:S(2)}) %collective-permute-start.1) | collective-permute-done | bytes 65568 | tf_op jit(solution)/shard_map/ppermute | solution.py:333
  109.2 1.7 %collective-permute-done.2 = f32[64,256]{1,0:T(8,128)S(1)} collective-permute-done((f32[64,256]{1,0:T(8,128)}, f32[64,256]{1,0:T(8,128)S(1)}, u32[]{:S(2)}, u32[]{:S(2)}) %collective-permute-start.2) | collective-permute-done | bytes 65568 | tf_op jit(solution)/shard_map/ppermute | solution.py:333
  110.9 0.9 select_select_fusion.3
  111.8 0.7 pad_maximum_fusion
  (8 shorter events, 0.0 us)
Async XLA Ops:
  31.8 12.0 %copy-start.1 = (bf16[256,256,1]{1,0,2:T(8,128)(2,1)S(1)}, bf16[256,256,1]{1,0,2:T(8,128)(2,1)}, u32[]{:S(2)}) copy-start(bf16[256,256,1]{1,0,2:T(8,128)(2,1)} %constant.56) | copy-start | bytes 393220
  31.8 12.0 %copy-start.2 = (s32[4,256]{1,0:T(4,128)S(1)}, s32[4,256]{1,0:T(4,128)}, u32[]{:S(2)}) copy-start(s32[4,256]{1,0:T(4,128)} %param.15) | copy-start | bytes 12292
  31.8 12.4 %copy-start = (bf16[256,256,1]{1,0,2:T(8,128)(2,1)S(1)}, bf16[256,256,1]{1,0,2:T(8,128)(2,1)}, u32[]{:S(2)}) copy-start(bf16[256,256,1]{1,0,2:T(8,128)(2,1)} %constant.57) | copy-start | bytes 393220
  31.8 63.9 %all-to-all-start = ((bf16[2,8,128,1024]{3,1,0,2:T(8,128)(2,1)}), bf16[2,8,128,1024]{3,1,0,2:T(8,128)(2,1)}, u32[]{:S(2)}, u32[]{:S(2)}) async-start(bf16[2,8,128,1024]{3,1,0,2:T(8,128)(2,1)} %copy.32), calls=%async_computation | async-start | bytes 8388608 | tf_op jit(solution)/shard_map/all_to_all | solution.py:320
  104.1 3.0 %collective-permute-start = (f32[64,256]{1,0:T(8,128)}, f32[64,256]{1,0:T(8,128)S(1)}, u32[]{:S(2)}, u32[]{:S(2)}) collective-permute-start(f32[64,256]{1,0:T(8,128)} %get-tuple-element.10), channel_id=1, source_target_pairs={{0,1},{1,0},{2,3},{3,2},{4,5},{5,4},{6,7},{7,6},{8,9},{9,8},{10,11... | collective-permute-start | bytes 196616 | tf_op jit(solution)/shard_map/ppermute | solution.py:333
  105.3 3.9 %collective-permute-start.1 = (f32[64,256]{1,0:T(8,128)}, f32[64,256]{1,0:T(8,128)S(1)}, u32[]{:S(2)}, u32[]{:S(2)}) collective-permute-start(f32[64,256]{1,0:T(8,128)} %get-tuple-element.11), channel_id=1, source_target_pairs={{0,2},{1,3},{2,0},{3,1},{4,6},{5,7},{6,4},{7,5},{8,10},{9,11},{10,... | collective-permute-start | bytes 196616 | tf_op jit(solution)/shard_map/ppermute | solution.py:333
  106.6 4.3 %collective-permute-start.2 = (f32[64,256]{1,0:T(8,128)}, f32[64,256]{1,0:T(8,128)S(1)}, u32[]{:S(2)}, u32[]{:S(2)}) collective-permute-start(f32[64,256]{1,0:T(8,128)} %get-tuple-element.12), channel_id=1, source_target_pairs={{0,3},{1,2},{2,1},{3,0},{4,7},{5,6},{6,5},{7,4},{8,11},{9,10},{10,... | collective-permute-start | bytes 196616 | tf_op jit(solution)/shard_map/ppermute | solution.py:333

commit v18 on v17

--- a/solution.py
+++ b/solution.py
@@ -177,11 +177,15 @@
             )
         )
     (a_re, a_im), (b_re, b_im), (c_re, c_im), (d_re, d_im) = parts
+    even_re, even_im = a_re + c_re, a_im + c_im
+    odd_re, odd_im = a_re - c_re, a_im - c_im
+    pair_re, pair_im = b_re + d_re, b_im + d_im
+    cross_re, cross_im = b_re - d_re, b_im - d_im
     beams = [
-        (a_re + b_re + c_re + d_re, a_im + b_im + c_im + d_im),
-        (a_re + b_im - c_re - d_im, a_im - b_re - c_im + d_re),
-        (a_re - b_re + c_re - d_re, a_im - b_im + c_im - d_im),
-        (a_re - b_im - c_re + d_im, a_im + b_re - c_im - d_re),
+        (even_re + pair_re, even_im + pair_im),
+        (odd_re + cross_im, odd_im - cross_re),
+        (even_re - pair_re, even_im - pair_im),
+        (odd_re - cross_im, odd_im + cross_re),
     ]
     for q in range(dish_count):
         beam_real, beam_imag = beams[q]
@@ -248,8 +252,10 @@
     feed_index = jnp.arange(dish_count, dtype=jnp.int32)
     positions = jnp.arange(grid_len, dtype=jnp.int32)
     twist_cos, twist_sin = rotation_constant(dish_count, grid_len, total_dishes)
-    twist_cos = jnp.asarray(twist_cos[:, :, None])
-    twist_sin = jnp.asarray(twist_sin[:, :, None])
+    twist_lanes = 4 * quarter
+    lane_shape = (dish_count, grid_len, twist_lanes)
+    twist_cos = jnp.broadcast_to(jnp.asarray(twist_cos[:, :, None]), lane_shape)
+    twist_sin = jnp.broadcast_to(jnp.asarray(twist_sin[:, :, None]), lane_shape)
     lane_block = 4 * quarter
 
     volts = voltages[:, 0].reshape(dish_rows, 2, samples // CHB, CHB)
@@ -290,7 +296,7 @@
             pl.BlockSpec((dests, 2, dish_rows, lane_block), lambda f: (0, 0, 0, f)),
             pl.BlockSpec((dish_count, 2 * grid_len, 2 * grid_len), lambda f: (0, 0, 0)),
         ]
-        in_specs += [pl.BlockSpec((dish_count, grid_len, 1), lambda f: (0, 0, 0))] * 2
+        in_specs += [pl.BlockSpec((dish_count, grid_len, twist_lanes), lambda f: (0, 0, 0))] * 2
         operands = [received, tables, twist_cos, twist_sin]
         if carry_in:
             in_specs.append(pl.BlockSpec((dish_count, grid_len, lane_block), lambda f: (0, 0, 0)))

time: 113 us -> 116 us (1.027)
  local copies, waits for them, and re-layouts: 19.8 us -> 22.2 us
    broadcast_in_dim x0 -> x2, local copies, waits for them, and re-layouts: none -> 2.4 us  [the longest x1 1.21 us: body(): twist_sin = jnp.broadcast_to(jnp.asarray(twist_sin[:, :, None]), lane_shape)]
where the time goes in v18:
time: 116 us; the launch traced here: 115 us
  waiting for transfers between devices  52.4 us (45%)
  local copies, waits for them, and re-layouts  22.2 us (19%)
  Pallas kernels  20.1 us (17%)
  starting transfers between devices  14.9 us (13%)
  matrix products  2.83 us (2%)
  other arithmetic  2.54 us (2%)
    all_to_all x1, waiting for transfers between devices, body(): lax.all_to_all(s, ('dish', 'freq'), 2, 2, tiled=True)  48.5 us
    all_to_all x1, starting transfers between devices, body(): lax.all_to_all(s, ('dish', 'freq'), 2, 2, tiled=True)  12 us
    pallas_call x1, Pallas kernels, channelize_chunk(): pl.pallas_call(functools.partial(channelize_kernel, first_pair, pairs), g...  11.6 us
    pallas_call x1, Pallas kernels, beamform_chunk(): pl.pallas_call(functools.partial(beam_kernel, dish_count, carry_in, finis...  8.48 us
    another operation x1, local copies, waits for them, and re-layouts, body(): volts = voltages[:, 0].reshape(dish_rows, 2, samples // CHB, CHB)  8.46 us
    pallas_call x1, local copies, waits for them, and re-layouts, channelize_chunk(): pl.pallas_call(functools.partial(channelize_kernel, first_pair, pairs), g...  6.53 us
    ppermute x3, waiting for transfers between devices, body(): pieces.append(lax.ppermute(outgoing, 'dish', pairs_list))  3.87 us
    ppermute x3, starting transfers between devices, body(): pieces.append(lax.ppermute(outgoing, 'dish', pairs_list))  2.94 us
  transfers between devices with their start and end apart: 4, of which 3 were waited for; matrix products, arithmetic and copies ran while one was open for 3% of the time, Pallas kernels for 0%

profile of v18, /device:TPU:1, one launch (start us, length us, event | category | flops | bytes accessed | tf_op | source)
XLA Modules:
  0.0 115.1 jit_solution(4914714880533943360)
XLA Ops:
  0.0 0.7 broadcast_multiply_fusion
  0.8 1.3 %reshape.54 = bf16[8,2,128,64]{3,2,1,0:T(8,128)(2,1)S(1)} reshape(bf16[8,1,2,8192]{3,2,1,0:T(2,128)(2,1)} %param.13) | data formatting | bytes 524288 | tf_op jit(solution)/shard_map/reshape;squeeze | solution.py:245
  2.1 0.3 convolution_convert_fusion.2
  2.4 1.0 copy.31
  3.4 1.8 %convolution_convert_fusion.3 = bf16[128,2,2,128]{3,0,2,1:T(8,128)(2,1)} fusion(bf16[2,2,128,128]{3,2,1,0:T(8,128)(2,1)} %constant.49.clone, s32[128]{0:T(128)S(1)} %fusion.9), kind=kOutput, calls=%fused_computation.6 | convolution fusion | flops 16859136 | bytes 262656 | tf_op jit(solution)/shard_map/je,qseb->qsjb/dot_general | solution.py:242
  5.2 8.5 %reshape_squeeze.6.v_ref = bf16[8,2,1216,128]{3,2,1,0:T(8,128)(2,1)} reshape(bf16[8,1,2,155648]{3,2,1,0:T(2,128)(2,1)} %param.12) | data formatting | bytes 9961472 | tf_op jit(solution)/shard_map/reshape;squeeze | solution.py:261
  13.7 11.6 %shard_map.118 = bf16[2,8,128,1024]{3,2,1,0:T(8,128)(2,1)} custom-call(bf16[8,2,1216,128]{3,2,1,0:T(8,128)(2,1)} %reshape_squeeze.6.v_ref, f32[4,64,128]{2,1,0:T(8,128)} %constant.46.clone.w_ref, bf16[128,128]{1,0:T(8,128)(2,1)} %constant.47.clone.t1_ref, f32[2,64,128]{2,1,0:T(8,128)} %constant.48.clone.tw_ref, bf16[2,256,128]{2,1,0:T(8,128)(2,1)} %bitcast.34, ...), custom_call_target="tpu_custom_call" | custom-call | flops 1610612736 | bytes 9175040 | tf_op jit(solution)/shard_map/pallas_call | solution.py:269
  25.3 6.5 %copy.32 = bf16[2,8,128,1024]{3,1,0,2:T(8,128)(2,1)} copy(bf16[2,8,128,1024]{3,2,1,0:T(8,128)(2,1)} %shard_map.118) | data formatting | bytes 8388608 | tf_op jit(solution)/shard_map/pallas_call | solution.py:269
  31.8 12.0 %all-to-all-start = ((bf16[2,8,128,1024]{3,1,0,2:T(8,128)(2,1)}), bf16[2,8,128,1024]{3,1,0,2:T(8,128)(2,1)}, u32[]{:S(2)}, u32[]{:S(2)}) async-start(bf16[2,8,128,1024]{3,1,0,2:T(8,128)(2,1)} %copy.32), calls=%async_computation | async-start | bytes 8388608 | tf_op jit(solution)/shard_map/all_to_all | solution.py:326
  43.8 0.4 fusion
  44.2 0.4 fusion.10
  44.6 0.3 maximum_maximum_fusion
  44.8 2.4 %copy.37.refs_1_ = bf16[4,512,512]{2,1,0:T(8,128)(2,1)} copy(bf16[4,512,512]{1,2,0:T(8,128)(2,1)S(1)} %bitcast.32) | data formatting | bytes 4194304 | tf_op jit(solution)/shard_map/reshape | solution.py:88
  47.2 48.5 %all-to-all-done = bf16[2,8,128,1024]{3,1,0,2:T(8,128)(2,1)} async-done(((bf16[2,8,128,1024]{3,1,0,2:T(8,128)(2,1)}), bf16[2,8,128,1024]{3,1,0,2:T(8,128)(2,1)}, u32[]{:S(2)}, u32[]{:S(2)}) %all-to-all-start) | async-done | bytes 4194336 | tf_op jit(solution)/shard_map/all_to_all | solution.py:326
  95.8 1.2 %broadcast_in_dim.21.refs_3_ = f32[4,256,256]{2,1,0:T(8,128)} broadcast(f32[4,256]{1,0:T(4,128)S(1)} %copy-done.4), dimensions={0,1} | broadcast | bytes 1052672 | tf_op jit(solution)/shard_map/broadcast_in_dim | solution.py:258
  97.0 1.2 %broadcast_in_dim.9.refs_2_ = f32[4,256,256]{2,1,0:T(8,128)} broadcast(f32[4,256]{1,0:T(4,128)S(1)} %copy-done.3), dimensions={0,1} | broadcast | bytes 1052672 | tf_op jit(solution)/shard_map/broadcast_in_dim | solution.py:257
  98.2 8.5 %shard_map.119 = (f32[64,256]{1,0:T(8,128)}, f32[64,256]{1,0:T(8,128)}, f32[64,256]{1,0:T(8,128)}, f32[64,256]{1,0:T(8,128)}) custom-call(bf16[128,2,8,1024]{3,2,1,0:T(8,128)(2,1)} %bitcast.6.refs_0_, bf16[4,512,512]{2,1,0:T(8,128)(2,1)} %copy.37.refs_1_, f32[4,256,256]{2,1,0:T(8,128)} %broadcast_in_dim.9.refs_2_, f32[4,256,256]{2,1,0:T(8,128)} %broadcast_in_dim.21.refs_3_), custom_call_target="tpu_custom_call" | custom-call | flops 2147483648 | bytes 6291456 | tf_op jit(solution)/shard_map/pallas_call | solution.py:310
  106.6 1.2 %collective-permute-start = (f32[64,256]{1,0:T(8,128)}, f32[64,256]{1,0:T(8,128)S(1)}, u32[]{:S(2)}, u32[]{:S(2)}) collective-permute-start(f32[64,256]{1,0:T(8,128)} %get-tuple-element.10), channel_id=1, source_target_pairs={{0,1},{1,0},{2,3},{3,2},{4,5},{5,4},{6,7},{7,6},{8,9},{9,8},{10,11... | collective-permute-start | bytes 196616 | tf_op jit(solution)/shard_map/ppermute | solution.py:339
  107.9 1.3 %collective-permute-start.1 = (f32[64,256]{1,0:T(8,128)}, f32[64,256]{1,0:T(8,128)S(1)}, u32[]{:S(2)}, u32[]{:S(2)}) collective-permute-start(f32[64,256]{1,0:T(8,128)} %get-tuple-element.11), channel_id=1, source_target_pairs={{0,2},{1,3},{2,0},{3,1},{4,6},{5,7},{6,4},{7,5},{8,10},{9,11},{10,... | collective-permute-start | bytes 196616 | tf_op jit(solution)/shard_map/ppermute | solution.py:339
  109.2 0.4 collective-permute-start.2
  109.6 2.2 %collective-permute-done.1 = f32[64,256]{1,0:T(8,128)S(1)} collective-permute-done((f32[64,256]{1,0:T(8,128)}, f32[64,256]{1,0:T(8,128)S(1)}, u32[]{:S(2)}, u32[]{:S(2)}) %collective-permute-start.1) | collective-permute-done | bytes 65568 | tf_op jit(solution)/shard_map/ppermute | solution.py:339
  111.8 1.7 %collective-permute-done.2 = f32[64,256]{1,0:T(8,128)S(1)} collective-permute-done((f32[64,256]{1,0:T(8,128)}, f32[64,256]{1,0:T(8,128)S(1)}, u32[]{:S(2)}, u32[]{:S(2)}) %collective-permute-start.2) | collective-permute-done | bytes 65568 | tf_op jit(solution)/shard_map/ppermute | solution.py:339
  113.5 0.9 select_select_fusion.3
  114.3 0.7 pad_maximum_fusion
  (14 shorter events, 0.1 us)
Async XLA Ops:
  31.8 12.0 %copy-start.1 = (bf16[256,256,1]{1,0,2:T(8,128)(2,1)S(1)}, bf16[256,256,1]{1,0,2:T(8,128)(2,1)}, u32[]{:S(2)}) copy-start(bf16[256,256,1]{1,0,2:T(8,128)(2,1)} %constant.58) | copy-start | bytes 393220
  31.8 12.0 %copy-start.2 = (s32[4,256]{1,0:T(4,128)S(1)}, s32[4,256]{1,0:T(4,128)}, u32[]{:S(2)}) copy-start(s32[4,256]{1,0:T(4,128)} %param.15) | copy-start | bytes 12292
  31.8 12.3 %copy-start = (bf16[256,256,1]{1,0,2:T(8,128)(2,1)S(1)}, bf16[256,256,1]{1,0,2:T(8,128)(2,1)}, u32[]{:S(2)}) copy-start(bf16[256,256,1]{1,0,2:T(8,128)(2,1)} %constant.59) | copy-start | bytes 393220
  31.8 63.9 %all-to-all-start = ((bf16[2,8,128,1024]{3,1,0,2:T(8,128)(2,1)}), bf16[2,8,128,1024]{3,1,0,2:T(8,128)(2,1)}, u32[]{:S(2)}, u32[]{:S(2)}) async-start(bf16[2,8,128,1024]{3,1,0,2:T(8,128)(2,1)} %copy.32), calls=%async_computation | async-start | bytes 8388608 | tf_op jit(solution)/shard_map/all_to_all | solution.py:326
  44.5 51.2 %copy-start.4 = (f32[4,256]{1,0:T(4,128)S(1)}, f32[4,256]{1,0:T(4,128)}, u32[]{:S(2)}) copy-start(f32[4,256]{1,0:T(4,128)} %constant.57) | copy-start | bytes 12292
  44.5 52.4 %copy-start.3 = (f32[4,256]{1,0:T(4,128)S(1)}, f32[4,256]{1,0:T(4,128)}, u32[]{:S(2)}) copy-start(f32[4,256]{1,0:T(4,128)} %constant.56) | copy-start | bytes 12292
  106.6 2.9 %collective-permute-start = (f32[64,256]{1,0:T(8,128)}, f32[64,256]{1,0:T(8,128)S(1)}, u32[]{:S(2)}, u32[]{:S(2)}) collective-permute-start(f32[64,256]{1,0:T(8,128)} %get-tuple-element.10), channel_id=1, source_target_pairs={{0,1},{1,0},{2,3},{3,2},{4,5},{5,4},{6,7},{7,6},{8,9},{9,8},{10,11... | collective-permute-start | bytes 196616 | tf_op jit(solution)/shard_map/ppermute | solution.py:339
  107.9 3.9 %collective-permute-start.1 = (f32[64,256]{1,0:T(8,128)}, f32[64,256]{1,0:T(8,128)S(1)}, u32[]{:S(2)}, u32[]{:S(2)}) collective-permute-start(f32[64,256]{1,0:T(8,128)} %get-tuple-element.11), channel_id=1, source_target_pairs={{0,2},{1,3},{2,0},{3,1},{4,6},{5,7},{6,4},{7,5},{8,10},{9,11},{10,... | collective-permute-start | bytes 196616 | tf_op jit(solution)/shard_map/ppermute | solution.py:339
  109.2 4.3 %collective-permute-start.2 = (f32[64,256]{1,0:T(8,128)}, f32[64,256]{1,0:T(8,128)S(1)}, u32[]{:S(2)}, u32[]{:S(2)}) collective-permute-start(f32[64,256]{1,0:T(8,128)} %get-tuple-element.12), channel_id=1, source_target_pairs={{0,3},{1,2},{2,1},{3,0},{4,7},{5,6},{6,5},{7,4},{8,11},{9,10},{10,... | collective-permute-start | bytes 196616 | tf_op jit(solution)/shard_map/ppermute | solution.py:339

commit v19 on v17

--- a/solution.py
+++ b/solution.py
@@ -79,13 +79,7 @@
     sine_table = jnp.einsum(
         "jg,dgm->djm", sine_base, picks, preferred_element_type=jnp.float32
     ).astype(jnp.bfloat16)
-    shape = (grid_rows.shape[0], grid_len, devices, 1, rows_per_device)
-    cosine_table = cosine_table.reshape(shape)
-    sine_table = sine_table.reshape(shape)
-    real_rows = jnp.concatenate([cosine_table, sine_table], axis=3)
-    imag_rows = jnp.concatenate([-sine_table, cosine_table], axis=3)
-    rows = jnp.concatenate([real_rows, imag_rows], axis=1)
-    return rows.reshape(grid_rows.shape[0], 2 * grid_len, 2 * grid_len)
+    return jnp.stack([cosine_table, sine_table], axis=1)
 
 
 def channelize_kernel(first_pair, pairs, v_ref, w_ref, t1_ref, tw_ref, t2_ref, g_ref, o_ref):
@@ -148,7 +142,7 @@
     step = pl.program_id(0)
     devices = x_ref.shape[0] // dish_count
     rows = x_ref.shape[2]
-    grid_len = t_ref.shape[1] // 2
+    grid_len = t_ref.shape[2]
     lane_window = slice(None)
 
     @pl.when(step == 0)
@@ -160,12 +154,16 @@
 
     parts = []
     for d in range(dish_count):
-        block = x_ref[pl.ds(d * devices, devices), :, :, lane_window].reshape(
-            2 * rows * devices, lanes
+        x_real = x_ref[pl.ds(d * devices, devices), 0, :, lane_window].reshape(rows * devices, lanes)
+        x_imag = x_ref[pl.ds(d * devices, devices), 1, :, lane_window].reshape(rows * devices, lanes)
+        cosine = t_ref[d, 0]
+        sine = t_ref[d, 1]
+        sum_real = jnp.dot(cosine, x_real, preferred_element_type=jnp.float32) + jnp.dot(
+            sine, x_imag, preferred_element_type=jnp.float32
         )
-        sums = jnp.dot(t_ref[d], block, preferred_element_type=jnp.float32)
-        sum_real = sums[:grid_len]
-        sum_imag = sums[grid_len:]
+        sum_imag = jnp.dot(cosine, x_imag, preferred_element_type=jnp.float32) - jnp.dot(
+            sine, x_real, preferred_element_type=jnp.float32
+        )
         cos_d = c_ref[d]
         sin_d = s_ref[d]
         part_real = sum_real * cos_d - sum_imag * sin_d
@@ -288,7 +286,7 @@
         chunk_lanes = received.shape[3]
         in_specs = [
             pl.BlockSpec((dests, 2, dish_rows, lane_block), lambda f: (0, 0, 0, f)),
-            pl.BlockSpec((dish_count, 2 * grid_len, 2 * grid_len), lambda f: (0, 0, 0)),
+            pl.BlockSpec((dish_count, 2, grid_len, grid_len), lambda f: (0, 0, 0, 0)),
         ]
         in_specs += [pl.BlockSpec((dish_count, grid_len, 1), lambda f: (0, 0, 0))] * 2
         operands = [received, tables, twist_cos, twist_sin]

time: 113 us -> 110 us (0.973)
  local copies, waits for them, and re-layouts: 19.8 us -> 16.5 us
  waiting for transfers between devices: 52.4 us -> 53.9 us
    reshape x1 -> x0, local copies, waits for them, and re-layouts: 2.38 us -> none  [beam_tables(): return rows.reshape(grid_rows.shape[0], 2 * grid_len, 2 * grid_len)]
    all_to_all x1, waiting for transfers between devices: 48.6 us -> 50 us  [body(): lax.all_to_all(s, ('dish', 'freq'), 2, 2, tiled=True)]
  transfers between devices with their start and end apart: 4 -> 4, of which waited for: 3 -> 3; matrix products, arithmetic and copies ran while one was open for 3% -> 2% of each run, Pallas kernels for 0% -> 0%
where the time goes in v19:
time: 110 us; the launch traced here: 109 us
  waiting for transfers between devices  53.9 us (49%)
  Pallas kernels  19.3 us (18%)
  local copies, waits for them, and re-layouts  16.5 us (15%)
  starting transfers between devices  14.9 us (14%)
  other arithmetic  2.66 us (2%)
  matrix products  2.08 us (2%)
    all_to_all x1, waiting for transfers between devices, body(): lax.all_to_all(s, ('dish', 'freq'), 2, 2, tiled=True)  50 us
    all_to_all x1, starting transfers between devices, body(): lax.all_to_all(s, ('dish', 'freq'), 2, 2, tiled=True)  12 us
    pallas_call x1, Pallas kernels, channelize_chunk(): pl.pallas_call(functools.partial(channelize_kernel, first_pair, pairs), g...  11.6 us
    another operation x1, local copies, waits for them, and re-layouts, body(): volts = voltages[:, 0].reshape(dish_rows, 2, samples // CHB, CHB)  8.52 us
    pallas_call x1, Pallas kernels, beamform_chunk(): pl.pallas_call(functools.partial(beam_kernel, dish_count, carry_in, finis...  7.73 us
    pallas_call x1, local copies, waits for them, and re-layouts, channelize_chunk(): pl.pallas_call(functools.partial(channelize_kernel, first_pair, pairs), g...  6.53 us
    ppermute x3, waiting for transfers between devices, body(): pieces.append(lax.ppermute(outgoing, 'dish', pairs_list))  3.86 us
    ppermute x3, starting transfers between devices, body(): pieces.append(lax.ppermute(outgoing, 'dish', pairs_list))  2.92 us
  transfers between devices with their start and end apart: 4, of which 3 were waited for; matrix products, arithmetic and copies ran while one was open for 2% of the time, Pallas kernels for 0%

profile of v19, /device:TPU:1, one launch (start us, length us, event | category | flops | bytes accessed | tf_op | source)
XLA Modules:
  0.0 109.4 jit_solution(10050829125382220424)
XLA Ops:
  0.0 8.5 %reshape_squeeze.6.v_ref = bf16[8,2,1216,128]{3,2,1,0:T(8,128)(2,1)} reshape(bf16[8,1,2,155648]{3,2,1,0:T(2,128)(2,1)} %param.12) | data formatting | bytes 9961472 | tf_op jit(solution)/shard_map/reshape;squeeze | solution.py:253
  8.5 0.0 copy-done.5
  8.5 0.1 mul.16
  8.6 0.0 copy-done
  8.6 0.3 reshape.30
  9.0 0.9 convolution_convert_fusion.3
  9.9 0.3 convolution_convert_fusion.2
  10.2 1.0 copy.26
  11.2 11.6 %shard_map.118 = bf16[2,8,128,1024]{3,2,1,0:T(8,128)(2,1)} custom-call(bf16[8,2,1216,128]{3,2,1,0:T(8,128)(2,1)} %reshape_squeeze.6.v_ref, f32[4,64,128]{2,1,0:T(8,128)} %constant.46.clone.w_ref, bf16[128,128]{1,0:T(8,128)(2,1)} %constant.47.clone.t1_ref, f32[2,64,128]{2,1,0:T(8,128)} %constant.48.clone.tw_ref, bf16[2,256,128]{2,1,0:T(8,128)(2,1)} %bitcast.26, ...), custom_call_target="tpu_custom_call" | custom-call | flops 1610612736 | bytes 9175040 | tf_op jit(solution)/shard_map/pallas_call | solution.py:261
  22.8 6.5 %copy.27 = bf16[2,8,128,1024]{3,1,0,2:T(8,128)(2,1)} copy(bf16[2,8,128,1024]{3,2,1,0:T(8,128)(2,1)} %shard_map.118) | data formatting | bytes 8388608 | tf_op jit(solution)/shard_map/pallas_call | solution.py:261
  29.4 12.0 %all-to-all-start = ((bf16[2,8,128,1024]{3,1,0,2:T(8,128)(2,1)}), bf16[2,8,128,1024]{3,1,0,2:T(8,128)(2,1)}, u32[]{:S(2)}, u32[]{:S(2)}) async-start(bf16[2,8,128,1024]{3,1,0,2:T(8,128)(2,1)} %copy.27), calls=%async_computation | async-start | bytes 8388608 | tf_op jit(solution)/shard_map/all_to_all | solution.py:318
  41.3 0.4 fusion.1
  41.8 0.4 fusion
  42.2 1.1 pad_maximum_fusion.refs_1_
  43.3 50.0 %all-to-all-done = bf16[2,8,128,1024]{3,1,0,2:T(8,128)(2,1)} async-done(((bf16[2,8,128,1024]{3,1,0,2:T(8,128)(2,1)}), bf16[2,8,128,1024]{3,1,0,2:T(8,128)(2,1)}, u32[]{:S(2)}, u32[]{:S(2)}) %all-to-all-start) | async-done | bytes 4194336 | tf_op jit(solution)/shard_map/all_to_all | solution.py:318
  93.3 7.7 %shard_map.119 = (f32[64,256]{1,0:T(8,128)}, f32[64,256]{1,0:T(8,128)}, f32[64,256]{1,0:T(8,128)}, f32[64,256]{1,0:T(8,128)}) custom-call(bf16[128,2,8,1024]{3,2,1,0:T(8,128)(2,1)} %bitcast.6.refs_0_, bf16[4,2,256,256]{3,2,1,0:T(8,128)(2,1)} %pad_maximum_fusion.refs_1_, f32[4,256,1]{2,1,0:T(8,128)} %constant.52.clone.refs_2_, ...), custom_call_target="tpu_custom_call" | custom-call | flops 2147483648 | bytes 5242880 | tf_op jit(solution)/shard_map/pallas_call | solution.py:302
  101.0 1.2 %collective-permute-start = (f32[64,256]{1,0:T(8,128)}, f32[64,256]{1,0:T(8,128)S(1)}, u32[]{:S(2)}, u32[]{:S(2)}) collective-permute-start(f32[64,256]{1,0:T(8,128)} %get-tuple-element.10), channel_id=1, source_target_pairs={{0,1},{1,0},{2,3},{3,2},{4,5},{5,4},{6,7},{7,6},{8,9},{9,8},{10,11... | collective-permute-start | bytes 196616 | tf_op jit(solution)/shard_map/ppermute | solution.py:331
  102.3 1.3 %collective-permute-start.1 = (f32[64,256]{1,0:T(8,128)}, f32[64,256]{1,0:T(8,128)S(1)}, u32[]{:S(2)}, u32[]{:S(2)}) collective-permute-start(f32[64,256]{1,0:T(8,128)} %get-tuple-element.11), channel_id=1, source_target_pairs={{0,2},{1,3},{2,0},{3,1},{4,6},{5,7},{6,4},{7,5},{8,10},{9,11},{10,... | collective-permute-start | bytes 196616 | tf_op jit(solution)/shard_map/ppermute | solution.py:331
  103.5 0.4 collective-permute-start.2
  104.0 0.0 collective-permute-done
  104.0 2.2 %collective-permute-done.1 = f32[64,256]{1,0:T(8,128)S(1)} collective-permute-done((f32[64,256]{1,0:T(8,128)}, f32[64,256]{1,0:T(8,128)S(1)}, u32[]{:S(2)}, u32[]{:S(2)}) %collective-permute-start.1) | collective-permute-done | bytes 65568 | tf_op jit(solution)/shard_map/ppermute | solution.py:331
  106.2 1.6 %collective-permute-done.2 = f32[64,256]{1,0:T(8,128)S(1)} collective-permute-done((f32[64,256]{1,0:T(8,128)}, f32[64,256]{1,0:T(8,128)S(1)}, u32[]{:S(2)}, u32[]{:S(2)}) %collective-permute-start.2) | collective-permute-done | bytes 65568 | tf_op jit(solution)/shard_map/ppermute | solution.py:331
  107.8 0.9 select_select_fusion.3
  108.7 0.7 pad_maximum_fusion.1
  (13 shorter events, 0.0 us)
Async XLA Ops:
  0.0 9.0 %copy-start.3 = (bf16[2,2,128,128]{3,2,1,0:T(8,128)(2,1)S(1)}, bf16[2,2,128,128]{3,2,1,0:T(8,128)(2,1)}, u32[]{:S(2)}) copy-start(bf16[2,2,128,128]{3,2,1,0:T(8,128)(2,1)} %constant.49.clone) | copy-start | bytes 393220
  0.0 8.5 %copy-start.5 = (s32[32]{0:T(128)S(1)}, s32[32]{0:T(128)}, u32[]{:S(2)}) copy-start(s32[32]{0:T(128)} %param.14) | copy-start | bytes 388
  0.0 8.6 %copy-start = (bf16[8,1,2,8192]{3,2,1,0:T(2,128)(2,1)S(1)}, bf16[8,1,2,8192]{3,2,1,0:T(2,128)(2,1)}, u32[]{:S(2)}) copy-start(bf16[8,1,2,8192]{3,2,1,0:T(2,128)(2,1)} %param.13) | copy-start | bytes 786436
  29.3 12.0 %copy-start.2 = (bf16[256,256,1]{1,0,2:T(8,128)(2,1)S(1)}, bf16[256,256,1]{1,0,2:T(8,128)(2,1)}, u32[]{:S(2)}) copy-start(bf16[256,256,1]{1,0,2:T(8,128)(2,1)} %constant.57) | copy-start | bytes 393220
  29.3 12.0 %copy-start.4 = (s32[4,256]{1,0:T(4,128)S(1)}, s32[4,256]{1,0:T(4,128)}, u32[]{:S(2)}) copy-start(s32[4,256]{1,0:T(4,128)} %param.15) | copy-start | bytes 12292
  29.4 12.4 %copy-start.1 = (bf16[256,256,1]{1,0,2:T(8,128)(2,1)S(1)}, bf16[256,256,1]{1,0,2:T(8,128)(2,1)}, u32[]{:S(2)}) copy-start(bf16[256,256,1]{1,0,2:T(8,128)(2,1)} %constant.56) | copy-start | bytes 393220
  29.4 63.9 %all-to-all-start = ((bf16[2,8,128,1024]{3,1,0,2:T(8,128)(2,1)}), bf16[2,8,128,1024]{3,1,0,2:T(8,128)(2,1)}, u32[]{:S(2)}, u32[]{:S(2)}) async-start(bf16[2,8,128,1024]{3,1,0,2:T(8,128)(2,1)} %copy.27), calls=%async_computation | async-start | bytes 8388608 | tf_op jit(solution)/shard_map/all_to_all | solution.py:318
  101.0 2.9 %collective-permute-start = (f32[64,256]{1,0:T(8,128)}, f32[64,256]{1,0:T(8,128)S(1)}, u32[]{:S(2)}, u32[]{:S(2)}) collective-permute-start(f32[64,256]{1,0:T(8,128)} %get-tuple-element.10), channel_id=1, source_target_pairs={{0,1},{1,0},{2,3},{3,2},{4,5},{5,4},{6,7},{7,6},{8,9},{9,8},{10,11... | collective-permute-start | bytes 196616 | tf_op jit(solution)/shard_map/ppermute | solution.py:331
  102.3 3.9 %collective-permute-start.1 = (f32[64,256]{1,0:T(8,128)}, f32[64,256]{1,0:T(8,128)S(1)}, u32[]{:S(2)}, u32[]{:S(2)}) collective-permute-start(f32[64,256]{1,0:T(8,128)} %get-tuple-element.11), channel_id=1, source_target_pairs={{0,2},{1,3},{2,0},{3,1},{4,6},{5,7},{6,4},{7,5},{8,10},{9,11},{10,... | collective-permute-start | bytes 196616 | tf_op jit(solution)/shard_map/ppermute | solution.py:331
  103.5 4.3 %collective-permute-start.2 = (f32[64,256]{1,0:T(8,128)}, f32[64,256]{1,0:T(8,128)S(1)}, u32[]{:S(2)}, u32[]{:S(2)}) collective-permute-start(f32[64,256]{1,0:T(8,128)} %get-tuple-element.12), channel_id=1, source_target_pairs={{0,3},{1,2},{2,1},{3,0},{4,7},{5,6},{6,5},{7,4},{8,11},{9,10},{10,... | collective-permute-start | bytes 196616 | tf_op jit(solution)/shard_map/ppermute | solution.py:331

commit v20 on v19

--- a/solution.py
+++ b/solution.py
@@ -248,7 +248,7 @@
     twist_cos, twist_sin = rotation_constant(dish_count, grid_len, total_dishes)
     twist_cos = jnp.asarray(twist_cos[:, :, None])
     twist_sin = jnp.asarray(twist_sin[:, :, None])
-    lane_block = 4 * quarter
+    lane_block = 2 * quarter
 
     volts = voltages[:, 0].reshape(dish_rows, 2, samples // CHB, CHB)
 

time: 110 us -> 113 us (1.027)
  Pallas kernels: 19.3 us -> 21.9 us
    pallas_call x1, Pallas kernels: 7.73 us -> 10.3 us  [beamform_chunk(): pl.pallas_call(functools.partial(beam_kernel, dish_count, carry_in, finis...]
where the time goes in v20:
time: 113 us; the launch traced here: 112 us
  waiting for transfers between devices  53.9 us (48%)
  Pallas kernels  21.9 us (19%)
  local copies, waits for them, and re-layouts  16.5 us (15%)
  starting transfers between devices  14.9 us (13%)
  other arithmetic  2.66 us (2%)
  matrix products  2.08 us (2%)
    all_to_all x1, waiting for transfers between devices, body(): lax.all_to_all(s, ('dish', 'freq'), 2, 2, tiled=True)  50 us
    all_to_all x1, starting transfers between devices, body(): lax.all_to_all(s, ('dish', 'freq'), 2, 2, tiled=True)  12 us
    pallas_call x1, Pallas kernels, channelize_chunk(): pl.pallas_call(functools.partial(channelize_kernel, first_pair, pairs), g...  11.6 us
    pallas_call x1, Pallas kernels, beamform_chunk(): pl.pallas_call(functools.partial(beam_kernel, dish_count, carry_in, finis...  10.3 us
    another operation x1, local copies, waits for them, and re-layouts, body(): volts = voltages[:, 0].reshape(dish_rows, 2, samples // CHB, CHB)  8.52 us
    pallas_call x1, local copies, waits for them, and re-layouts, channelize_chunk(): pl.pallas_call(functools.partial(channelize_kernel, first_pair, pairs), g...  6.53 us
    ppermute x3, waiting for transfers between devices, body(): pieces.append(lax.ppermute(outgoing, 'dish', pairs_list))  3.85 us
    ppermute x3, starting transfers between devices, body(): pieces.append(lax.ppermute(outgoing, 'dish', pairs_list))  2.94 us
  transfers between devices with their start and end apart: 4, of which 3 were waited for; matrix products, arithmetic and copies ran while one was open for 2% of the time, Pallas kernels for 0%

profile of v20, /device:TPU:1, one launch (start us, length us, event | category | flops | bytes accessed | tf_op | source)
XLA Modules:
  0.0 112.0 jit_solution(4399685069610562291)
XLA Ops:
  0.0 8.5 %reshape_squeeze.6.v_ref = bf16[8,2,1216,128]{3,2,1,0:T(8,128)(2,1)} reshape(bf16[8,1,2,155648]{3,2,1,0:T(2,128)(2,1)} %param.12) | data formatting | bytes 9961472 | tf_op jit(solution)/shard_map/reshape;squeeze | solution.py:253
  8.5 0.0 copy-done.5
  8.5 0.1 mul.16
  8.6 0.0 copy-done
  8.6 0.3 reshape.30
  9.0 0.9 convolution_convert_fusion.3
  9.9 0.3 convolution_convert_fusion.2
  10.2 1.0 copy.26
  11.2 11.6 %shard_map.118 = bf16[2,8,128,1024]{3,2,1,0:T(8,128)(2,1)} custom-call(bf16[8,2,1216,128]{3,2,1,0:T(8,128)(2,1)} %reshape_squeeze.6.v_ref, f32[4,64,128]{2,1,0:T(8,128)} %constant.46.clone.w_ref, bf16[128,128]{1,0:T(8,128)(2,1)} %constant.47.clone.t1_ref, f32[2,64,128]{2,1,0:T(8,128)} %constant.48.clone.tw_ref, bf16[2,256,128]{2,1,0:T(8,128)(2,1)} %bitcast.26, ...), custom_call_target="tpu_custom_call" | custom-call | flops 1610612736 | bytes 9175040 | tf_op jit(solution)/shard_map/pallas_call | solution.py:261
  22.8 6.5 %copy.27 = bf16[2,8,128,1024]{3,1,0,2:T(8,128)(2,1)} copy(bf16[2,8,128,1024]{3,2,1,0:T(8,128)(2,1)} %shard_map.118) | data formatting | bytes 8388608 | tf_op jit(solution)/shard_map/pallas_call | solution.py:261
  29.4 12.0 %all-to-all-start = ((bf16[2,8,128,1024]{3,1,0,2:T(8,128)(2,1)}), bf16[2,8,128,1024]{3,1,0,2:T(8,128)(2,1)}, u32[]{:S(2)}, u32[]{:S(2)}) async-start(bf16[2,8,128,1024]{3,1,0,2:T(8,128)(2,1)} %copy.27), calls=%async_computation | async-start | bytes 8388608 | tf_op jit(solution)/shard_map/all_to_all | solution.py:318
  41.3 0.4 fusion.1
  41.8 0.4 fusion
  42.2 1.1 pad_maximum_fusion.refs_1_
  43.3 50.0 %all-to-all-done = bf16[2,8,128,1024]{3,1,0,2:T(8,128)(2,1)} async-done(((bf16[2,8,128,1024]{3,1,0,2:T(8,128)(2,1)}), bf16[2,8,128,1024]{3,1,0,2:T(8,128)(2,1)}, u32[]{:S(2)}, u32[]{:S(2)}) %all-to-all-start) | async-done | bytes 4194336 | tf_op jit(solution)/shard_map/all_to_all | solution.py:318
  93.3 10.3 %shard_map.119 = (f32[64,256]{1,0:T(8,128)}, f32[64,256]{1,0:T(8,128)}, f32[64,256]{1,0:T(8,128)}, f32[64,256]{1,0:T(8,128)}) custom-call(bf16[128,2,8,1024]{3,2,1,0:T(8,128)(2,1)} %bitcast.6.refs_0_, bf16[4,2,256,256]{3,2,1,0:T(8,128)(2,1)} %pad_maximum_fusion.refs_1_, f32[4,256,1]{2,1,0:T(8,128)} %constant.52.clone.refs_2_, ...), custom_call_target="tpu_custom_call" | custom-call | flops 2147483648 | bytes 5242880 | tf_op jit(solution)/shard_map/pallas_call | solution.py:302
  103.6 1.3 %collective-permute-start = (f32[64,256]{1,0:T(8,128)}, f32[64,256]{1,0:T(8,128)S(1)}, u32[]{:S(2)}, u32[]{:S(2)}) collective-permute-start(f32[64,256]{1,0:T(8,128)} %get-tuple-element.10), channel_id=1, source_target_pairs={{0,1},{1,0},{2,3},{3,2},{4,5},{5,4},{6,7},{7,6},{8,9},{9,8},{10,11... | collective-permute-start | bytes 196616 | tf_op jit(solution)/shard_map/ppermute | solution.py:331
  104.9 1.3 %collective-permute-start.1 = (f32[64,256]{1,0:T(8,128)}, f32[64,256]{1,0:T(8,128)S(1)}, u32[]{:S(2)}, u32[]{:S(2)}) collective-permute-start(f32[64,256]{1,0:T(8,128)} %get-tuple-element.11), channel_id=1, source_target_pairs={{0,2},{1,3},{2,0},{3,1},{4,6},{5,7},{6,4},{7,5},{8,10},{9,11},{10,... | collective-permute-start | bytes 196616 | tf_op jit(solution)/shard_map/ppermute | solution.py:331
  106.1 0.4 collective-permute-start.2
  106.6 0.0 collective-permute-done
  106.6 2.2 %collective-permute-done.1 = f32[64,256]{1,0:T(8,128)S(1)} collective-permute-done((f32[64,256]{1,0:T(8,128)}, f32[64,256]{1,0:T(8,128)S(1)}, u32[]{:S(2)}, u32[]{:S(2)}) %collective-permute-start.1) | collective-permute-done | bytes 65568 | tf_op jit(solution)/shard_map/ppermute | solution.py:331
  108.8 1.6 %collective-permute-done.2 = f32[64,256]{1,0:T(8,128)S(1)} collective-permute-done((f32[64,256]{1,0:T(8,128)}, f32[64,256]{1,0:T(8,128)S(1)}, u32[]{:S(2)}, u32[]{:S(2)}) %collective-permute-start.2) | collective-permute-done | bytes 65568 | tf_op jit(solution)/shard_map/ppermute | solution.py:331
  110.4 0.9 select_select_fusion.3
  111.3 0.7 pad_maximum_fusion.1
  (13 shorter events, 0.0 us)
Async XLA Ops:
  0.0 9.0 %copy-start.3 = (bf16[2,2,128,128]{3,2,1,0:T(8,128)(2,1)S(1)}, bf16[2,2,128,128]{3,2,1,0:T(8,128)(2,1)}, u32[]{:S(2)}) copy-start(bf16[2,2,128,128]{3,2,1,0:T(8,128)(2,1)} %constant.49.clone) | copy-start | bytes 393220
  0.0 8.5 %copy-start.5 = (s32[32]{0:T(128)S(1)}, s32[32]{0:T(128)}, u32[]{:S(2)}) copy-start(s32[32]{0:T(128)} %param.14) | copy-start | bytes 388
  0.0 8.6 %copy-start = (bf16[8,1,2,8192]{3,2,1,0:T(2,128)(2,1)S(1)}, bf16[8,1,2,8192]{3,2,1,0:T(2,128)(2,1)}, u32[]{:S(2)}) copy-start(bf16[8,1,2,8192]{3,2,1,0:T(2,128)(2,1)} %param.13) | copy-start | bytes 786436
  29.3 12.0 %copy-start.2 = (bf16[256,256,1]{1,0,2:T(8,128)(2,1)S(1)}, bf16[256,256,1]{1,0,2:T(8,128)(2,1)}, u32[]{:S(2)}) copy-start(bf16[256,256,1]{1,0,2:T(8,128)(2,1)} %constant.57) | copy-start | bytes 393220
  29.3 12.0 %copy-start.4 = (s32[4,256]{1,0:T(4,128)S(1)}, s32[4,256]{1,0:T(4,128)}, u32[]{:S(2)}) copy-start(s32[4,256]{1,0:T(4,128)} %param.15) | copy-start | bytes 12292
  29.4 12.4 %copy-start.1 = (bf16[256,256,1]{1,0,2:T(8,128)(2,1)S(1)}, bf16[256,256,1]{1,0,2:T(8,128)(2,1)}, u32[]{:S(2)}) copy-start(bf16[256,256,1]{1,0,2:T(8,128)(2,1)} %constant.56) | copy-start | bytes 393220
  29.4 63.9 %all-to-all-start = ((bf16[2,8,128,1024]{3,1,0,2:T(8,128)(2,1)}), bf16[2,8,128,1024]{3,1,0,2:T(8,128)(2,1)}, u32[]{:S(2)}, u32[]{:S(2)}) async-start(bf16[2,8,128,1024]{3,1,0,2:T(8,128)(2,1)} %copy.27), calls=%async_computation | async-start | bytes 8388608 | tf_op jit(solution)/shard_map/all_to_all | solution.py:318
  103.6 2.9 %collective-permute-start = (f32[64,256]{1,0:T(8,128)}, f32[64,256]{1,0:T(8,128)S(1)}, u32[]{:S(2)}, u32[]{:S(2)}) collective-permute-start(f32[64,256]{1,0:T(8,128)} %get-tuple-element.10), channel_id=1, source_target_pairs={{0,1},{1,0},{2,3},{3,2},{4,5},{5,4},{6,7},{7,6},{8,9},{9,8},{10,11... | collective-permute-start | bytes 196616 | tf_op jit(solution)/shard_map/ppermute | solution.py:331
  104.9 3.9 %collective-permute-start.1 = (f32[64,256]{1,0:T(8,128)}, f32[64,256]{1,0:T(8,128)S(1)}, u32[]{:S(2)}, u32[]{:S(2)}) collective-permute-start(f32[64,256]{1,0:T(8,128)} %get-tuple-element.11), channel_id=1, source_target_pairs={{0,2},{1,3},{2,0},{3,1},{4,6},{5,7},{6,4},{7,5},{8,10},{9,11},{10,... | collective-permute-start | bytes 196616 | tf_op jit(solution)/shard_map/ppermute | solution.py:331
  106.1 4.3 %collective-permute-start.2 = (f32[64,256]{1,0:T(8,128)}, f32[64,256]{1,0:T(8,128)S(1)}, u32[]{:S(2)}, u32[]{:S(2)}) collective-permute-start(f32[64,256]{1,0:T(8,128)} %get-tuple-element.12), channel_id=1, source_target_pairs={{0,3},{1,2},{2,1},{3,0},{4,7},{5,6},{6,5},{7,4},{8,11},{9,10},{10,... | collective-permute-start | bytes 196616 | tf_op jit(solution)/shard_map/ppermute | solution.py:331

commit v21 on v20

--- a/solution.py
+++ b/solution.py
@@ -248,7 +248,7 @@
     twist_cos, twist_sin = rotation_constant(dish_count, grid_len, total_dishes)
     twist_cos = jnp.asarray(twist_cos[:, :, None])
     twist_sin = jnp.asarray(twist_sin[:, :, None])
-    lane_block = 2 * quarter
+    lane_block = 8 * quarter
 
     volts = voltages[:, 0].reshape(dish_rows, 2, samples // CHB, CHB)
 

time: 113 us -> 111 us (0.982)
  Pallas kernels: 21.9 us -> 20.1 us
    pallas_call x1, Pallas kernels: 10.3 us -> 8.49 us  [beamform_chunk(): pl.pallas_call(functools.partial(beam_kernel, dish_count, carry_in, finis...]
where the time goes in v21:
time: 111 us; the launch traced here: 110 us
  waiting for transfers between devices  53.8 us (48%)
  Pallas kernels  20.1 us (18%)
  local copies, waits for them, and re-layouts  16.5 us (15%)
  starting transfers between devices  14.9 us (13%)
  other arithmetic  2.66 us (2%)
  matrix products  2.08 us (2%)
    all_to_all x1, waiting for transfers between devices, body(): lax.all_to_all(s, ('dish', 'freq'), 2, 2, tiled=True)  50 us
    all_to_all x1, starting transfers between devices, body(): lax.all_to_all(s, ('dish', 'freq'), 2, 2, tiled=True)  12 us
    pallas_call x1, Pallas kernels, channelize_chunk(): pl.pallas_call(functools.partial(channelize_kernel, first_pair, pairs), g...  11.6 us
    another operation x1, local copies, waits for them, and re-layouts, body(): volts = voltages[:, 0].reshape(dish_rows, 2, samples // CHB, CHB)  8.52 us
    pallas_call x1, Pallas kernels, beamform_chunk(): pl.pallas_call(functools.partial(beam_kernel, dish_count, carry_in, finis...  8.49 us
    pallas_call x1, local copies, waits for them, and re-layouts, channelize_chunk(): pl.pallas_call(functools.partial(channelize_kernel, first_pair, pairs), g...  6.53 us
    ppermute x3, waiting for transfers between devices, body(): pieces.append(lax.ppermute(outgoing, 'dish', pairs_list))  3.85 us
    ppermute x3, starting transfers between devices, body(): pieces.append(lax.ppermute(outgoing, 'dish', pairs_list))  2.92 us
  transfers between devices with their start and end apart: 4, of which 3 were waited for; matrix products, arithmetic and copies ran while one was open for 2% of the time, Pallas kernels for 0%

profile of v21, /device:TPU:1, one launch (start us, length us, event | category | flops | bytes accessed | tf_op | source)
XLA Modules:
  0.0 110.2 jit_solution(6329060088829464209)
XLA Ops:
  0.0 8.5 %reshape_squeeze.6.v_ref = bf16[8,2,1216,128]{3,2,1,0:T(8,128)(2,1)} reshape(bf16[8,1,2,155648]{3,2,1,0:T(2,128)(2,1)} %param.12) | data formatting | bytes 9961472 | tf_op jit(solution)/shard_map/reshape;squeeze | solution.py:253
  8.5 0.1 mul.16
  8.6 0.0 copy-done
  8.6 0.3 reshape.30
  9.0 0.0 copy-done.3
  9.0 0.9 convolution_convert_fusion.3
  9.9 0.3 convolution_convert_fusion.2
  10.2 1.0 copy.26
  11.2 11.6 %shard_map.118 = bf16[2,8,128,1024]{3,2,1,0:T(8,128)(2,1)} custom-call(bf16[8,2,1216,128]{3,2,1,0:T(8,128)(2,1)} %reshape_squeeze.6.v_ref, f32[4,64,128]{2,1,0:T(8,128)} %constant.46.clone.w_ref, bf16[128,128]{1,0:T(8,128)(2,1)} %constant.47.clone.t1_ref, f32[2,64,128]{2,1,0:T(8,128)} %constant.48.clone.tw_ref, bf16[2,256,128]{2,1,0:T(8,128)(2,1)} %bitcast.26, ...), custom_call_target="tpu_custom_call" | custom-call | flops 1610612736 | bytes 9175040 | tf_op jit(solution)/shard_map/pallas_call | solution.py:261
  22.8 6.5 %copy.27 = bf16[2,8,128,1024]{3,1,0,2:T(8,128)(2,1)} copy(bf16[2,8,128,1024]{3,2,1,0:T(8,128)(2,1)} %shard_map.118) | data formatting | bytes 8388608 | tf_op jit(solution)/shard_map/pallas_call | solution.py:261
  29.4 12.0 %all-to-all-start = ((bf16[2,8,128,1024]{3,1,0,2:T(8,128)(2,1)}), bf16[2,8,128,1024]{3,1,0,2:T(8,128)(2,1)}, u32[]{:S(2)}, u32[]{:S(2)}) async-start(bf16[2,8,128,1024]{3,1,0,2:T(8,128)(2,1)} %copy.27), calls=%async_computation | async-start | bytes 8388608 | tf_op jit(solution)/shard_map/all_to_all | solution.py:318
  41.3 0.4 fusion.1
  41.8 0.4 fusion
  42.2 1.1 pad_maximum_fusion.refs_1_
  43.3 50.0 %all-to-all-done = bf16[2,8,128,1024]{3,1,0,2:T(8,128)(2,1)} async-done(((bf16[2,8,128,1024]{3,1,0,2:T(8,128)(2,1)}), bf16[2,8,128,1024]{3,1,0,2:T(8,128)(2,1)}, u32[]{:S(2)}, u32[]{:S(2)}) %all-to-all-start) | async-done | bytes 4194336 | tf_op jit(solution)/shard_map/all_to_all | solution.py:318
  93.3 8.5 %shard_map.119 = (f32[64,256]{1,0:T(8,128)}, f32[64,256]{1,0:T(8,128)}, f32[64,256]{1,0:T(8,128)}, f32[64,256]{1,0:T(8,128)}) custom-call(bf16[128,2,8,1024]{3,2,1,0:T(8,128)(2,1)} %bitcast.6.refs_0_, bf16[4,2,256,256]{3,2,1,0:T(8,128)(2,1)} %pad_maximum_fusion.refs_1_, f32[4,256,1]{2,1,0:T(8,128)} %constant.52.clone.refs_2_, ...), custom_call_target="tpu_custom_call" | custom-call | flops 2147483648 | bytes 5242880 | tf_op jit(solution)/shard_map/pallas_call | solution.py:302
  101.8 1.2 %collective-permute-start = (f32[64,256]{1,0:T(8,128)}, f32[64,256]{1,0:T(8,128)S(1)}, u32[]{:S(2)}, u32[]{:S(2)}) collective-permute-start(f32[64,256]{1,0:T(8,128)} %get-tuple-element.10), channel_id=1, source_target_pairs={{0,1},{1,0},{2,3},{3,2},{4,5},{5,4},{6,7},{7,6},{8,9},{9,8},{10,11... | collective-permute-start | bytes 196616 | tf_op jit(solution)/shard_map/ppermute | solution.py:331
  103.0 1.3 %collective-permute-start.1 = (f32[64,256]{1,0:T(8,128)}, f32[64,256]{1,0:T(8,128)S(1)}, u32[]{:S(2)}, u32[]{:S(2)}) collective-permute-start(f32[64,256]{1,0:T(8,128)} %get-tuple-element.11), channel_id=1, source_target_pairs={{0,2},{1,3},{2,0},{3,1},{4,6},{5,7},{6,4},{7,5},{8,10},{9,11},{10,... | collective-permute-start | bytes 196616 | tf_op jit(solution)/shard_map/ppermute | solution.py:331
  104.3 0.4 collective-permute-start.2
  104.7 0.0 collective-permute-done
  104.7 2.2 %collective-permute-done.1 = f32[64,256]{1,0:T(8,128)S(1)} collective-permute-done((f32[64,256]{1,0:T(8,128)}, f32[64,256]{1,0:T(8,128)S(1)}, u32[]{:S(2)}, u32[]{:S(2)}) %collective-permute-start.1) | collective-permute-done | bytes 65568 | tf_op jit(solution)/shard_map/ppermute | solution.py:331
  106.9 1.6 %collective-permute-done.2 = f32[64,256]{1,0:T(8,128)S(1)} collective-permute-done((f32[64,256]{1,0:T(8,128)}, f32[64,256]{1,0:T(8,128)S(1)}, u32[]{:S(2)}, u32[]{:S(2)}) %collective-permute-start.2) | collective-permute-done | bytes 65568 | tf_op jit(solution)/shard_map/ppermute | solution.py:331
  108.6 0.9 select_select_fusion.3
  109.4 0.7 pad_maximum_fusion.1
  (13 shorter events, 0.0 us)
Async XLA Ops:
  0.0 9.0 %copy-start.3 = (bf16[2,2,128,128]{3,2,1,0:T(8,128)(2,1)S(1)}, bf16[2,2,128,128]{3,2,1,0:T(8,128)(2,1)}, u32[]{:S(2)}) copy-start(bf16[2,2,128,128]{3,2,1,0:T(8,128)(2,1)} %constant.49.clone) | copy-start | bytes 393220
  0.0 8.5 %copy-start.5 = (s32[32]{0:T(128)S(1)}, s32[32]{0:T(128)}, u32[]{:S(2)}) copy-start(s32[32]{0:T(128)} %param.14) | copy-start | bytes 388
  0.0 8.6 %copy-start = (bf16[8,1,2,8192]{3,2,1,0:T(2,128)(2,1)S(1)}, bf16[8,1,2,8192]{3,2,1,0:T(2,128)(2,1)}, u32[]{:S(2)}) copy-start(bf16[8,1,2,8192]{3,2,1,0:T(2,128)(2,1)} %param.13) | copy-start | bytes 786436
  29.3 12.0 %copy-start.2 = (bf16[256,256,1]{1,0,2:T(8,128)(2,1)S(1)}, bf16[256,256,1]{1,0,2:T(8,128)(2,1)}, u32[]{:S(2)}) copy-start(bf16[256,256,1]{1,0,2:T(8,128)(2,1)} %constant.57) | copy-start | bytes 393220
  29.3 12.0 %copy-start.4 = (s32[4,256]{1,0:T(4,128)S(1)}, s32[4,256]{1,0:T(4,128)}, u32[]{:S(2)}) copy-start(s32[4,256]{1,0:T(4,128)} %param.15) | copy-start | bytes 12292
  29.3 12.4 %copy-start.1 = (bf16[256,256,1]{1,0,2:T(8,128)(2,1)S(1)}, bf16[256,256,1]{1,0,2:T(8,128)(2,1)}, u32[]{:S(2)}) copy-start(bf16[256,256,1]{1,0,2:T(8,128)(2,1)} %constant.56) | copy-start | bytes 393220
  29.4 63.9 %all-to-all-start = ((bf16[2,8,128,1024]{3,1,0,2:T(8,128)(2,1)}), bf16[2,8,128,1024]{3,1,0,2:T(8,128)(2,1)}, u32[]{:S(2)}, u32[]{:S(2)}) async-start(bf16[2,8,128,1024]{3,1,0,2:T(8,128)(2,1)} %copy.27), calls=%async_computation | async-start | bytes 8388608 | tf_op jit(solution)/shard_map/all_to_all | solution.py:318
  101.8 2.9 %collective-permute-start = (f32[64,256]{1,0:T(8,128)}, f32[64,256]{1,0:T(8,128)S(1)}, u32[]{:S(2)}, u32[]{:S(2)}) collective-permute-start(f32[64,256]{1,0:T(8,128)} %get-tuple-element.10), channel_id=1, source_target_pairs={{0,1},{1,0},{2,3},{3,2},{4,5},{5,4},{6,7},{7,6},{8,9},{9,8},{10,11... | collective-permute-start | bytes 196616 | tf_op jit(solution)/shard_map/ppermute | solution.py:331
  103.0 3.9 %collective-permute-start.1 = (f32[64,256]{1,0:T(8,128)}, f32[64,256]{1,0:T(8,128)S(1)}, u32[]{:S(2)}, u32[]{:S(2)}) collective-permute-start(f32[64,256]{1,0:T(8,128)} %get-tuple-element.11), channel_id=1, source_target_pairs={{0,2},{1,3},{2,0},{3,1},{4,6},{5,7},{6,4},{7,5},{8,10},{9,11},{10,... | collective-permute-start | bytes 196616 | tf_op jit(solution)/shard_map/ppermute | solution.py:331
  104.3 4.3 %collective-permute-start.2 = (f32[64,256]{1,0:T(8,128)}, f32[64,256]{1,0:T(8,128)S(1)}, u32[]{:S(2)}, u32[]{:S(2)}) collective-permute-start(f32[64,256]{1,0:T(8,128)} %get-tuple-element.12), channel_id=1, source_target_pairs={{0,3},{1,2},{2,1},{3,0},{4,7},{5,6},{6,5},{7,4},{8,11},{9,10},{10,... | collective-permute-start | bytes 196616 | tf_op jit(solution)/shard_map/ppermute | solution.py:331

commit v22 on v19

--- a/solution.py
+++ b/solution.py
@@ -15,7 +15,7 @@
 CHB = 128
 TAPS = 4
 FRAMES = 16
-FEEDS_PER_STEP = 4
+FEEDS_PER_STEP = 2
 
 
 full_turn = 2.0 * math.pi

time: 110 us -> 110 us (level)
  no operation moved by 1% of the time
where the time goes in v22:
time: 110 us; the launch traced here: 109 us
  waiting for transfers between devices  53.9 us (49%)
  Pallas kernels  19 us (17%)
  local copies, waits for them, and re-layouts  16.5 us (15%)
  starting transfers between devices  14.9 us (14%)
  other arithmetic  2.66 us (2%)
  matrix products  2.08 us (2%)
    all_to_all x1, waiting for transfers between devices, body(): lax.all_to_all(s, ('dish', 'freq'), 2, 2, tiled=True)  50 us
    all_to_all x1, starting transfers between devices, body(): lax.all_to_all(s, ('dish', 'freq'), 2, 2, tiled=True)  12 us
    pallas_call x1, Pallas kernels, channelize_chunk(): pl.pallas_call(functools.partial(channelize_kernel, first_pair, pairs), g...  11.2 us
    another operation x1, local copies, waits for them, and re-layouts, body(): volts = voltages[:, 0].reshape(dish_rows, 2, samples // CHB, CHB)  8.52 us
    pallas_call x1, Pallas kernels, beamform_chunk(): pl.pallas_call(functools.partial(beam_kernel, dish_count, carry_in, finis...  7.73 us
    pallas_call x1, local copies, waits for them, and re-layouts, channelize_chunk(): pl.pallas_call(functools.partial(channelize_kernel, first_pair, pairs), g...  6.53 us
    ppermute x3, waiting for transfers between devices, body(): pieces.append(lax.ppermute(outgoing, 'dish', pairs_list))  3.85 us
    ppermute x3, starting transfers between devices, body(): pieces.append(lax.ppermute(outgoing, 'dish', pairs_list))  2.93 us
  transfers between devices with their start and end apart: 4, of which 3 were waited for; matrix products, arithmetic and copies ran while one was open for 2% of the time, Pallas kernels for 0%

profile of v22, /device:TPU:1, one launch (start us, length us, event | category | flops | bytes accessed | tf_op | source)
XLA Modules:
  0.0 109.1 jit_solution(15805468248037711763)
XLA Ops:
  0.0 8.5 %reshape_squeeze.6.v_ref = bf16[8,2,1216,128]{3,2,1,0:T(8,128)(2,1)} reshape(bf16[8,1,2,155648]{3,2,1,0:T(2,128)(2,1)} %param.12) | data formatting | bytes 9961472 | tf_op jit(solution)/shard_map/reshape;squeeze | solution.py:253
  8.5 0.0 copy-done.5
  8.5 0.1 mul.16
  8.6 0.0 copy-done
  8.6 0.3 reshape.30
  9.0 0.9 convolution_convert_fusion.3
  9.9 0.3 convolution_convert_fusion.2
  10.2 1.0 copy.26
  11.2 11.2 %shard_map.118 = bf16[2,8,128,1024]{3,2,1,0:T(8,128)(2,1)} custom-call(bf16[8,2,1216,128]{3,2,1,0:T(8,128)(2,1)} %reshape_squeeze.6.v_ref, f32[4,64,128]{2,1,0:T(8,128)} %constant.46.clone.w_ref, bf16[128,128]{1,0:T(8,128)(2,1)} %constant.47.clone.t1_ref, f32[2,64,128]{2,1,0:T(8,128)} %constant.48.clone.tw_ref, bf16[2,256,128]{2,1,0:T(8,128)(2,1)} %bitcast.26, ...), custom_call_target="tpu_custom_call" | custom-call | flops 1610612736 | bytes 9175040 | tf_op jit(solution)/shard_map/pallas_call | solution.py:261
  22.5 6.5 %copy.27 = bf16[2,8,128,1024]{3,1,0,2:T(8,128)(2,1)} copy(bf16[2,8,128,1024]{3,2,1,0:T(8,128)(2,1)} %shard_map.118) | data formatting | bytes 8388608 | tf_op jit(solution)/shard_map/pallas_call | solution.py:261
  29.0 12.0 %all-to-all-start = ((bf16[2,8,128,1024]{3,1,0,2:T(8,128)(2,1)}), bf16[2,8,128,1024]{3,1,0,2:T(8,128)(2,1)}, u32[]{:S(2)}, u32[]{:S(2)}) async-start(bf16[2,8,128,1024]{3,1,0,2:T(8,128)(2,1)} %copy.27), calls=%async_computation | async-start | bytes 8388608 | tf_op jit(solution)/shard_map/all_to_all | solution.py:318
  41.0 0.4 fusion.1
  41.5 0.4 fusion
  41.9 1.1 pad_maximum_fusion.refs_1_
  42.9 50.0 %all-to-all-done = bf16[2,8,128,1024]{3,1,0,2:T(8,128)(2,1)} async-done(((bf16[2,8,128,1024]{3,1,0,2:T(8,128)(2,1)}), bf16[2,8,128,1024]{3,1,0,2:T(8,128)(2,1)}, u32[]{:S(2)}, u32[]{:S(2)}) %all-to-all-start) | async-done | bytes 4194336 | tf_op jit(solution)/shard_map/all_to_all | solution.py:318
  93.0 7.7 %shard_map.119 = (f32[64,256]{1,0:T(8,128)}, f32[64,256]{1,0:T(8,128)}, f32[64,256]{1,0:T(8,128)}, f32[64,256]{1,0:T(8,128)}) custom-call(bf16[128,2,8,1024]{3,2,1,0:T(8,128)(2,1)} %bitcast.6.refs_0_, bf16[4,2,256,256]{3,2,1,0:T(8,128)(2,1)} %pad_maximum_fusion.refs_1_, f32[4,256,1]{2,1,0:T(8,128)} %constant.52.clone.refs_2_, ...), custom_call_target="tpu_custom_call" | custom-call | flops 2147483648 | bytes 5242880 | tf_op jit(solution)/shard_map/pallas_call | solution.py:302
  100.7 1.3 %collective-permute-start = (f32[64,256]{1,0:T(8,128)}, f32[64,256]{1,0:T(8,128)S(1)}, u32[]{:S(2)}, u32[]{:S(2)}) collective-permute-start(f32[64,256]{1,0:T(8,128)} %get-tuple-element.10), channel_id=1, source_target_pairs={{0,1},{1,0},{2,3},{3,2},{4,5},{5,4},{6,7},{7,6},{8,9},{9,8},{10,11... | collective-permute-start | bytes 196616 | tf_op jit(solution)/shard_map/ppermute | solution.py:331
  101.9 1.3 %collective-permute-start.1 = (f32[64,256]{1,0:T(8,128)}, f32[64,256]{1,0:T(8,128)S(1)}, u32[]{:S(2)}, u32[]{:S(2)}) collective-permute-start(f32[64,256]{1,0:T(8,128)} %get-tuple-element.11), channel_id=1, source_target_pairs={{0,2},{1,3},{2,0},{3,1},{4,6},{5,7},{6,4},{7,5},{8,10},{9,11},{10,... | collective-permute-start | bytes 196616 | tf_op jit(solution)/shard_map/ppermute | solution.py:331
  103.2 0.4 collective-permute-start.2
  103.6 0.0 collective-permute-done
  103.6 2.2 %collective-permute-done.1 = f32[64,256]{1,0:T(8,128)S(1)} collective-permute-done((f32[64,256]{1,0:T(8,128)}, f32[64,256]{1,0:T(8,128)S(1)}, u32[]{:S(2)}, u32[]{:S(2)}) %collective-permute-start.1) | collective-permute-done | bytes 65568 | tf_op jit(solution)/shard_map/ppermute | solution.py:331
  105.8 1.6 %collective-permute-done.2 = f32[64,256]{1,0:T(8,128)S(1)} collective-permute-done((f32[64,256]{1,0:T(8,128)}, f32[64,256]{1,0:T(8,128)S(1)}, u32[]{:S(2)}, u32[]{:S(2)}) %collective-permute-start.2) | collective-permute-done | bytes 65568 | tf_op jit(solution)/shard_map/ppermute | solution.py:331
  107.5 0.9 select_select_fusion.3
  108.4 0.7 pad_maximum_fusion.1
  (13 shorter events, 0.0 us)
Async XLA Ops:
  0.0 9.0 %copy-start.3 = (bf16[2,2,128,128]{3,2,1,0:T(8,128)(2,1)S(1)}, bf16[2,2,128,128]{3,2,1,0:T(8,128)(2,1)}, u32[]{:S(2)}) copy-start(bf16[2,2,128,128]{3,2,1,0:T(8,128)(2,1)} %constant.49.clone) | copy-start | bytes 393220
  0.0 8.5 %copy-start.5 = (s32[32]{0:T(128)S(1)}, s32[32]{0:T(128)}, u32[]{:S(2)}) copy-start(s32[32]{0:T(128)} %param.14) | copy-start | bytes 388
  0.0 8.6 %copy-start = (bf16[8,1,2,8192]{3,2,1,0:T(2,128)(2,1)S(1)}, bf16[8,1,2,8192]{3,2,1,0:T(2,128)(2,1)}, u32[]{:S(2)}) copy-start(bf16[8,1,2,8192]{3,2,1,0:T(2,128)(2,1)} %param.13) | copy-start | bytes 786436
  29.0 12.0 %copy-start.2 = (bf16[256,256,1]{1,0,2:T(8,128)(2,1)S(1)}, bf16[256,256,1]{1,0,2:T(8,128)(2,1)}, u32[]{:S(2)}) copy-start(bf16[256,256,1]{1,0,2:T(8,128)(2,1)} %constant.57) | copy-start | bytes 393220
  29.0 12.0 %copy-start.4 = (s32[4,256]{1,0:T(4,128)S(1)}, s32[4,256]{1,0:T(4,128)}, u32[]{:S(2)}) copy-start(s32[4,256]{1,0:T(4,128)} %param.15) | copy-start | bytes 12292
  29.0 12.4 %copy-start.1 = (bf16[256,256,1]{1,0,2:T(8,128)(2,1)S(1)}, bf16[256,256,1]{1,0,2:T(8,128)(2,1)}, u32[]{:S(2)}) copy-start(bf16[256,256,1]{1,0,2:T(8,128)(2,1)} %constant.56) | copy-start | bytes 393220
  29.0 63.9 %all-to-all-start = ((bf16[2,8,128,1024]{3,1,0,2:T(8,128)(2,1)}), bf16[2,8,128,1024]{3,1,0,2:T(8,128)(2,1)}, u32[]{:S(2)}, u32[]{:S(2)}) async-start(bf16[2,8,128,1024]{3,1,0,2:T(8,128)(2,1)} %copy.27), calls=%async_computation | async-start | bytes 8388608 | tf_op jit(solution)/shard_map/all_to_all | solution.py:318
  100.7 2.9 %collective-permute-start = (f32[64,256]{1,0:T(8,128)}, f32[64,256]{1,0:T(8,128)S(1)}, u32[]{:S(2)}, u32[]{:S(2)}) collective-permute-start(f32[64,256]{1,0:T(8,128)} %get-tuple-element.10), channel_id=1, source_target_pairs={{0,1},{1,0},{2,3},{3,2},{4,5},{5,4},{6,7},{7,6},{8,9},{9,8},{10,11... | collective-permute-start | bytes 196616 | tf_op jit(solution)/shard_map/ppermute | solution.py:331
  101.9 3.9 %collective-permute-start.1 = (f32[64,256]{1,0:T(8,128)}, f32[64,256]{1,0:T(8,128)S(1)}, u32[]{:S(2)}, u32[]{:S(2)}) collective-permute-start(f32[64,256]{1,0:T(8,128)} %get-tuple-element.11), channel_id=1, source_target_pairs={{0,2},{1,3},{2,0},{3,1},{4,6},{5,7},{6,4},{7,5},{8,10},{9,11},{10,... | collective-permute-start | bytes 196616 | tf_op jit(solution)/shard_map/ppermute | solution.py:331
  103.2 4.3 %collective-permute-start.2 = (f32[64,256]{1,0:T(8,128)}, f32[64,256]{1,0:T(8,128)S(1)}, u32[]{:S(2)}, u32[]{:S(2)}) collective-permute-start(f32[64,256]{1,0:T(8,128)} %get-tuple-element.12), channel_id=1, source_target_pairs={{0,3},{1,2},{2,1},{3,0},{4,7},{5,6},{6,5},{7,4},{8,11},{9,10},{10,... | collective-permute-start | bytes 196616 | tf_op jit(solution)/shard_map/ppermute | solution.py:331
